TPU v7x, 32 devices: a whole 2x2x4 slice. The times are simulated.
32 devices in a mesh: wave: 4 (over z), lev: 8 (over y, x, core).
Axes of the slice: x: 2, y: 2, z: 4, core: 2. Of those that a mesh axis runs over, the one named last changes fastest.
Arguments:
- spec: bfloat16 [1280, 2, 16, 1280], P('wave', None, 'lev'), may hold values from -0.119628906 to 0.119628906
- legendre: bfloat16 [1280, 16, 1280], P(('wave', 'lev')), may hold values from -0.15625 to 0.15625
- slot_wave: int32 [1280], replicated, may hold values from 0 to 1280, as said below
- row_lons: int32 [32], replicated, may hold values from 20 to 5136, as said below
- band_rows: int32 [32], replicated, may hold values from 0 to 31, as said below
Outputs:
- grid: float32 [32, 16, 5136], P('wave', 'lev')
Inputs may be any that keep to these rules, and one draw needn't show every extreme that they name: `slot_wave`: every zonal wavenumber 0 to 1279 stands in exactly one slot; any other slot holds 1280. `row_lons`: row 16 + j has as many points as row j; each count is 20 plus a multiple of 4; some row has 5136. `band_rows`: a permutation of the latitude rows.
All inputs are finite; a program needn't handle non-finite values.
Results may differ from a plain program's by a relative error of at most 0.0037.
Values may be sent and summed in bfloat16 or wider, within the bound.
No kernel may reach another device: no remote copies, remote signals or barrier semaphores. Data moves between devices by JAX's collectives and lax.ppermute only.
A program may use at most 64 MiB of HBM per device.

v0:
```python
import math

import jax
import jax.numpy as jnp
from jax import lax
from jax.sharding import PartitionSpec as P


def angles(remainder, points):
    return 2.0 * math.pi * remainder.astype(jnp.float32) / points.astype(jnp.float32)


def row_synthesis(coef_row, points):
    fields = coef_row.shape[1]
    waves = coef_row.shape[2]
    ablocks = waves // 64
    lon_len = 20 + 4 * (waves - 1)
    lon_idx = jnp.arange(lon_len, dtype=jnp.int32)
    inner = jnp.arange(64, dtype=jnp.int32)
    remainder = inner[:, None] * lon_idx[None, :] % points
    theta = angles(remainder, points)
    cosb = jnp.cos(theta).astype(jnp.bfloat16)
    sinb = jnp.sin(theta).astype(jnp.bfloat16)
    table = jnp.stack([jnp.stack([cosb, sinb], 1), jnp.stack([-sinb, cosb], 1)], 0)
    blocks = coef_row.reshape(2, fields, ablocks, 64)
    part = jnp.einsum("cfab,cbdi->dfai", blocks, table, preferred_element_type=jnp.float32)
    outer = jnp.arange(ablocks, dtype=jnp.int32) * 64
    phase = angles(outer[:, None] * lon_idx[None, :] % points, points)
    total = jnp.sum(part[0] * jnp.cos(phase)[None] - part[1] * jnp.sin(phase)[None], axis=1)
    return jnp.where(lon_idx[None, :] < points, total, jnp.zeros_like(total))


def on_device(spec, legendre, slot_wave, row_lons, band_rows):
    n_wave = lax.axis_size("wave")
    n_lev = lax.axis_size("lev")
    per_dev = legendre.shape[0]
    nlath = legendre.shape[1]
    waves = spec.shape[-1]
    trunc_top = waves - 1
    gathered = lax.all_to_all(spec, "lev", split_axis=0, concat_axis=2, tiled=True)
    fields = gathered.shape[2]
    first_slot = (lax.axis_index("wave") * n_lev + lax.axis_index("lev")) * per_dev
    my_waves = lax.dynamic_slice_in_dim(slot_wave, first_slot, per_dev)
    degree = jnp.arange(waves, dtype=jnp.int32)
    live_k = degree[None, :] <= trunc_top - my_waves[:, None]
    even_mask = (live_k & (degree[None, :] % 2 == 0))[:, None, None, :]
    odd_mask = (live_k & (degree[None, :] % 2 == 1))[:, None, None, :]
    zeros = jnp.zeros_like(gathered)
    stacked = jnp.stack(
        [jnp.where(even_mask, gathered, zeros), jnp.where(odd_mask, gathered, zeros)], 1
    )
    flat = stacked.reshape(per_dev, 4 * fields, waves)
    width_k = 256
    longest = jnp.max(jnp.maximum(trunc_top + 1 - my_waves, 0))
    count = (longest + width_k - 1) // width_k

    def accumulate(index, total):
        start = index * width_k
        piece = lax.dynamic_slice_in_dim(flat, start, width_k, 2)
        tab_piece = lax.dynamic_slice_in_dim(legendre, start, width_k, 2)
        return total + jnp.einsum(
            "sxk,sjk->sxj", piece, tab_piece, preferred_element_type=jnp.float32
        )

    start_total = jnp.zeros((per_dev, 4 * fields, nlath), jnp.float32)
    sums = lax.fori_loop(0, count, accumulate, start_total)
    sums = sums.reshape(per_dev, 2, 2, fields, nlath)
    north = band_rows < nlath
    lat_idx = jnp.where(north, band_rows, band_rows - nlath)
    parity_sign = jnp.where(north, 1.0, -1.0).astype(jnp.float32)
    fourier = (sums[:, 0][..., lat_idx] + parity_sign * sums[:, 1][..., lat_idx]).astype(
        jnp.bfloat16
    )
    fourier = jnp.transpose(fourier, (1, 2, 3, 0))
    banded = lax.all_to_all(
        lax.all_to_all(fourier, "wave", split_axis=2, concat_axis=3, tiled=True),
        "lev",
        split_axis=1,
        concat_axis=3,
        tiled=True,
    )
    slot_order = jnp.transpose(slot_wave.reshape(n_wave, n_lev, per_dev), (1, 0, 2)).reshape(-1)
    wave_idx = jnp.arange(waves, dtype=jnp.int32)
    onehot = (slot_order[:, None] == wave_idx[None, :]).astype(jnp.bfloat16)
    coef = jnp.einsum("cfrs,sm->cfrm", banded, onehot, preferred_element_type=jnp.float32)
    row_dev = banded.shape[2]
    my_rows = lax.dynamic_slice_in_dim(band_rows, lax.axis_index("wave") * row_dev, row_dev)
    row_points = row_lons[my_rows]
    keep = 2 * wave_idx[None, :] < row_points[:, None]
    factor = jnp.where(keep, jnp.where(wave_idx[None, :] == 0, 1.0, 2.0), 0.0).astype(jnp.float32)
    coef = (coef * factor[None, None]).astype(jnp.bfloat16)
    coef_rows = jnp.moveaxis(coef, 2, 0)
    return lax.map(lambda item: row_synthesis(item[0], item[1]), (coef_rows, row_points))


def solution(mesh):
    return jax.shard_map(
        on_device,
        mesh=mesh,
        in_specs=(P("wave", None, "lev", None), P(("wave", "lev"), None, None), P(), P(), P()),
        out_specs=P("wave", "lev", None),
        check_vma=False,
    )
```

profile of v0, /device:TPU:0, one launch (start us, length us, event | category | flops | bytes accessed | tf_op | source)
XLA Modules:
  0.0 472.2 jit_solution(5588244557851422227)
XLA Ops:
  7.0 37.6 %all-to-all-done = bf16[320,2,2,1280]{3,2,1,0:T(2,128)(2,1)S(1)} async-done(((bf16[320,2,2,1280]{3,2,1,0:T(2,128)(2,1)}), bf16[320,2,2,1280]{3,2,1,0:T(2,128)(2,1)S(1)}, u32[]{:S(2)}, u32[]{:S(2)}) %all-to-all-start) | async-done | bytes 3276832 | tf_op jit(solution)/shard_map/all_to_all | solution.py:40
  60.4 9.3 %while.20 = (s32[]{:T(128)}, f32[40,64,16]{1,2,0:T(8,128)S(1)}, s32[]{:T(128)}, bf16[40,64,1280]{2,1,0:T(8,128)(2,1)}, bf16[40,16,1280]{2,1,0:T(8,128)(2,1)}, /*index=5*/s32[]{:T(128)}, s32[]{:T(128)}, s32[]{:T(128)}, s32[]{:T(128)}) while((s32[]{:T(128)}, f32[40,64,16]{1,2,0:T(8,128)S(1)}, s32[]{:T(128)}, bf16[40,64,1280]{2,1,0:T(8,128)(2,1)}, ...), condition=%wide.region_2.3_spmd, body=%wide.region_1.2_spmd.sunk | while | flops 21012484 | bytes 1967243 | solution.py:66
  95.2 376.2 %while.21 = (s32[]{:T(128)}, f32[8,2,5136]{2,1,0:T(2,128)S(1)}, s32[8]{0:T(128)S(1)}, bf16[8,2,2,1280]{3,2,1,0:T(2,128)(2,1)S(1)}, s32[]{:T(128)}, /*index=5*/s32[]{:T(128)}) while((s32[]{:T(128)}, f32[8,2,5136]{2,1,0:T(2,128)S(1)}, s32[8]{0:T(128)S(1)}, bf16[8,2,2,1280]{3,2,1,0:T(2,128)(2,1)S(1)}, s32[]{:T(128)}, /*index=5*/s32[]{:T(128)}) %tuple.52), condition=%wide.region_5.6_spmd, body=%wide.region_3.5_spmd.sunk | while | flops 122919920 | bytes 14322127 | solution.py:93
  98.0 18.2 %sine_convert_fusion.2 = (bf16[64,1,5136]{2,0,1:T(8,128)(2,1)S(1)}, bf16[64,1,5136]{2,0,1:T(8,128)(2,1)S(1)}) fusion(f32[]{:T(128)S(6)} %convert_element_type.119, pred[]{:T(512)S(6)} %lt.166, s32[]{:T(128)S(6)} %select_n.198), kind=kLoop, calls=%fused_computation.18.clone.2 | loop fusion | flops 4273152 | bytes 1314825 | tf_op jit(solution)/shard_map/while/body/eval_jaxpr/convert_element_type | solution.py:23
  116.2 17.6 %fusion.71 = bf16[64,1,5136]{2,0,1:T(8,128)(2,1)S(1)} fusion(f32[]{:T(128)S(6)} %convert_element_type.119, pred[]{:T(512)S(6)} %lt.166, s32[]{:T(128)S(6)} %select_n.198), kind=kLoop, calls=%fused_computation.40.clone.1 | loop fusion | flops 4930560 | bytes 657417 | tf_op jit(solution)/shard_map/while/body/eval_jaxpr/neg | solution.py:24
  134.7 6.7 %fusion.72 = (f32[20,5136]{1,0:T(8,128)S(1)}, f32[20,5136]{1,0:T(8,128)S(1)}) fusion(f32[]{:T(128)S(6)} %convert_element_type.119, pred[]{:T(512)S(6)} %lt.166, s32[]{:T(128)S(6)} %select_n.198, s32[20]{0:T(128)S(1)} %iota_multiply_fusion.3), kind=kLoop, calls=%fused_computation.42.clone.1 | loop fusion | flops 1129920 | bytes 821849 | tf_op jit(solution)/shard_map/while/body/eval_jaxpr/cos | solution.py:29
  145.0 18.2 %sine_convert_fusion.2 = (bf16[64,1,5136]{2,0,1:T(8,128)(2,1)S(1)}, bf16[64,1,5136]{2,0,1:T(8,128)(2,1)S(1)}) fusion(f32[]{:T(128)S(6)} %convert_element_type.119, pred[]{:T(512)S(6)} %lt.166, s32[]{:T(128)S(6)} %select_n.198), kind=kLoop, calls=%fused_computation.18.clone.2 | loop fusion | flops 4273152 | bytes 1314825 | tf_op jit(solution)/shard_map/while/body/eval_jaxpr/convert_element_type | solution.py:23
  163.2 17.6 %fusion.71 = bf16[64,1,5136]{2,0,1:T(8,128)(2,1)S(1)} fusion(f32[]{:T(128)S(6)} %convert_element_type.119, pred[]{:T(512)S(6)} %lt.166, s32[]{:T(128)S(6)} %select_n.198), kind=kLoop, calls=%fused_computation.40.clone.1 | loop fusion | flops 4930560 | bytes 657417 | tf_op jit(solution)/shard_map/while/body/eval_jaxpr/neg | solution.py:24
  181.7 6.7 %fusion.72 = (f32[20,5136]{1,0:T(8,128)S(1)}, f32[20,5136]{1,0:T(8,128)S(1)}) fusion(f32[]{:T(128)S(6)} %convert_element_type.119, pred[]{:T(512)S(6)} %lt.166, s32[]{:T(128)S(6)} %select_n.198, s32[20]{0:T(128)S(1)} %iota_multiply_fusion.3), kind=kLoop, calls=%fused_computation.42.clone.1 | loop fusion | flops 1129920 | bytes 821849 | tf_op jit(solution)/shard_map/while/body/eval_jaxpr/cos | solution.py:29
  192.0 18.2 %sine_convert_fusion.2 = (bf16[64,1,5136]{2,0,1:T(8,128)(2,1)S(1)}, bf16[64,1,5136]{2,0,1:T(8,128)(2,1)S(1)}) fusion(f32[]{:T(128)S(6)} %convert_element_type.119, pred[]{:T(512)S(6)} %lt.166, s32[]{:T(128)S(6)} %select_n.198), kind=kLoop, calls=%fused_computation.18.clone.2 | loop fusion | flops 4273152 | bytes 1314825 | tf_op jit(solution)/shard_map/while/body/eval_jaxpr/convert_element_type | solution.py:23
  210.2 17.6 %fusion.71 = bf16[64,1,5136]{2,0,1:T(8,128)(2,1)S(1)} fusion(f32[]{:T(128)S(6)} %convert_element_type.119, pred[]{:T(512)S(6)} %lt.166, s32[]{:T(128)S(6)} %select_n.198), kind=kLoop, calls=%fused_computation.40.clone.1 | loop fusion | flops 4930560 | bytes 657417 | tf_op jit(solution)/shard_map/while/body/eval_jaxpr/neg | solution.py:24
  228.7 6.7 %fusion.72 = (f32[20,5136]{1,0:T(8,128)S(1)}, f32[20,5136]{1,0:T(8,128)S(1)}) fusion(f32[]{:T(128)S(6)} %convert_element_type.119, pred[]{:T(512)S(6)} %lt.166, s32[]{:T(128)S(6)} %select_n.198, s32[20]{0:T(128)S(1)} %iota_multiply_fusion.3), kind=kLoop, calls=%fused_computation.42.clone.1 | loop fusion | flops 1129920 | bytes 821849 | tf_op jit(solution)/shard_map/while/body/eval_jaxpr/cos | solution.py:29
  239.0 18.2 %sine_convert_fusion.2 = (bf16[64,1,5136]{2,0,1:T(8,128)(2,1)S(1)}, bf16[64,1,5136]{2,0,1:T(8,128)(2,1)S(1)}) fusion(f32[]{:T(128)S(6)} %convert_element_type.119, pred[]{:T(512)S(6)} %lt.166, s32[]{:T(128)S(6)} %select_n.198), kind=kLoop, calls=%fused_computation.18.clone.2 | loop fusion | flops 4273152 | bytes 1314825 | tf_op jit(solution)/shard_map/while/body/eval_jaxpr/convert_element_type | solution.py:23
  257.2 17.6 %fusion.71 = bf16[64,1,5136]{2,0,1:T(8,128)(2,1)S(1)} fusion(f32[]{:T(128)S(6)} %convert_element_type.119, pred[]{:T(512)S(6)} %lt.166, s32[]{:T(128)S(6)} %select_n.198), kind=kLoop, calls=%fused_computation.40.clone.1 | loop fusion | flops 4930560 | bytes 657417 | tf_op jit(solution)/shard_map/while/body/eval_jaxpr/neg | solution.py:24
  286.0 18.2 %sine_convert_fusion.2 = (bf16[64,1,5136]{2,0,1:T(8,128)(2,1)S(1)}, bf16[64,1,5136]{2,0,1:T(8,128)(2,1)S(1)}) fusion(f32[]{:T(128)S(6)} %convert_element_type.119, pred[]{:T(512)S(6)} %lt.166, s32[]{:T(128)S(6)} %select_n.198), kind=kLoop, calls=%fused_computation.18.clone.2 | loop fusion | flops 4273152 | bytes 1314825 | tf_op jit(solution)/shard_map/while/body/eval_jaxpr/convert_element_type | solution.py:23
  304.2 17.6 %fusion.71 = bf16[64,1,5136]{2,0,1:T(8,128)(2,1)S(1)} fusion(f32[]{:T(128)S(6)} %convert_element_type.119, pred[]{:T(512)S(6)} %lt.166, s32[]{:T(128)S(6)} %select_n.198), kind=kLoop, calls=%fused_computation.40.clone.1 | loop fusion | flops 4930560 | bytes 657417 | tf_op jit(solution)/shard_map/while/body/eval_jaxpr/neg | solution.py:24
  322.7 6.7 %fusion.72 = (f32[20,5136]{1,0:T(8,128)S(1)}, f32[20,5136]{1,0:T(8,128)S(1)}) fusion(f32[]{:T(128)S(6)} %convert_element_type.119, pred[]{:T(512)S(6)} %lt.166, s32[]{:T(128)S(6)} %select_n.198, s32[20]{0:T(128)S(1)} %iota_multiply_fusion.3), kind=kLoop, calls=%fused_computation.42.clone.1 | loop fusion | flops 1129920 | bytes 821849 | tf_op jit(solution)/shard_map/while/body/eval_jaxpr/cos | solution.py:29
  333.0 18.2 %sine_convert_fusion.2 = (bf16[64,1,5136]{2,0,1:T(8,128)(2,1)S(1)}, bf16[64,1,5136]{2,0,1:T(8,128)(2,1)S(1)}) fusion(f32[]{:T(128)S(6)} %convert_element_type.119, pred[]{:T(512)S(6)} %lt.166, s32[]{:T(128)S(6)} %select_n.198), kind=kLoop, calls=%fused_computation.18.clone.2 | loop fusion | flops 4273152 | bytes 1314825 | tf_op jit(solution)/shard_map/while/body/eval_jaxpr/convert_element_type | solution.py:23
  351.2 17.6 %fusion.71 = bf16[64,1,5136]{2,0,1:T(8,128)(2,1)S(1)} fusion(f32[]{:T(128)S(6)} %convert_element_type.119, pred[]{:T(512)S(6)} %lt.166, s32[]{:T(128)S(6)} %select_n.198), kind=kLoop, calls=%fused_computation.40.clone.1 | loop fusion | flops 4930560 | bytes 657417 | tf_op jit(solution)/shard_map/while/body/eval_jaxpr/neg | solution.py:24
  369.7 6.7 %fusion.72 = (f32[20,5136]{1,0:T(8,128)S(1)}, f32[20,5136]{1,0:T(8,128)S(1)}) fusion(f32[]{:T(128)S(6)} %convert_element_type.119, pred[]{:T(512)S(6)} %lt.166, s32[]{:T(128)S(6)} %select_n.198, s32[20]{0:T(128)S(1)} %iota_multiply_fusion.3), kind=kLoop, calls=%fused_computation.42.clone.1 | loop fusion | flops 1129920 | bytes 821849 | tf_op jit(solution)/shard_map/while/body/eval_jaxpr/cos | solution.py:29
  380.0 18.2 %sine_convert_fusion.2 = (bf16[64,1,5136]{2,0,1:T(8,128)(2,1)S(1)}, bf16[64,1,5136]{2,0,1:T(8,128)(2,1)S(1)}) fusion(f32[]{:T(128)S(6)} %convert_element_type.119, pred[]{:T(512)S(6)} %lt.166, s32[]{:T(128)S(6)} %select_n.198), kind=kLoop, calls=%fused_computation.18.clone.2 | loop fusion | flops 4273152 | bytes 1314825 | tf_op jit(solution)/shard_map/while/body/eval_jaxpr/convert_element_type | solution.py:23
  398.2 17.6 %fusion.71 = bf16[64,1,5136]{2,0,1:T(8,128)(2,1)S(1)} fusion(f32[]{:T(128)S(6)} %convert_element_type.119, pred[]{:T(512)S(6)} %lt.166, s32[]{:T(128)S(6)} %select_n.198), kind=kLoop, calls=%fused_computation.40.clone.1 | loop fusion | flops 4930560 | bytes 657417 | tf_op jit(solution)/shard_map/while/body/eval_jaxpr/neg | solution.py:24
  427.0 18.2 %sine_convert_fusion.2 = (bf16[64,1,5136]{2,0,1:T(8,128)(2,1)S(1)}, bf16[64,1,5136]{2,0,1:T(8,128)(2,1)S(1)}) fusion(f32[]{:T(128)S(6)} %convert_element_type.119, pred[]{:T(512)S(6)} %lt.166, s32[]{:T(128)S(6)} %select_n.198), kind=kLoop, calls=%fused_computation.18.clone.2 | loop fusion | flops 4273152 | bytes 1314825 | tf_op jit(solution)/shard_map/while/body/eval_jaxpr/convert_element_type | solution.py:23
  445.2 17.6 %fusion.71 = bf16[64,1,5136]{2,0,1:T(8,128)(2,1)S(1)} fusion(f32[]{:T(128)S(6)} %convert_element_type.119, pred[]{:T(512)S(6)} %lt.166, s32[]{:T(128)S(6)} %select_n.198), kind=kLoop, calls=%fused_computation.40.clone.1 | loop fusion | flops 4930560 | bytes 657417 | tf_op jit(solution)/shard_map/while/body/eval_jaxpr/neg | solution.py:24
  (130 shorter events, 97.8 us)
Async XLA Ops:
  0.0 77.4 %copy-start = (s32[32]{0:T(128)S(1)}, s32[32]{0:T(128)}, u32[]{:S(2)}) copy-start(s32[32]{0:T(128)} %param.12) | copy-start | bytes 388
  0.0 5.3 %copy-start.1 = (s32[1280]{0:T(1024)S(1)}, s32[1280]{0:T(1024)}, u32[]{:S(2)}) copy-start(s32[1280]{0:T(1024)} %param.11) | copy-start | bytes 15364
  0.0 6.7 %copy-start.3 = (s32[32]{0:T(128)S(1)}, s32[32]{0:T(128)}, u32[]{:S(2)}) copy-start(s32[32]{0:T(128)} %param.13) | copy-start | bytes 388
  0.0 44.6 %all-to-all-start = ((bf16[320,2,2,1280]{3,2,1,0:T(2,128)(2,1)}), bf16[320,2,2,1280]{3,2,1,0:T(2,128)(2,1)S(1)}, u32[]{:S(2)}, u32[]{:S(2)}) async-start(bf16[320,2,2,1280]{3,2,1,0:T(2,128)(2,1)} %param.9), calls=%async_computation | async-start | bytes 6553600 | tf_op jit(solution)/shard_map/all_to_all | solution.py:40
  72.6 10.7 %all-to-all-start.1 = ((bf16[4,2,5120]{2,1,0:T(2,128)(2,1)}), bf16[4,2,5120]{2,1,0:T(2,128)(2,1)S(1)}, u32[]{:S(2)}, u32[]{:S(2)}) async-start(bf16[4,2,5120]{2,1,0:T(2,128)(2,1)} %reshape.354), calls=%async_computation.1 | async-start | bytes 163840 | tf_op jit(solution)/shard_map/all_to_all | solution.py:76
  84.7 8.8 %all-to-all-start.2 = ((bf16[2,16,8,160]{3,2,0,1:T(8,128)(2,1)}), bf16[2,16,8,160]{3,2,0,1:T(8,128)(2,1)S(1)}, u32[]{:S(2)}, u32[]{:S(2)}) async-start(bf16[2,16,8,160]{3,2,0,1:T(8,128)(2,1)} %copy.33), calls=%async_computation.2 | async-start | bytes 262144 | tf_op jit(solution)/shard_map/all_to_all | solution.py:75
  471.4 0.7 copy-start.2
where the time goes:
time: 473 us; the launch traced here: 472 us
  other arithmetic  355 us (75%)
  waiting for transfers between devices  47.9 us (10%)
  local copies, waits for them, and re-layouts  23.4 us (5%)
  loops' own time  16.4 us (3%)
  matrix products  14.9 us (3%)
  starting transfers between devices  13.6 us (3%)
    convert_element_type x8, other arithmetic, row_synthesis(): sinb = jnp.sin(theta).astype(jnp.bfloat16)  146 us
    neg x8, other arithmetic, row_synthesis(): -sinb  140 us
    cos x8, other arithmetic, row_synthesis(): jnp.cos(phase)[None]  53.7 us
    all_to_all x1, waiting for transfers between devices, on_device(): lax.all_to_all(spec, 'lev', split_axis=0, concat_axis=2, tiled=True)  37.6 us
    another operation x1, loops' own time, on_device(): lax.map(lambda item: row_synthesis(item[0], item[1]), (coef_rows, row_poi...  16.3 us
    all_to_all x2, local copies, waits for them, and re-layouts, on_device(): lax.all_to_all(spec, 'lev', split_axis=0, concat_axis=2, tiled=True)  11.8 us
  transfers between devices with their start and end apart: 3, of which 3 were waited for; matrix products, arithmetic and copies ran while one was open for 0% of the time, Pallas kernels for 0%

commit v1 on v0

v1 whole, which is shorter than its diff:
```python
import math

import jax
import jax.numpy as jnp
import numpy as np
from jax import lax
from jax.sharding import Mesh
from jax.sharding import PartitionSpec as P


def angles(remainder, points):
    return 2.0 * math.pi * remainder.astype(jnp.float32) / points.astype(jnp.float32)


def row_synthesis(coef_row, points):
    fields = coef_row.shape[1]
    waves = coef_row.shape[2]
    ablocks = waves // 64
    lon_len = 20 + 4 * (waves - 1)
    lon_idx = jnp.arange(lon_len, dtype=jnp.int32)
    inner = jnp.arange(64, dtype=jnp.int32)
    remainder = inner[:, None] * lon_idx[None, :] % points
    theta = angles(remainder, points)
    cosb = jnp.cos(theta).astype(jnp.bfloat16)
    sinb = jnp.sin(theta).astype(jnp.bfloat16)
    table = jnp.stack([jnp.stack([cosb, sinb], 1), jnp.stack([-sinb, cosb], 1)], 0)
    blocks = coef_row.reshape(2, fields, ablocks, 64)
    part = jnp.einsum("cfab,cbdi->dfai", blocks, table, preferred_element_type=jnp.float32)
    outer = jnp.arange(ablocks, dtype=jnp.int32) * 64
    phase = angles(outer[:, None] * lon_idx[None, :] % points, points)
    total = jnp.sum(part[0] * jnp.cos(phase)[None] - part[1] * jnp.sin(phase)[None], axis=1)
    return jnp.where(lon_idx[None, :] < points, total, jnp.zeros_like(total))


def on_device(spec, legendre, slot_wave, row_lons, band_rows, rows_per_dev):
    n_wave = lax.axis_size("wave")
    n_g = lax.axis_size("lev_g")
    n_r = lax.axis_size("lev_r")
    n_lev = n_g * n_r
    per_dev = legendre.shape[0]
    nlath = legendre.shape[1]
    waves = spec.shape[-1]
    trunc_top = waves - 1
    lev_idx = lax.axis_index("lev_g") * n_r + lax.axis_index("lev_r")
    gathered = lax.all_to_all(spec, ("lev_g", "lev_r"), split_axis=0, concat_axis=2, tiled=True)
    fields = gathered.shape[2]
    first_slot = (lax.axis_index("wave") * n_lev + lev_idx) * per_dev
    my_waves = lax.dynamic_slice_in_dim(slot_wave, first_slot, per_dev)
    degree = jnp.arange(waves, dtype=jnp.int32)
    live_k = degree[None, :] <= trunc_top - my_waves[:, None]
    even_mask = (live_k & (degree[None, :] % 2 == 0))[:, None, :]
    odd_mask = (live_k & (degree[None, :] % 2 == 1))[:, None, :]
    zeros = jnp.zeros_like(legendre)
    leg2 = jnp.concatenate(
        [jnp.where(even_mask, legendre, zeros), jnp.where(odd_mask, legendre, zeros)], 1
    )
    flat = gathered.reshape(per_dev, 2 * fields, waves)
    sums = jnp.einsum("sxk,sjk->sxj", flat, leg2, preferred_element_type=jnp.float32)
    sums = sums.reshape(per_dev, 2, fields, 2, nlath)
    north = band_rows < nlath
    lat_idx = jnp.where(north, band_rows, band_rows - nlath)
    parity_sign = jnp.where(north, 1.0, -1.0).astype(jnp.float32)
    fourier = (sums[:, :, :, 0][..., lat_idx] + parity_sign * sums[:, :, :, 1][..., lat_idx]).astype(
        jnp.bfloat16
    )
    rows = band_rows.shape[0]
    fpg = fields // n_g
    fourier = fourier.reshape(per_dev, 2, n_g, fpg, n_wave, n_r, rows_per_dev)
    fourier = jnp.transpose(fourier, (4, 2, 5, 1, 3, 6, 0))
    fourier = fourier.reshape(n_wave * n_g * n_r, 2, fpg, rows_per_dev, per_dev)
    banded = lax.all_to_all(
        fourier, ("wave", "lev_g", "lev_r"), split_axis=0, concat_axis=0, tiled=True
    )
    banded = jnp.transpose(banded, (1, 2, 3, 0, 4)).reshape(2, fpg, rows_per_dev, -1)
    wave_idx = jnp.arange(waves, dtype=jnp.int32)
    onehot = (slot_wave[:, None] == wave_idx[None, :]).astype(jnp.bfloat16)
    coef = jnp.einsum("cfrs,sm->cfrm", banded, onehot, preferred_element_type=jnp.float32)
    first_row = (lax.axis_index("wave") * n_r + lax.axis_index("lev_r")) * rows_per_dev
    my_rows = lax.dynamic_slice_in_dim(band_rows, first_row, rows_per_dev)
    row_points = row_lons[my_rows]
    keep = 2 * wave_idx[None, :] < row_points[:, None]
    factor = jnp.where(keep, jnp.where(wave_idx[None, :] == 0, 1.0, 2.0), 0.0).astype(jnp.float32)
    coef = (coef * factor[None, None]).astype(jnp.bfloat16)
    coef_rows = jnp.moveaxis(coef, 2, 0)
    if rows_per_dev == 1:
        grid = row_synthesis(coef_rows[0], row_points[0])[None]
    else:
        grid = lax.map(lambda item: row_synthesis(item[0], item[1]), (coef_rows, row_points))
    lon = grid.shape[-1]
    fpd = fpg // n_r
    grid = grid.reshape(rows_per_dev, n_r, fpd, lon)
    grid = lax.all_to_all(grid, "lev_r", split_axis=1, concat_axis=0, tiled=True)
    return grid.reshape(n_r * rows_per_dev, fpd, lon)


def solution(mesh):
    def run(spec, legendre, slot_wave, row_lons, band_rows):
        n_wave = mesh.shape["wave"]
        n_lev = mesh.shape["lev"]
        rows_w = band_rows.shape[0] // n_wave
        if n_lev >= rows_w:
            n_r = rows_w
            rows_per_dev = 1
        else:
            n_r = n_lev
            rows_per_dev = rows_w // n_lev
        n_g = n_lev // n_r
        devs = np.asarray(mesh.devices).reshape(n_wave, n_g, n_r)
        mesh2 = Mesh(devs, ("wave", "lev_g", "lev_r"))
        lev = ("lev_g", "lev_r")
        fn = jax.shard_map(
            lambda *a: on_device(*a, rows_per_dev=rows_per_dev),
            mesh=mesh2,
            in_specs=(P("wave", None, lev, None), P(("wave",) + lev, None, None), P(), P(), P()),
            out_specs=P("wave", lev, None),
            check_vma=False,
        )
        return fn(spec, legendre, slot_wave, row_lons, band_rows)

    return run
```

time: 473 us -> 113 us (0.24)
  other arithmetic: 355 us -> 53.2 us
  waiting for transfers between devices: 47.9 us -> 6.36 us
  loops' own time: 16.4 us -> 0 us
  blocking collectives: 0 us -> 10.1 us
  matrix products: 14.9 us -> 7.47 us
    convert_element_type x8 -> x1, other arithmetic: 146 us -> 18.2 us  [row_synthesis(): sinb = jnp.sin(theta).astype(jnp.bfloat16)]
    neg x8 -> x1, other arithmetic: 140 us -> 18.2 us  [row_synthesis(): -sinb]
    cos x8 -> x1, other arithmetic: 53.7 us -> 7.73 us  [row_synthesis(): jnp.cos(phase)[None]]
    all_to_all x3 -> x2, waiting for transfers between devices: 47.9 us -> 6.36 us  [the longest x1 6.36 us: on_device(): lax.all_to_all(fourier, ('wave', 'lev_g', 'lev_r'), split_axis=0, concat_...]
    another operation x2 -> x0, loops' own time: 16.4 us -> none  [the longest x1 16.3 us: on_device(): lax.map(lambda item: row_synthesis(item[0], item[1]), (coef_rows, row_poi...]
    all_to_all x0 -> x1, blocking collectives: none -> 10.1 us  [on_device(): lax.all_to_all(grid, 'lev_r', split_axis=1, concat_axis=0, tiled=True)]
    all_to_all x7 -> x1, local copies, waits for them, and re-layouts: 13.1 us -> 5.21 us  [on_device(): lax.all_to_all(spec, ('lev_g', 'lev_r'), split_axis=0, concat_axis=2, til...]
    reshape x9 -> x1, local copies, waits for them, and re-layouts: 0.82 us -> 6.61 us  [on_device(): flat = gathered.reshape(per_dev, 2 * fields, waves)]
  transfers between devices with their start and end apart: 3 -> 2, of which waited for: 3 -> 1; matrix products, arithmetic and copies ran while one was open for 0% -> 47% of each run, Pallas kernels for 0% -> 0%
where the time goes in v1:
time: 113 us; the launch traced here: 112 us
  other arithmetic  53.2 us (47%)
  local copies, waits for them, and re-layouts  19.1 us (17%)
  starting transfers between devices  11.6 us (10%)
  blocking collectives  10.1 us (9%)
  matrix products  7.47 us (7%)
  waiting for transfers between devices  6.36 us (6%)
  between operations  4.07 us (4%)
    neg x1, other arithmetic, row_synthesis(): -sinb  18.2 us
    convert_element_type x1, other arithmetic, row_synthesis(): sinb = jnp.sin(theta).astype(jnp.bfloat16)  18.2 us
    all_to_all x1, blocking collectives, on_device(): lax.all_to_all(grid, 'lev_r', split_axis=1, concat_axis=0, tiled=True)  10.1 us
    cos x1, other arithmetic, row_synthesis(): jnp.cos(phase)[None]  7.73 us
    reshape x1, local copies, waits for them, and re-layouts, on_device(): flat = gathered.reshape(per_dev, 2 * fields, waves)  6.61 us
    all_to_all x1, waiting for transfers between devices, on_device(): lax.all_to_all(fourier, ('wave', 'lev_g', 'lev_r'), split_axis=0, concat_...  6.36 us
    all_to_all x1, starting transfers between devices, on_device(): lax.all_to_all(fourier, ('wave', 'lev_g', 'lev_r'), split_axis=0, concat_...  6.33 us
    all_to_all x1, starting transfers between devices, on_device(): lax.all_to_all(spec, ('lev_g', 'lev_r'), split_axis=0, concat_axis=2, til...  5.32 us
  transfers between devices with their start and end apart: 2, of which 1 were waited for; matrix products, arithmetic and copies ran while one was open for 47% of the time, Pallas kernels for 0%

profile of v1, /device:TPU:0, one launch (start us, length us, event | category | flops | bytes accessed | tf_op | source)
XLA Modules:
  0.0 112.0 jit_solution(5712427975865913089)
XLA Ops:
  0.0 5.3 %all-to-all-start = ((bf16[320,2,2,1280]{3,2,1,0:T(2,128)(2,1)}), bf16[320,2,2,1280]{3,2,1,0:T(2,128)(2,1)S(1)}, u32[]{:S(2)}, u32[]{:S(2)}) async-start(bf16[320,2,2,1280]{3,2,1,0:T(2,128)(2,1)} %param.5), calls=%async_computation | async-start | bytes 6553600 | tf_op jit(solution)/shard_map/all_to_all | solution.py:45
  5.4 0.6 dynamic_slice.6
  7.9 0.6 dynamic-slice.2
  10.5 18.2 %fusion.37 = bf16[64,1,5136]{2,0,1:T(8,128)(2,1)} fusion(f32[]{:T(128)S(6)} %convert_element_type.72, pred[]{:T(512)S(6)} %lt.92, s32[]{:T(128)S(6)} %select_n.116), kind=kLoop, calls=%fused_computation.52 | loop fusion | flops 4930560 | bytes 657417 | tf_op jit(solution)/shard_map/neg | solution.py:26
  28.8 3.6 %broadcast_select_fusion.1 = (bf16[40,16,1280]{2,1,0:T(8,128)(2,1)}, bf16[40,16,1280]{2,1,0:T(8,128)(2,1)}) fusion(bf16[40,16,1280]{2,1,0:T(8,128)(2,1)} %param.6, pred[40,1280]{1,0:T(8,128)(4,1)S(1)} %get-tuple-element.24, pred[40,1280]{1,0:T(8,128)(4,1)S(1)} %get-tuple-element.25), kind=kLoop, calls=%fused_computation.25 | loop fusion | flops 1638400 | bytes 5017600 | tf_op jit(solution)/shard_map/jit(_where)/select_n | solution.py:55
  32.6 18.2 %sine_convert_fusion = (bf16[64,1,5136]{2,0,1:T(8,128)(2,1)S(1)}, bf16[64,1,5136]{2,0,1:T(8,128)(2,1)S(1)}) fusion(f32[]{:T(128)S(6)} %convert_element_type.72, pred[]{:T(512)S(6)} %lt.92, s32[]{:T(128)S(6)} %select_n.116), kind=kLoop, calls=%fused_computation.31 | loop fusion | flops 4273152 | bytes 1314825 | tf_op jit(solution)/shard_map/convert_element_type | solution.py:25
  50.8 1.9 %maximum_bitcast_fusion.2 = (bf16[1,64,2,5136]{3,1,0,2:T(8,128)(2,1)}, bf16[1,64,2,5136]{3,1,0,2:T(8,128)(2,1)}) fusion(bf16[64,1,5136]{2,0,1:T(8,128)(2,1)S(1)} %get-tuple-element.26, bf16[64,1,5136]{2,0,1:T(8,128)(2,1)S(1)} %get-tuple-element.27, bf16[64,1,5136]{2,0,1:T(8,128)(2,1)S(1)} %copy-done.2), kind=kLoop, calls=%fused_computation.29 | loop fusion | flops 1314816 | bytes 4601856 | tf_op jit(solution)/shard_map/stack | solution.py:26
  52.6 7.7 %fusion.39 = (f32[20,5136]{1,0:T(8,128)}, f32[20,5136]{1,0:T(8,128)}) fusion(f32[]{:T(128)S(6)} %convert_element_type.72, pred[]{:T(512)S(6)} %lt.92, s32[]{:T(128)S(6)} %select_n.116, s32[20]{0:T(128)S(1)} %iota_multiply_fusion), kind=kLoop, calls=%fused_computation.54 | loop fusion | flops 1129920 | bytes 821849 | tf_op jit(solution)/shard_map/cos | solution.py:31
  60.3 5.2 %copy.39 = bf16[8,40,2,2,1280]{4,3,0,2,1:T(2,128)(2,1)} copy(bf16[8,40,2,2,1280]{4,3,2,1,0:T(2,128)(2,1)S(1)} %bitcast.76) | data formatting | bytes 6553600 | tf_op jit(solution)/shard_map/all_to_all | solution.py:45
  65.6 6.6 %reshape.294 = bf16[40,32,1280]{2,1,0:T(8,128)(2,1)S(1)} reshape(bf16[40,2,8,2,1280]{4,3,2,1,0:T(2,128)(2,1)} %bitcast.77) | data formatting | bytes 6553600 | tf_op jit(solution)/shard_map/reshape | solution.py:57
  72.2 3.8 %fusion.27 = f32[40,32,32]{1,2,0:T(8,128)} fusion(bf16[40,32,1280]{2,1,0:T(8,128)(2,1)S(1)} %reshape.294, bf16[40,16,1280]{2,1,0:T(8,128)(2,1)} %get-tuple-element.17, bf16[40,16,1280]{2,1,0:T(8,128)(2,1)} %get-tuple-element.16), kind=kOutput, calls=%fused_computation.38 | convolution fusion | flops 111411200 | bytes 6717440 | tf_op jit(solution)/shard_map/sxk,sjk->sxj/dot_general | solution.py:58
  75.9 1.7 %copy.23 = f32[40,32,32]{0,2,1:T(8,128)S(1)} copy(f32[40,32,32]{1,2,0:T(8,128)} %fusion.27) | data formatting | bytes 327680 | tf_op jit(solution)/shard_map/sxk,sjk->sxj/dot_general | solution.py:58
  77.8 0.6 gather_fusion
  78.4 0.6 gather_fusion.1
  79.1 1.0 reshape.342
  80.1 6.3 %all-to-all-start.1 = ((bf16[32,2,640]{2,1,0:T(2,128)(2,1)}), bf16[32,2,640]{2,1,0:T(2,128)(2,1)S(1)}, u32[]{:S(2)}, u32[]{:S(2)}) async-start(bf16[32,2,640]{2,1,0:T(2,128)(2,1)} %reshape.342), calls=%async_computation.1 | async-start | bytes 163840 | tf_op jit(solution)/shard_map/all_to_all | solution.py:71
  86.5 0.6 iota_compare_fusion.2
  87.1 0.6 select_select_fusion
  87.7 6.4 %all-to-all-done.1 = bf16[32,2,640]{2,1,0:T(2,128)(2,1)S(1)} async-done(((bf16[32,2,640]{2,1,0:T(2,128)(2,1)}), bf16[32,2,640]{2,1,0:T(2,128)(2,1)S(1)}, u32[]{:S(2)}, u32[]{:S(2)}) %all-to-all-start.1) | async-done | bytes 81952 | tf_op jit(solution)/shard_map/all_to_all | solution.py:71
  95.0 1.4 %fusion.17 = bf16[2,16,1280]{2,1,0:T(8,128)(2,1)S(1)} fusion(bf16[2,16,1280]{2,1,0:T(8,128)(2,1)S(1)} %reshape.297, s32[1280]{0:T(1024)S(1)} %copy-done.5, f32[1280]{0:T(1024)S(1)} %select_select_fusion), kind=kOutput, calls=%fused_computation.22 | convolution fusion | flops 106577920 | bytes 174080 | tf_op jit(solution)/shard_map/cfrs,sm->cfrm/dot_general | solution.py:77
  96.6 2.3 %convolution_bitcast_fusion = f32[2,16,20,5136]{3,2,1,0:T(8,128)S(1)} fusion(bf16[1,64,2,5136]{3,1,0,2:T(8,128)(2,1)S(1)} %copy-done.1, bf16[1,64,2,5136]{3,1,0,2:T(8,128)(2,1)S(1)} %copy-done, bf16[2,16,20,64]{3,2,1,0:T(8,128)(2,1)S(1)} %reshape_squeeze_transpose.3), kind=kOutput, calls=%fused_computation.2 | convolution fusion | flops 846741504 | bytes 15859712 | tf_op jit(solution)/shard_map/cfab,cbdi->dfai/dot_general | solution.py:28
  98.9 1.9 %fusion.2 = f32[16,5136]{1,0:T(8,128)S(1)} fusion(f32[2,16,20,5136]{3,2,1,0:T(8,128)S(1)} %convolution_bitcast_fusion, f32[20,5136]{1,0:T(8,128)S(1)} %copy-done.4, f32[20,5136]{1,0:T(8,128)S(1)} %copy-done.3), kind=kLoop, calls=%fused_computation.6 | loop fusion | flops 6491904 | bytes 14298624 | tf_op jit(solution)/shard_map/reduce_sum | solution.py:31
  101.1 10.1 %all_to_all.29 = f32[1,8,2,5136]{3,2,0,1:T(2,128)S(1)} all-to-all(f32[1,8,2,5136]{3,2,0,1:T(2,128)S(1)} %broadcast_select_fusion.2), channel_id=1, replica_groups=mesh['wave'=4,'lev'=8] {'lev'}, dimensions={1} | all-to-all | bytes 657408 | tf_op jit(solution)/shard_map/all_to_all | solution.py:92
  111.2 0.7 copy.43
  (36 shorter events, 2.0 us)
Async XLA Ops:
  0.0 5.3 %copy-start.6 = (s32[32]{0:T(128)S(1)}, s32[32]{0:T(128)}, u32[]{:S(2)}) copy-start(s32[32]{0:T(128)} %param.9) | copy-start | bytes 388
  0.0 7.9 %copy-start.7 = (s32[32]{0:T(128)S(1)}, s32[32]{0:T(128)}, u32[]{:S(2)}) copy-start(s32[32]{0:T(128)} %param.8) | copy-start | bytes 388
  0.0 10.4 %copy-start.5 = (s32[1280]{0:T(1024)S(1)}, s32[1280]{0:T(1024)}, u32[]{:S(2)}) copy-start(s32[1280]{0:T(1024)} %param.7) | copy-start | bytes 15364
  0.0 60.3 %all-to-all-start = ((bf16[320,2,2,1280]{3,2,1,0:T(2,128)(2,1)}), bf16[320,2,2,1280]{3,2,1,0:T(2,128)(2,1)S(1)}, u32[]{:S(2)}, u32[]{:S(2)}) async-start(bf16[320,2,2,1280]{3,2,1,0:T(2,128)(2,1)} %param.5), calls=%async_computation | async-start | bytes 6553600 | tf_op jit(solution)/shard_map/all_to_all | solution.py:45
  32.6 18.2 %copy-start.2 = (bf16[64,1,5136]{2,0,1:T(8,128)(2,1)S(1)}, bf16[64,1,5136]{2,0,1:T(8,128)(2,1)}, u32[]{:S(2)}) copy-start(bf16[64,1,5136]{2,0,1:T(8,128)(2,1)} %fusion.37) | copy-start | bytes 1972228
  80.1 13.9 %all-to-all-start.1 = ((bf16[32,2,640]{2,1,0:T(2,128)(2,1)}), bf16[32,2,640]{2,1,0:T(2,128)(2,1)S(1)}, u32[]{:S(2)}, u32[]{:S(2)}) async-start(bf16[32,2,640]{2,1,0:T(2,128)(2,1)} %reshape.342), calls=%async_computation.1 | async-start | bytes 163840 | tf_op jit(solution)/shard_map/all_to_all | solution.py:71
  94.5 2.0 %copy-start = (bf16[1,64,2,5136]{3,1,0,2:T(8,128)(2,1)S(1)}, bf16[1,64,2,5136]{3,1,0,2:T(8,128)(2,1)}, u32[]{:S(2)}) copy-start(bf16[1,64,2,5136]{3,1,0,2:T(8,128)(2,1)} %get-tuple-element.18) | copy-start | bytes 3944452
  94.5 2.0 %copy-start.1 = (bf16[1,64,2,5136]{3,1,0,2:T(8,128)(2,1)S(1)}, bf16[1,64,2,5136]{3,1,0,2:T(8,128)(2,1)}, u32[]{:S(2)}) copy-start(bf16[1,64,2,5136]{3,1,0,2:T(8,128)(2,1)} %get-tuple-element.19) | copy-start | bytes 3944452
  96.6 2.3 %copy-start.3 = (f32[20,5136]{1,0:T(8,128)S(1)}, f32[20,5136]{1,0:T(8,128)}, u32[]{:S(2)}) copy-start(f32[20,5136]{1,0:T(8,128)} %get-tuple-element.22) | copy-start | bytes 1232644
  96.6 2.3 %copy-start.4 = (f32[20,5136]{1,0:T(8,128)S(1)}, f32[20,5136]{1,0:T(8,128)}, u32[]{:S(2)}) copy-start(f32[20,5136]{1,0:T(8,128)} %get-tuple-element.23) | copy-start | bytes 1232644

commit v2 on v1

--- a/solution.py
+++ b/solution.py
@@ -12,23 +12,44 @@
     return 2.0 * math.pi * remainder.astype(jnp.float32) / points.astype(jnp.float32)
 
 
+def trig_pair(step, lon_idx, points, count):
+    mult = jnp.arange(count, dtype=jnp.int32)[:, None] * step
+    theta = angles(mult * lon_idx[None, :] % points, points)
+    return jnp.cos(theta), jnp.sin(theta)
+
+
+def compose(first, second):
+    c0, s0 = first
+    c1, s1 = second
+    cos = c1[:, None] * c0[None] - s1[:, None] * s0[None]
+    sin = s1[:, None] * c0[None] + c1[:, None] * s0[None]
+    return cos.reshape(-1, cos.shape[-1]), sin.reshape(-1, sin.shape[-1])
+
+
 def row_synthesis(coef_row, points):
     fields = coef_row.shape[1]
     waves = coef_row.shape[2]
     ablocks = waves // 64
     lon_len = 20 + 4 * (waves - 1)
     lon_idx = jnp.arange(lon_len, dtype=jnp.int32)
-    inner = jnp.arange(64, dtype=jnp.int32)
-    remainder = inner[:, None] * lon_idx[None, :] % points
-    theta = angles(remainder, points)
-    cosb = jnp.cos(theta).astype(jnp.bfloat16)
-    sinb = jnp.sin(theta).astype(jnp.bfloat16)
-    table = jnp.stack([jnp.stack([cosb, sinb], 1), jnp.stack([-sinb, cosb], 1)], 0)
+    cos_t, sin_t = compose(trig_pair(1, lon_idx, points, 8), trig_pair(8, lon_idx, points, 8))
+    cosb = cos_t.astype(jnp.bfloat16)
+    sinb = sin_t.astype(jnp.bfloat16)
+    n_a1 = -(-ablocks // 4)
+    cosp, sinp = compose(
+        trig_pair(64, lon_idx, points, 4), trig_pair(256, lon_idx, points, n_a1)
+    )
+    cosp = cosp[:ablocks]
+    sinp = sinp[:ablocks]
     blocks = coef_row.reshape(2, fields, ablocks, 64)
-    part = jnp.einsum("cfab,cbdi->dfai", blocks, table, preferred_element_type=jnp.float32)
-    outer = jnp.arange(ablocks, dtype=jnp.int32) * 64
-    phase = angles(outer[:, None] * lon_idx[None, :] % points, points)
-    total = jnp.sum(part[0] * jnp.cos(phase)[None] - part[1] * jnp.sin(phase)[None], axis=1)
+    c0 = blocks[0]
+    c1 = blocks[1]
+    lhs = jnp.stack(
+        [jnp.concatenate([c0, -c1], -1), jnp.concatenate([c1, c0], -1)], 0
+    )
+    rhs = jnp.concatenate([cosb, sinb], 0)
+    part = jnp.einsum("dfab,bi->dfai", lhs, rhs, preferred_element_type=jnp.float32)
+    total = jnp.sum(part[0] * cosp[None] - part[1] * sinp[None], axis=1)
     return jnp.where(lon_idx[None, :] < points, total, jnp.zeros_like(total))
 
 

time: 113 us -> 95.7 us (0.85)
  other arithmetic: 53.2 us -> 22.6 us
  waiting for transfers between devices: 6.36 us -> 15.6 us
  local copies, waits for them, and re-layouts: 19.1 us -> 25.1 us
  starting transfers between devices: 11.6 us -> 9.3 us
    neg x1, other arithmetic: 18.2 us -> 0.02 us  [row_synthesis(): -c1]
    convert_element_type x1, other arithmetic: 18.2 us -> 1.4 us  [row_synthesis(): cosb = cos_t.astype(jnp.bfloat16)]
    all_to_all x1, waiting for transfers between devices: 0.01 us -> 14.9 us  [on_device(): lax.all_to_all(spec, ('lev_g', 'lev_r'), split_axis=0, concat_axis=2, til...]
    all_to_all x1, waiting for transfers between devices: 6.36 us -> 0.66 us  [on_device(): lax.all_to_all(fourier, ('wave', 'lev_g', 'lev_r'), split_axis=0, concat_...]
    sin x0 -> x1, other arithmetic: none -> 2.94 us  [trig_pair(): return (jnp.cos(theta), jnp.sin(theta))]
    convert_element_type x0 -> x2, local copies, waits for them, and re-layouts: none -> 2.61 us  [the longest x1 1.31 us: row_synthesis(): cosb = cos_t.astype(jnp.bfloat16)]
    all_to_all x1, starting transfers between devices: 6.33 us -> 4 us  [on_device(): lax.all_to_all(fourier, ('wave', 'lev_g', 'lev_r'), split_axis=0, concat_...]
    sub x0 -> x1, local copies, waits for them, and re-layouts: none -> 1.95 us  [compose(): cos = c1[:, None] * c0[None] - s1[:, None] * s0[None]]
  transfers between devices with their start and end apart: 2 -> 2, of which waited for: 1 -> 2; matrix products, arithmetic and copies ran while one was open for 47% -> 29% of each run, Pallas kernels for 0% -> 0%
where the time goes in v2:
time: 95.7 us; the launch traced here: 95.1 us
  local copies, waits for them, and re-layouts  25.1 us (26%)
  other arithmetic  22.6 us (24%)
  waiting for transfers between devices  15.6 us (16%)
  blocking collectives  10.8 us (11%)
  starting transfers between devices  9.3 us (10%)
  matrix products  7.62 us (8%)
  between operations  4.07 us (4%)
    all_to_all x1, waiting for transfers between devices, on_device(): lax.all_to_all(spec, ('lev_g', 'lev_r'), split_axis=0, concat_axis=2, til...  14.9 us
    all_to_all x1, blocking collectives, on_device(): lax.all_to_all(grid, 'lev_r', split_axis=1, concat_axis=0, tiled=True)  10.8 us
    cos x3, other arithmetic, trig_pair(): return (jnp.cos(theta), jnp.sin(theta))  9.1 us
    reshape x1, local copies, waits for them, and re-layouts, on_device(): flat = gathered.reshape(per_dev, 2 * fields, waves)  6.61 us
    all_to_all x1, local copies, waits for them, and re-layouts, on_device(): lax.all_to_all(spec, ('lev_g', 'lev_r'), split_axis=0, concat_axis=2, til...  5.38 us
    all_to_all x1, starting transfers between devices, on_device(): lax.all_to_all(spec, ('lev_g', 'lev_r'), split_axis=0, concat_axis=2, til...  5.3 us
    all_to_all x1, starting transfers between devices, on_device(): lax.all_to_all(fourier, ('wave', 'lev_g', 'lev_r'), split_axis=0, concat_...  4 us
    dot_general x1, matrix products, on_device(): jnp.einsum('sxk,sjk->sxj', flat, leg2, preferred_element_type=jnp.float32)  3.78 us
  transfers between devices with their start and end apart: 2, of which 2 were waited for; matrix products, arithmetic and copies ran while one was open for 29% of the time, Pallas kernels for 0%

profile of v2, /device:TPU:0, one launch (start us, length us, event | category | flops | bytes accessed | tf_op | source)
XLA Modules:
  0.0 95.1 jit_solution(3790226199187932912)
XLA Ops:
  0.0 5.3 %all-to-all-start = ((bf16[320,2,2,1280]{3,2,1,0:T(2,128)(2,1)}), bf16[320,2,2,1280]{3,2,1,0:T(2,128)(2,1)S(1)}, u32[]{:S(2)}, u32[]{:S(2)}) async-start(bf16[320,2,2,1280]{3,2,1,0:T(2,128)(2,1)} %param.5), calls=%async_computation | async-start | bytes 6553600 | tf_op jit(solution)/shard_map/all_to_all | solution.py:66
  10.3 2.9 %fusion.61 = (f32[8,5136]{1,0:T(8,128)S(1)}, f32[8,5136]{1,0:T(8,128)}) fusion(f32[]{:T(128)S(6)} %convert_element_type.76, pred[]{:T(512)S(6)} %lt.114, s32[]{:T(128)S(6)} %select_n.141), kind=kLoop, calls=%fused_computation.82 | loop fusion | flops 451968 | bytes 328713 | tf_op jit(solution)/shard_map/sin | solution.py:18
  13.3 3.1 %fusion.64 = (f32[8,5136]{1,0:T(8,128)}, f32[8,5136]{1,0:T(8,128)}) fusion(f32[]{:T(128)S(6)} %convert_element_type.76, pred[]{:T(512)S(6)} %lt.114, s32[]{:T(128)S(6)} %select_n.141, s32[8]{0:T(128)S(1)} %iota_multiply_fusion.2), kind=kLoop, calls=%fused_computation.85 | loop fusion | flops 451968 | bytes 328745 | tf_op jit(solution)/shard_map/cos | solution.py:18
  16.4 3.1 %fusion.60 = (f32[5,5136]{1,0:T(8,128)}, f32[5,5136]{1,0:T(8,128)}) fusion(f32[]{:T(128)S(6)} %convert_element_type.76, pred[]{:T(512)S(6)} %lt.114, s32[]{:T(128)S(6)} %select_n.141, s32[5]{0:T(128)S(1)} %iota_multiply_fusion.1), kind=kLoop, calls=%fused_computation.81 | loop fusion | flops 282480 | bytes 205469 | tf_op jit(solution)/shard_map/cos | solution.py:18
  19.4 3.0 %fusion.66 = (f32[4,5136]{1,0:T(4,128)S(1)}, f32[4,5136]{1,0:T(4,128)}) fusion(f32[]{:T(128)S(6)} %convert_element_type.76, pred[]{:T(512)S(6)} %lt.114, s32[]{:T(128)S(6)} %select_n.141, s32[4]{0:T(128)S(1)} %iota_multiply_fusion), kind=kLoop, calls=%fused_computation.87 | loop fusion | flops 225984 | bytes 164377 | tf_op jit(solution)/shard_map/cos | solution.py:18
  22.4 0.8 dynamic-slice_subtract_fusion
  23.3 3.7 %broadcast_select_fusion.1 = (bf16[40,16,1280]{2,1,0:T(8,128)(2,1)}, bf16[40,16,1280]{2,1,0:T(8,128)(2,1)}) fusion(bf16[40,16,1280]{2,1,0:T(8,128)(2,1)} %param.6, pred[40,1280]{1,0:T(8,128)(4,1)S(1)} %get-tuple-element.32, pred[40,1280]{1,0:T(8,128)(4,1)S(1)} %get-tuple-element.33), kind=kLoop, calls=%fused_computation.20 | loop fusion | flops 1638400 | bytes 5017600 | tf_op jit(solution)/shard_map/jit(_where)/select_n | solution.py:76
  27.1 1.1 %multiply_subtract_fusion = (f32[5,4,5136]{2,1,0:T(4,128)}, f32[5,4,5136]{2,1,0:T(4,128)}) fusion(f32[4,5136]{1,0:T(4,128)S(1)} %copy-done.8, f32[5,5136]{1,0:T(8,128)S(1)} %copy-done.7, f32[4,5136]{1,0:T(4,128)S(1)} %get-tuple-element.30, f32[5,5136]{1,0:T(8,128)S(1)} %copy-done.6), kind=kLoop, calls=%fused_computation.32 | loop fusion | flops 616320 | bytes 1191552 | tf_op jit(solution)/shard_map/sub | solution.py:24
  28.3 1.4 %fusion.24 = (bf16[64,5136]{1,0:T(8,128)(2,1)}, bf16[64,5136]{1,0:T(8,128)(2,1)}) fusion(f32[8,5136]{1,0:T(8,128)S(1)} %get-tuple-element.36, f32[8,5136]{1,0:T(8,128)S(1)} %copy-done.5, f32[8,5136]{1,0:T(8,128)S(1)} %copy-done.3, f32[8,5136]{1,0:T(8,128)S(1)} %copy-done.4), kind=kLoop, calls=%fused_computation.28 | loop fusion | flops 2629632 | bytes 1972224 | tf_op jit(solution)/shard_map/convert_element_type | solution.py:36
  29.7 14.9 %all-to-all-done = bf16[320,2,2,1280]{3,2,1,0:T(2,128)(2,1)S(1)} async-done(((bf16[320,2,2,1280]{3,2,1,0:T(2,128)(2,1)}), bf16[320,2,2,1280]{3,2,1,0:T(2,128)(2,1)S(1)}, u32[]{:S(2)}, u32[]{:S(2)}) %all-to-all-start) | async-done | bytes 3276832 | tf_op jit(solution)/shard_map/all_to_all | solution.py:66
  44.6 5.4 %copy.32 = bf16[8,40,2,2,1280]{4,3,0,2,1:T(2,128)(2,1)} copy(bf16[8,40,2,2,1280]{4,3,2,1,0:T(2,128)(2,1)S(1)} %bitcast.70) | data formatting | bytes 6553600 | tf_op jit(solution)/shard_map/all_to_all | solution.py:66
  50.0 6.6 %reshape.439 = bf16[40,32,1280]{2,1,0:T(8,128)(2,1)S(1)} reshape(bf16[40,2,8,2,1280]{4,3,2,1,0:T(2,128)(2,1)} %bitcast.71) | data formatting | bytes 6553600 | tf_op jit(solution)/shard_map/reshape | solution.py:78
  56.6 3.8 %fusion.21 = f32[40,32,32]{1,2,0:T(8,128)} fusion(bf16[40,32,1280]{2,1,0:T(8,128)(2,1)S(1)} %reshape.439, bf16[40,16,1280]{2,1,0:T(8,128)(2,1)} %get-tuple-element.17, bf16[40,16,1280]{2,1,0:T(8,128)(2,1)} %get-tuple-element.16), kind=kOutput, calls=%fused_computation.27 | convolution fusion | flops 111411200 | bytes 6717440 | tf_op jit(solution)/shard_map/sxk,sjk->sxj/dot_general | solution.py:79
  60.4 1.7 %copy.20 = f32[40,32,32]{0,2,1:T(8,128)S(1)} copy(f32[40,32,32]{1,2,0:T(8,128)} %fusion.21) | data formatting | bytes 327680 | tf_op jit(solution)/shard_map/sxk,sjk->sxj/dot_general | solution.py:79
  63.6 1.0 %reshape.485 = bf16[32,2,640]{2,1,0:T(2,128)(2,1)} reshape(bf16[32,1,2,16,40]{4,3,2,1,0:T(8,128)(2,1)S(1)} %bitcast.78) | data formatting | bytes 163840
  64.6 4.0 %all-to-all-start.1 = ((bf16[32,2,640]{2,1,0:T(2,128)(2,1)}), bf16[32,2,640]{2,1,0:T(2,128)(2,1)S(1)}, u32[]{:S(2)}, u32[]{:S(2)}) async-start(bf16[32,2,640]{2,1,0:T(2,128)(2,1)} %reshape.485), calls=%async_computation.1 | async-start | bytes 163840 | tf_op jit(solution)/shard_map/all_to_all | solution.py:92
  69.2 1.3 %copy.24 = bf16[64,5136]{0,1:T(8,128)(2,1)S(1)} copy(bf16[64,5136]{1,0:T(8,128)(2,1)S(1)} %copy-done.1) | data formatting | bytes 1314816 | tf_op jit(solution)/shard_map/convert_element_type | solution.py:36
  70.5 1.3 %copy.25 = bf16[64,5136]{0,1:T(8,128)(2,1)S(1)} copy(bf16[64,5136]{1,0:T(8,128)(2,1)S(1)} %copy-done) | data formatting | bytes 1314816 | tf_op jit(solution)/shard_map/convert_element_type | solution.py:37
  71.9 1.2 %add.125 = f32[20,5136]{1,0:T(8,128)S(1)} reshape(f32[5,4,5136]{2,1,0:T(4,128)} %get-tuple-element.23) | data formatting | bytes 821760 | tf_op jit(solution)/shard_map/add | solution.py:25
  73.0 2.0 %sub.33 = f32[20,5136]{1,0:T(8,128)} reshape(f32[5,4,5136]{2,1,0:T(4,128)} %get-tuple-element.22) | data formatting | bytes 821760 | tf_op jit(solution)/shard_map/sub | solution.py:24
  77.1 1.4 %fusion.15 = bf16[2,16,1280]{2,1,0:T(8,128)(2,1)S(1)} fusion(bf16[2,16,1280]{2,1,0:T(8,128)(2,1)S(1)} %reshape.442, s32[1280]{0:T(1024)S(1)} %copy-done.9, f32[1280]{0:T(1024)S(1)} %select_select_fusion), kind=kOutput, calls=%fused_computation.18 | convolution fusion | flops 106577920 | bytes 174080 | tf_op jit(solution)/shard_map/cfrs,sm->cfrm/dot_general | solution.py:98
  78.9 2.4 %fusion.18 = f32[2,16,20,5136]{3,2,1,0:T(8,128)S(1)} fusion(bf16[64,5136]{0,1:T(8,128)(2,1)S(1)} %copy.25, bf16[64,5136]{0,1:T(8,128)(2,1)S(1)} %copy.24, bf16[1,16,20,128]{3,2,1,0:T(8,128)(2,1)S(1)} %get-tuple-element.25, bf16[1,16,20,128]{3,2,1,0:T(8,128)(2,1)S(1)} %get-tuple-element.24), kind=kOutput, calls=%fused_computation.24 | convolution fusion | flops 844193792 | bytes 14626816 | tf_op jit(solution)/shard_map/dfab,bi->dfai/dot_general | solution.py:51
  81.4 1.8 %fusion.2 = f32[16,5136]{1,0:T(8,128)S(1)} fusion(f32[2,16,20,5136]{3,2,1,0:T(8,128)S(1)} %fusion.18, f32[20,5136]{1,0:T(8,128)S(1)} %add.125, f32[20,5136]{1,0:T(8,128)S(1)} %copy-done.2), kind=kLoop, calls=%fused_computation.5 | loop fusion | flops 6491904 | bytes 14298624 | tf_op jit(solution)/shard_map/reduce_sum | solution.py:52
  83.5 10.8 %all_to_all.29 = f32[1,8,2,5136]{3,2,0,1:T(2,128)S(1)} all-to-all(f32[1,8,2,5136]{3,2,0,1:T(2,128)S(1)} %broadcast_select_fusion.2), channel_id=1, replica_groups=mesh['wave'=4,'lev'=8] {'lev'}, dimensions={1} | all-to-all | bytes 657408 | tf_op jit(solution)/shard_map/all_to_all | solution.py:113
  (56 shorter events, 7.1 us)
Async XLA Ops:
  0.0 5.3 %copy-start.10 = (s32[32]{0:T(128)S(1)}, s32[32]{0:T(128)}, u32[]{:S(2)}) copy-start(s32[32]{0:T(128)} %param.9) | copy-start | bytes 388
  0.0 7.9 %copy-start.11 = (s32[32]{0:T(128)S(1)}, s32[32]{0:T(128)}, u32[]{:S(2)}) copy-start(s32[32]{0:T(128)} %param.8) | copy-start | bytes 388
  0.0 44.6 %all-to-all-start = ((bf16[320,2,2,1280]{3,2,1,0:T(2,128)(2,1)}), bf16[320,2,2,1280]{3,2,1,0:T(2,128)(2,1)S(1)}, u32[]{:S(2)}, u32[]{:S(2)}) async-start(bf16[320,2,2,1280]{3,2,1,0:T(2,128)(2,1)} %param.5), calls=%async_computation | async-start | bytes 6553600 | tf_op jit(solution)/shard_map/all_to_all | solution.py:66
  23.3 3.8 %copy-start.6 = (f32[5,5136]{1,0:T(8,128)S(1)}, f32[5,5136]{1,0:T(8,128)}, u32[]{:S(2)}) copy-start(f32[5,5136]{1,0:T(8,128)} %get-tuple-element.28) | copy-start | bytes 308164
  23.3 3.8 %copy-start.7 = (f32[5,5136]{1,0:T(8,128)S(1)}, f32[5,5136]{1,0:T(8,128)}, u32[]{:S(2)}) copy-start(f32[5,5136]{1,0:T(8,128)} %get-tuple-element.29) | copy-start | bytes 308164
  23.3 3.8 %copy-start.8 = (f32[4,5136]{1,0:T(4,128)S(1)}, f32[4,5136]{1,0:T(4,128)}, u32[]{:S(2)}) copy-start(f32[4,5136]{1,0:T(4,128)} %get-tuple-element.31) | copy-start | bytes 246532
  23.3 4.9 %copy-start.3 = (f32[8,5136]{1,0:T(8,128)S(1)}, f32[8,5136]{1,0:T(8,128)}, u32[]{:S(2)}) copy-start(f32[8,5136]{1,0:T(8,128)} %get-tuple-element.37) | copy-start | bytes 493060
  23.3 4.9 %copy-start.4 = (f32[8,5136]{1,0:T(8,128)S(1)}, f32[8,5136]{1,0:T(8,128)}, u32[]{:S(2)}) copy-start(f32[8,5136]{1,0:T(8,128)} %get-tuple-element.34) | copy-start | bytes 493060
  23.3 4.9 %copy-start.5 = (f32[8,5136]{1,0:T(8,128)S(1)}, f32[8,5136]{1,0:T(8,128)}, u32[]{:S(2)}) copy-start(f32[8,5136]{1,0:T(8,128)} %get-tuple-element.35) | copy-start | bytes 493060
  62.8 6.3 %copy-start.1 = (bf16[64,5136]{1,0:T(8,128)(2,1)S(1)}, bf16[64,5136]{1,0:T(8,128)(2,1)}, u32[]{:S(2)}) copy-start(bf16[64,5136]{1,0:T(8,128)(2,1)} %get-tuple-element.18) | copy-start | bytes 1972228
  63.4 7.1 %copy-start = (bf16[64,5136]{1,0:T(8,128)(2,1)S(1)}, bf16[64,5136]{1,0:T(8,128)(2,1)}, u32[]{:S(2)}) copy-start(bf16[64,5136]{1,0:T(8,128)(2,1)} %get-tuple-element.19) | copy-start | bytes 1972228
  64.6 11.6 %all-to-all-start.1 = ((bf16[32,2,640]{2,1,0:T(2,128)(2,1)}), bf16[32,2,640]{2,1,0:T(2,128)(2,1)S(1)}, u32[]{:S(2)}, u32[]{:S(2)}) async-start(bf16[32,2,640]{2,1,0:T(2,128)(2,1)} %reshape.485), calls=%async_computation.1 | async-start | bytes 163840 | tf_op jit(solution)/shard_map/all_to_all | solution.py:92
  71.8 5.2 %copy-start.9 = (s32[1280]{0:T(1024)S(1)}, s32[1280]{0:T(1024)}, u32[]{:S(2)}) copy-start(s32[1280]{0:T(1024)} %param.7) | copy-start | bytes 15364
  78.9 2.4 %copy-start.2 = (f32[20,5136]{1,0:T(8,128)S(1)}, f32[20,5136]{1,0:T(8,128)}, u32[]{:S(2)}) copy-start(f32[20,5136]{1,0:T(8,128)} %sub.33) | copy-start | bytes 1232644

commit v3 on v2

--- a/solution.py
+++ b/solution.py
@@ -63,8 +63,9 @@
     waves = spec.shape[-1]
     trunc_top = waves - 1
     lev_idx = lax.axis_index("lev_g") * n_r + lax.axis_index("lev_r")
-    gathered = lax.all_to_all(spec, ("lev_g", "lev_r"), split_axis=0, concat_axis=2, tiled=True)
-    fields = gathered.shape[2]
+    spec_v = spec.reshape((n_lev, per_dev) + spec.shape[1:])
+    gathered = lax.all_to_all(spec_v, ("lev_g", "lev_r"), split_axis=0, concat_axis=0, tiled=True)
+    fields = gathered.shape[3] * n_lev
     first_slot = (lax.axis_index("wave") * n_lev + lev_idx) * per_dev
     my_waves = lax.dynamic_slice_in_dim(slot_wave, first_slot, per_dev)
     degree = jnp.arange(waves, dtype=jnp.int32)
@@ -75,8 +76,7 @@
     leg2 = jnp.concatenate(
         [jnp.where(even_mask, legendre, zeros), jnp.where(odd_mask, legendre, zeros)], 1
     )
-    flat = gathered.reshape(per_dev, 2 * fields, waves)
-    sums = jnp.einsum("sxk,sjk->sxj", flat, leg2, preferred_element_type=jnp.float32)
+    sums = jnp.einsum("lscfk,sjk->sclfj", gathered, leg2, preferred_element_type=jnp.float32)
     sums = sums.reshape(per_dev, 2, fields, 2, nlath)
     north = band_rows < nlath
     lat_idx = jnp.where(north, band_rows, band_rows - nlath)

time: 95.7 us -> 84.7 us (0.89)
  local copies, waits for them, and re-layouts: 25.1 us -> 12.9 us
  matrix products: 7.62 us -> 8.82 us
    reshape x1, local copies, waits for them, and re-layouts: 6.61 us -> 0.33 us  [run(): return fn(spec, legendre, slot_wave, row_lons, band_rows)]
    all_to_all x1 -> x0, local copies, waits for them, and re-layouts: 5.38 us -> none  [on_device(): lax.all_to_all(spec, ('lev_g', 'lev_r'), split_axis=0, concat_axis=2, til...]
    dot_general x1 -> x0, local copies, waits for them, and re-layouts: 1.65 us -> none  [on_device(): jnp.einsum('sxk,sjk->sxj', flat, leg2, preferred_element_type=jnp.float32)]
    transpose x0 -> x1, local copies, waits for them, and re-layouts: none -> 1.44 us  [on_device(): jnp.einsum('lscfk,sjk->sclfj', gathered, leg2, preferred_element_type=jnp...]
    dot_general x1, matrix products: 3.78 us -> 4.98 us  [on_device(): jnp.einsum('lscfk,sjk->sclfj', gathered, leg2, preferred_element_type=jnp...]
  transfers between devices with their start and end apart: 2 -> 2, of which waited for: 2 -> 2; matrix products, arithmetic and copies ran while one was open for 29% -> 33% of each run, Pallas kernels for 0% -> 0%
where the time goes in v3:
time: 84.7 us; the launch traced here: 84.2 us
  other arithmetic  22.6 us (27%)
  waiting for transfers between devices  15.4 us (18%)
  local copies, waits for them, and re-layouts  12.9 us (15%)
  blocking collectives  10.9 us (13%)
  starting transfers between devices  9.31 us (11%)
  matrix products  8.82 us (10%)
  between operations  4.24 us (5%)
    all_to_all x1, waiting for transfers between devices, on_device(): lax.all_to_all(spec_v, ('lev_g', 'lev_r'), split_axis=0, concat_axis=0, t...  14.9 us
    all_to_all x1, blocking collectives, on_device(): lax.all_to_all(grid, 'lev_r', split_axis=1, concat_axis=0, tiled=True)  10.9 us
    cos x3, other arithmetic, trig_pair(): return (jnp.cos(theta), jnp.sin(theta))  9.06 us
    all_to_all x1, starting transfers between devices, on_device(): lax.all_to_all(spec_v, ('lev_g', 'lev_r'), split_axis=0, concat_axis=0, t...  5.3 us
    dot_general x1, matrix products, on_device(): jnp.einsum('lscfk,sjk->sclfj', gathered, leg2, preferred_element_type=jnp...  4.98 us
    all_to_all x1, starting transfers between devices, on_device(): lax.all_to_all(fourier, ('wave', 'lev_g', 'lev_r'), split_axis=0, concat_...  4 us
    select_n x1, other arithmetic, on_device(): jnp.where(even_mask, legendre, zeros)  3.67 us
    sin x1, other arithmetic, trig_pair(): return (jnp.cos(theta), jnp.sin(theta))  2.94 us
  transfers between devices with their start and end apart: 2, of which 2 were waited for; matrix products, arithmetic and copies ran while one was open for 33% of the time, Pallas kernels for 0%

profile of v3, /device:TPU:0, one launch (start us, length us, event | category | flops | bytes accessed | tf_op | source)
XLA Modules:
  0.0 84.2 jit_solution(5961895452045900970)
XLA Ops:
  0.0 5.3 %all-to-all-start = ((bf16[8,40,2,2,1280]{4,3,2,1,0:T(2,128)(2,1)}), bf16[8,40,2,2,1280]{4,3,2,1,0:T(2,128)(2,1)S(1)}, u32[]{:S(2)}, u32[]{:S(2)}) async-start(bf16[8,40,2,2,1280]{4,3,2,1,0:T(2,128)(2,1)} %bitcast.73), calls=%async_computation | async-start | bytes 6553600 | tf_op jit(solution)/shard_map/all_to_all | solution.py:67
  10.5 2.9 %fusion.61 = (f32[8,5136]{1,0:T(8,128)S(1)}, f32[8,5136]{1,0:T(8,128)}) fusion(f32[]{:T(128)S(6)} %convert_element_type.76, pred[]{:T(512)S(6)} %lt.114, s32[]{:T(128)S(6)} %select_n.141), kind=kLoop, calls=%fused_computation.82 | loop fusion | flops 451968 | bytes 328713 | tf_op jit(solution)/shard_map/sin | solution.py:18
  13.5 3.1 %fusion.64 = (f32[8,5136]{1,0:T(8,128)}, f32[8,5136]{1,0:T(8,128)}) fusion(f32[]{:T(128)S(6)} %convert_element_type.76, pred[]{:T(512)S(6)} %lt.114, s32[]{:T(128)S(6)} %select_n.141, s32[8]{0:T(128)S(1)} %iota_multiply_fusion.2), kind=kLoop, calls=%fused_computation.85 | loop fusion | flops 451968 | bytes 328745 | tf_op jit(solution)/shard_map/cos | solution.py:18
  16.5 3.0 %fusion.60 = (f32[5,5136]{1,0:T(8,128)}, f32[5,5136]{1,0:T(8,128)}) fusion(f32[]{:T(128)S(6)} %convert_element_type.76, pred[]{:T(512)S(6)} %lt.114, s32[]{:T(128)S(6)} %select_n.141, s32[5]{0:T(128)S(1)} %iota_multiply_fusion.1), kind=kLoop, calls=%fused_computation.81 | loop fusion | flops 282480 | bytes 205469 | tf_op jit(solution)/shard_map/cos | solution.py:18
  19.6 3.0 %fusion.66 = (f32[4,5136]{1,0:T(4,128)S(1)}, f32[4,5136]{1,0:T(4,128)}) fusion(f32[]{:T(128)S(6)} %convert_element_type.76, pred[]{:T(512)S(6)} %lt.114, s32[]{:T(128)S(6)} %select_n.141, s32[4]{0:T(128)S(1)} %iota_multiply_fusion), kind=kLoop, calls=%fused_computation.87 | loop fusion | flops 225984 | bytes 164377 | tf_op jit(solution)/shard_map/cos | solution.py:18
  22.5 0.8 dynamic-slice_subtract_fusion
  23.5 3.7 %broadcast_select_fusion.1 = (bf16[40,16,1280]{2,1,0:T(8,128)(2,1)}, bf16[40,16,1280]{2,1,0:T(8,128)(2,1)}) fusion(bf16[40,16,1280]{2,1,0:T(8,128)(2,1)} %param.6, pred[40,1280]{1,0:T(8,128)(4,1)S(1)} %get-tuple-element.32, pred[40,1280]{1,0:T(8,128)(4,1)S(1)} %get-tuple-element.33), kind=kLoop, calls=%fused_computation.20 | loop fusion | flops 1638400 | bytes 5017600 | tf_op jit(solution)/shard_map/jit(_where)/select_n | solution.py:77
  27.2 1.1 %multiply_subtract_fusion = (f32[5,4,5136]{2,1,0:T(4,128)}, f32[5,4,5136]{2,1,0:T(4,128)}) fusion(f32[4,5136]{1,0:T(4,128)S(1)} %copy-done.8, f32[5,5136]{1,0:T(8,128)S(1)} %copy-done.7, f32[4,5136]{1,0:T(4,128)S(1)} %get-tuple-element.30, f32[5,5136]{1,0:T(8,128)S(1)} %copy-done.6), kind=kLoop, calls=%fused_computation.32 | loop fusion | flops 616320 | bytes 1191552 | tf_op jit(solution)/shard_map/sub | solution.py:24
  28.3 1.4 %fusion.24 = (bf16[64,5136]{1,0:T(8,128)(2,1)}, bf16[64,5136]{1,0:T(8,128)(2,1)}) fusion(f32[8,5136]{1,0:T(8,128)S(1)} %get-tuple-element.36, f32[8,5136]{1,0:T(8,128)S(1)} %copy-done.5, f32[8,5136]{1,0:T(8,128)S(1)} %copy-done.3, f32[8,5136]{1,0:T(8,128)S(1)} %copy-done.4), kind=kLoop, calls=%fused_computation.28 | loop fusion | flops 2629632 | bytes 1972224 | tf_op jit(solution)/shard_map/convert_element_type | solution.py:36
  29.7 14.9 %all-to-all-done = bf16[8,40,2,2,1280]{4,3,2,1,0:T(2,128)(2,1)S(1)} async-done(((bf16[8,40,2,2,1280]{4,3,2,1,0:T(2,128)(2,1)}), bf16[8,40,2,2,1280]{4,3,2,1,0:T(2,128)(2,1)S(1)}, u32[]{:S(2)}, u32[]{:S(2)}) %all-to-all-start) | async-done | bytes 3276832 | tf_op jit(solution)/shard_map/all_to_all | solution.py:67
  44.6 5.0 %fusion.21 = f32[40,2,8,2,32]{4,2,3,1,0:T(8,128)} fusion(bf16[8,40,2,2,1280]{4,3,2,1,0:T(2,128)(2,1)S(1)} %all-to-all-done, bf16[40,16,1280]{2,1,0:T(8,128)(2,1)} %get-tuple-element.17, bf16[40,16,1280]{2,1,0:T(8,128)(2,1)} %get-tuple-element.16), kind=kOutput, calls=%fused_computation.27 | convolution fusion | flops 111411200 | bytes 6717440 | tf_op jit(solution)/shard_map/lscfk,sjk->sclfj/dot_general | solution.py:79
  49.6 1.4 %copy.17 = f32[40,2,8,2,32]{0,4,3,2,1:T(8,128)S(1)} copy(f32[40,2,8,2,32]{4,2,3,1,0:T(8,128)} %fusion.21) | data formatting | bytes 327680 | tf_op jit(solution)/shard_map/lscfk,sjk->sclfj/transpose | solution.py:79
  52.6 1.0 %reshape.485 = bf16[32,2,640]{2,1,0:T(2,128)(2,1)} reshape(bf16[32,1,2,16,40]{4,3,2,1,0:T(8,128)(2,1)S(1)} %bitcast.80) | data formatting | bytes 163840
  53.6 4.0 %all-to-all-start.1 = ((bf16[32,2,640]{2,1,0:T(2,128)(2,1)}), bf16[32,2,640]{2,1,0:T(2,128)(2,1)S(1)}, u32[]{:S(2)}, u32[]{:S(2)}) async-start(bf16[32,2,640]{2,1,0:T(2,128)(2,1)} %reshape.485), calls=%async_computation.1 | async-start | bytes 163840 | tf_op jit(solution)/shard_map/all_to_all | solution.py:92
  57.6 0.6 iota_compare_fusion.2
  58.2 1.3 %copy.21 = bf16[64,5136]{0,1:T(8,128)(2,1)S(1)} copy(bf16[64,5136]{1,0:T(8,128)(2,1)S(1)} %copy-done.1) | data formatting | bytes 1314816 | tf_op jit(solution)/shard_map/convert_element_type | solution.py:36
  59.6 1.3 %copy.22 = bf16[64,5136]{0,1:T(8,128)(2,1)S(1)} copy(bf16[64,5136]{1,0:T(8,128)(2,1)S(1)} %copy-done) | data formatting | bytes 1314816 | tf_op jit(solution)/shard_map/convert_element_type | solution.py:37
  60.9 1.2 %add.125 = f32[20,5136]{1,0:T(8,128)S(1)} reshape(f32[5,4,5136]{2,1,0:T(4,128)} %get-tuple-element.23) | data formatting | bytes 821760 | tf_op jit(solution)/shard_map/add | solution.py:25
  62.1 2.0 %sub.33 = f32[20,5136]{1,0:T(8,128)} reshape(f32[5,4,5136]{2,1,0:T(4,128)} %get-tuple-element.22) | data formatting | bytes 821760 | tf_op jit(solution)/shard_map/sub | solution.py:24
  66.1 1.4 %fusion.15 = bf16[2,16,1280]{2,1,0:T(8,128)(2,1)S(1)} fusion(bf16[2,16,1280]{2,1,0:T(8,128)(2,1)S(1)} %reshape.441, s32[1280]{0:T(1024)S(1)} %copy-done.9, f32[1280]{0:T(1024)S(1)} %select_select_fusion), kind=kOutput, calls=%fused_computation.18 | convolution fusion | flops 106577920 | bytes 174080 | tf_op jit(solution)/shard_map/cfrs,sm->cfrm/dot_general | solution.py:98
  67.9 2.4 %fusion.18 = f32[2,16,20,5136]{3,2,1,0:T(8,128)S(1)} fusion(bf16[64,5136]{0,1:T(8,128)(2,1)S(1)} %copy.22, bf16[64,5136]{0,1:T(8,128)(2,1)S(1)} %copy.21, bf16[1,16,20,128]{3,2,1,0:T(8,128)(2,1)S(1)} %get-tuple-element.25, bf16[1,16,20,128]{3,2,1,0:T(8,128)(2,1)S(1)} %get-tuple-element.24), kind=kOutput, calls=%fused_computation.24 | convolution fusion | flops 844193792 | bytes 14626816 | tf_op jit(solution)/shard_map/dfab,bi->dfai/dot_general | solution.py:51
  70.4 1.8 %fusion.2 = f32[16,5136]{1,0:T(8,128)S(1)} fusion(f32[2,16,20,5136]{3,2,1,0:T(8,128)S(1)} %fusion.18, f32[20,5136]{1,0:T(8,128)S(1)} %add.125, f32[20,5136]{1,0:T(8,128)S(1)} %copy-done.2), kind=kLoop, calls=%fused_computation.5 | loop fusion | flops 6491904 | bytes 14298624 | tf_op jit(solution)/shard_map/reduce_sum | solution.py:52
  72.5 10.9 %all_to_all.19 = f32[1,8,2,5136]{3,2,0,1:T(2,128)S(1)} all-to-all(f32[1,8,2,5136]{3,2,0,1:T(2,128)S(1)} %broadcast_select_fusion.2), channel_id=1, replica_groups=mesh['wave'=4,'lev'=8] {'lev'}, dimensions={1} | all-to-all | bytes 657408 | tf_op jit(solution)/shard_map/all_to_all | solution.py:113
  83.5 0.7 copy.37
  (54 shorter events, 5.8 us)
Async XLA Ops:
  0.0 5.3 %copy-start.10 = (s32[32]{0:T(128)S(1)}, s32[32]{0:T(128)}, u32[]{:S(2)}) copy-start(s32[32]{0:T(128)} %param.9) | copy-start | bytes 388
  0.0 7.9 %copy-start.11 = (s32[32]{0:T(128)S(1)}, s32[32]{0:T(128)}, u32[]{:S(2)}) copy-start(s32[32]{0:T(128)} %param.8) | copy-start | bytes 388
  0.0 44.6 %all-to-all-start = ((bf16[8,40,2,2,1280]{4,3,2,1,0:T(2,128)(2,1)}), bf16[8,40,2,2,1280]{4,3,2,1,0:T(2,128)(2,1)S(1)}, u32[]{:S(2)}, u32[]{:S(2)}) async-start(bf16[8,40,2,2,1280]{4,3,2,1,0:T(2,128)(2,1)} %bitcast.73), calls=%async_computation | async-start | bytes 6553600 | tf_op jit(solution)/shard_map/all_to_all | solution.py:67
  23.4 3.7 %copy-start.6 = (f32[5,5136]{1,0:T(8,128)S(1)}, f32[5,5136]{1,0:T(8,128)}, u32[]{:S(2)}) copy-start(f32[5,5136]{1,0:T(8,128)} %get-tuple-element.28) | copy-start | bytes 308164
  23.4 3.7 %copy-start.7 = (f32[5,5136]{1,0:T(8,128)S(1)}, f32[5,5136]{1,0:T(8,128)}, u32[]{:S(2)}) copy-start(f32[5,5136]{1,0:T(8,128)} %get-tuple-element.29) | copy-start | bytes 308164
  23.5 3.7 %copy-start.8 = (f32[4,5136]{1,0:T(4,128)S(1)}, f32[4,5136]{1,0:T(4,128)}, u32[]{:S(2)}) copy-start(f32[4,5136]{1,0:T(4,128)} %get-tuple-element.31) | copy-start | bytes 246532
  23.5 4.8 %copy-start.3 = (f32[8,5136]{1,0:T(8,128)S(1)}, f32[8,5136]{1,0:T(8,128)}, u32[]{:S(2)}) copy-start(f32[8,5136]{1,0:T(8,128)} %get-tuple-element.37) | copy-start | bytes 493060
  23.5 4.8 %copy-start.4 = (f32[8,5136]{1,0:T(8,128)S(1)}, f32[8,5136]{1,0:T(8,128)}, u32[]{:S(2)}) copy-start(f32[8,5136]{1,0:T(8,128)} %get-tuple-element.34) | copy-start | bytes 493060
  23.5 4.8 %copy-start.5 = (f32[8,5136]{1,0:T(8,128)S(1)}, f32[8,5136]{1,0:T(8,128)}, u32[]{:S(2)}) copy-start(f32[8,5136]{1,0:T(8,128)} %get-tuple-element.35) | copy-start | bytes 493060
  51.8 6.4 %copy-start.1 = (bf16[64,5136]{1,0:T(8,128)(2,1)S(1)}, bf16[64,5136]{1,0:T(8,128)(2,1)}, u32[]{:S(2)}) copy-start(bf16[64,5136]{1,0:T(8,128)(2,1)} %get-tuple-element.18) | copy-start | bytes 1972228
  52.4 7.1 %copy-start = (bf16[64,5136]{1,0:T(8,128)(2,1)S(1)}, bf16[64,5136]{1,0:T(8,128)(2,1)}, u32[]{:S(2)}) copy-start(bf16[64,5136]{1,0:T(8,128)(2,1)} %get-tuple-element.19) | copy-start | bytes 1972228
  53.6 11.6 %all-to-all-start.1 = ((bf16[32,2,640]{2,1,0:T(2,128)(2,1)}), bf16[32,2,640]{2,1,0:T(2,128)(2,1)S(1)}, u32[]{:S(2)}, u32[]{:S(2)}) async-start(bf16[32,2,640]{2,1,0:T(2,128)(2,1)} %reshape.485), calls=%async_computation.1 | async-start | bytes 163840 | tf_op jit(solution)/shard_map/all_to_all | solution.py:92
  60.9 5.2 %copy-start.9 = (s32[1280]{0:T(1024)S(1)}, s32[1280]{0:T(1024)}, u32[]{:S(2)}) copy-start(s32[1280]{0:T(1024)} %param.7) | copy-start | bytes 15364
  67.9 2.4 %copy-start.2 = (f32[20,5136]{1,0:T(8,128)S(1)}, f32[20,5136]{1,0:T(8,128)}, u32[]{:S(2)}) copy-start(f32[20,5136]{1,0:T(8,128)} %sub.33) | copy-start | bytes 1232644

commit v4 on v3

--- a/solution.py
+++ b/solution.py
@@ -63,9 +63,11 @@
     waves = spec.shape[-1]
     trunc_top = waves - 1
     lev_idx = lax.axis_index("lev_g") * n_r + lax.axis_index("lev_r")
-    spec_v = spec.reshape((n_lev, per_dev) + spec.shape[1:])
+    fpd = spec.shape[2]
+    spec_v = spec.reshape(n_lev, per_dev * 2 * fpd, waves)
     gathered = lax.all_to_all(spec_v, ("lev_g", "lev_r"), split_axis=0, concat_axis=0, tiled=True)
-    fields = gathered.shape[3] * n_lev
+    gathered = gathered.reshape(n_lev, per_dev, 2, fpd, waves)
+    fields = fpd * n_lev
     first_slot = (lax.axis_index("wave") * n_lev + lev_idx) * per_dev
     my_waves = lax.dynamic_slice_in_dim(slot_wave, first_slot, per_dev)
     degree = jnp.arange(waves, dtype=jnp.int32)

time: 84.7 us -> 89.6 us (1.058)
  local copies, waits for them, and re-layouts: 12.9 us -> 21.6 us
  matrix products: 8.82 us -> 4.81 us
    reshape x0 -> x1, local copies, waits for them, and re-layouts: none -> 7.68 us  [on_device(): spec_v = spec.reshape(n_lev, per_dev * 2 * fpd, waves)]
    dot_general x1, matrix products: 4.98 us -> 0.98 us  [on_device(): jnp.einsum('lscfk,sjk->sclfj', gathered, leg2, preferred_element_type=jnp...]
    all_to_all x0 -> x1, local copies, waits for them, and re-layouts: none -> 1.97 us  [on_device(): lax.all_to_all(spec_v, ('lev_g', 'lev_r'), split_axis=0, concat_axis=0, t...]
    transpose x1, local copies, waits for them, and re-layouts: 1.44 us -> 0.41 us  [on_device(): jnp.einsum('lscfk,sjk->sclfj', gathered, leg2, preferred_element_type=jnp...]
    unnamed x29 -> x33, local copies, waits for them, and re-layouts: 2.34 us -> 2.35 us
  transfers between devices with their start and end apart: 2 -> 2, of which waited for: 2 -> 2; matrix products, arithmetic and copies ran while one was open for 33% -> 31% of each run, Pallas kernels for 0% -> 0%
where the time goes in v4:
time: 89.6 us; the launch traced here: 88.9 us
  other arithmetic  22.9 us (26%)
  local copies, waits for them, and re-layouts  21.6 us (24%)
  waiting for transfers between devices  14.9 us (17%)
  blocking collectives  11 us (12%)
  starting transfers between devices  9.31 us (10%)
  matrix products  4.81 us (5%)
  between operations  4.43 us (5%)
    all_to_all x1, waiting for transfers between devices, on_device(): lax.all_to_all(spec_v, ('lev_g', 'lev_r'), split_axis=0, concat_axis=0, t...  14.5 us
    all_to_all x1, blocking collectives, on_device(): lax.all_to_all(grid, 'lev_r', split_axis=1, concat_axis=0, tiled=True)  11 us
    cos x3, other arithmetic, trig_pair(): return (jnp.cos(theta), jnp.sin(theta))  9.09 us
    reshape x1, local copies, waits for them, and re-layouts, on_device(): spec_v = spec.reshape(n_lev, per_dev * 2 * fpd, waves)  7.68 us
    all_to_all x1, starting transfers between devices, on_device(): lax.all_to_all(spec_v, ('lev_g', 'lev_r'), split_axis=0, concat_axis=0, t...  5.3 us
    all_to_all x1, starting transfers between devices, on_device(): lax.all_to_all(fourier, ('wave', 'lev_g', 'lev_r'), split_axis=0, concat_...  4 us
    select_n x1, other arithmetic, on_device(): jnp.where(even_mask, legendre, zeros)  3.74 us
    sin x1, other arithmetic, trig_pair(): return (jnp.cos(theta), jnp.sin(theta))  2.94 us
  transfers between devices with their start and end apart: 2, of which 2 were waited for; matrix products, arithmetic and copies ran while one was open for 31% of the time, Pallas kernels for 0%

profile of v4, /device:TPU:0, one launch (start us, length us, event | category | flops | bytes accessed | tf_op | source)
XLA Modules:
  0.0 88.9 jit_solution(4236769617720743688)
XLA Ops:
  0.0 7.7 %reshape.441 = bf16[8,160,1280]{2,1,0:T(8,128)(2,1)} reshape(bf16[320,2,2,1280]{3,2,1,0:T(2,128)(2,1)} %param.5) | data formatting | bytes 6553600 | tf_op jit(solution)/shard_map/reshape | solution.py:67
  7.7 5.3 %all-to-all-start = ((bf16[8,160,1280]{2,1,0:T(8,128)(2,1)}), bf16[8,160,1280]{2,1,0:T(8,128)(2,1)S(1)}, u32[]{:S(2)}, u32[]{:S(2)}) async-start(bf16[8,160,1280]{2,1,0:T(8,128)(2,1)} %reshape.441), calls=%async_computation | async-start | bytes 6553600 | tf_op jit(solution)/shard_map/all_to_all | solution.py:68
  18.4 2.9 %fusion.58 = (f32[8,5136]{1,0:T(8,128)S(1)}, f32[8,5136]{1,0:T(8,128)}) fusion(f32[]{:T(128)S(6)} %convert_element_type.76, pred[]{:T(512)S(6)} %lt.114, s32[]{:T(128)S(6)} %select_n.141), kind=kLoop, calls=%fused_computation.81 | loop fusion | flops 451968 | bytes 328713 | tf_op jit(solution)/shard_map/sin | solution.py:18
  21.4 3.1 %fusion.61 = (f32[8,5136]{1,0:T(8,128)}, f32[8,5136]{1,0:T(8,128)}) fusion(f32[]{:T(128)S(6)} %convert_element_type.76, pred[]{:T(512)S(6)} %lt.114, s32[]{:T(128)S(6)} %select_n.141, s32[8]{0:T(128)S(1)} %iota_multiply_fusion.2), kind=kLoop, calls=%fused_computation.84 | loop fusion | flops 451968 | bytes 328745 | tf_op jit(solution)/shard_map/cos | solution.py:18
  24.5 3.1 %fusion.57 = (f32[5,5136]{1,0:T(8,128)}, f32[5,5136]{1,0:T(8,128)}) fusion(f32[]{:T(128)S(6)} %convert_element_type.76, pred[]{:T(512)S(6)} %lt.114, s32[]{:T(128)S(6)} %select_n.141, s32[5]{0:T(128)S(1)} %iota_multiply_fusion.1), kind=kLoop, calls=%fused_computation.80 | loop fusion | flops 282480 | bytes 205469 | tf_op jit(solution)/shard_map/cos | solution.py:18
  27.5 3.0 %fusion.63 = (f32[4,5136]{1,0:T(4,128)S(1)}, f32[4,5136]{1,0:T(4,128)}) fusion(f32[]{:T(128)S(6)} %convert_element_type.76, pred[]{:T(512)S(6)} %lt.114, s32[]{:T(128)S(6)} %select_n.141, s32[4]{0:T(128)S(1)} %iota_multiply_fusion), kind=kLoop, calls=%fused_computation.86 | loop fusion | flops 225984 | bytes 164377 | tf_op jit(solution)/shard_map/cos | solution.py:18
  30.5 0.8 dynamic-slice_subtract_fusion
  31.4 3.7 %broadcast_select_fusion.1 = (bf16[40,16,1280]{2,1,0:T(8,128)(2,1)}, bf16[40,16,1280]{2,1,0:T(8,128)(2,1)}) fusion(bf16[40,16,1280]{2,1,0:T(8,128)(2,1)} %param.6, pred[40,1280]{1,0:T(8,128)(4,1)S(1)} %get-tuple-element.32, pred[40,1280]{1,0:T(8,128)(4,1)S(1)} %get-tuple-element.33), kind=kLoop, calls=%fused_computation.19 | loop fusion | flops 1638400 | bytes 5017600 | tf_op jit(solution)/shard_map/jit(_where)/select_n | solution.py:79
  35.2 1.1 %multiply_subtract_fusion = (f32[5,4,5136]{2,1,0:T(4,128)}, f32[5,4,5136]{2,1,0:T(4,128)}) fusion(f32[4,5136]{1,0:T(4,128)S(1)} %copy-done.10, f32[5,5136]{1,0:T(8,128)S(1)} %copy-done.9, f32[4,5136]{1,0:T(4,128)S(1)} %get-tuple-element.30, f32[5,5136]{1,0:T(8,128)S(1)} %copy-done.8), kind=kLoop, calls=%fused_computation.31 | loop fusion | flops 616320 | bytes 1191552 | tf_op jit(solution)/shard_map/sub | solution.py:24
  36.4 1.4 %fusion.21 = (bf16[64,5136]{1,0:T(8,128)(2,1)}, bf16[64,5136]{1,0:T(8,128)(2,1)}) fusion(f32[8,5136]{1,0:T(8,128)S(1)} %get-tuple-element.36, f32[8,5136]{1,0:T(8,128)S(1)} %copy-done.7, f32[8,5136]{1,0:T(8,128)S(1)} %copy-done.5, f32[8,5136]{1,0:T(8,128)S(1)} %copy-done.6), kind=kLoop, calls=%fused_computation.27 | loop fusion | flops 2629632 | bytes 1972224 | tf_op jit(solution)/shard_map/convert_element_type | solution.py:36
  37.8 14.5 %all-to-all-done = bf16[8,160,1280]{2,1,0:T(8,128)(2,1)S(1)} async-done(((bf16[8,160,1280]{2,1,0:T(8,128)(2,1)}), bf16[8,160,1280]{2,1,0:T(8,128)(2,1)S(1)}, u32[]{:S(2)}, u32[]{:S(2)}) %all-to-all-start) | async-done | bytes 3276832 | tf_op jit(solution)/shard_map/all_to_all | solution.py:68
  52.3 2.0 %copy.14 = bf16[8,160,1280]{2,0,1:T(8,128)(2,1)S(1)} copy(bf16[8,160,1280]{2,1,0:T(8,128)(2,1)S(1)} %all-to-all-done) | data formatting | bytes 6553600 | tf_op jit(solution)/shard_map/all_to_all | solution.py:68
  54.3 1.0 %fusion.20 = f32[40,2,8,2,32]{4,2,3,1,0:T(8,128)S(1)} fusion(bf16[8,40,2,2,1280]{4,0,3,2,1:T(8,128)(2,1)S(1)} %bitcast.74, bf16[40,16,1280]{2,1,0:T(8,128)(2,1)S(1)} %copy-done.4, bf16[40,16,1280]{2,1,0:T(8,128)(2,1)S(1)} %copy-done.3), kind=kOutput, calls=%fused_computation.26 | convolution fusion | flops 111411200 | bytes 6717440 | tf_op jit(solution)/shard_map/lscfk,sjk->sclfj/dot_general | solution.py:81
  57.2 1.0 %reshape.489 = bf16[32,2,640]{2,1,0:T(2,128)(2,1)} reshape(bf16[32,1,2,16,40]{4,3,2,1,0:T(8,128)(2,1)S(1)} %bitcast.81) | data formatting | bytes 163840
  58.2 4.0 %all-to-all-start.1 = ((bf16[32,2,640]{2,1,0:T(2,128)(2,1)}), bf16[32,2,640]{2,1,0:T(2,128)(2,1)S(1)}, u32[]{:S(2)}, u32[]{:S(2)}) async-start(bf16[32,2,640]{2,1,0:T(2,128)(2,1)} %reshape.489), calls=%async_computation.1 | async-start | bytes 163840 | tf_op jit(solution)/shard_map/all_to_all | solution.py:94
  63.0 1.3 %copy.19 = bf16[64,5136]{0,1:T(8,128)(2,1)S(1)} copy(bf16[64,5136]{1,0:T(8,128)(2,1)S(1)} %copy-done.1) | data formatting | bytes 1314816 | tf_op jit(solution)/shard_map/convert_element_type | solution.py:36
  64.3 1.3 %copy.20 = bf16[64,5136]{0,1:T(8,128)(2,1)S(1)} copy(bf16[64,5136]{1,0:T(8,128)(2,1)S(1)} %copy-done) | data formatting | bytes 1314816 | tf_op jit(solution)/shard_map/convert_element_type | solution.py:37
  65.6 1.2 %add.125 = f32[20,5136]{1,0:T(8,128)S(1)} reshape(f32[5,4,5136]{2,1,0:T(4,128)} %get-tuple-element.23) | data formatting | bytes 821760 | tf_op jit(solution)/shard_map/add | solution.py:25
  66.8 1.9 %sub.33 = f32[20,5136]{1,0:T(8,128)} reshape(f32[5,4,5136]{2,1,0:T(4,128)} %get-tuple-element.22) | data formatting | bytes 821760 | tf_op jit(solution)/shard_map/sub | solution.py:24
  70.7 1.4 %fusion.14 = bf16[2,16,1280]{2,1,0:T(8,128)(2,1)S(1)} fusion(bf16[2,16,1280]{2,1,0:T(8,128)(2,1)S(1)} %reshape.445, s32[1280]{0:T(1024)S(1)} %copy-done.11, f32[1280]{0:T(1024)S(1)} %select_select_fusion), kind=kOutput, calls=%fused_computation.17 | convolution fusion | flops 106577920 | bytes 174080 | tf_op jit(solution)/shard_map/cfrs,sm->cfrm/dot_general | solution.py:100
  72.6 2.4 %fusion.17 = f32[2,16,20,5136]{3,2,1,0:T(8,128)S(1)} fusion(bf16[64,5136]{0,1:T(8,128)(2,1)S(1)} %copy.20, bf16[64,5136]{0,1:T(8,128)(2,1)S(1)} %copy.19, bf16[1,16,20,128]{3,2,1,0:T(8,128)(2,1)S(1)} %get-tuple-element.25, bf16[1,16,20,128]{3,2,1,0:T(8,128)(2,1)S(1)} %get-tuple-element.24), kind=kOutput, calls=%fused_computation.23 | convolution fusion | flops 844193792 | bytes 14626816 | tf_op jit(solution)/shard_map/dfab,bi->dfai/dot_general | solution.py:51
  75.0 1.8 %fusion.2 = f32[16,5136]{1,0:T(8,128)S(1)} fusion(f32[2,16,20,5136]{3,2,1,0:T(8,128)S(1)} %fusion.17, f32[20,5136]{1,0:T(8,128)S(1)} %add.125, f32[20,5136]{1,0:T(8,128)S(1)} %copy-done.2), kind=kLoop, calls=%fused_computation.5 | loop fusion | flops 6491904 | bytes 14298624 | tf_op jit(solution)/shard_map/reduce_sum | solution.py:52
  77.2 11.0 %all_to_all.19 = f32[1,8,2,5136]{3,2,0,1:T(2,128)S(1)} all-to-all(f32[1,8,2,5136]{3,2,0,1:T(2,128)S(1)} %broadcast_select_fusion.2), channel_id=1, replica_groups=mesh['wave'=4,'lev'=8] {'lev'}, dimensions={1} | all-to-all | bytes 657408 | tf_op jit(solution)/shard_map/all_to_all | solution.py:115
  88.2 0.7 copy.30
  (60 shorter events, 6.9 us)
Async XLA Ops:
  7.7 5.3 %copy-start.12 = (s32[32]{0:T(128)S(1)}, s32[32]{0:T(128)}, u32[]{:S(2)}) copy-start(s32[32]{0:T(128)} %param.9) | copy-start | bytes 388
  7.7 7.9 %copy-start.13 = (s32[32]{0:T(128)S(1)}, s32[32]{0:T(128)}, u32[]{:S(2)}) copy-start(s32[32]{0:T(128)} %param.8) | copy-start | bytes 388
  7.7 44.6 %all-to-all-start = ((bf16[8,160,1280]{2,1,0:T(8,128)(2,1)}), bf16[8,160,1280]{2,1,0:T(8,128)(2,1)S(1)}, u32[]{:S(2)}, u32[]{:S(2)}) async-start(bf16[8,160,1280]{2,1,0:T(8,128)(2,1)} %reshape.441), calls=%async_computation | async-start | bytes 6553600 | tf_op jit(solution)/shard_map/all_to_all | solution.py:68
  31.4 3.8 %copy-start.8 = (f32[5,5136]{1,0:T(8,128)S(1)}, f32[5,5136]{1,0:T(8,128)}, u32[]{:S(2)}) copy-start(f32[5,5136]{1,0:T(8,128)} %get-tuple-element.28) | copy-start | bytes 308164
  31.4 3.8 %copy-start.9 = (f32[5,5136]{1,0:T(8,128)S(1)}, f32[5,5136]{1,0:T(8,128)}, u32[]{:S(2)}) copy-start(f32[5,5136]{1,0:T(8,128)} %get-tuple-element.29) | copy-start | bytes 308164
  31.4 3.8 %copy-start.10 = (f32[4,5136]{1,0:T(4,128)S(1)}, f32[4,5136]{1,0:T(4,128)}, u32[]{:S(2)}) copy-start(f32[4,5136]{1,0:T(4,128)} %get-tuple-element.31) | copy-start | bytes 246532
  31.4 4.9 %copy-start.5 = (f32[8,5136]{1,0:T(8,128)S(1)}, f32[8,5136]{1,0:T(8,128)}, u32[]{:S(2)}) copy-start(f32[8,5136]{1,0:T(8,128)} %get-tuple-element.37) | copy-start | bytes 493060
  31.4 4.9 %copy-start.6 = (f32[8,5136]{1,0:T(8,128)S(1)}, f32[8,5136]{1,0:T(8,128)}, u32[]{:S(2)}) copy-start(f32[8,5136]{1,0:T(8,128)} %get-tuple-element.34) | copy-start | bytes 493060
  31.4 4.9 %copy-start.7 = (f32[8,5136]{1,0:T(8,128)S(1)}, f32[8,5136]{1,0:T(8,128)}, u32[]{:S(2)}) copy-start(f32[8,5136]{1,0:T(8,128)} %get-tuple-element.35) | copy-start | bytes 493060
  52.3 2.0 %copy-start.3 = (bf16[40,16,1280]{2,1,0:T(8,128)(2,1)S(1)}, bf16[40,16,1280]{2,1,0:T(8,128)(2,1)}, u32[]{:S(2)}) copy-start(bf16[40,16,1280]{2,1,0:T(8,128)(2,1)} %get-tuple-element.16) | copy-start | bytes 4915204
  52.3 2.0 %copy-start.4 = (bf16[40,16,1280]{2,1,0:T(8,128)(2,1)S(1)}, bf16[40,16,1280]{2,1,0:T(8,128)(2,1)}, u32[]{:S(2)}) copy-start(bf16[40,16,1280]{2,1,0:T(8,128)(2,1)} %get-tuple-element.17) | copy-start | bytes 4915204
  56.5 6.5 %copy-start.1 = (bf16[64,5136]{1,0:T(8,128)(2,1)S(1)}, bf16[64,5136]{1,0:T(8,128)(2,1)}, u32[]{:S(2)}) copy-start(bf16[64,5136]{1,0:T(8,128)(2,1)} %get-tuple-element.18) | copy-start | bytes 1972228
  57.1 7.2 %copy-start = (bf16[64,5136]{1,0:T(8,128)(2,1)S(1)}, bf16[64,5136]{1,0:T(8,128)(2,1)}, u32[]{:S(2)}) copy-start(bf16[64,5136]{1,0:T(8,128)(2,1)} %get-tuple-element.19) | copy-start | bytes 1972228
  58.2 11.6 %all-to-all-start.1 = ((bf16[32,2,640]{2,1,0:T(2,128)(2,1)}), bf16[32,2,640]{2,1,0:T(2,128)(2,1)S(1)}, u32[]{:S(2)}, u32[]{:S(2)}) async-start(bf16[32,2,640]{2,1,0:T(2,128)(2,1)} %reshape.489), calls=%async_computation.1 | async-start | bytes 163840 | tf_op jit(solution)/shard_map/all_to_all | solution.py:94
  65.6 5.1 %copy-start.11 = (s32[1280]{0:T(1024)S(1)}, s32[1280]{0:T(1024)}, u32[]{:S(2)}) copy-start(s32[1280]{0:T(1024)} %param.7) | copy-start | bytes 15364
  72.6 2.4 %copy-start.2 = (f32[20,5136]{1,0:T(8,128)S(1)}, f32[20,5136]{1,0:T(8,128)}, u32[]{:S(2)}) copy-start(f32[20,5136]{1,0:T(8,128)} %sub.33) | copy-start | bytes 1232644

commit v5 on v3

--- a/solution.py
+++ b/solution.py
@@ -12,42 +12,63 @@
     return 2.0 * math.pi * remainder.astype(jnp.float32) / points.astype(jnp.float32)
 
 
-def trig_pair(step, lon_idx, points, count):
-    mult = jnp.arange(count, dtype=jnp.int32)[:, None] * step
-    theta = angles(mult * lon_idx[None, :] % points, points)
-    return jnp.cos(theta), jnp.sin(theta)
+def cmul(x, y):
+    return x[0] * y[0] - x[1] * y[1], x[0] * y[1] + x[1] * y[0]
 
 
-def compose(first, second):
+def powers(base, count):
+    out = [(jnp.ones_like(base[0]), jnp.zeros_like(base[1])), base]
+    while len(out) < count:
+        out.append(cmul(out[-1], base))
+    out = out[:count]
+    return jnp.stack([o[0] for o in out], 1), jnp.stack([o[1] for o in out], 1)
+
+
+def outer(first, second):
     c0, s0 = first
     c1, s1 = second
-    cos = c1[:, None] * c0[None] - s1[:, None] * s0[None]
-    sin = s1[:, None] * c0[None] + c1[:, None] * s0[None]
-    return cos.reshape(-1, cos.shape[-1]), sin.reshape(-1, sin.shape[-1])
+    cos = c1[:, :, None] * c0[:, None] - s1[:, :, None] * s0[:, None]
+    sin = s1[:, :, None] * c0[:, None] + c1[:, :, None] * s0[:, None]
+    shape = (cos.shape[0], -1, cos.shape[-1])
+    return cos.reshape(shape), sin.reshape(shape)
 
 
-def row_synthesis(coef_row, points):
+def rows_tables(points, waves):
+    ablocks = waves // 64
+    lon_len = 20 + 4 * (waves - 1)
+    lon_idx = jnp.arange(lon_len, dtype=jnp.int32)
+    pts = points[:, None]
+    steps = jnp.array([1, 64], dtype=jnp.int32)[:, None, None]
+    theta = angles(steps * lon_idx[None, None, :] % pts[None], pts[None])
+    dc, ds = lax.optimization_barrier((jnp.cos(theta), jnp.sin(theta)))
+    e1 = (dc[0], ds[0])
+    e64 = (dc[1], ds[1])
+    lo = powers(e1, 8)
+    e8 = cmul((lo[0][:, 7], lo[1][:, 7]), e1)
+    hi = powers(e8, 8)
+    cos_t, sin_t = outer(lo, hi)
+    rhs = jnp.concatenate([cos_t.astype(jnp.bfloat16), sin_t.astype(jnp.bfloat16)], 1)
+    p0 = powers(e64, 4)
+    e256 = cmul((p0[0][:, 3], p0[1][:, 3]), e64)
+    n_a1 = -(-ablocks // 4)
+    p1 = powers(e256, n_a1)
+    return rhs, p0, p1
+
+
+def row_synthesis(coef_row, rhs, p0c, p0s, p1c, p1s, points):
     fields = coef_row.shape[1]
     waves = coef_row.shape[2]
     ablocks = waves // 64
-    lon_len = 20 + 4 * (waves - 1)
-    lon_idx = jnp.arange(lon_len, dtype=jnp.int32)
-    cos_t, sin_t = compose(trig_pair(1, lon_idx, points, 8), trig_pair(8, lon_idx, points, 8))
-    cosb = cos_t.astype(jnp.bfloat16)
-    sinb = sin_t.astype(jnp.bfloat16)
-    n_a1 = -(-ablocks // 4)
-    cosp, sinp = compose(
-        trig_pair(64, lon_idx, points, 4), trig_pair(256, lon_idx, points, n_a1)
-    )
-    cosp = cosp[:ablocks]
-    sinp = sinp[:ablocks]
+    lon_idx = jnp.arange(rhs.shape[-1], dtype=jnp.int32)
+    cosp, sinp = outer((p0c[None], p0s[None]), (p1c[None], p1s[None]))
+    cosp = cosp[0, :ablocks]
+    sinp = sinp[0, :ablocks]
     blocks = coef_row.reshape(2, fields, ablocks, 64)
     c0 = blocks[0]
     c1 = blocks[1]
     lhs = jnp.stack(
         [jnp.concatenate([c0, -c1], -1), jnp.concatenate([c1, c0], -1)], 0
     )
-    rhs = jnp.concatenate([cosb, sinb], 0)
     part = jnp.einsum("dfab,bi->dfai", lhs, rhs, preferred_element_type=jnp.float32)
     total = jnp.sum(part[0] * cosp[None] - part[1] * sinp[None], axis=1)
     return jnp.where(lon_idx[None, :] < points, total, jnp.zeros_like(total))
@@ -66,6 +87,10 @@
     spec_v = spec.reshape((n_lev, per_dev) + spec.shape[1:])
     gathered = lax.all_to_all(spec_v, ("lev_g", "lev_r"), split_axis=0, concat_axis=0, tiled=True)
     fields = gathered.shape[3] * n_lev
+    first_row = (lax.axis_index("wave") * n_r + lax.axis_index("lev_r")) * rows_per_dev
+    my_rows = lax.dynamic_slice_in_dim(band_rows, first_row, rows_per_dev)
+    row_points = row_lons[my_rows]
+    rhs_all, p0_all, p1_all = rows_tables(row_points, waves)
     first_slot = (lax.axis_index("wave") * n_lev + lev_idx) * per_dev
     my_waves = lax.dynamic_slice_in_dim(slot_wave, first_slot, per_dev)
     degree = jnp.arange(waves, dtype=jnp.int32)
@@ -96,17 +121,13 @@
     wave_idx = jnp.arange(waves, dtype=jnp.int32)
     onehot = (slot_wave[:, None] == wave_idx[None, :]).astype(jnp.bfloat16)
     coef = jnp.einsum("cfrs,sm->cfrm", banded, onehot, preferred_element_type=jnp.float32)
-    first_row = (lax.axis_index("wave") * n_r + lax.axis_index("lev_r")) * rows_per_dev
-    my_rows = lax.dynamic_slice_in_dim(band_rows, first_row, rows_per_dev)
-    row_points = row_lons[my_rows]
     keep = 2 * wave_idx[None, :] < row_points[:, None]
     factor = jnp.where(keep, jnp.where(wave_idx[None, :] == 0, 1.0, 2.0), 0.0).astype(jnp.float32)
     coef = (coef * factor[None, None]).astype(jnp.bfloat16)
     coef_rows = jnp.moveaxis(coef, 2, 0)
-    if rows_per_dev == 1:
-        grid = row_synthesis(coef_rows[0], row_points[0])[None]
-    else:
-        grid = lax.map(lambda item: row_synthesis(item[0], item[1]), (coef_rows, row_points))
+    grid = lax.map(
+        lambda item: row_synthesis(*item), (coef_rows, rhs_all, p0_all[0], p0_all[1], p1_all[0], p1_all[1], row_points)
+    )
     lon = grid.shape[-1]
     fpd = fpg // n_r
     grid = grid.reshape(rows_per_dev, n_r, fpd, lon)
@@ -119,12 +140,8 @@
         n_wave = mesh.shape["wave"]
         n_lev = mesh.shape["lev"]
         rows_w = band_rows.shape[0] // n_wave
-        if n_lev >= rows_w:
-            n_r = rows_w
-            rows_per_dev = 1
-        else:
-            n_r = n_lev
-            rows_per_dev = rows_w // n_lev
+        n_r = 1
+        rows_per_dev = rows_w
         n_g = n_lev // n_r
         devs = np.asarray(mesh.devices).reshape(n_wave, n_g, n_r)
         mesh2 = Mesh(devs, ("wave", "lev_g", "lev_r"))

time: 84.7 us -> 146 us (1.72)
  local copies, waits for them, and re-layouts: 12.9 us -> 65 us
  other arithmetic: 22.6 us -> 42.8 us
  waiting for transfers between devices: 15.4 us -> 0.01 us
  matrix products: 8.82 us -> 23.9 us
  blocking collectives: 10.9 us -> 0 us
  between operations: 4.24 us -> 0.35 us
  starting transfers between devices: 9.31 us -> 12.3 us
    dynamic_slice x1 -> x56, local copies, waits for them, and re-layouts: 0.59 us -> 29.4 us  [on_device(): lax.map(lambda item: row_synthesis(*item), (coef_rows, rhs_all, p0_all[0]...]
    dot_general x1 -> x8, matrix products: 2.43 us -> 18 us  [row_synthesis(): jnp.einsum('dfab,bi->dfai', lhs, rhs, preferred_element_type=jnp.float32)]
    all_to_all x1, waiting for transfers between devices: 14.9 us -> 0.01 us  [on_device(): lax.all_to_all(spec_v, ('lev_g', 'lev_r'), split_axis=0, concat_axis=0, t...]
    while x0 -> x2, local copies, waits for them, and re-layouts: none -> 14 us  [on_device(): lax.map(lambda item: row_synthesis(*item), (coef_rows, rhs_all, p0_all[0]...]
    all_to_all x1 -> x0, blocking collectives: 10.9 us -> none  [on_device(): lax.all_to_all(grid, 'lev_r', split_axis=1, concat_axis=0, tiled=True)]
    cos x3 -> x0, other arithmetic: 9.06 us -> none  [trig_pair(): return (jnp.cos(theta), jnp.sin(theta))]
    unnamed x0 -> x17, other arithmetic: none -> 7.41 us
    unnamed x29 -> x40, local copies, waits for them, and re-layouts: 2.34 us -> 9.64 us
  transfers between devices with their start and end apart: 2 -> 2, of which waited for: 2 -> 0; matrix products, arithmetic and copies ran while one was open for 33% -> 35% of each run, Pallas kernels for 0% -> 0%
where the time goes in v5:
time: 146 us; the launch traced here: 145 us
  local copies, waits for them, and re-layouts  65 us (45%)
  other arithmetic  42.8 us (29%)
  matrix products  23.9 us (16%)
  starting transfers between devices  12.3 us (8%)
    dynamic_slice x56, local copies, waits for them, and re-layouts, on_device(): lax.map(lambda item: row_synthesis(*item), (coef_rows, rhs_all, p0_all[0]...  29.4 us
    dot_general x8, matrix products, row_synthesis(): jnp.einsum('dfab,bi->dfai', lhs, rhs, preferred_element_type=jnp.float32)  18 us
    while x2, local copies, waits for them, and re-layouts, on_device(): lax.map(lambda item: row_synthesis(*item), (coef_rows, rhs_all, p0_all[0]...  14 us
    unnamed x40, local copies, waits for them, and re-layouts  9.64 us
    unnamed x17, other arithmetic  7.41 us
    all_to_all x1, starting transfers between devices, on_device(): lax.all_to_all(fourier, ('wave', 'lev_g', 'lev_r'), split_axis=0, concat_...  6.95 us
    concatenate x1, other arithmetic, rows_tables(): jnp.concatenate([cos_t.astype(jnp.bfloat16), sin_t.astype(jnp.bfloat16)], 1)  5.5 us
    all_to_all x1, starting transfers between devices, on_device(): lax.all_to_all(spec_v, ('lev_g', 'lev_r'), split_axis=0, concat_axis=0, t...  5.3 us
  transfers between devices with their start and end apart: 2, of which 0 were waited for; matrix products, arithmetic and copies ran while one was open for 35% of the time, Pallas kernels for 0%

profile of v5, /device:TPU:0, one launch (start us, length us, event | category | flops | bytes accessed | tf_op | source)
XLA Modules:
  0.0 144.9 jit_solution(637917910465926185)
XLA Ops:
  0.0 5.3 %all-to-all-start = ((bf16[8,40,2,2,1280]{4,3,2,1,0:T(2,128)(2,1)}), bf16[8,40,2,2,1280]{4,3,2,1,0:T(2,128)(2,1)}, u32[]{:S(2)}, u32[]{:S(2)}) async-start(bf16[8,40,2,2,1280]{4,3,2,1,0:T(2,128)(2,1)} %bitcast.393), calls=%async_computation | async-start | bytes 6553600 | tf_op jit(solution)/shard_map/all_to_all | solution.py:88
  9.0 4.5 %fusion.81 = (f32[2,8,5136]{2,1,0:T(8,128)S(1)}, f32[2,8,5136]{2,1,0:T(8,128)S(1)}) fusion(f32[8]{0:T(128)S(1)} %get-tuple-element.176, pred[8]{0:T(512)(128)(4,1)S(1)} %broadcast_compare_fusion, s32[8]{0:T(128)S(1)} %get-tuple-element.175, s32[2,5136]{1,0:T(2,128)S(1)} %iota_multiply_fusion), kind=kLoop, calls=%fused_computation.165 | loop fusion | flops 821760 | bytes 698568 | tf_op jit(solution)/shard_map/sin | solution.py:43
  23.9 1.7 %copy.57 = f32[8,8,5136]{2,1,0:T(8,128)S(1)} copy(f32[8,8,5136]{2,0,1:T(8,128)} %copy-done.2) | data formatting | bytes 2629632 | tf_op jit(solution)/shard_map/stack | solution.py:24
  30.4 4.5 %fusion.16 = (bf16[8,64,5136]{2,1,0:T(8,128)(2,1)S(1)}, bf16[8,64,5136]{2,1,0:T(8,128)(2,1)S(1)}) fusion(f32[8,8,5136]{2,1,0:T(8,128)S(1)} %copy.58, f32[8,8,5136]{2,1,0:T(8,128)S(1)} %copy.57, f32[8,8,5136]{2,1,0:T(8,128)} %copy.56, f32[8,8,5136]{2,1,0:T(8,128)} %copy.55), kind=kLoop, calls=%fused_computation.40 | loop fusion | flops 21037056 | bytes 15777792 | tf_op jit(solution)/shard_map/convert_element_type | solution.py:50
  34.9 5.5 %pad_maximum_fusion = bf16[8,128,5136]{2,1,0:T(8,128)(2,1)} fusion(bf16[8,64,5136]{2,1,0:T(8,128)(2,1)S(1)} %get-tuple-element.141, bf16[8,64,5136]{2,1,0:T(8,128)(2,1)S(1)} %get-tuple-element.140), kind=kLoop, calls=%fused_computation.34 | loop fusion | flops 21037056 | bytes 21037056 | tf_op jit(solution)/shard_map/concatenate | solution.py:50
  40.6 1.7 %broadcast_select_fusion.1 = (bf16[40,16,1280]{2,1,0:T(8,128)(2,1)S(1)}, bf16[40,16,1280]{2,1,0:T(8,128)(2,1)}) fusion(bf16[40,16,1280]{2,1,0:T(8,128)(2,1)S(1)} %copy-done.7, pred[40,1280]{1,0:T(8,128)(4,1)S(1)} %get-tuple-element.177, pred[40,1280]{1,0:T(8,128)(4,1)S(1)} %get-tuple-element.178), kind=kLoop, calls=%fused_computation.52 | loop fusion | flops 1638400 | bytes 5017600 | tf_op jit(solution)/shard_map/jit(_where)/select_n | solution.py:102
  45.9 4.5 %fusion.32 = f32[40,2,8,2,32]{4,2,3,1,0:T(8,128)S(1)} fusion(bf16[8,40,2,2,1280]{4,3,2,1,0:T(2,128)(2,1)} %all-to-all-done, bf16[40,16,1280]{2,1,0:T(8,128)(2,1)} %get-tuple-element.143, bf16[40,16,1280]{2,1,0:T(8,128)(2,1)S(1)} %get-tuple-element.142), kind=kOutput, calls=%fused_computation.53 | convolution fusion | flops 111411200 | bytes 6717440 | tf_op jit(solution)/shard_map/lscfk,sjk->sclfj/dot_general | solution.py:104
  54.1 6.9 %all-to-all-start.1 = ((bf16[32,2,640]{2,1,0:T(2,128)(2,1)}), bf16[32,2,640]{2,1,0:T(2,128)(2,1)S(1)}, u32[]{:S(2)}, u32[]{:S(2)}) async-start(bf16[32,2,640]{2,1,0:T(2,128)(2,1)} %reshape.2830), calls=%async_computation.1 | async-start | bytes 163840 | tf_op jit(solution)/shard_map/all_to_all | solution.py:117
  61.1 13.9 %copy.60 = bf16[8,128,5136]{1,2,0:T(8,128)(2,1)} copy(bf16[8,128,5136]{2,1,0:T(8,128)(2,1)} %pad_maximum_fusion) | data formatting | bytes 21037056 | tf_op jit(solution)/shard_map/while | solution.py:128
  77.3 67.0 %while.10 = (s32[]{:T(128)}, f32[8,2,5136]{2,1,0:T(2,128)}, s32[8]{0:T(128)S(1)}, bf16[8,2,2,1280]{3,2,1,0:T(2,128)(2,1)S(1)}, bf16[8,128,5136]{1,2,0:T(8,128)(2...) while((s32[]{:T(128)}, f32[8,2,5136]{2,1,0:T(2,128)}, ...), condition=%wide.region_2.3_spmd, body=%wide.region_0.2_spmd.sunk | while | flops 106682256 | bytes 9979985 | solution.py:128
  77.6 2.3 %fusion.106 = f32[2,2,20,5136]{3,2,1,0:T(8,128)S(1)} fusion(bf16[8,128,5136]{1,2,0:T(8,128)(2,1)} %get-tuple-element.288, s32[]{:T(128)S(6)} %copy.138, bf16[1,2,20,128]{3,2,1,0:T(8,128)(2,1)S(1)} %get-tuple-element.252, bf16[1,2,20,128]{3,2,1,0:T(8,128)(2,1)S(1)} %get-tuple-element.253), kind=kOutput, calls=%fused_computation.3.clone.1 | convolution fusion | flops 105195520 | bytes 2978820 | tf_op jit(solution)/shard_map/while/body/eval_jaxpr/dfab,bi->dfai/dot_general | solution.py:72
  81.3 1.6 %constant_dynamic-slice_fusion.11 = (f32[1,5,5136]{2,0,1:T(1,128)S(1)}, f32[1,5,5136]{2,0,1:T(1,128)S(1)}) fusion(f32[8,5,5136]{2,0,1:T(8,128)} %get-tuple-element.291, s32[]{:T(128)S(6)} %copy.138, f32[8,5,5136]{2,0,1:T(8,128)} %get-tuple-element.289), kind=kLoop, calls=%fused_computation.28.clone.1 | loop fusion | bytes 410884 | tf_op jit(solution)/shard_map/while/body/jit(dynamic_index_in_dim)/dynamic_slice | solution.py:128
  86.0 2.3 %fusion.106 = f32[2,2,20,5136]{3,2,1,0:T(8,128)S(1)} fusion(bf16[8,128,5136]{1,2,0:T(8,128)(2,1)} %get-tuple-element.288, s32[]{:T(128)S(6)} %copy.138, bf16[1,2,20,128]{3,2,1,0:T(8,128)(2,1)S(1)} %get-tuple-element.252, bf16[1,2,20,128]{3,2,1,0:T(8,128)(2,1)S(1)} %get-tuple-element.253), kind=kOutput, calls=%fused_computation.3.clone.1 | convolution fusion | flops 105195520 | bytes 2978820 | tf_op jit(solution)/shard_map/while/body/eval_jaxpr/dfab,bi->dfai/dot_general | solution.py:72
  89.7 1.6 %constant_dynamic-slice_fusion.11 = (f32[1,5,5136]{2,0,1:T(1,128)S(1)}, f32[1,5,5136]{2,0,1:T(1,128)S(1)}) fusion(f32[8,5,5136]{2,0,1:T(8,128)} %get-tuple-element.291, s32[]{:T(128)S(6)} %copy.138, f32[8,5,5136]{2,0,1:T(8,128)} %get-tuple-element.289), kind=kLoop, calls=%fused_computation.28.clone.1 | loop fusion | bytes 410884 | tf_op jit(solution)/shard_map/while/body/jit(dynamic_index_in_dim)/dynamic_slice | solution.py:128
  94.4 2.3 %fusion.106 = f32[2,2,20,5136]{3,2,1,0:T(8,128)S(1)} fusion(bf16[8,128,5136]{1,2,0:T(8,128)(2,1)} %get-tuple-element.288, s32[]{:T(128)S(6)} %copy.138, bf16[1,2,20,128]{3,2,1,0:T(8,128)(2,1)S(1)} %get-tuple-element.252, bf16[1,2,20,128]{3,2,1,0:T(8,128)(2,1)S(1)} %get-tuple-element.253), kind=kOutput, calls=%fused_computation.3.clone.1 | convolution fusion | flops 105195520 | bytes 2978820 | tf_op jit(solution)/shard_map/while/body/eval_jaxpr/dfab,bi->dfai/dot_general | solution.py:72
  98.1 1.6 %constant_dynamic-slice_fusion.11 = (f32[1,5,5136]{2,0,1:T(1,128)S(1)}, f32[1,5,5136]{2,0,1:T(1,128)S(1)}) fusion(f32[8,5,5136]{2,0,1:T(8,128)} %get-tuple-element.291, s32[]{:T(128)S(6)} %copy.138, f32[8,5,5136]{2,0,1:T(8,128)} %get-tuple-element.289), kind=kLoop, calls=%fused_computation.28.clone.1 | loop fusion | bytes 410884 | tf_op jit(solution)/shard_map/while/body/jit(dynamic_index_in_dim)/dynamic_slice | solution.py:128
  102.7 2.3 %fusion.106 = f32[2,2,20,5136]{3,2,1,0:T(8,128)S(1)} fusion(bf16[8,128,5136]{1,2,0:T(8,128)(2,1)} %get-tuple-element.288, s32[]{:T(128)S(6)} %copy.138, bf16[1,2,20,128]{3,2,1,0:T(8,128)(2,1)S(1)} %get-tuple-element.252, bf16[1,2,20,128]{3,2,1,0:T(8,128)(2,1)S(1)} %get-tuple-element.253), kind=kOutput, calls=%fused_computation.3.clone.1 | convolution fusion | flops 105195520 | bytes 2978820 | tf_op jit(solution)/shard_map/while/body/eval_jaxpr/dfab,bi->dfai/dot_general | solution.py:72
  106.4 1.6 %constant_dynamic-slice_fusion.11 = (f32[1,5,5136]{2,0,1:T(1,128)S(1)}, f32[1,5,5136]{2,0,1:T(1,128)S(1)}) fusion(f32[8,5,5136]{2,0,1:T(8,128)} %get-tuple-element.291, s32[]{:T(128)S(6)} %copy.138, f32[8,5,5136]{2,0,1:T(8,128)} %get-tuple-element.289), kind=kLoop, calls=%fused_computation.28.clone.1 | loop fusion | bytes 410884 | tf_op jit(solution)/shard_map/while/body/jit(dynamic_index_in_dim)/dynamic_slice | solution.py:128
  111.1 2.3 %fusion.106 = f32[2,2,20,5136]{3,2,1,0:T(8,128)S(1)} fusion(bf16[8,128,5136]{1,2,0:T(8,128)(2,1)} %get-tuple-element.288, s32[]{:T(128)S(6)} %copy.138, bf16[1,2,20,128]{3,2,1,0:T(8,128)(2,1)S(1)} %get-tuple-element.252, bf16[1,2,20,128]{3,2,1,0:T(8,128)(2,1)S(1)} %get-tuple-element.253), kind=kOutput, calls=%fused_computation.3.clone.1 | convolution fusion | flops 105195520 | bytes 2978820 | tf_op jit(solution)/shard_map/while/body/eval_jaxpr/dfab,bi->dfai/dot_general | solution.py:72
  114.8 1.6 %constant_dynamic-slice_fusion.11 = (f32[1,5,5136]{2,0,1:T(1,128)S(1)}, f32[1,5,5136]{2,0,1:T(1,128)S(1)}) fusion(f32[8,5,5136]{2,0,1:T(8,128)} %get-tuple-element.291, s32[]{:T(128)S(6)} %copy.138, f32[8,5,5136]{2,0,1:T(8,128)} %get-tuple-element.289), kind=kLoop, calls=%fused_computation.28.clone.1 | loop fusion | bytes 410884 | tf_op jit(solution)/shard_map/while/body/jit(dynamic_index_in_dim)/dynamic_slice | solution.py:128
  119.5 2.3 %fusion.106 = f32[2,2,20,5136]{3,2,1,0:T(8,128)S(1)} fusion(bf16[8,128,5136]{1,2,0:T(8,128)(2,1)} %get-tuple-element.288, s32[]{:T(128)S(6)} %copy.138, bf16[1,2,20,128]{3,2,1,0:T(8,128)(2,1)S(1)} %get-tuple-element.252, bf16[1,2,20,128]{3,2,1,0:T(8,128)(2,1)S(1)} %get-tuple-element.253), kind=kOutput, calls=%fused_computation.3.clone.1 | convolution fusion | flops 105195520 | bytes 2978820 | tf_op jit(solution)/shard_map/while/body/eval_jaxpr/dfab,bi->dfai/dot_general | solution.py:72
  127.8 2.3 %fusion.106 = f32[2,2,20,5136]{3,2,1,0:T(8,128)S(1)} fusion(bf16[8,128,5136]{1,2,0:T(8,128)(2,1)} %get-tuple-element.288, s32[]{:T(128)S(6)} %copy.138, bf16[1,2,20,128]{3,2,1,0:T(8,128)(2,1)S(1)} %get-tuple-element.252, bf16[1,2,20,128]{3,2,1,0:T(8,128)(2,1)S(1)} %get-tuple-element.253), kind=kOutput, calls=%fused_computation.3.clone.1 | convolution fusion | flops 105195520 | bytes 2978820 | tf_op jit(solution)/shard_map/while/body/eval_jaxpr/dfab,bi->dfai/dot_general | solution.py:72
  136.2 2.3 %fusion.106 = f32[2,2,20,5136]{3,2,1,0:T(8,128)S(1)} fusion(bf16[8,128,5136]{1,2,0:T(8,128)(2,1)} %get-tuple-element.288, s32[]{:T(128)S(6)} %copy.138, bf16[1,2,20,128]{3,2,1,0:T(8,128)(2,1)S(1)} %get-tuple-element.252, bf16[1,2,20,128]{3,2,1,0:T(8,128)(2,1)S(1)} %get-tuple-element.253), kind=kOutput, calls=%fused_computation.3.clone.1 | convolution fusion | flops 105195520 | bytes 2978820 | tf_op jit(solution)/shard_map/while/body/eval_jaxpr/dfab,bi->dfai/dot_general | solution.py:72
  139.9 1.6 %constant_dynamic-slice_fusion.11 = (f32[1,5,5136]{2,0,1:T(1,128)S(1)}, f32[1,5,5136]{2,0,1:T(1,128)S(1)}) fusion(f32[8,5,5136]{2,0,1:T(8,128)} %get-tuple-element.291, s32[]{:T(128)S(6)} %copy.138, f32[8,5,5136]{2,0,1:T(8,128)} %get-tuple-element.289), kind=kLoop, calls=%fused_computation.28.clone.1 | loop fusion | bytes 410884 | tf_op jit(solution)/shard_map/while/body/jit(dynamic_index_in_dim)/dynamic_slice | solution.py:128
  (237 shorter events, 68.1 us)
Async XLA Ops:
  0.0 6.1 %copy-start = (s32[32]{0:T(128)S(1)}, s32[32]{0:T(128)}, u32[]{:S(2)}) copy-start(s32[32]{0:T(128)} %param.11) | copy-start | bytes 388
  0.0 5.3 %copy-start.13 = (s32[32]{0:T(128)S(1)}, s32[32]{0:T(128)}, u32[]{:S(2)}) copy-start(s32[32]{0:T(128)} %param.12) | copy-start | bytes 388
  0.0 45.9 %all-to-all-start = ((bf16[8,40,2,2,1280]{4,3,2,1,0:T(2,128)(2,1)}), bf16[8,40,2,2,1280]{4,3,2,1,0:T(2,128)(2,1)}, u32[]{:S(2)}, u32[]{:S(2)}) async-start(bf16[8,40,2,2,1280]{4,3,2,1,0:T(2,128)(2,1)} %bitcast.393), calls=%async_computation | async-start | bytes 6553600 | tf_op jit(solution)/shard_map/all_to_all | solution.py:88
  5.3 3.6 %copy-start.11 = (s32[2]{0:T(128)S(1)}, s32[2]{0:T(128)}, u32[]{:S(2)}) copy-start(s32[2]{0:T(128)} %constant.93.clone) | copy-start | bytes 28
  14.8 3.2 %copy-start.5 = (f32[8,8,5136]{2,0,1:T(8,128)S(1)}, f32[8,8,5136]{2,0,1:T(8,128)}, u32[]{:S(2)}) copy-start(f32[8,8,5136]{2,0,1:T(8,128)} %constant_dynamic-update-slice_fusion.1) | copy-start | bytes 3944452
  19.1 1.3 copy-start.6
  20.6 1.1 copy-start.3
  22.8 1.1 copy-start.2
  23.9 1.7 %copy-start.4 = (f32[8,8,5136]{2,0,1:T(8,128)S(1)}, f32[8,8,5136]{2,0,1:T(8,128)}, u32[]{:S(2)}) copy-start(f32[8,8,5136]{2,0,1:T(8,128)} %copy-done.3) | copy-start | bytes 3944452
  34.9 5.6 %copy-start.7 = (bf16[40,16,1280]{2,1,0:T(8,128)(2,1)S(1)}, bf16[40,16,1280]{2,1,0:T(8,128)(2,1)}, u32[]{:S(2)}) copy-start(bf16[40,16,1280]{2,1,0:T(8,128)(2,1)} %param.9) | copy-start | bytes 4915204
  40.6 1.7 %copy-start.9 = (f32[8,1,5136]{2,0,1:T(8,128)S(1)}, f32[8,1,5136]{2,0,1:T(8,128)}, u32[]{:S(2)}) copy-start(f32[8,1,5136]{2,0,1:T(8,128)} %get-tuple-element.146) | copy-start | bytes 493060
  40.6 1.7 %copy-start.10 = (f32[8,1,5136]{2,0,1:T(8,128)S(1)}, f32[8,1,5136]{2,0,1:T(8,128)}, u32[]{:S(2)}) copy-start(f32[8,1,5136]{2,0,1:T(8,128)} %get-tuple-element.147) | copy-start | bytes 493060
  42.3 1.0 copy-start.8
  54.1 20.9 %all-to-all-start.1 = ((bf16[32,2,640]{2,1,0:T(2,128)(2,1)}), bf16[32,2,640]{2,1,0:T(2,128)(2,1)S(1)}, u32[]{:S(2)}, u32[]{:S(2)}) async-start(bf16[32,2,640]{2,1,0:T(2,128)(2,1)} %reshape.2830), calls=%async_computation.1 | async-start | bytes 163840 | tf_op jit(solution)/shard_map/all_to_all | solution.py:117
  61.1 14.7 %copy-start.12 = (s32[1280]{0:T(1024)S(1)}, s32[1280]{0:T(1024)}, u32[]{:S(2)}) copy-start(s32[1280]{0:T(1024)} %param.10) | copy-start | bytes 15364
  144.3 0.7 copy-start.1

commit v6 on v3

--- a/solution.py
+++ b/solution.py
@@ -26,28 +26,30 @@
     return cos.reshape(-1, cos.shape[-1]), sin.reshape(-1, sin.shape[-1])
 
 
-def row_synthesis(coef_row, points):
-    fields = coef_row.shape[1]
-    waves = coef_row.shape[2]
+def row_tables(points, waves):
     ablocks = waves // 64
     lon_len = 20 + 4 * (waves - 1)
     lon_idx = jnp.arange(lon_len, dtype=jnp.int32)
     cos_t, sin_t = compose(trig_pair(1, lon_idx, points, 8), trig_pair(8, lon_idx, points, 8))
-    cosb = cos_t.astype(jnp.bfloat16)
-    sinb = sin_t.astype(jnp.bfloat16)
+    rhs = jnp.concatenate([cos_t.astype(jnp.bfloat16), sin_t.astype(jnp.bfloat16)], 0)
     n_a1 = -(-ablocks // 4)
     cosp, sinp = compose(
         trig_pair(64, lon_idx, points, 4), trig_pair(256, lon_idx, points, n_a1)
     )
-    cosp = cosp[:ablocks]
-    sinp = sinp[:ablocks]
+    return rhs, cosp[:ablocks], sinp[:ablocks]
+
+
+def row_synthesis(coef_row, rhs, cosp, sinp, points):
+    fields = coef_row.shape[1]
+    waves = coef_row.shape[2]
+    ablocks = waves // 64
+    lon_idx = jnp.arange(rhs.shape[-1], dtype=jnp.int32)
     blocks = coef_row.reshape(2, fields, ablocks, 64)
     c0 = blocks[0]
     c1 = blocks[1]
     lhs = jnp.stack(
         [jnp.concatenate([c0, -c1], -1), jnp.concatenate([c1, c0], -1)], 0
     )
-    rhs = jnp.concatenate([cosb, sinb], 0)
     part = jnp.einsum("dfab,bi->dfai", lhs, rhs, preferred_element_type=jnp.float32)
     total = jnp.sum(part[0] * cosp[None] - part[1] * sinp[None], axis=1)
     return jnp.where(lon_idx[None, :] < points, total, jnp.zeros_like(total))
@@ -66,6 +68,14 @@
     spec_v = spec.reshape((n_lev, per_dev) + spec.shape[1:])
     gathered = lax.all_to_all(spec_v, ("lev_g", "lev_r"), split_axis=0, concat_axis=0, tiled=True)
     fields = gathered.shape[3] * n_lev
+    first_row = (lax.axis_index("wave") * n_r + lax.axis_index("lev_r")) * rows_per_dev
+    my_rows = lax.dynamic_slice_in_dim(band_rows, first_row, rows_per_dev)
+    row_points = row_lons[my_rows]
+    if rows_per_dev == 1:
+        tables = tuple(t[None] for t in row_tables(row_points[0], waves))
+    else:
+        tables = lax.map(lambda p: row_tables(p, waves), row_points)
+    gathered, tables = lax.optimization_barrier((gathered, tables))
     first_slot = (lax.axis_index("wave") * n_lev + lev_idx) * per_dev
     my_waves = lax.dynamic_slice_in_dim(slot_wave, first_slot, per_dev)
     degree = jnp.arange(waves, dtype=jnp.int32)
@@ -96,17 +106,14 @@
     wave_idx = jnp.arange(waves, dtype=jnp.int32)
     onehot = (slot_wave[:, None] == wave_idx[None, :]).astype(jnp.bfloat16)
     coef = jnp.einsum("cfrs,sm->cfrm", banded, onehot, preferred_element_type=jnp.float32)
-    first_row = (lax.axis_index("wave") * n_r + lax.axis_index("lev_r")) * rows_per_dev
-    my_rows = lax.dynamic_slice_in_dim(band_rows, first_row, rows_per_dev)
-    row_points = row_lons[my_rows]
     keep = 2 * wave_idx[None, :] < row_points[:, None]
     factor = jnp.where(keep, jnp.where(wave_idx[None, :] == 0, 1.0, 2.0), 0.0).astype(jnp.float32)
     coef = (coef * factor[None, None]).astype(jnp.bfloat16)
     coef_rows = jnp.moveaxis(coef, 2, 0)
     if rows_per_dev == 1:
-        grid = row_synthesis(coef_rows[0], row_points[0])[None]
+        grid = row_synthesis(coef_rows[0], *(t[0] for t in tables), row_points[0])[None]
     else:
-        grid = lax.map(lambda item: row_synthesis(item[0], item[1]), (coef_rows, row_points))
+        grid = lax.map(lambda item: row_synthesis(*item), (coef_rows,) + tuple(tables) + (row_points,))
     lon = grid.shape[-1]
     fpd = fpg // n_r
     grid = grid.reshape(rows_per_dev, n_r, fpd, lon)

time: 84.7 us -> 84.9 us (level)
  waiting for transfers between devices: 15.4 us -> 26.8 us
  other arithmetic: 22.6 us -> 15.9 us
  local copies, waits for them, and re-layouts: 12.9 us -> 8.25 us
    all_to_all x1, waiting for transfers between devices: 14.9 us -> 20.6 us  [on_device(): lax.all_to_all(spec_v, ('lev_g', 'lev_r'), split_axis=0, concat_axis=0, t...]
    all_to_all x1, waiting for transfers between devices: 0.53 us -> 6.23 us  [on_device(): lax.all_to_all(fourier, ('wave', 'lev_g', 'lev_r'), split_axis=0, concat_...]
    convert_element_type x2 -> x0, local copies, waits for them, and re-layouts: 2.61 us -> none  [the longest x1 1.31 us: row_synthesis(): cosb = cos_t.astype(jnp.bfloat16)]
    cos x3, other arithmetic: 9.06 us -> 6.98 us  [trig_pair(): return (jnp.cos(theta), jnp.sin(theta))]
    select_n x1, other arithmetic: 3.67 us -> 2.2 us  [on_device(): jnp.where(even_mask, legendre, zeros)]
    sub x1 -> x0, other arithmetic: 1.09 us -> none  [compose(): cos = c1[:, None] * c0[None] - s1[:, None] * s0[None]]
    convert_element_type x1, other arithmetic: 1.4 us -> 0.32 us  [row_tables(): cos_t.astype(jnp.bfloat16)]
    sub x1, local copies, waits for them, and re-layouts: 1.95 us -> 0.94 us  [compose(): cos = c1[:, None] * c0[None] - s1[:, None] * s0[None]]
  transfers between devices with their start and end apart: 2 -> 2, of which waited for: 2 -> 2; matrix products, arithmetic and copies ran while one was open for 33% -> 19% of each run, Pallas kernels for 0% -> 0%
where the time goes in v6:
time: 84.9 us; the launch traced here: 84.5 us
  waiting for transfers between devices  26.8 us (32%)
  other arithmetic  15.9 us (19%)
  blocking collectives  10.1 us (12%)
  starting transfers between devices  9.95 us (12%)
  matrix products  9.22 us (11%)
  local copies, waits for them, and re-layouts  8.25 us (10%)
  between operations  4.27 us (5%)
    all_to_all x1, waiting for transfers between devices, on_device(): lax.all_to_all(spec_v, ('lev_g', 'lev_r'), split_axis=0, concat_axis=0, t...  20.6 us
    all_to_all x1, blocking collectives, on_device(): lax.all_to_all(grid, 'lev_r', split_axis=1, concat_axis=0, tiled=True)  10.1 us
    cos x3, other arithmetic, trig_pair(): return (jnp.cos(theta), jnp.sin(theta))  6.98 us
    all_to_all x1, waiting for transfers between devices, on_device(): lax.all_to_all(fourier, ('wave', 'lev_g', 'lev_r'), split_axis=0, concat_...  6.23 us
    dot_general x1, matrix products, on_device(): jnp.einsum('lscfk,sjk->sclfj', gathered, leg2, preferred_element_type=jnp...  5.51 us
    all_to_all x1, starting transfers between devices, on_device(): lax.all_to_all(spec_v, ('lev_g', 'lev_r'), split_axis=0, concat_axis=0, t...  5.3 us
    all_to_all x1, starting transfers between devices, on_device(): lax.all_to_all(fourier, ('wave', 'lev_g', 'lev_r'), split_axis=0, concat_...  4.65 us
    unnamed x17, local copies, waits for them, and re-layouts  2.32 us
  transfers between devices with their start and end apart: 2, of which 2 were waited for; matrix products, arithmetic and copies ran while one was open for 19% of the time, Pallas kernels for 0%

profile of v6, /device:TPU:0, one launch (start us, length us, event | category | flops | bytes accessed | tf_op | source)
XLA Modules:
  0.0 84.5 jit_solution(6244546915750172796)
XLA Ops:
  0.0 5.3 %all-to-all-start = ((bf16[8,40,2,2,1280]{4,3,2,1,0:T(2,128)(2,1)}), bf16[8,40,2,2,1280]{4,3,2,1,0:T(2,128)(2,1)}, u32[]{:S(2)}, u32[]{:S(2)}) async-start(bf16[8,40,2,2,1280]{4,3,2,1,0:T(2,128)(2,1)} %bitcast.77), calls=%async_computation | async-start | bytes 6553600 | tf_op jit(solution)/shard_map/all_to_all | solution.py:69
  5.3 0.6 dynamic_slice.6
  7.9 0.7 dynamic-slice.2
  10.6 2.3 %fusion.63 = (f32[8,5136]{1,0:T(8,128)S(1)}, f32[8,5136]{1,0:T(8,128)S(1)}) fusion(f32[]{:T(128)S(6)} %convert_element_type.74, pred[]{:T(512)S(6)} %lt.110, s32[]{:T(128)S(6)} %select_n.136, s32[8]{0:T(128)S(1)} %iota_multiply_fusion.2), kind=kLoop, calls=%fused_computation.84 | loop fusion | flops 451968 | bytes 328745 | tf_op jit(solution)/shard_map/cos | solution.py:18
  12.9 2.3 %fusion.59 = (f32[5,5136]{1,0:T(8,128)S(1)}, f32[5,5136]{1,0:T(8,128)S(1)}) fusion(f32[]{:T(128)S(6)} %convert_element_type.74, pred[]{:T(512)S(6)} %lt.110, s32[]{:T(128)S(6)} %select_n.136, s32[5]{0:T(128)S(1)} %iota_multiply_fusion.1), kind=kLoop, calls=%fused_computation.80 | loop fusion | flops 282480 | bytes 205469 | tf_op jit(solution)/shard_map/cos | solution.py:18
  15.3 2.3 %fusion.65 = (f32[4,5136]{1,0:T(4,128)S(1)}, f32[4,5136]{1,0:T(4,128)S(1)}) fusion(f32[]{:T(128)S(6)} %convert_element_type.74, pred[]{:T(512)S(6)} %lt.110, s32[]{:T(128)S(6)} %select_n.136, s32[4]{0:T(128)S(1)} %iota_multiply_fusion), kind=kLoop, calls=%fused_computation.86 | loop fusion | flops 225984 | bytes 164377 | tf_op jit(solution)/shard_map/cos | solution.py:18
  18.0 0.9 %sub.35 = f32[1,20,5136]{2,1,0:T(8,128)} reshape(f32[5,4,5136]{2,1,0:T(4,128)S(1)} %get-tuple-element.31) | data formatting | bytes 821760 | tf_op jit(solution)/shard_map/sub | solution.py:24
  19.2 2.2 %broadcast_select_fusion.1 = (bf16[40,16,1280]{2,1,0:T(8,128)(2,1)}, bf16[40,16,1280]{2,1,0:T(8,128)(2,1)}) fusion(bf16[40,16,1280]{2,1,0:T(8,128)(2,1)S(1)} %copy-done.1, pred[40,1280]{1,0:T(8,128)(4,1)S(1)} %get-tuple-element.36, pred[40,1280]{1,0:T(8,128)(4,1)S(1)} %get-tuple-element.37), kind=kLoop, calls=%fused_computation.20 | loop fusion | flops 1638400 | bytes 5017600 | tf_op jit(solution)/shard_map/jit(_where)/select_n | solution.py:87
  21.4 2.3 %fusion.60 = (f32[8,5136]{1,0:T(8,128)S(1)}, f32[8,5136]{1,0:T(8,128)S(1)}) fusion(f32[]{:T(128)S(6)} %convert_element_type.74, pred[]{:T(512)S(6)} %lt.110, s32[]{:T(128)S(6)} %select_n.136), kind=kLoop, calls=%fused_computation.81 | loop fusion | flops 451968 | bytes 328713 | tf_op jit(solution)/shard_map/sin | solution.py:18
  24.1 20.6 %all-to-all-done = bf16[8,40,2,2,1280]{4,3,2,1,0:T(2,128)(2,1)} async-done(((bf16[8,40,2,2,1280]{4,3,2,1,0:T(2,128)(2,1)}), bf16[8,40,2,2,1280]{4,3,2,1,0:T(2,128)(2,1)}, u32[]{:S(2)}, u32[]{:S(2)}) %all-to-all-start) | async-done | bytes 3276832 | tf_op jit(solution)/shard_map/all_to_all | solution.py:69
  44.7 5.5 %fusion.20 = f32[40,2,8,2,32]{4,2,3,1,0:T(8,128)} fusion(bf16[8,40,2,2,1280]{4,3,2,1,0:T(2,128)(2,1)} %all-to-all-done, bf16[40,16,1280]{2,1,0:T(8,128)(2,1)} %get-tuple-element.25, bf16[40,16,1280]{2,1,0:T(8,128)(2,1)S(1)} %copy-done.2), kind=kOutput, calls=%fused_computation.26 | convolution fusion | flops 111411200 | bytes 6717440 | tf_op jit(solution)/shard_map/lscfk,sjk->sclfj/dot_general | solution.py:89
  50.2 1.4 %copy.14 = f32[40,2,8,2,32]{0,4,3,2,1:T(8,128)S(1)} copy(f32[40,2,8,2,32]{4,2,3,1,0:T(8,128)} %fusion.20) | data formatting | bytes 327680 | tf_op jit(solution)/shard_map/lscfk,sjk->sclfj/transpose | solution.py:89
  51.9 0.6 gather_fusion
  52.5 0.6 gather_fusion.1
  53.2 1.0 %reshape.521 = bf16[32,2,640]{2,1,0:T(2,128)(2,1)} reshape(bf16[32,1,2,16,40]{4,3,2,1,0:T(8,128)(2,1)S(1)} %bitcast.86) | data formatting | bytes 163840
  54.2 4.6 %all-to-all-start.1 = ((bf16[32,2,640]{2,1,0:T(2,128)(2,1)}), bf16[32,2,640]{2,1,0:T(2,128)(2,1)S(1)}, u32[]{:S(2)}, u32[]{:S(2)}) async-start(bf16[32,2,640]{2,1,0:T(2,128)(2,1)} %reshape.521), calls=%async_computation.1 | async-start | bytes 163840 | tf_op jit(solution)/shard_map/all_to_all | solution.py:102
  58.8 0.7 iota_compare_fusion.2
  59.5 0.7 select_select_fusion
  60.2 6.2 %all-to-all-done.1 = bf16[32,2,640]{2,1,0:T(2,128)(2,1)S(1)} async-done(((bf16[32,2,640]{2,1,0:T(2,128)(2,1)}), bf16[32,2,640]{2,1,0:T(2,128)(2,1)S(1)}, u32[]{:S(2)}, u32[]{:S(2)}) %all-to-all-start.1) | async-done | bytes 81952 | tf_op jit(solution)/shard_map/all_to_all | solution.py:102
  67.3 1.4 %fusion.15 = bf16[2,16,1280]{2,1,0:T(8,128)(2,1)S(1)} fusion(bf16[2,16,1280]{2,1,0:T(8,128)(2,1)S(1)} %reshape.477, s32[1280]{0:T(1024)S(1)} %copy-done.3, f32[1280]{0:T(1024)S(1)} %select_select_fusion), kind=kOutput, calls=%fused_computation.18 | convolution fusion | flops 106577920 | bytes 174080 | tf_op jit(solution)/shard_map/cfrs,sm->cfrm/dot_general | solution.py:108
  69.2 2.3 %fusion.18 = f32[2,16,20,5136]{3,2,1,0:T(8,128)S(1)} fusion(bf16[1,128,5136]{2,1,0:T(8,128)(2,1)S(1)} %maximum_bitcast_fusion.2, bf16[1,16,20,128]{3,2,1,0:T(8,128)(2,1)S(1)} %get-tuple-element.33, bf16[1,16,20,128]{3,2,1,0:T(8,128)(2,1)S(1)} %get-tuple-element.32), kind=kOutput, calls=%fused_computation.22 | convolution fusion | flops 841564160 | bytes 14626816 | tf_op jit(solution)/shard_map/dfab,bi->dfai/dot_general | solution.py:53
  71.5 1.8 %fusion.2 = f32[16,5136]{1,0:T(8,128)S(1)} fusion(f32[2,16,20,5136]{3,2,1,0:T(8,128)S(1)} %fusion.18, f32[20,5136]{1,0:T(8,128)S(1)} %bitcast.83, f32[20,5136]{1,0:T(8,128)S(1)} %bitcast.84), kind=kLoop, calls=%fused_computation.5 | loop fusion | flops 6491904 | bytes 14298624 | tf_op jit(solution)/shard_map/reduce_sum | solution.py:54
  73.6 10.1 %all_to_all.19 = f32[1,8,2,5136]{3,2,0,1:T(2,128)S(1)} all-to-all(f32[1,8,2,5136]{3,2,0,1:T(2,128)S(1)} %broadcast_select_fusion.2), channel_id=1, replica_groups=mesh['wave'=4,'lev'=8] {'lev'}, dimensions={1} | all-to-all | bytes 657408 | tf_op jit(solution)/shard_map/all_to_all | solution.py:120
  83.8 0.7 copy.33
  (41 shorter events, 3.0 us)
Async XLA Ops:
  0.0 5.3 %copy-start.5 = (s32[32]{0:T(128)S(1)}, s32[32]{0:T(128)}, u32[]{:S(2)}) copy-start(s32[32]{0:T(128)} %param.9) | copy-start | bytes 388
  0.0 7.8 %copy-start.4 = (s32[32]{0:T(128)S(1)}, s32[32]{0:T(128)}, u32[]{:S(2)}) copy-start(s32[32]{0:T(128)} %param.8) | copy-start | bytes 388
  0.0 44.7 %all-to-all-start = ((bf16[8,40,2,2,1280]{4,3,2,1,0:T(2,128)(2,1)}), bf16[8,40,2,2,1280]{4,3,2,1,0:T(2,128)(2,1)}, u32[]{:S(2)}, u32[]{:S(2)}) async-start(bf16[8,40,2,2,1280]{4,3,2,1,0:T(2,128)(2,1)} %bitcast.77), calls=%async_computation | async-start | bytes 6553600 | tf_op jit(solution)/shard_map/all_to_all | solution.py:69
  17.6 1.4 %copy-start.3 = (s32[1280]{0:T(1024)S(1)}, s32[1280]{0:T(1024)}, u32[]{:S(2)}) copy-start(s32[1280]{0:T(1024)} %param.7) | copy-start | bytes 15364
  17.6 1.6 %copy-start.1 = (bf16[40,16,1280]{2,1,0:T(8,128)(2,1)S(1)}, bf16[40,16,1280]{2,1,0:T(8,128)(2,1)}, u32[]{:S(2)}) copy-start(bf16[40,16,1280]{2,1,0:T(8,128)(2,1)} %param.6) | copy-start | bytes 4915204
  24.0 20.7 %copy-start.2 = (bf16[40,16,1280]{2,1,0:T(8,128)(2,1)S(1)}, bf16[40,16,1280]{2,1,0:T(8,128)(2,1)}, u32[]{:S(2)}) copy-start(bf16[40,16,1280]{2,1,0:T(8,128)(2,1)} %get-tuple-element.24) | copy-start | bytes 4915204
  54.2 12.3 %all-to-all-start.1 = ((bf16[32,2,640]{2,1,0:T(2,128)(2,1)}), bf16[32,2,640]{2,1,0:T(2,128)(2,1)S(1)}, u32[]{:S(2)}, u32[]{:S(2)}) async-start(bf16[32,2,640]{2,1,0:T(2,128)(2,1)} %reshape.521), calls=%async_computation.1 | async-start | bytes 163840 | tf_op jit(solution)/shard_map/all_to_all | solution.py:102
  69.2 2.3 %copy-start = (f32[1,20,5136]{2,1,0:T(8,128)S(1)}, f32[1,20,5136]{2,1,0:T(8,128)}, u32[]{:S(2)}) copy-start(f32[1,20,5136]{2,1,0:T(8,128)} %sub.35) | copy-start | bytes 1232644

commit v7 on v6

--- a/solution.py
+++ b/solution.py
@@ -117,7 +117,16 @@
     lon = grid.shape[-1]
     fpd = fpg // n_r
     grid = grid.reshape(rows_per_dev, n_r, fpd, lon)
-    grid = lax.all_to_all(grid, "lev_r", split_axis=1, concat_axis=0, tiled=True)
+    me = lax.axis_index("lev_r")
+    got = []
+    for d in range(n_r):
+        piece = lax.dynamic_index_in_dim(grid, (me + d) % n_r, 1, keepdims=False)
+        if d > 0:
+            piece = lax.ppermute(piece, "lev_r", [(j, (j + d) % n_r) for j in range(n_r)])
+        got.append(piece)
+    got = jnp.stack(got, 0)
+    order = (me - jnp.arange(n_r, dtype=jnp.int32)) % n_r
+    grid = jnp.take(got, order, axis=0)
     return grid.reshape(n_r * rows_per_dev, fpd, lon)
 
 

time: 84.9 us -> 85.5 us (level)
  blocking collectives: 10.1 us -> 0 us
  starting transfers between devices: 9.95 us -> 16.6 us
  waiting for transfers between devices: 26.8 us -> 29.5 us
    all_to_all x1 -> x0, blocking collectives: 10.1 us -> none  [on_device(): lax.all_to_all(grid, 'lev_r', split_axis=1, concat_axis=0, tiled=True)]
    ppermute x0 -> x7, starting transfers between devices: none -> 6.61 us  [on_device(): lax.ppermute(piece, 'lev_r', [(j, (j + d) % n_r) for j in range(n_r)])]
    ppermute x0 -> x7, waiting for transfers between devices: none -> 2.5 us  [on_device(): lax.ppermute(piece, 'lev_r', [(j, (j + d) % n_r) for j in range(n_r)])]
    select_n x0 -> x2, other arithmetic: none -> 0.95 us  [on_device(): grid = jnp.take(got, order, axis=0)]
    gather x0 -> x1, local copies, waits for them, and re-layouts: none -> 0.91 us  [on_device(): grid = jnp.take(got, order, axis=0)]
    unnamed x17 -> x22, local copies, waits for them, and re-layouts: 2.32 us -> 1.66 us
  transfers between devices with their start and end apart: 2 -> 9, of which waited for: 2 -> 5; matrix products, arithmetic and copies ran while one was open for 19% -> 19% of each run, Pallas kernels for 0% -> 0%
where the time goes in v7:
time: 85.5 us; the launch traced here: 84.9 us
  waiting for transfers between devices  29.5 us (35%)
  other arithmetic  16.7 us (20%)
  starting transfers between devices  16.6 us (19%)
  matrix products  9.25 us (11%)
  local copies, waits for them, and re-layouts  8.53 us (10%)
  between operations  4.26 us (5%)
    all_to_all x1, waiting for transfers between devices, on_device(): lax.all_to_all(spec_v, ('lev_g', 'lev_r'), split_axis=0, concat_axis=0, t...  20.2 us
    cos x3, other arithmetic, trig_pair(): return (jnp.cos(theta), jnp.sin(theta))  6.98 us
    all_to_all x1, waiting for transfers between devices, on_device(): lax.all_to_all(fourier, ('wave', 'lev_g', 'lev_r'), split_axis=0, concat_...  6.86 us
    ppermute x7, starting transfers between devices, on_device(): lax.ppermute(piece, 'lev_r', [(j, (j + d) % n_r) for j in range(n_r)])  6.61 us
    dot_general x1, matrix products, on_device(): jnp.einsum('lscfk,sjk->sclfj', gathered, leg2, preferred_element_type=jnp...  5.54 us
    all_to_all x1, starting transfers between devices, on_device(): lax.all_to_all(spec_v, ('lev_g', 'lev_r'), split_axis=0, concat_axis=0, t...  5.3 us
    all_to_all x1, starting transfers between devices, on_device(): lax.all_to_all(fourier, ('wave', 'lev_g', 'lev_r'), split_axis=0, concat_...  4.64 us
    ppermute x7, waiting for transfers between devices, on_device(): lax.ppermute(piece, 'lev_r', [(j, (j + d) % n_r) for j in range(n_r)])  2.5 us
  transfers between devices with their start and end apart: 9, of which 5 were waited for; matrix products, arithmetic and copies ran while one was open for 19% of the time, Pallas kernels for 0%

profile of v7, /device:TPU:0, one launch (start us, length us, event | category | flops | bytes accessed | tf_op | source)
XLA Modules:
  0.0 84.9 jit_solution(2533634062613013576)
XLA Ops:
  0.0 5.3 %all-to-all-start = ((bf16[8,40,2,2,1280]{4,3,2,1,0:T(2,128)(2,1)}), bf16[8,40,2,2,1280]{4,3,2,1,0:T(2,128)(2,1)}, u32[]{:S(2)}, u32[]{:S(2)}) async-start(bf16[8,40,2,2,1280]{4,3,2,1,0:T(2,128)(2,1)} %bitcast.107), calls=%async_computation | async-start | bytes 6553600 | tf_op jit(solution)/shard_map/all_to_all | solution.py:69
  11.0 2.3 %fusion.63 = (f32[8,5136]{1,0:T(8,128)S(1)}, f32[8,5136]{1,0:T(8,128)S(1)}) fusion(f32[]{:T(128)S(6)} %convert_element_type.74, pred[]{:T(512)S(6)} %lt.194, s32[]{:T(128)S(6)} %select_n.237, s32[8]{0:T(128)S(1)} %iota_multiply_fusion.2), kind=kLoop, calls=%fused_computation.86 | loop fusion | flops 451968 | bytes 328745 | tf_op jit(solution)/shard_map/cos | solution.py:18
  13.3 2.3 %fusion.59 = (f32[5,5136]{1,0:T(8,128)S(1)}, f32[5,5136]{1,0:T(8,128)S(1)}) fusion(f32[]{:T(128)S(6)} %convert_element_type.74, pred[]{:T(512)S(6)} %lt.194, s32[]{:T(128)S(6)} %select_n.237, s32[5]{0:T(128)S(1)} %iota_multiply_fusion.1), kind=kLoop, calls=%fused_computation.82 | loop fusion | flops 282480 | bytes 205469 | tf_op jit(solution)/shard_map/cos | solution.py:18
  15.7 2.3 %fusion.65 = (f32[4,5136]{1,0:T(4,128)S(1)}, f32[4,5136]{1,0:T(4,128)S(1)}) fusion(f32[]{:T(128)S(6)} %convert_element_type.74, pred[]{:T(512)S(6)} %lt.194, s32[]{:T(128)S(6)} %select_n.237, s32[4]{0:T(128)S(1)} %iota_multiply_fusion), kind=kLoop, calls=%fused_computation.103 | loop fusion | flops 225984 | bytes 164377 | tf_op jit(solution)/shard_map/cos | solution.py:18
  18.4 0.9 %sub.56 = f32[1,20,5136]{2,1,0:T(8,128)} reshape(f32[5,4,5136]{2,1,0:T(4,128)S(1)} %get-tuple-element.31) | data formatting | bytes 821760 | tf_op jit(solution)/shard_map/sub | solution.py:24
  19.6 2.2 %broadcast_select_fusion.1 = (bf16[40,16,1280]{2,1,0:T(8,128)(2,1)}, bf16[40,16,1280]{2,1,0:T(8,128)(2,1)}) fusion(bf16[40,16,1280]{2,1,0:T(8,128)(2,1)S(1)} %copy-done.1, pred[40,1280]{1,0:T(8,128)(4,1)S(1)} %get-tuple-element.44, pred[40,1280]{1,0:T(8,128)(4,1)S(1)} %get-tuple-element.45), kind=kLoop, calls=%fused_computation.21 | loop fusion | flops 1638400 | bytes 5017600 | tf_op jit(solution)/shard_map/jit(_where)/select_n | solution.py:87
  21.8 2.3 %fusion.60 = (f32[8,5136]{1,0:T(8,128)S(1)}, f32[8,5136]{1,0:T(8,128)S(1)}) fusion(f32[]{:T(128)S(6)} %convert_element_type.74, pred[]{:T(512)S(6)} %lt.194, s32[]{:T(128)S(6)} %select_n.237), kind=kLoop, calls=%fused_computation.83 | loop fusion | flops 451968 | bytes 328713 | tf_op jit(solution)/shard_map/sin | solution.py:18
  24.5 20.2 %all-to-all-done = bf16[8,40,2,2,1280]{4,3,2,1,0:T(2,128)(2,1)} async-done(((bf16[8,40,2,2,1280]{4,3,2,1,0:T(2,128)(2,1)}), bf16[8,40,2,2,1280]{4,3,2,1,0:T(2,128)(2,1)}, u32[]{:S(2)}, u32[]{:S(2)}) %all-to-all-start) | async-done | bytes 3276832 | tf_op jit(solution)/shard_map/all_to_all | solution.py:69
  44.7 5.5 %fusion.20 = f32[40,2,8,2,32]{4,2,3,1,0:T(8,128)} fusion(bf16[8,40,2,2,1280]{4,3,2,1,0:T(2,128)(2,1)} %all-to-all-done, bf16[40,16,1280]{2,1,0:T(8,128)(2,1)} %get-tuple-element.25, bf16[40,16,1280]{2,1,0:T(8,128)(2,1)S(1)} %copy-done.2), kind=kOutput, calls=%fused_computation.27 | convolution fusion | flops 111411200 | bytes 6717440 | tf_op jit(solution)/shard_map/lscfk,sjk->sclfj/dot_general | solution.py:89
  50.2 1.4 %copy.14 = f32[40,2,8,2,32]{0,4,3,2,1:T(8,128)S(1)} copy(f32[40,2,8,2,32]{4,2,3,1,0:T(8,128)} %fusion.20) | data formatting | bytes 327680 | tf_op jit(solution)/shard_map/lscfk,sjk->sclfj/transpose | solution.py:89
  53.2 1.0 %reshape.582 = bf16[32,2,640]{2,1,0:T(2,128)(2,1)} reshape(bf16[32,1,2,16,40]{4,3,2,1,0:T(8,128)(2,1)S(1)} %bitcast.115) | data formatting | bytes 163840
  54.2 4.6 %all-to-all-start.1 = ((bf16[32,2,640]{2,1,0:T(2,128)(2,1)}), bf16[32,2,640]{2,1,0:T(2,128)(2,1)S(1)}, u32[]{:S(2)}, u32[]{:S(2)}) async-start(bf16[32,2,640]{2,1,0:T(2,128)(2,1)} %reshape.582), calls=%async_computation.1 | async-start | bytes 163840 | tf_op jit(solution)/shard_map/all_to_all | solution.py:102
  59.6 6.9 %all-to-all-done.1 = bf16[32,2,640]{2,1,0:T(2,128)(2,1)S(1)} async-done(((bf16[32,2,640]{2,1,0:T(2,128)(2,1)}), bf16[32,2,640]{2,1,0:T(2,128)(2,1)S(1)}, u32[]{:S(2)}, u32[]{:S(2)}) %all-to-all-start.1) | async-done | bytes 81952 | tf_op jit(solution)/shard_map/all_to_all | solution.py:102
  67.3 1.4 %fusion.15 = bf16[2,16,1280]{2,1,0:T(8,128)(2,1)S(1)} fusion(bf16[2,16,1280]{2,1,0:T(8,128)(2,1)S(1)} %reshape.528, s32[1280]{0:T(1024)S(1)} %copy-done.3, f32[1280]{0:T(1024)S(1)} %select_select_fusion), kind=kOutput, calls=%fused_computation.19 | convolution fusion | flops 106577920 | bytes 174080 | tf_op jit(solution)/shard_map/cfrs,sm->cfrm/dot_general | solution.py:108
  69.2 2.3 %fusion.18 = f32[2,16,20,5136]{3,2,1,0:T(8,128)S(1)} fusion(bf16[1,128,5136]{2,1,0:T(8,128)(2,1)S(1)} %maximum_bitcast_fusion.2, bf16[1,16,20,128]{3,2,1,0:T(8,128)(2,1)S(1)} %get-tuple-element.41, bf16[1,16,20,128]{3,2,1,0:T(8,128)(2,1)S(1)} %get-tuple-element.40), kind=kOutput, calls=%fused_computation.23 | convolution fusion | flops 841564160 | bytes 14626816 | tf_op jit(solution)/shard_map/dfab,bi->dfai/dot_general | solution.py:53
  71.5 1.8 %fusion.2 = f32[16,5136]{1,0:T(8,128)S(1)} fusion(f32[2,16,20,5136]{3,2,1,0:T(8,128)S(1)} %fusion.18, f32[20,5136]{1,0:T(8,128)S(1)} %bitcast.113, f32[20,5136]{1,0:T(8,128)S(1)} %bitcast.114), kind=kLoop, calls=%fused_computation.6 | loop fusion | flops 6491904 | bytes 14298624 | tf_op jit(solution)/shard_map/reduce_sum | solution.py:54
  74.4 1.7 %collective-permute-start.2 = (f32[1,2,5136]{2,1,0:T(2,128)S(1)}, f32[1,2,5136]{2,1,0:T(2,128)S(1)}, u32[]{:S(2)}, u32[]{:S(2)}) collective-permute-start(f32[1,2,5136]{2,1,0:T(2,128)S(1)} %get-tuple-element.36), channel_id=1, source_target_pairs={{0,3},{1,4},{2,5},{3,6},{4,7},{5,0},{6,1},{7,2},{8,11},{9,12},{10,... | collective-permute-start | bytes 123272 | tf_op jit(solution)/shard_map/ppermute | solution.py:125
  76.1 1.1 %collective-permute-start.3 = (f32[1,2,5136]{2,1,0:T(2,128)S(1)}, f32[1,2,5136]{2,1,0:T(2,128)S(1)}, u32[]{:S(2)}, u32[]{:S(2)}) collective-permute-start(f32[1,2,5136]{2,1,0:T(2,128)S(1)} %get-tuple-element.35), channel_id=1, source_target_pairs={{0,4},{1,5},{2,6},{3,7},{4,0},{5,1},{6,2},{7,3},{8,12},{9,13},{10,... | collective-permute-start | bytes 123272 | tf_op jit(solution)/shard_map/ppermute | solution.py:125
  77.2 0.9 %collective-permute-done = f32[1,2,5136]{2,1,0:T(2,128)S(1)} collective-permute-done((f32[1,2,5136]{2,1,0:T(2,128)S(1)}, f32[1,2,5136]{2,1,0:T(2,128)S(1)}, u32[]{:S(2)}, u32[]{:S(2)}) %collective-permute-start) | collective-permute-done | bytes 41120 | tf_op jit(solution)/shard_map/ppermute | solution.py:125
  78.2 1.6 %collective-permute-start.5 = (f32[1,2,5136]{2,1,0:T(2,128)S(1)}, f32[1,2,5136]{2,1,0:T(2,128)S(1)}, u32[]{:S(2)}, u32[]{:S(2)}) collective-permute-start(f32[1,2,5136]{2,1,0:T(2,128)S(1)} %get-tuple-element.33), channel_id=1, source_target_pairs={{0,6},{1,7},{2,0},{3,1},{4,2},{5,3},{6,4},{7,5},{8,14},{9,15},{10,... | collective-permute-start | bytes 123272 | tf_op jit(solution)/shard_map/ppermute | solution.py:125
  79.8 1.5 %collective-permute-start.6 = (f32[1,2,5136]{2,1,0:T(2,128)S(1)}, f32[1,2,5136]{2,1,0:T(2,128)S(1)}, u32[]{:S(2)}, u32[]{:S(2)}) collective-permute-start(f32[1,2,5136]{2,1,0:T(2,128)S(1)} %get-tuple-element.32), channel_id=1, source_target_pairs={{0,7},{1,0},{2,1},{3,2},{4,3},{5,4},{6,5},{7,6},{8,15},{9,8},{10,9... | collective-permute-start | bytes 123272 | tf_op jit(solution)/shard_map/ppermute | solution.py:125
  82.2 0.8 collective-permute-done.6
  83.0 0.9 %gather_fusion.2 = f32[8,2,5136]{2,1,0:T(2,128)S(1)} fusion(f32[8,2,5136]{2,1,0:T(2,128)S(1)} %bitcast.116, s32[1024]{0:T(1024)S(1)} %pad_clamp_fusion), kind=kCustom, calls=%fused_computation.2 | custom fusion | bytes 657440 | tf_op jit(solution)/shard_map/jit(_take)/gather | solution.py:129
  83.9 0.9 %broadcast_select_fusion.2 = f32[8,2,5136]{2,1,0:T(2,128)} fusion(f32[8,2,5136]{2,1,0:T(2,128)S(1)} %gather_fusion.2, pred[8]{0:T(512)(128)(4,1)S(1)} %compare_and_fusion), kind=kLoop, calls=%fused_computation.33 | loop fusion | flops 82176 | bytes 657416 | tf_op jit(solution)/shard_map/jit(_take)/select_n | solution.py:129
  (66 shorter events, 8.2 us)
Async XLA Ops:
  0.0 5.3 %copy-start.5 = (s32[32]{0:T(128)S(1)}, s32[32]{0:T(128)}, u32[]{:S(2)}) copy-start(s32[32]{0:T(128)} %param.9) | copy-start | bytes 388
  0.0 7.8 %copy-start.4 = (s32[32]{0:T(128)S(1)}, s32[32]{0:T(128)}, u32[]{:S(2)}) copy-start(s32[32]{0:T(128)} %param.8) | copy-start | bytes 388
  0.0 44.7 %all-to-all-start = ((bf16[8,40,2,2,1280]{4,3,2,1,0:T(2,128)(2,1)}), bf16[8,40,2,2,1280]{4,3,2,1,0:T(2,128)(2,1)}, u32[]{:S(2)}, u32[]{:S(2)}) async-start(bf16[8,40,2,2,1280]{4,3,2,1,0:T(2,128)(2,1)} %bitcast.107), calls=%async_computation | async-start | bytes 6553600 | tf_op jit(solution)/shard_map/all_to_all | solution.py:69
  18.0 1.4 %copy-start.3 = (s32[1280]{0:T(1024)S(1)}, s32[1280]{0:T(1024)}, u32[]{:S(2)}) copy-start(s32[1280]{0:T(1024)} %param.7) | copy-start | bytes 15364
  18.0 1.6 %copy-start.1 = (bf16[40,16,1280]{2,1,0:T(8,128)(2,1)S(1)}, bf16[40,16,1280]{2,1,0:T(8,128)(2,1)}, u32[]{:S(2)}) copy-start(bf16[40,16,1280]{2,1,0:T(8,128)(2,1)} %param.6) | copy-start | bytes 4915204
  24.4 20.3 %copy-start.2 = (bf16[40,16,1280]{2,1,0:T(8,128)(2,1)S(1)}, bf16[40,16,1280]{2,1,0:T(8,128)(2,1)}, u32[]{:S(2)}) copy-start(bf16[40,16,1280]{2,1,0:T(8,128)(2,1)} %get-tuple-element.24) | copy-start | bytes 4915204
  54.2 12.3 %all-to-all-start.1 = ((bf16[32,2,640]{2,1,0:T(2,128)(2,1)}), bf16[32,2,640]{2,1,0:T(2,128)(2,1)S(1)}, u32[]{:S(2)}, u32[]{:S(2)}) async-start(bf16[32,2,640]{2,1,0:T(2,128)(2,1)} %reshape.582), calls=%async_computation.1 | async-start | bytes 163840 | tf_op jit(solution)/shard_map/all_to_all | solution.py:102
  69.2 2.3 %copy-start = (f32[1,20,5136]{2,1,0:T(8,128)S(1)}, f32[1,20,5136]{2,1,0:T(8,128)}, u32[]{:S(2)}) copy-start(f32[1,20,5136]{2,1,0:T(8,128)} %sub.56) | copy-start | bytes 1232644
  73.8 4.4 %collective-permute-start = (f32[1,2,5136]{2,1,0:T(2,128)S(1)}, f32[1,2,5136]{2,1,0:T(2,128)S(1)}, u32[]{:S(2)}, u32[]{:S(2)}) collective-permute-start(f32[1,2,5136]{2,1,0:T(2,128)S(1)} %get-tuple-element.38), channel_id=1, source_target_pairs={{0,1},{1,2},{2,3},{3,4},{4,5},{5,6},{6,7},{7,0},{8,9},{9,10},{10,1... | collective-permute-start | bytes 123272 | tf_op jit(solution)/shard_map/ppermute | solution.py:125
  73.9 5.8 %collective-permute-start.1 = (f32[1,2,5136]{2,1,0:T(2,128)S(1)}, f32[1,2,5136]{2,1,0:T(2,128)S(1)}, u32[]{:S(2)}, u32[]{:S(2)}) collective-permute-start(f32[1,2,5136]{2,1,0:T(2,128)S(1)} %get-tuple-element.37), channel_id=1, source_target_pairs={{0,2},{1,3},{2,4},{3,5},{4,6},{5,7},{6,0},{7,1},{8,10},{9,11},{10,... | collective-permute-start | bytes 123272 | tf_op jit(solution)/shard_map/ppermute | solution.py:125
  74.4 6.9 %collective-permute-start.2 = (f32[1,2,5136]{2,1,0:T(2,128)S(1)}, f32[1,2,5136]{2,1,0:T(2,128)S(1)}, u32[]{:S(2)}, u32[]{:S(2)}) collective-permute-start(f32[1,2,5136]{2,1,0:T(2,128)S(1)} %get-tuple-element.36), channel_id=1, source_target_pairs={{0,3},{1,4},{2,5},{3,6},{4,7},{5,0},{6,1},{7,2},{8,11},{9,12},{10,... | collective-permute-start | bytes 123272 | tf_op jit(solution)/shard_map/ppermute | solution.py:125
  76.1 5.3 %collective-permute-start.3 = (f32[1,2,5136]{2,1,0:T(2,128)S(1)}, f32[1,2,5136]{2,1,0:T(2,128)S(1)}, u32[]{:S(2)}, u32[]{:S(2)}) collective-permute-start(f32[1,2,5136]{2,1,0:T(2,128)S(1)} %get-tuple-element.35), channel_id=1, source_target_pairs={{0,4},{1,5},{2,6},{3,7},{4,0},{5,1},{6,2},{7,3},{8,12},{9,13},{10,... | collective-permute-start | bytes 123272 | tf_op jit(solution)/shard_map/ppermute | solution.py:125
  77.2 4.2 %collective-permute-start.4 = (f32[1,2,5136]{2,1,0:T(2,128)S(1)}, f32[1,2,5136]{2,1,0:T(2,128)S(1)}, u32[]{:S(2)}, u32[]{:S(2)}) collective-permute-start(f32[1,2,5136]{2,1,0:T(2,128)S(1)} %get-tuple-element.34), channel_id=1, source_target_pairs={{0,5},{1,6},{2,7},{3,0},{4,1},{5,2},{6,3},{7,4},{8,13},{9,14},{10,... | collective-permute-start | bytes 123272 | tf_op jit(solution)/shard_map/ppermute | solution.py:125
  78.2 4.0 %collective-permute-start.5 = (f32[1,2,5136]{2,1,0:T(2,128)S(1)}, f32[1,2,5136]{2,1,0:T(2,128)S(1)}, u32[]{:S(2)}, u32[]{:S(2)}) collective-permute-start(f32[1,2,5136]{2,1,0:T(2,128)S(1)} %get-tuple-element.33), channel_id=1, source_target_pairs={{0,6},{1,7},{2,0},{3,1},{4,2},{5,3},{6,4},{7,5},{8,14},{9,15},{10,... | collective-permute-start | bytes 123272 | tf_op jit(solution)/shard_map/ppermute | solution.py:125
  79.8 3.2 %collective-permute-start.6 = (f32[1,2,5136]{2,1,0:T(2,128)S(1)}, f32[1,2,5136]{2,1,0:T(2,128)S(1)}, u32[]{:S(2)}, u32[]{:S(2)}) collective-permute-start(f32[1,2,5136]{2,1,0:T(2,128)S(1)} %get-tuple-element.32), channel_id=1, source_target_pairs={{0,7},{1,0},{2,1},{3,2},{4,3},{5,4},{6,5},{7,6},{8,15},{9,8},{10,9... | collective-permute-start | bytes 123272 | tf_op jit(solution)/shard_map/ppermute | solution.py:125

commit v8 on v5

--- a/solution.py
+++ b/solution.py
@@ -16,12 +16,14 @@
     return x[0] * y[0] - x[1] * y[1], x[0] * y[1] + x[1] * y[0]
 
 
-def powers(base, count):
-    out = [(jnp.ones_like(base[0]), jnp.zeros_like(base[1])), base]
-    while len(out) < count:
-        out.append(cmul(out[-1], base))
-    out = out[:count]
-    return jnp.stack([o[0] for o in out], 1), jnp.stack([o[1] for o in out], 1)
+def bit_powers(bases, count):
+    j = jnp.arange(count, dtype=jnp.int32)[None, :, None]
+    c = jnp.ones((bases[0][0].shape[0], count, bases[0][0].shape[1]), jnp.float32)
+    s = jnp.zeros_like(c)
+    for k, (bc, bs) in enumerate(bases):
+        bit = (j >> k) & 1 == 1
+        c, s = cmul((c, s), (jnp.where(bit, bc[:, None], 1.0), jnp.where(bit, bs[:, None], 0.0)))
+    return c, s
 
 
 def outer(first, second):
@@ -41,37 +43,44 @@
     steps = jnp.array([1, 64], dtype=jnp.int32)[:, None, None]
     theta = angles(steps * lon_idx[None, None, :] % pts[None], pts[None])
     dc, ds = lax.optimization_barrier((jnp.cos(theta), jnp.sin(theta)))
-    e1 = (dc[0], ds[0])
-    e64 = (dc[1], ds[1])
-    lo = powers(e1, 8)
-    e8 = cmul((lo[0][:, 7], lo[1][:, 7]), e1)
-    hi = powers(e8, 8)
-    cos_t, sin_t = outer(lo, hi)
-    rhs = jnp.concatenate([cos_t.astype(jnp.bfloat16), sin_t.astype(jnp.bfloat16)], 1)
-    p0 = powers(e64, 4)
-    e256 = cmul((p0[0][:, 3], p0[1][:, 3]), e64)
+    sq = [(dc[0], ds[0])]
+    while len(sq) < 6:
+        sq.append(cmul(sq[-1], sq[-1]))
+    lo = bit_powers(sq[:3], 8)
+    hi = bit_powers(sq[3:6], 8)
+    c0, s0 = (jnp.swapaxes(x, 1, 2)[:, :, None, :] for x in lo)
+    c1, s1 = (jnp.swapaxes(x, 1, 2)[:, :, :, None] for x in hi)
+    rows_n, lon_n = c0.shape[0], c0.shape[1]
+    cos_t = (c1 * c0 - s1 * s0).astype(jnp.bfloat16).reshape(rows_n, lon_n, 64)
+    sin_t = (s1 * c0 + c1 * s0).astype(jnp.bfloat16).reshape(rows_n, lon_n, 64)
+    rhs = jnp.concatenate([cos_t, sin_t], -1)
+    sq = [(dc[1], ds[1])]
+    while len(sq) < 5:
+        sq.append(cmul(sq[-1], sq[-1]))
     n_a1 = -(-ablocks // 4)
-    p1 = powers(e256, n_a1)
+    p0 = bit_powers(sq[:2], 4)
+    p1 = bit_powers(sq[2:5], n_a1)
     return rhs, p0, p1
 
 
-def row_synthesis(coef_row, rhs, p0c, p0s, p1c, p1s, points):
-    fields = coef_row.shape[1]
-    waves = coef_row.shape[2]
+def rows_synthesis(coef, rhs, p0, p1, points):
+    rows = coef.shape[0]
+    fields = coef.shape[2]
+    waves = coef.shape[3]
     ablocks = waves // 64
-    lon_idx = jnp.arange(rhs.shape[-1], dtype=jnp.int32)
-    cosp, sinp = outer((p0c[None], p0s[None]), (p1c[None], p1s[None]))
-    cosp = cosp[0, :ablocks]
-    sinp = sinp[0, :ablocks]
-    blocks = coef_row.reshape(2, fields, ablocks, 64)
-    c0 = blocks[0]
-    c1 = blocks[1]
+    lon_idx = jnp.arange(rhs.shape[1], dtype=jnp.int32)
+    blocks = coef.reshape(rows, 2, fields, ablocks, 64)
+    c0 = blocks[:, 0]
+    c1 = blocks[:, 1]
     lhs = jnp.stack(
-        [jnp.concatenate([c0, -c1], -1), jnp.concatenate([c1, c0], -1)], 0
+        [jnp.concatenate([c0, -c1], -1), jnp.concatenate([c1, c0], -1)], 1
     )
-    part = jnp.einsum("dfab,bi->dfai", lhs, rhs, preferred_element_type=jnp.float32)
-    total = jnp.sum(part[0] * cosp[None] - part[1] * sinp[None], axis=1)
-    return jnp.where(lon_idx[None, :] < points, total, jnp.zeros_like(total))
+    part = jnp.einsum("rdfab,rib->rdfai", lhs, rhs, preferred_element_type=jnp.float32)
+    cosp, sinp = outer(p0, p1)
+    cosp = cosp[:, :ablocks]
+    sinp = sinp[:, :ablocks]
+    total = jnp.sum(part[:, 0] * cosp[:, None] - part[:, 1] * sinp[:, None], axis=2)
+    return jnp.where(lon_idx[None, None, :] < points[:, None, None], total, jnp.zeros_like(total))
 
 
 def on_device(spec, legendre, slot_wave, row_lons, band_rows, rows_per_dev):
@@ -90,7 +99,8 @@
     first_row = (lax.axis_index("wave") * n_r + lax.axis_index("lev_r")) * rows_per_dev
     my_rows = lax.dynamic_slice_in_dim(band_rows, first_row, rows_per_dev)
     row_points = row_lons[my_rows]
-    rhs_all, p0_all, p1_all = rows_tables(row_points, waves)
+    tables = rows_tables(row_points, waves)
+    gathered, tables = lax.optimization_barrier((gathered, tables))
     first_slot = (lax.axis_index("wave") * n_lev + lev_idx) * per_dev
     my_waves = lax.dynamic_slice_in_dim(slot_wave, first_slot, per_dev)
     degree = jnp.arange(waves, dtype=jnp.int32)
@@ -125,13 +135,21 @@
     factor = jnp.where(keep, jnp.where(wave_idx[None, :] == 0, 1.0, 2.0), 0.0).astype(jnp.float32)
     coef = (coef * factor[None, None]).astype(jnp.bfloat16)
     coef_rows = jnp.moveaxis(coef, 2, 0)
-    grid = lax.map(
-        lambda item: row_synthesis(*item), (coef_rows, rhs_all, p0_all[0], p0_all[1], p1_all[0], p1_all[1], row_points)
-    )
+    rhs_all, (p0c, p0s), (p1c, p1s) = tables
+    half = rows_per_dev // 2 if rows_per_dev % 2 == 0 else rows_per_dev
+    outs = []
+    for h in range(0, rows_per_dev, half):
+        sl = slice(h, h + half)
+        piece = (coef_rows[sl], rhs_all[sl], (p0c[sl], p0s[sl]), (p1c[sl], p1s[sl]), row_points[sl])
+        if outs:
+            outs[-1], piece = lax.optimization_barrier((outs[-1], piece))
+        outs.append(rows_synthesis(*piece))
+    grid = jnp.concatenate(outs, 0) if len(outs) > 1 else outs[0]
     lon = grid.shape[-1]
     fpd = fpg // n_r
-    grid = grid.reshape(rows_per_dev, n_r, fpd, lon)
-    grid = lax.all_to_all(grid, "lev_r", split_axis=1, concat_axis=0, tiled=True)
+    if n_r > 1:
+        grid = grid.reshape(rows_per_dev, n_r, fpd, lon)
+        grid = lax.all_to_all(grid, "lev_r", split_axis=1, concat_axis=0, tiled=True)
     return grid.reshape(n_r * rows_per_dev, fpd, lon)
 
 

time: 146 us -> 114 us (0.78)
  local copies, waits for them, and re-layouts: 65 us -> 36 us
  matrix products: 23.9 us -> 14.4 us
  waiting for transfers between devices: 0.01 us -> 4.97 us
  other arithmetic: 42.8 us -> 44.4 us
    dynamic_slice x56 -> x0, local copies, waits for them, and re-layouts: 29.4 us -> none  [on_device(): lax.map(lambda item: row_synthesis(*item), (coef_rows, rhs_all, p0_all[0]...]
    convert_element_type x0 -> x2, local copies, waits for them, and re-layouts: none -> 21.3 us  [the longest x1 10.7 us: rows_tables(): cos_t = (c1 * c0 - s1 * s0).astype(jnp.bfloat16).reshape(rows_n, lon_n, 64)]
    while x2 -> x0, local copies, waits for them, and re-layouts: 14 us -> none  [on_device(): lax.map(lambda item: row_synthesis(*item), (coef_rows, rhs_all, p0_all[0]...]
    concatenate x1 -> x2, other arithmetic: 5.5 us -> 15.6 us  [the longest x1 14.7 us: rows_tables(): rhs = jnp.concatenate([cos_t, sin_t], -1)]
    dot_general x8 -> x2, matrix products: 18 us -> 8.98 us  [rows_synthesis(): jnp.einsum('rdfab,rib->rdfai', lhs, rhs, preferred_element_type=jnp.float32)]
    unnamed x17 -> x0, other arithmetic: 7.41 us -> none
    unnamed x40 -> x42, local copies, waits for them, and re-layouts: 9.64 us -> 2.27 us
    slice x8 -> x10, local copies, waits for them, and re-layouts: 0.08 us -> 5.7 us  [the longest x2 1.34 us: on_device(): rhs_all[sl]]
  transfers between devices with their start and end apart: 2 -> 2, of which waited for: 0 -> 1; matrix products, arithmetic and copies ran while one was open for 35% -> 57% of each run, Pallas kernels for 0% -> 0%
where the time goes in v8:
time: 114 us; the launch traced here: 113 us
  other arithmetic  44.4 us (39%)
  local copies, waits for them, and re-layouts  36 us (32%)
  matrix products  14.4 us (13%)
  starting transfers between devices  12.5 us (11%)
  waiting for transfers between devices  4.97 us (4%)
    concatenate x1, other arithmetic, rows_tables(): rhs = jnp.concatenate([cos_t, sin_t], -1)  14.7 us
    convert_element_type x1, local copies, waits for them, and re-layouts, rows_tables(): cos_t = (c1 * c0 - s1 * s0).astype(jnp.bfloat16).reshape(rows_n, lon_n, 64)  10.7 us
    convert_element_type x1, local copies, waits for them, and re-layouts, rows_tables(): sin_t = (s1 * c0 + c1 * s0).astype(jnp.bfloat16).reshape(rows_n, lon_n, 64)  10.6 us
    dot_general x2, matrix products, rows_synthesis(): jnp.einsum('rdfab,rib->rdfai', lhs, rhs, preferred_element_type=jnp.float32)  8.98 us
    all_to_all x1, starting transfers between devices, on_device(): lax.all_to_all(fourier, ('wave', 'lev_g', 'lev_r'), split_axis=0, concat_...  7.2 us
    convert_element_type x1, other arithmetic, rows_tables(): cos_t = (c1 * c0 - s1 * s0).astype(jnp.bfloat16).reshape(rows_n, lon_n, 64)  5.83 us
    all_to_all x1, starting transfers between devices, on_device(): lax.all_to_all(spec_v, ('lev_g', 'lev_r'), split_axis=0, concat_axis=0, t...  5.32 us
    all_to_all x1, waiting for transfers between devices, on_device(): lax.all_to_all(fourier, ('wave', 'lev_g', 'lev_r'), split_axis=0, concat_...  4.97 us
  transfers between devices with their start and end apart: 2, of which 1 were waited for; matrix products, arithmetic and copies ran while one was open for 57% of the time, Pallas kernels for 0%

profile of v8, /device:TPU:0, one launch (start us, length us, event | category | flops | bytes accessed | tf_op | source)
XLA Modules:
  0.0 112.8 jit_solution(5059483739783035032)
XLA Ops:
  0.0 5.3 %all-to-all-start = ((bf16[8,40,2,2,1280]{4,3,2,1,0:T(2,128)(2,1)}), bf16[8,40,2,2,1280]{4,3,2,1,0:T(2,128)(2,1)}, u32[]{:S(2)}, u32[]{:S(2)}) async-start(bf16[8,40,2,2,1280]{4,3,2,1,0:T(2,128)(2,1)} %bitcast.159), calls=%async_computation | async-start | bytes 6553600 | tf_op jit(solution)/shard_map/all_to_all | solution.py:97
  6.2 4.5 %fusion.57 = (f32[2,8,5136]{2,1,0:T(8,128)S(1)}, f32[2,8,5136]{2,1,0:T(8,128)S(1)}) fusion(f32[8]{0:T(128)S(1)} %get-tuple-element.109, pred[8]{0:T(512)(128)(4,1)S(1)} %broadcast_compare_fusion, s32[8]{0:T(128)S(1)} %get-tuple-element.108, s32[2,5136]{1,0:T(2,128)S(1)} %iota_multiply_fusion), kind=kLoop, calls=%fused_computation.141 | loop fusion | flops 821760 | bytes 698568 | tf_op jit(solution)/shard_map/sin | solution.py:45
  10.7 1.0 multiply_subtract_fusion.2
  14.9 2.0 %fusion.34 = (f32[8,5136,8]{1,2,0:T(8,128)S(1)}, f32[8,5136,8]{1,2,0:T(8,128)S(1)}, f32[8,5136,8]{1,2,0:T(8,128)S(1)}, f32[8,5136,8]{1,2,0:T(8,128)S(1)}) fusion(f32[8,5136]{1,0:T(8,128)S(1)} %get-tuple-element.113, f32[8,5136]{1,0:T(8,128)S(1)} %get-tuple-element.76, f32[8,5136]{1,0:T(8,128)S(1)} %get-tuple-element.77, f32[8,5136]{1,0:T(8,128)S(1)} %get-tuple-element.78, ...), kind=kLoop, calls=%fused_computation.69 | loop fusion | flops 14462976 | bytes 7231512 | tf_op jit(solution)/shard_map/sub | solution.py:16
  16.9 5.8 %fusion.3 = (bf16[8,5136,64]{1,2,0:T(8,128)(2,1)}, bf16[8,5136,64]{1,2,0:T(8,128)(2,1)}) fusion(f32[8,5136,8]{1,2,0:T(8,128)S(1)} %get-tuple-element.102, f32[8,5136,8]{1,2,0:T(8,128)S(1)} %get-tuple-element.63, f32[8,5136,8]{1,2,0:T(8,128)S(1)} %get-tuple-element.103, f32[8,5136,8]{1,2,0:T(8,128)S(1)} %get-tuple-element.62), kind=kLoop, calls=%fused_computation.9 | loop fusion | flops 21037056 | bytes 15777792 | tf_op jit(solution)/shard_map/convert_element_type | solution.py:54
  22.7 10.7 %copy.63 = bf16[8,5136,64]{2,1,0:T(8,128)(2,1)} copy(bf16[8,5136,64]{1,2,0:T(8,128)(2,1)} %get-tuple-element.52) | data formatting | bytes 10518528 | tf_op jit(solution)/shard_map/convert_element_type | solution.py:54
  33.4 10.6 %copy.64 = bf16[8,5136,64]{2,1,0:T(8,128)(2,1)} copy(bf16[8,5136,64]{1,2,0:T(8,128)(2,1)} %get-tuple-element.53) | data formatting | bytes 10518528 | tf_op jit(solution)/shard_map/convert_element_type | solution.py:55
  44.7 14.7 %pad_maximum_fusion = bf16[8,5136,128]{2,1,0:T(8,128)(2,1)} fusion(bf16[8,5136,64]{2,1,0:T(8,128)(2,1)} %copy.64, bf16[8,5136,64]{2,1,0:T(8,128)(2,1)} %copy.63), kind=kLoop, calls=%fused_computation.5 | loop fusion | flops 21037056 | bytes 21037056 | tf_op jit(solution)/shard_map/concatenate | solution.py:56
  61.1 2.3 %broadcast_select_fusion.1 = (bf16[40,16,1280]{2,1,0:T(8,128)(2,1)}, bf16[40,16,1280]{2,1,0:T(8,128)(2,1)}) fusion(bf16[40,16,1280]{2,1,0:T(8,128)(2,1)S(1)} %copy-done.6, pred[40,1280]{1,0:T(8,128)(4,1)S(1)} %get-tuple-element.106, pred[40,1280]{1,0:T(8,128)(4,1)S(1)} %get-tuple-element.107), kind=kLoop, calls=%fused_computation.66 | loop fusion | flops 1638400 | bytes 5017600 | tf_op jit(solution)/shard_map/jit(_where)/select_n | solution.py:112
  64.0 1.5 %fusion.48 = (f32[8,4,5136]{2,0,1:T(8,128)S(1)}, f32[8,4,5136]{2,0,1:T(8,128)S(1)}) fusion(f32[8,5136]{1,0:T(8,128)} %get-tuple-element.43, f32[8,5136]{1,0:T(8,128)S(1)} %get-tuple-element.42, f32[8,5136]{1,0:T(8,128)} %get-tuple-element.88, f32[8,5136]{1,0:T(8,128)} %get-tuple-element.111, pred[4]{0:T(512)(128)(4,1)} %get-tuple-element.116, ...), kind=kLoop, calls=%fused_computation.105 | loop fusion | flops 2300928 | bytes 1972232 | tf_op jit(solution)/shard_map/add | solution.py:16
  65.4 1.8 %fusion.46 = (f32[8,5,5136]{2,0,1:T(8,128)S(1)}, f32[8,5,5136]{2,0,1:T(8,128)S(1)}) fusion(f32[8,5136]{1,0:T(8,128)} %get-tuple-element.112, f32[8,5136]{1,0:T(8,128)} %get-tuple-element.37, f32[8,5136]{1,0:T(8,128)S(1)} %get-tuple-element.39, f32[8,5136]{1,0:T(8,128)S(1)} %get-tuple-element.38, f32[8,5136]{1,0:T(8,128)} %get-tuple-element.41, ...), kind=kLoop, calls=%fused_computation.99 | loop fusion | flops 4519680 | bytes 2629647 | tf_op jit(solution)/shard_map/add | solution.py:16
  68.2 1.0 fusion.77
  71.0 4.0 %fusion.40 = f32[40,2,8,2,32]{4,2,3,1,0:T(8,128)S(1)} fusion(bf16[8,40,2,2,1280]{4,3,2,1,0:T(2,128)(2,1)} %all-to-all-done, bf16[40,16,1280]{2,1,0:T(8,128)(2,1)S(1)} %copy-done.8, bf16[40,16,1280]{2,1,0:T(8,128)(2,1)S(1)} %copy-done.7), kind=kOutput, calls=%fused_computation.75 | convolution fusion | flops 111411200 | bytes 6717440 | tf_op jit(solution)/shard_map/lscfk,sjk->sclfj/dot_general | solution.py:114
  78.0 1.0 reshape.775
  79.0 7.2 %all-to-all-start.1 = ((bf16[32,2,640]{2,1,0:T(2,128)(2,1)}), bf16[32,2,640]{2,1,0:T(2,128)(2,1)S(1)}, u32[]{:S(2)}, u32[]{:S(2)}) async-start(bf16[32,2,640]{2,1,0:T(2,128)(2,1)} %reshape.775), calls=%async_computation.1 | async-start | bytes 163840 | tf_op jit(solution)/shard_map/all_to_all | solution.py:127
  87.1 1.5 %copy.79 = f32[4,20,5136]{2,1,0:T(8,128)} copy(f32[4,20,5136]{2,0,1:T(4,128)S(1)} %bitcast.155) | data formatting | bytes 3287040 | tf_op jit(solution)/shard_map/add | solution.py:33
  88.6 5.0 %all-to-all-done.1 = bf16[32,2,640]{2,1,0:T(2,128)(2,1)S(1)} async-done(((bf16[32,2,640]{2,1,0:T(2,128)(2,1)}), bf16[32,2,640]{2,1,0:T(2,128)(2,1)S(1)}, u32[]{:S(2)}, u32[]{:S(2)}) %all-to-all-start.1) | async-done | bytes 81952 | tf_op jit(solution)/shard_map/all_to_all | solution.py:127
  94.4 1.4 %fusion.29 = bf16[8,2,2,1280]{3,0,2,1:T(8,128)(2,1)S(1)} fusion(bf16[2,2,8,1280]{3,2,1,0:T(8,128)(2,1)S(1)} %reshape.739, s32[1280]{0:T(1024)S(1)} %copy-done.15, f32[8,1280]{1,0:T(8,128)S(1)} %copy-done.11), kind=kOutput, calls=%fused_computation.36 | convolution fusion | flops 106577920 | bytes 209920 | tf_op jit(solution)/shard_map/cfrs,sm->cfrm/dot_general | solution.py:133
  96.2 5.8 %fusion.7 = f32[4,2,2,20,5136]{4,3,2,1,0:T(8,128)S(1)} fusion(bf16[8,5136,128]{2,1,0:T(8,128)(2,1)} %pad_maximum_fusion, bf16[4,1,2,20,128]{4,3,2,1,0:T(8,128)(2,1)S(1)} %get-tuple-element.99, bf16[4,1,2,20,128]{4,3,2,1,0:T(8,128)(2,1)S(1)} %get-tuple-element.98), kind=kOutput, calls=%fused_computation.13 | convolution fusion | flops 420782080 | bytes 11915264 | tf_op jit(solution)/shard_map/rdfab,rib->rdfai/dot_general | solution.py:78
  102.0 1.1 fusion.16
  103.4 1.7 %multiply_subtract_fusion = (f32[4,5,4,5136]{3,0,2,1:T(4,128)S(1)}, f32[4,5,4,5136]{3,0,2,1:T(4,128)S(1)}) fusion(f32[4,4,5136]{2,0,1:T(4,128)S(1)} %copy-done.9, f32[4,5,5136]{2,0,1:T(4,128)S(1)} %get-tuple-element.35, f32[4,4,5136]{2,0,1:T(4,128)} %get-tuple-element.34, f32[4,5,5136]{2,0,1:T(4,128)S(1)} %copy-done.3), kind=kLoop, calls=%fused_computation.62 | loop fusion | flops 2465280 | bytes 4766208 | tf_op jit(solution)/shard_map/sub | solution.py:32
  106.3 1.3 %slice-done = bf16[4,5136,128]{2,1,0:T(8,128)(2,1)S(1)} async-done(((bf16[8,5136,128]{2,1,0:T(8,128)(2,1)}), bf16[4,5136,128]{2,1,0:T(8,128)(2,1)S(1)}, s32[]{:S(2)}) %slice-start) | async-done | bytes 5259288 | tf_op jit(solution)/shard_map/slice | solution.py:143
  107.6 3.2 %fusion.5 = f32[4,2,2,20,5136]{4,3,2,1,0:T(8,128)S(1)} fusion(bf16[4,5136,128]{2,1,0:T(8,128)(2,1)S(1)} %slice-done, bf16[4,1,2,20,128]{4,3,2,1,0:T(8,128)(2,1)S(1)} %get-tuple-element.97, bf16[4,1,2,20,128]{4,3,2,1,0:T(8,128)(2,1)S(1)} %get-tuple-element.96), kind=kOutput, calls=%fused_computation.11 | convolution fusion | flops 420782080 | bytes 11915264 | tf_op jit(solution)/shard_map/rdfab,rib->rdfai/dot_general | solution.py:78
  110.8 1.0 fusion.12
  (99 shorter events, 16.9 us)
Async XLA Ops:
  0.0 5.4 %copy-start = (s32[32]{0:T(128)S(1)}, s32[32]{0:T(128)}, u32[]{:S(2)}) copy-start(s32[32]{0:T(128)} %param.9) | copy-start | bytes 388
  0.0 5.3 %copy-start.16 = (s32[32]{0:T(128)S(1)}, s32[32]{0:T(128)}, u32[]{:S(2)}) copy-start(s32[32]{0:T(128)} %param.10) | copy-start | bytes 388
  0.0 6.1 %copy-start.13 = (s32[2]{0:T(128)S(1)}, s32[2]{0:T(128)}, u32[]{:S(2)}) copy-start(s32[2]{0:T(128)} %constant.43.clone) | copy-start | bytes 28
  0.0 67.3 %all-to-all-start = ((bf16[8,40,2,2,1280]{4,3,2,1,0:T(2,128)(2,1)}), bf16[8,40,2,2,1280]{4,3,2,1,0:T(2,128)(2,1)}, u32[]{:S(2)}, u32[]{:S(2)}) async-start(bf16[8,40,2,2,1280]{4,3,2,1,0:T(2,128)(2,1)} %bitcast.159), calls=%async_computation | async-start | bytes 6553600 | tf_op jit(solution)/shard_map/all_to_all | solution.py:97
  44.7 16.3 %copy-start.6 = (bf16[40,16,1280]{2,1,0:T(8,128)(2,1)S(1)}, bf16[40,16,1280]{2,1,0:T(8,128)(2,1)}, u32[]{:S(2)}) copy-start(bf16[40,16,1280]{2,1,0:T(8,128)(2,1)} %param.7) | copy-start | bytes 4915204
  63.9 1.5 %copy-start.14 = (pred[5]{0:T(512)(128)(4,1)S(1)}, pred[5]{0:T(512)(128)(4,1)}, u32[]{:S(2)}) copy-start(pred[5]{0:T(512)(128)(4,1)} %and_compare_fusion.2) | copy-start | bytes 19
  68.2 2.8 %copy-start.8 = (bf16[40,16,1280]{2,1,0:T(8,128)(2,1)S(1)}, bf16[40,16,1280]{2,1,0:T(8,128)(2,1)}, u32[]{:S(2)}) copy-start(bf16[40,16,1280]{2,1,0:T(8,128)(2,1)} %get-tuple-element.55) | copy-start | bytes 4915204
  69.2 1.8 %copy-start.7 = (bf16[40,16,1280]{2,1,0:T(8,128)(2,1)S(1)}, bf16[40,16,1280]{2,1,0:T(8,128)(2,1)}, u32[]{:S(2)}) copy-start(bf16[40,16,1280]{2,1,0:T(8,128)(2,1)} %get-tuple-element.54) | copy-start | bytes 4915204
  77.4 8.8 %copy-start.4 = (f32[4,5,5136]{2,0,1:T(4,128)S(1)}, f32[4,5,5136]{2,0,1:T(4,128)}, u32[]{:S(2)}) copy-start(f32[4,5,5136]{2,0,1:T(4,128)} %get-tuple-element.67) | copy-start | bytes 1232644
  77.4 8.8 %copy-start.5 = (f32[4,5,5136]{2,0,1:T(4,128)S(1)}, f32[4,5,5136]{2,0,1:T(4,128)}, u32[]{:S(2)}) copy-start(f32[4,5,5136]{2,0,1:T(4,128)} %get-tuple-element.69) | copy-start | bytes 1232644
  77.4 8.8 %copy-start.10 = (f32[4,4,5136]{2,0,1:T(4,128)S(1)}, f32[4,4,5136]{2,0,1:T(4,128)}, u32[]{:S(2)}) copy-start(f32[4,4,5136]{2,0,1:T(4,128)} %get-tuple-element.73) | copy-start | bytes 986116
  79.0 14.6 %all-to-all-start.1 = ((bf16[32,2,640]{2,1,0:T(2,128)(2,1)}), bf16[32,2,640]{2,1,0:T(2,128)(2,1)S(1)}, u32[]{:S(2)}, u32[]{:S(2)}) async-start(bf16[32,2,640]{2,1,0:T(2,128)(2,1)} %reshape.775), calls=%async_computation.1 | async-start | bytes 163840 | tf_op jit(solution)/shard_map/all_to_all | solution.py:127
  88.6 5.8 %copy-start.11 = (f32[8,1280]{1,0:T(8,128)S(1)}, f32[8,1280]{1,0:T(8,128)}, u32[]{:S(2)}) copy-start(f32[8,1280]{1,0:T(8,128)} %compare_select_fusion) | copy-start | bytes 122884
  88.6 5.8 %copy-start.15 = (s32[1280]{0:T(1024)S(1)}, s32[1280]{0:T(1024)}, u32[]{:S(2)}) copy-start(s32[1280]{0:T(1024)} %param.8) | copy-start | bytes 15364
  96.2 5.8 %copy-start.2 = (f32[4,20,5136]{2,1,0:T(8,128)S(1)}, f32[4,20,5136]{2,1,0:T(8,128)}, u32[]{:S(2)}) copy-start(f32[4,20,5136]{2,1,0:T(8,128)} %copy.79) | copy-start | bytes 4930564
  102.0 1.4 %copy-start.3 = (f32[4,5,5136]{2,0,1:T(4,128)S(1)}, f32[4,5,5136]{2,0,1:T(4,128)}, u32[]{:S(2)}) copy-start(f32[4,5,5136]{2,0,1:T(4,128)} %get-tuple-element.33) | copy-start | bytes 1232644
  102.0 1.4 %copy-start.9 = (f32[4,4,5136]{2,0,1:T(4,128)S(1)}, f32[4,4,5136]{2,0,1:T(4,128)}, u32[]{:S(2)}) copy-start(f32[4,4,5136]{2,0,1:T(4,128)} %get-tuple-element.36) | copy-start | bytes 986116
  105.1 2.5 %slice-start = ((bf16[8,5136,128]{2,1,0:T(8,128)(2,1)}), bf16[4,5136,128]{2,1,0:T(8,128)(2,1)S(1)}, s32[]{:S(2)}) async-start(bf16[8,5136,128]{2,1,0:T(8,128)(2,1)} %pad_maximum_fusion), calls=%async_computation.2 | async-start | bytes 10518528 | tf_op jit(solution)/shard_map/slice | solution.py:143
  105.3 0.8 copy-start.12
  110.8 2.0 %copy-start.1 = (s32[32]{0:T(128)S(1)}, s32[32]{0:T(128)}, u32[]{:S(2)}) copy-start(s32[32]{0:T(128)} %param.9) | copy-start | bytes 388

commit v9 on v6

--- a/solution.py
+++ b/solution.py
@@ -13,30 +13,32 @@
 
 
 def trig_pair(step, lon_idx, points, count):
-    mult = jnp.arange(count, dtype=jnp.int32)[:, None] * step
-    theta = angles(mult * lon_idx[None, :] % points, points)
+    mult = jnp.arange(count, dtype=jnp.int32)[None, :, None] * step
+    pts = points[:, None, None]
+    theta = angles(mult * lon_idx[None, None, :] % pts, pts)
     return jnp.cos(theta), jnp.sin(theta)
 
 
 def compose(first, second):
     c0, s0 = first
     c1, s1 = second
-    cos = c1[:, None] * c0[None] - s1[:, None] * s0[None]
-    sin = s1[:, None] * c0[None] + c1[:, None] * s0[None]
-    return cos.reshape(-1, cos.shape[-1]), sin.reshape(-1, sin.shape[-1])
+    cos = c1[:, :, None] * c0[:, None] - s1[:, :, None] * s0[:, None]
+    sin = s1[:, :, None] * c0[:, None] + c1[:, :, None] * s0[:, None]
+    shape = (cos.shape[0], -1, cos.shape[-1])
+    return cos.reshape(shape), sin.reshape(shape)
 
 
-def row_tables(points, waves):
+def rows_tables(points, waves):
     ablocks = waves // 64
     lon_len = 20 + 4 * (waves - 1)
     lon_idx = jnp.arange(lon_len, dtype=jnp.int32)
     cos_t, sin_t = compose(trig_pair(1, lon_idx, points, 8), trig_pair(8, lon_idx, points, 8))
-    rhs = jnp.concatenate([cos_t.astype(jnp.bfloat16), sin_t.astype(jnp.bfloat16)], 0)
+    rhs = jnp.concatenate([cos_t.astype(jnp.bfloat16), sin_t.astype(jnp.bfloat16)], 1)
     n_a1 = -(-ablocks // 4)
     cosp, sinp = compose(
         trig_pair(64, lon_idx, points, 4), trig_pair(256, lon_idx, points, n_a1)
     )
-    return rhs, cosp[:ablocks], sinp[:ablocks]
+    return rhs, cosp[:, :ablocks], sinp[:, :ablocks]
 
 
 def row_synthesis(coef_row, rhs, cosp, sinp, points):
@@ -71,10 +73,10 @@
     first_row = (lax.axis_index("wave") * n_r + lax.axis_index("lev_r")) * rows_per_dev
     my_rows = lax.dynamic_slice_in_dim(band_rows, first_row, rows_per_dev)
     row_points = row_lons[my_rows]
-    if rows_per_dev == 1:
-        tables = tuple(t[None] for t in row_tables(row_points[0], waves))
+    if rows_per_dev <= 2:
+        tables = rows_tables(row_points, waves)
     else:
-        tables = lax.map(lambda p: row_tables(p, waves), row_points)
+        tables = lax.map(lambda p: tuple(t[0] for t in rows_tables(p[None], waves)), row_points)
     gathered, tables = lax.optimization_barrier((gathered, tables))
     first_slot = (lax.axis_index("wave") * n_lev + lev_idx) * per_dev
     my_waves = lax.dynamic_slice_in_dim(slot_wave, first_slot, per_dev)
@@ -112,6 +114,14 @@
     coef_rows = jnp.moveaxis(coef, 2, 0)
     if rows_per_dev == 1:
         grid = row_synthesis(coef_rows[0], *(t[0] for t in tables), row_points[0])[None]
+    elif rows_per_dev <= 2:
+        grid = jnp.stack(
+            [
+                row_synthesis(coef_rows[t], *(x[t] for x in tables), row_points[t])
+                for t in range(rows_per_dev)
+            ],
+            0,
+        )
     else:
         grid = lax.map(lambda item: row_synthesis(*item), (coef_rows,) + tuple(tables) + (row_points,))
     lon = grid.shape[-1]
@@ -126,12 +136,10 @@
         n_wave = mesh.shape["wave"]
         n_lev = mesh.shape["lev"]
         rows_w = band_rows.shape[0] // n_wave
-        if n_lev >= rows_w:
-            n_r = rows_w
-            rows_per_dev = 1
-        else:
-            n_r = n_lev
+        rows_per_dev = 2 if rows_w % 2 == 0 and n_lev % (rows_w // 2) == 0 else 1
+        if n_lev < rows_w // rows_per_dev:
             rows_per_dev = rows_w // n_lev
+        n_r = rows_w // rows_per_dev
         n_g = n_lev // n_r
         devs = np.asarray(mesh.devices).reshape(n_wave, n_g, n_r)
         mesh2 = Mesh(devs, ("wave", "lev_g", "lev_r"))

time: 84.9 us -> 118 us (1.39)
  other arithmetic: 15.9 us -> 47.7 us
  local copies, waits for them, and re-layouts: 8.25 us -> 33.7 us
  waiting for transfers between devices: 26.8 us -> 3.38 us
  between operations: 4.27 us -> 0.37 us
  starting transfers between devices: 9.95 us -> 12.3 us
    cos x3, other arithmetic: 6.98 us -> 29.6 us  [trig_pair(): return (jnp.cos(theta), jnp.sin(theta))]
    all_to_all x1, waiting for transfers between devices: 20.6 us -> 0.01 us  [on_device(): lax.all_to_all(spec_v, ('lev_g', 'lev_r'), split_axis=0, concat_axis=0, t...]
    unnamed x17 -> x27, local copies, waits for them, and re-layouts: 2.32 us -> 9.18 us
    convert_element_type x0 -> x2, local copies, waits for them, and re-layouts: none -> 5.18 us  [the longest x1 2.59 us: rows_tables(): cos_t.astype(jnp.bfloat16)]
    slice x0 -> x3, local copies, waits for them, and re-layouts: none -> 4.48 us  [the longest x2 3.82 us: on_device(): x[t]]
    concatenate x0 -> x1, other arithmetic: none -> 4.1 us  [rows_tables(): jnp.concatenate([cos_t.astype(jnp.bfloat16), sin_t.astype(jnp.bfloat16)], 1)]
    gather x1 -> x2, local copies, waits for them, and re-layouts: 0.58 us -> 4.22 us  [on_device(): sums[:, :, :, 1][..., lat_idx]]
    all_to_all x1, waiting for transfers between devices: 6.23 us -> 3.38 us  [on_device(): lax.all_to_all(fourier, ('wave', 'lev_g', 'lev_r'), split_axis=0, concat_...]
  transfers between devices with their start and end apart: 2 -> 2, of which waited for: 2 -> 1; matrix products, arithmetic and copies ran while one was open for 19% -> 46% of each run, Pallas kernels for 0% -> 0%
where the time goes in v9:
time: 118 us; the launch traced here: 117 us
  other arithmetic  47.7 us (40%)
  local copies, waits for them, and re-layouts  33.7 us (29%)
  starting transfers between devices  12.3 us (10%)
  matrix products  10.4 us (9%)
  blocking collectives  9.2 us (8%)
  waiting for transfers between devices  3.38 us (3%)
    cos x3, other arithmetic, trig_pair(): return (jnp.cos(theta), jnp.sin(theta))  29.6 us
    all_to_all x1, blocking collectives, on_device(): lax.all_to_all(grid, 'lev_r', split_axis=1, concat_axis=0, tiled=True)  9.2 us
    unnamed x27, local copies, waits for them, and re-layouts  9.18 us
    all_to_all x1, starting transfers between devices, on_device(): lax.all_to_all(fourier, ('wave', 'lev_g', 'lev_r'), split_axis=0, concat_...  6.95 us
    dot_general x1, matrix products, on_device(): jnp.einsum('lscfk,sjk->sclfj', gathered, leg2, preferred_element_type=jnp...  5.79 us
    all_to_all x1, starting transfers between devices, on_device(): lax.all_to_all(spec_v, ('lev_g', 'lev_r'), split_axis=0, concat_axis=0, t...  5.3 us
    gather x2, local copies, waits for them, and re-layouts, on_device(): sums[:, :, :, 1][..., lat_idx]  4.22 us
    concatenate x1, other arithmetic, rows_tables(): jnp.concatenate([cos_t.astype(jnp.bfloat16), sin_t.astype(jnp.bfloat16)], 1)  4.1 us
  transfers between devices with their start and end apart: 2, of which 1 were waited for; matrix products, arithmetic and copies ran while one was open for 46% of the time, Pallas kernels for 0%

profile of v9, /device:TPU:0, one launch (start us, length us, event | category | flops | bytes accessed | tf_op | source)
XLA Modules:
  0.0 117.0 jit_solution(5353735122317302742)
XLA Ops:
  0.0 5.3 %all-to-all-start = ((bf16[8,40,2,2,1280]{4,3,2,1,0:T(2,128)(2,1)}), bf16[8,40,2,2,1280]{4,3,2,1,0:T(2,128)(2,1)}, u32[]{:S(2)}, u32[]{:S(2)}) async-start(bf16[8,40,2,2,1280]{4,3,2,1,0:T(2,128)(2,1)} %bitcast.156), calls=%async_computation | async-start | bytes 6553600 | tf_op jit(solution)/shard_map/all_to_all | solution.py:71
  8.1 1.3 %iota_compare_fusion.2 = pred[5136]{0:T(1024)(128)(4,1)} fusion(s32[]{:T(128)} %bitcast.36), kind=kLoop, calls=%fused_computation.101 | loop fusion | flops 5136 | bytes 5140 | tf_op jit(solution)/shard_map/lt | solution.py:57
  9.7 8.8 %fusion.58 = (f32[2,8,5136]{2,1,0:T(8,128)S(1)}, f32[2,8,5136]{2,1,0:T(8,128)S(1)}, f32[2,8,5136]{2,1,0:T(8,128)S(1)}, f32[2,8,5136]{2,1,0:T(8,128)S(1)}) fusion(f32[2]{0:T(128)S(1)} %get-tuple-element.49, pred[2]{0:T(512)(128)(4,1)S(1)} %compare_bitcast_fusion, s32[2]{0:T(128)S(1)} %fusion.73, s32[8,5136]{1,0:T(8,128)S(1)} %get-tuple-element.51, ...), kind=kLoop, calls=%fused_computation.87 | loop fusion | flops 1643520 | bytes 1643538 | tf_op jit(solution)/shard_map/cos | solution.py:19
  19.2 2.6 %copy.26 = bf16[2,64,5136]{1,2,0:T(8,128)(2,1)} copy(bf16[2,64,5136]{2,1,0:T(8,128)(2,1)S(1)} %get-tuple-element.16) | data formatting | bytes 2629632 | tf_op jit(solution)/shard_map/convert_element_type | solution.py:36
  21.8 2.6 %copy.27 = bf16[2,64,5136]{1,2,0:T(8,128)(2,1)} copy(bf16[2,64,5136]{2,1,0:T(8,128)(2,1)S(1)} %get-tuple-element.17) | data formatting | bytes 2629632 | tf_op jit(solution)/shard_map/convert_element_type | solution.py:36
  25.8 4.1 %pad_maximum_fusion = bf16[2,128,5136]{1,2,0:T(8,128)(2,1)S(1)} fusion(bf16[2,64,5136]{1,2,0:T(8,128)(2,1)} %copy.27, bf16[2,64,5136]{1,2,0:T(8,128)(2,1)} %copy.26), kind=kLoop, calls=%fused_computation.26 | loop fusion | flops 5259264 | bytes 5259264 | tf_op jit(solution)/shard_map/concatenate | solution.py:36
  30.0 9.0 %fusion.66 = (f32[2,4,5136]{2,0,1:T(2,128)S(1)}, f32[2,4,5136]{2,0,1:T(2,128)S(1)}) fusion(f32[2]{0:T(128)S(1)} %get-tuple-element.49, pred[2]{0:T(512)(128)(4,1)S(1)} %broadcast_compare_fusion, s32[2]{0:T(128)S(1)} %get-tuple-element.48, s32[4,5136]{1,0:T(4,128)S(1)} %iota_multiply_fusion.1), kind=kLoop, calls=%fused_computation.106 | loop fusion | flops 410880 | bytes 410898 | tf_op jit(solution)/shard_map/cos | solution.py:19
  39.1 2.2 %broadcast_select_fusion.1 = (bf16[40,16,1280]{2,1,0:T(8,128)(2,1)}, bf16[40,16,1280]{2,1,0:T(8,128)(2,1)}) fusion(bf16[40,16,1280]{2,1,0:T(8,128)(2,1)S(1)} %copy-done.5, pred[40,1280]{1,0:T(8,128)(4,1)S(1)} %get-tuple-element.46, pred[40,1280]{1,0:T(8,128)(4,1)S(1)} %get-tuple-element.47), kind=kLoop, calls=%fused_computation.31 | loop fusion | flops 1638400 | bytes 5017600 | tf_op jit(solution)/shard_map/jit(_where)/select_n | solution.py:89
  41.3 11.8 %fusion.78 = (f32[2,5,5136]{2,0,1:T(2,128)S(1)}, f32[2,5,5136]{2,0,1:T(2,128)S(1)}) fusion(f32[2]{0:T(128)S(1)} %get-tuple-element.49, pred[2]{0:T(512)(128)(4,1)S(1)} %broadcast_compare_fusion, s32[2]{0:T(128)S(1)} %get-tuple-element.48, s32[5,5136]{1,0:T(8,128)S(1)} %iota_multiply_fusion), kind=kLoop, calls=%fused_computation.135 | loop fusion | flops 513600 | bytes 513618 | tf_op jit(solution)/shard_map/cos | solution.py:19
  53.1 1.6 %multiply_add_fusion = (f32[2,5,4,5136]{3,0,2,1:T(2,128)S(1)}, f32[2,5,4,5136]{3,0,2,1:T(2,128)}) fusion(f32[2,4,5136]{2,0,1:T(2,128)S(1)} %get-tuple-element.33, f32[2,5,5136]{2,0,1:T(2,128)S(1)} %get-tuple-element.27, f32[2,4,5136]{2,0,1:T(2,128)S(1)} %get-tuple-element.32, f32[2,5,5136]{2,0,1:T(2,128)S(1)} %get-tuple-element.26), kind=kLoop, calls=%fused_computation.41 | loop fusion | flops 1232640 | bytes 2383104 | tf_op jit(solution)/shard_map/add | solution.py:26
  54.7 3.2 %fusion.79 = (f32[1,20,5136]{2,0,1:T(1,128)}, f32[1,20,5136]{2,0,1:T(1,128)}) fusion(f32[2,20,5136]{2,0,1:T(2,128)} %bitcast.155), kind=kLoop, calls=%fused_computation.136 | loop fusion | bytes 1643520 | tf_op jit(solution)/shard_map/slice | solution.py:120
  57.9 5.8 %fusion.33 = f32[40,2,8,2,32]{4,2,3,1,0:T(8,128)} fusion(bf16[8,40,2,2,1280]{4,3,2,1,0:T(2,128)(2,1)} %all-to-all-done, bf16[40,16,1280]{2,1,0:T(8,128)(2,1)} %get-tuple-element.15, bf16[40,16,1280]{2,1,0:T(8,128)(2,1)} %get-tuple-element.14), kind=kOutput, calls=%fused_computation.40 | convolution fusion | flops 111411200 | bytes 6717440 | tf_op jit(solution)/shard_map/lscfk,sjk->sclfj/dot_general | solution.py:91
  63.7 2.2 %copy.29 = f32[40,2,8,2,32]{0,4,3,2,1:T(8,128)} copy(f32[40,2,8,2,32]{4,2,3,1,0:T(8,128)} %fusion.33) | data formatting | bytes 327680 | tf_op jit(solution)/shard_map/lscfk,sjk->sclfj/transpose | solution.py:91
  65.9 1.8 %fusion.81 = (f32[40,2,16,1,16]{0,4,3,2,1:T(8,128)S(1)}, f32[40,2,16,1,16]{0,4,3,2,1:T(8,128)}) fusion(f32[40,2,16,2,16]{0,4,3,2,1:T(8,128)} %bitcast.162), kind=kLoop, calls=%fused_computation.138 | loop fusion | bytes 327680 | tf_op jit(solution)/shard_map/slice | solution.py:96
  68.5 2.3 %gather_fusion.2 = f32[32,40,2,16]{1,3,2,0:T(8,128)} fusion(f32[40,2,16,16]{0,2,3,1:T(8,128)} %bitcast.158, s32[1024]{0:T(1024)S(1)} %pad_clamp_fusion), kind=kCustom, calls=%fused_computation.2 | custom fusion | bytes 327808 | tf_op jit(solution)/shard_map/gather | solution.py:96
  70.8 1.9 %copy.33 = f32[40,2,16,32]{0,2,3,1:T(8,128)} copy(f32[40,2,16,32]{0,2,1,3:T(8,128)} %bitcast.160) | data formatting | bytes 327680 | tf_op jit(solution)/shard_map/gather | solution.py:96
  72.7 1.7 %copy.61 = f32[40,2,16,1,16]{0,2,4,1,3:T(8,128)} copy(f32[40,2,16,1,16]{0,4,3,2,1:T(8,128)} %get-tuple-element.25) | data formatting | bytes 163840
  74.5 2.3 %gather_fusion.1 = f32[32,40,2,16]{1,3,2,0:T(8,128)} fusion(f32[40,2,16,16]{0,2,3,1:T(8,128)} %bitcast.157, s32[1024]{0:T(1024)S(1)} %pad_clamp_fusion), kind=kCustom, calls=%fused_computation.1 | custom fusion | bytes 327808 | tf_op jit(solution)/shard_map/gather | solution.py:96
  79.8 1.9 %reshape.439 = bf16[32,2,640]{2,1,0:T(2,128)(2,1)} reshape(bf16[32,2,2,8,40]{4,3,2,1,0:T(8,128)(2,1)} %bitcast.169) | data formatting | bytes 163840
  81.8 7.0 %all-to-all-start.1 = ((bf16[32,2,640]{2,1,0:T(2,128)(2,1)}), bf16[32,2,640]{2,1,0:T(2,128)(2,1)S(1)}, u32[]{:S(2)}, u32[]{:S(2)}) async-start(bf16[32,2,640]{2,1,0:T(2,128)(2,1)} %reshape.439), calls=%async_computation.1 | async-start | bytes 163840 | tf_op jit(solution)/shard_map/all_to_all | solution.py:104
  89.4 1.8 %copy.59 = f32[1,20,5136]{2,1,0:T(8,128)} copy(f32[1,20,5136]{2,0,1:T(1,128)} %get-tuple-element.18) | data formatting | bytes 821760
  93.0 3.4 %all-to-all-done.1 = bf16[32,2,640]{2,1,0:T(2,128)(2,1)S(1)} async-done(((bf16[32,2,640]{2,1,0:T(2,128)(2,1)}), bf16[32,2,640]{2,1,0:T(2,128)(2,1)S(1)}, u32[]{:S(2)}, u32[]{:S(2)}) %all-to-all-start.1) | async-done | bytes 81952 | tf_op jit(solution)/shard_map/all_to_all | solution.py:104
  97.2 2.1 %fusion.22 = bf16[2,2,8,1280]{3,2,0,1:T(8,128)(2,1)S(1)} fusion(bf16[2,8,2,1280]{3,1,2,0:T(8,128)(2,1)S(1)} %reshape.406, s32[1280]{0:T(1024)} %param.9, f32[2,1280]{1,0:T(2,128)} %compare_select_fusion), kind=kOutput, calls=%fused_computation.29 | convolution fusion | flops 106577920 | bytes 179200 | tf_op jit(solution)/shard_map/cfrs,sm->cfrm/dot_general | solution.py:110
  107.1 9.2 %all_to_all.25 = f32[2,4,2,5136]{3,2,0,1:T(2,128)S(1)} all-to-all(f32[2,4,2,5136]{3,2,0,1:T(2,128)S(1)} %pad_maximum_fusion.1), channel_id=1, replica_groups=mesh['wave'=4,'lev_g'=2,'lev_r'=4] {'lev_r'}, dimensions={1} | all-to-all | bytes 657408 | tf_op jit(solution)/shard_map/all_to_all | solution.py:130
  (76 shorter events, 20.6 us)
Async XLA Ops:
  0.0 5.5 %copy-start = (s32[32]{0:T(128)S(1)}, s32[32]{0:T(128)}, u32[]{:S(2)}) copy-start(s32[32]{0:T(128)} %param.10) | copy-start | bytes 388
  0.0 5.3 %copy-start.8 = (s32[32]{0:T(128)S(1)}, s32[32]{0:T(128)}, u32[]{:S(2)}) copy-start(s32[32]{0:T(128)} %param.11) | copy-start | bytes 388
  0.0 54.7 %all-to-all-start = ((bf16[8,40,2,2,1280]{4,3,2,1,0:T(2,128)(2,1)}), bf16[8,40,2,2,1280]{4,3,2,1,0:T(2,128)(2,1)}, u32[]{:S(2)}, u32[]{:S(2)}) async-start(bf16[8,40,2,2,1280]{4,3,2,1,0:T(2,128)(2,1)} %bitcast.156), calls=%async_computation | async-start | bytes 6553600 | tf_op jit(solution)/shard_map/all_to_all | solution.py:71
  25.8 13.3 %copy-start.5 = (bf16[40,16,1280]{2,1,0:T(8,128)(2,1)S(1)}, bf16[40,16,1280]{2,1,0:T(8,128)(2,1)}, u32[]{:S(2)}) copy-start(bf16[40,16,1280]{2,1,0:T(8,128)(2,1)} %param.8) | copy-start | bytes 4915204
  81.8 14.6 %all-to-all-start.1 = ((bf16[32,2,640]{2,1,0:T(2,128)(2,1)}), bf16[32,2,640]{2,1,0:T(2,128)(2,1)S(1)}, u32[]{:S(2)}, u32[]{:S(2)}) async-start(bf16[32,2,640]{2,1,0:T(2,128)(2,1)} %reshape.439), calls=%async_computation.1 | async-start | bytes 163840 | tf_op jit(solution)/shard_map/all_to_all | solution.py:104
  88.7 2.5 %copy-start.4 = (f32[1,20,5136]{2,0,1:T(1,128)S(1)}, f32[1,20,5136]{2,0,1:T(1,128)}, u32[]{:S(2)}) copy-start(f32[1,20,5136]{2,0,1:T(1,128)} %get-tuple-element.19) | copy-start | bytes 1232644
  101.1 1.3 %copy-start.2 = (f32[1,20,5136]{2,1,0:T(8,128)S(1)}, f32[1,20,5136]{2,1,0:T(8,128)}, u32[]{:S(2)}) copy-start(f32[1,20,5136]{2,1,0:T(8,128)} %copy.59) | copy-start | bytes 1232644
  101.1 1.3 %copy-start.3 = (f32[1,20,5136]{2,1,0:T(8,128)S(1)}, f32[1,20,5136]{2,1,0:T(8,128)}, u32[]{:S(2)}) copy-start(f32[1,20,5136]{2,1,0:T(8,128)} %copy.58) | copy-start | bytes 1232644
  104.4 1.3 %copy-start.1 = (f32[1,20,5136]{2,1,0:T(8,128)S(1)}, f32[1,20,5136]{2,1,0:T(8,128)}, u32[]{:S(2)}) copy-start(f32[1,20,5136]{2,1,0:T(8,128)} %copy.56) | copy-start | bytes 1232644
  105.7 1.0 copy-start.6
  105.7 1.1 copy-start.7

commit v10 on v3

--- a/solution.py
+++ b/solution.py
@@ -70,20 +70,16 @@
     my_waves = lax.dynamic_slice_in_dim(slot_wave, first_slot, per_dev)
     degree = jnp.arange(waves, dtype=jnp.int32)
     live_k = degree[None, :] <= trunc_top - my_waves[:, None]
-    even_mask = (live_k & (degree[None, :] % 2 == 0))[:, None, :]
-    odd_mask = (live_k & (degree[None, :] % 2 == 1))[:, None, :]
-    zeros = jnp.zeros_like(legendre)
-    leg2 = jnp.concatenate(
-        [jnp.where(even_mask, legendre, zeros), jnp.where(odd_mask, legendre, zeros)], 1
-    )
-    sums = jnp.einsum("lscfk,sjk->sclfj", gathered, leg2, preferred_element_type=jnp.float32)
-    sums = sums.reshape(per_dev, 2, fields, 2, nlath)
     north = band_rows < nlath
     lat_idx = jnp.where(north, band_rows, band_rows - nlath)
-    parity_sign = jnp.where(north, 1.0, -1.0).astype(jnp.float32)
-    fourier = (sums[:, :, :, 0][..., lat_idx] + parity_sign * sums[:, :, :, 1][..., lat_idx]).astype(
-        jnp.bfloat16
+    parity_sign = jnp.where(north, 1.0, -1.0).astype(jnp.bfloat16)
+    even_k = (degree % 2 == 0)[None, None, :]
+    factor = jnp.where(
+        live_k[:, None, :], jnp.where(even_k, jnp.bfloat16(1), parity_sign[None, :, None]), jnp.bfloat16(0)
     )
+    leg_rows = jnp.take(legendre, lat_idx, axis=1) * factor
+    sums = jnp.einsum("lscfk,spk->sclfp", gathered, leg_rows, preferred_element_type=jnp.float32)
+    fourier = sums.reshape(per_dev, 2, fields, band_rows.shape[0]).astype(jnp.bfloat16)
     rows = band_rows.shape[0]
     fpg = fields // n_g
     fourier = fourier.reshape(per_dev, 2, n_g, fpg, n_wave, n_r, rows_per_dev)

time: 84.7 us -> 95.4 us (1.13)
  local copies, waits for them, and re-layouts: 12.9 us -> 30.3 us
  waiting for transfers between devices: 15.4 us -> 10.3 us
  other arithmetic: 22.6 us -> 17.8 us
  matrix products: 8.82 us -> 10.7 us
    gather x2 -> x1, local copies, waits for them, and re-layouts: 1.16 us -> 11.8 us  [on_device(): leg_rows = jnp.take(legendre, lat_idx, axis=1) * factor]
    all_to_all x1, waiting for transfers between devices: 14.9 us -> 10.3 us  [on_device(): lax.all_to_all(spec_v, ('lev_g', 'lev_r'), split_axis=0, concat_axis=0, t...]
    select_n x3 -> x1, other arithmetic: 3.68 us -> 0.08 us  [on_device(): jnp.where(even_k, jnp.bfloat16(1), parity_sign[None, :, None])]
    cos x3, other arithmetic: 9.06 us -> 6.98 us  [trig_pair(): return (jnp.cos(theta), jnp.sin(theta))]
    transpose x2, local copies, waits for them, and re-layouts: 0.12 us -> 1.77 us  [on_device(): jnp.transpose(banded, (1, 2, 3, 0, 4)).reshape(2, fpg, rows_per_dev, -1)]
    transpose x1 -> x0, local copies, waits for them, and re-layouts: 1.44 us -> none  [on_device(): jnp.einsum('lscfk,sjk->sclfj', gathered, leg2, preferred_element_type=jnp...]
    squeeze x1, local copies, waits for them, and re-layouts: 0.12 us -> 1.55 us  [row_synthesis(): c0 = blocks[0]]
    dot_general x1, matrix products: 2.43 us -> 3.8 us  [row_synthesis(): jnp.einsum('dfab,bi->dfai', lhs, rhs, preferred_element_type=jnp.float32)]
  transfers between devices with their start and end apart: 2 -> 2, of which waited for: 2 -> 1; matrix products, arithmetic and copies ran while one was open for 33% -> 37% of each run, Pallas kernels for 0% -> 0%
where the time goes in v10:
time: 95.4 us; the launch traced here: 94.7 us
  local copies, waits for them, and re-layouts  30.3 us (32%)
  other arithmetic  17.8 us (19%)
  blocking collectives  11.3 us (12%)
  matrix products  10.7 us (11%)
  waiting for transfers between devices  10.3 us (11%)
  starting transfers between devices  10.2 us (11%)
  between operations  4.09 us (4%)
    gather x1, local copies, waits for them, and re-layouts, on_device(): leg_rows = jnp.take(legendre, lat_idx, axis=1) * factor  11.8 us
    all_to_all x1, blocking collectives, on_device(): lax.all_to_all(grid, 'lev_r', split_axis=1, concat_axis=0, tiled=True)  11.3 us
    all_to_all x1, waiting for transfers between devices, on_device(): lax.all_to_all(spec_v, ('lev_g', 'lev_r'), split_axis=0, concat_axis=0, t...  10.3 us
    cos x3, other arithmetic, trig_pair(): return (jnp.cos(theta), jnp.sin(theta))  6.98 us
    dot_general x1, matrix products, on_device(): jnp.einsum('lscfk,spk->sclfp', gathered, leg_rows, preferred_element_type...  5.47 us
    all_to_all x1, starting transfers between devices, on_device(): lax.all_to_all(spec_v, ('lev_g', 'lev_r'), split_axis=0, concat_axis=0, t...  5.32 us
    all_to_all x1, starting transfers between devices, on_device(): lax.all_to_all(fourier, ('wave', 'lev_g', 'lev_r'), split_axis=0, concat_...  4.87 us
    dot_general x1, matrix products, row_synthesis(): jnp.einsum('dfab,bi->dfai', lhs, rhs, preferred_element_type=jnp.float32)  3.8 us
  transfers between devices with their start and end apart: 2, of which 1 were waited for; matrix products, arithmetic and copies ran while one was open for 37% of the time, Pallas kernels for 0%

profile of v10, /device:TPU:0, one launch (start us, length us, event | category | flops | bytes accessed | tf_op | source)
XLA Modules:
  0.0 94.7 jit_solution(16603988355262399024)
XLA Ops:
  0.0 5.3 %all-to-all-start = ((bf16[8,40,2,2,1280]{4,3,2,1,0:T(2,128)(2,1)}), bf16[8,40,2,2,1280]{4,3,2,1,0:T(2,128)(2,1)}, u32[]{:S(2)}, u32[]{:S(2)}) async-start(bf16[8,40,2,2,1280]{4,3,2,1,0:T(2,128)(2,1)} %bitcast.75), calls=%async_computation | async-start | bytes 6553600 | tf_op jit(solution)/shard_map/all_to_all | solution.py:67
  10.7 2.3 %fusion.72 = (f32[8,5136]{1,0:T(8,128)S(1)}, f32[8,5136]{1,0:T(8,128)S(1)}) fusion(f32[]{:T(128)S(6)} %convert_element_type.88, pred[]{:T(512)S(6)} %lt.115, s32[]{:T(128)S(6)} %select_n.144), kind=kLoop, calls=%fused_computation.81 | loop fusion | flops 451968 | bytes 328713 | tf_op jit(solution)/shard_map/sin | solution.py:18
  12.9 2.3 %fusion.75 = (f32[8,5136]{1,0:T(8,128)S(1)}, f32[8,5136]{1,0:T(8,128)S(1)}) fusion(f32[]{:T(128)S(6)} %convert_element_type.88, pred[]{:T(512)S(6)} %lt.115, s32[]{:T(128)S(6)} %select_n.144, s32[8]{0:T(128)S(1)} %iota_multiply_fusion.2), kind=kLoop, calls=%fused_computation.84 | loop fusion | flops 451968 | bytes 328745 | tf_op jit(solution)/shard_map/cos | solution.py:18
  15.3 2.3 %fusion.71 = (f32[5,5136]{1,0:T(8,128)S(1)}, f32[5,5136]{1,0:T(8,128)S(1)}) fusion(f32[]{:T(128)S(6)} %convert_element_type.88, pred[]{:T(512)S(6)} %lt.115, s32[]{:T(128)S(6)} %select_n.144, s32[5]{0:T(128)S(1)} %iota_multiply_fusion.1), kind=kLoop, calls=%fused_computation.80 | loop fusion | flops 282480 | bytes 205469 | tf_op jit(solution)/shard_map/cos | solution.py:18
  17.6 2.3 %fusion.77 = (f32[4,5136]{1,0:T(4,128)S(1)}, f32[4,5136]{1,0:T(4,128)S(1)}) fusion(f32[]{:T(128)S(6)} %convert_element_type.88, pred[]{:T(512)S(6)} %lt.115, s32[]{:T(128)S(6)} %select_n.144, s32[4]{0:T(128)S(1)} %iota_multiply_fusion), kind=kLoop, calls=%fused_computation.87 | loop fusion | flops 225984 | bytes 164377 | tf_op jit(solution)/shard_map/cos | solution.py:18
  20.0 11.8 %gather_fusion = bf16[32,40,1280]{2,0,1:T(8,128)(2,1)} fusion(bf16[40,16,1280]{2,1,0:T(8,128)(2,1)S(1)} %copy-done, s32[1024]{0:T(1024)S(1)} %pad_clamp_fusion), kind=kCustom, calls=%fused_computation | custom fusion | bytes 6553728 | tf_op jit(solution)/shard_map/jit(_take)/gather | solution.py:80
  31.8 1.2 %multiply_subtract_fusion = (f32[5,4,5136]{2,1,0:T(4,128)}, f32[5,4,5136]{2,1,0:T(4,128)}) fusion(f32[4,5136]{1,0:T(4,128)S(1)} %get-tuple-element.29, f32[5,5136]{1,0:T(8,128)S(1)} %get-tuple-element.27, f32[4,5136]{1,0:T(4,128)S(1)} %get-tuple-element.28, f32[5,5136]{1,0:T(8,128)S(1)} %get-tuple-element.26), kind=kLoop, calls=%fused_computation.35 | loop fusion | flops 616320 | bytes 1191552 | tf_op jit(solution)/shard_map/sub | solution.py:24
  33.0 1.4 %fusion.37 = (bf16[64,5136]{1,0:T(8,128)(2,1)}, bf16[64,5136]{1,0:T(8,128)(2,1)}) fusion(f32[8,5136]{1,0:T(8,128)S(1)} %get-tuple-element.32, f32[8,5136]{1,0:T(8,128)S(1)} %get-tuple-element.31, f32[8,5136]{1,0:T(8,128)S(1)} %get-tuple-element.33, f32[8,5136]{1,0:T(8,128)S(1)} %get-tuple-element.30), kind=kLoop, calls=%fused_computation.32 | loop fusion | flops 2629632 | bytes 1972224 | tf_op jit(solution)/shard_map/convert_element_type | solution.py:36
  34.4 10.3 %all-to-all-done = bf16[8,40,2,2,1280]{4,3,2,1,0:T(2,128)(2,1)} async-done(((bf16[8,40,2,2,1280]{4,3,2,1,0:T(2,128)(2,1)}), bf16[8,40,2,2,1280]{4,3,2,1,0:T(2,128)(2,1)}, u32[]{:S(2)}, u32[]{:S(2)}) %all-to-all-start) | async-done | bytes 3276832 | tf_op jit(solution)/shard_map/all_to_all | solution.py:67
  44.7 5.5 %fusion.32 = bf16[40,2,8,2,32]{4,2,3,1,0:T(8,128)(2,1)S(1)} fusion(bf16[8,40,2,2,1280]{4,3,2,1,0:T(2,128)(2,1)} %all-to-all-done, bf16[32,40,1280]{2,0,1:T(8,128)(2,1)} %gather_fusion, pred[32]{0:T(512)(128)(4,1)S(1)} %get-tuple-element.16, pred[40,1280]{1,0:T(8,128)(4,1)S(1)} %iota_compare_fusion.1, bf16[32,1280]{1,0:T(8,128)(2,1)S(1)} %broadcast_select_fusion.1), kind=kOutput, calls=%fused_computation.31 | convolution fusion | flops 114728960 | bytes 6768672 | tf_op jit(solution)/shard_map/lscfk,spk->sclfp/dot_general | solution.py:81
  51.7 4.9 %all-to-all-start.1 = ((bf16[32,2,640]{2,1,0:T(2,128)(2,1)}), bf16[32,2,640]{2,1,0:T(2,128)(2,1)S(1)}, u32[]{:S(2)}, u32[]{:S(2)}) async-start(bf16[32,2,640]{2,1,0:T(2,128)(2,1)} %reshape.447), calls=%async_computation.1 | async-start | bytes 163840 | tf_op jit(solution)/shard_map/all_to_all | solution.py:88
  56.6 1.2 %iota_compare_fusion.2 = pred[5136]{0:T(1024)(128)(4,1)} fusion(s32[]{:T(128)} %bitcast.1), kind=kLoop, calls=%fused_computation.88 | loop fusion | flops 5136 | bytes 5140 | tf_op jit(solution)/shard_map/lt | solution.py:53
  57.8 2.2 %copy.17 = bf16[64,5136]{0,1:T(8,128)(2,1)S(1)} copy(bf16[64,5136]{1,0:T(8,128)(2,1)} %get-tuple-element.18) | data formatting | bytes 1314816 | tf_op jit(solution)/shard_map/convert_element_type | solution.py:36
  60.0 2.4 %copy.18 = bf16[64,5136]{0,1:T(8,128)(2,1)} copy(bf16[64,5136]{1,0:T(8,128)(2,1)} %get-tuple-element.19) | data formatting | bytes 1314816 | tf_op jit(solution)/shard_map/convert_element_type | solution.py:37
  62.4 1.1 %add.108 = f32[20,5136]{1,0:T(8,128)S(1)} reshape(f32[5,4,5136]{2,1,0:T(4,128)} %get-tuple-element.21) | data formatting | bytes 821760 | tf_op jit(solution)/shard_map/add | solution.py:25
  63.5 2.0 %sub.33 = f32[20,5136]{1,0:T(8,128)} reshape(f32[5,4,5136]{2,1,0:T(4,128)} %get-tuple-element.20) | data formatting | bytes 821760 | tf_op jit(solution)/shard_map/sub | solution.py:24
  66.1 1.1 %reshape.448 = bf16[32,1,2,16,40]{4,3,2,1,0:T(8,128)(2,1)} reshape(bf16[32,2,640]{2,1,0:T(2,128)(2,1)S(1)} %all-to-all-done.1) | data formatting | bytes 163840
  69.0 1.3 %reshape.412 = bf16[2,16,1280]{2,1,0:T(8,128)(2,1)S(1)} reshape(bf16[2,16,1,32,40]{4,3,1,0,2:T(8,128)(2,1)} %copy.16) | data formatting | bytes 163840 | tf_op jit(solution)/shard_map/reshape.3 | solution.py:135
  70.3 1.4 %fusion.18 = bf16[2,16,1280]{2,1,0:T(8,128)(2,1)S(1)} fusion(bf16[2,16,1280]{2,1,0:T(8,128)(2,1)S(1)} %reshape.412, s32[1280]{0:T(1024)S(1)} %copy-done.3, f32[1280]{0:T(1024)S(1)} %select_select_fusion), kind=kOutput, calls=%fused_computation.20 | convolution fusion | flops 106577920 | bytes 174080 | tf_op jit(solution)/shard_map/cfrs,sm->cfrm/dot_general | solution.py:94
  73.9 1.5 %squeeze.16 = bf16[16,20,64]{2,1,0:T(8,128)(2,1)} reshape(bf16[1,16,1280]{2,1,0:T(8,128)(2,1)} %get-tuple-element.25) | data formatting | bytes 81920 | tf_op jit(solution)/shard_map/squeeze | solution.py:45
  75.5 1.1 %maximum_bitcast_fusion.2 = (bf16[1,16,20,128]{3,2,1,0:T(8,128)(2,1)S(1)}, bf16[1,16,20,128]{3,2,1,0:T(8,128)(2,1)S(1)}) fusion(bf16[16,20,64]{2,1,0:T(8,128)(2,1)} %neg.3, bf16[16,20,64]{2,1,0:T(8,128)(2,1)} %squeeze.16, bf16[16,20,64]{2,1,0:T(8,128)(2,1)S(1)} %squeeze.17), kind=kLoop, calls=%fused_computation.69 | loop fusion | flops 327680 | bytes 286720 | tf_op jit(solution)/shard_map/stack | solution.py:47
  76.6 3.8 %fusion.24 = f32[2,16,20,5136]{3,2,1,0:T(8,128)S(1)} fusion(bf16[64,5136]{0,1:T(8,128)(2,1)} %copy.18, bf16[64,5136]{0,1:T(8,128)(2,1)S(1)} %copy.17, bf16[1,16,20,128]{3,2,1,0:T(8,128)(2,1)S(1)} %get-tuple-element.23, bf16[1,16,20,128]{3,2,1,0:T(8,128)(2,1)S(1)} %get-tuple-element.22), kind=kOutput, calls=%fused_computation.27 | convolution fusion | flops 844193792 | bytes 14626816 | tf_op jit(solution)/shard_map/dfab,bi->dfai/dot_general | solution.py:51
  80.4 1.9 %fusion.2 = f32[16,5136]{1,0:T(8,128)S(1)} fusion(f32[2,16,20,5136]{3,2,1,0:T(8,128)S(1)} %fusion.24, f32[20,5136]{1,0:T(8,128)S(1)} %add.108, f32[20,5136]{1,0:T(8,128)S(1)} %copy-done.1), kind=kLoop, calls=%fused_computation.4 | loop fusion | flops 6491904 | bytes 14298624 | tf_op jit(solution)/shard_map/reduce_sum | solution.py:52
  82.7 11.3 %all_to_all.19 = f32[1,8,2,5136]{3,2,0,1:T(2,128)S(1)} all-to-all(f32[1,8,2,5136]{3,2,0,1:T(2,128)S(1)} %broadcast_select_fusion), channel_id=1, replica_groups=mesh['wave'=4,'lev'=8] {'lev'}, dimensions={1} | all-to-all | bytes 657408 | tf_op jit(solution)/shard_map/all_to_all | solution.py:109
  (37 shorter events, 8.7 us)
Async XLA Ops:
  0.0 20.0 %copy-start = (bf16[40,16,1280]{2,1,0:T(8,128)(2,1)S(1)}, bf16[40,16,1280]{2,1,0:T(8,128)(2,1)}, u32[]{:S(2)}) copy-start(bf16[40,16,1280]{2,1,0:T(8,128)(2,1)} %param.6) | copy-start | bytes 4915204
  0.0 5.3 %copy-start.4 = (s32[32]{0:T(128)S(1)}, s32[32]{0:T(128)}, u32[]{:S(2)}) copy-start(s32[32]{0:T(128)} %param.9) | copy-start | bytes 388
  0.0 7.9 %copy-start.5 = (s32[32]{0:T(128)S(1)}, s32[32]{0:T(128)}, u32[]{:S(2)}) copy-start(s32[32]{0:T(128)} %param.8) | copy-start | bytes 388
  0.0 9.8 %copy-start.3 = (s32[1280]{0:T(1024)S(1)}, s32[1280]{0:T(1024)}, u32[]{:S(2)}) copy-start(s32[1280]{0:T(1024)} %param.7) | copy-start | bytes 15364
  0.0 44.7 %all-to-all-start = ((bf16[8,40,2,2,1280]{4,3,2,1,0:T(2,128)(2,1)}), bf16[8,40,2,2,1280]{4,3,2,1,0:T(2,128)(2,1)}, u32[]{:S(2)}, u32[]{:S(2)}) async-start(bf16[8,40,2,2,1280]{4,3,2,1,0:T(2,128)(2,1)} %bitcast.75), calls=%async_computation | async-start | bytes 6553600 | tf_op jit(solution)/shard_map/all_to_all | solution.py:67
  51.7 14.4 %all-to-all-start.1 = ((bf16[32,2,640]{2,1,0:T(2,128)(2,1)}), bf16[32,2,640]{2,1,0:T(2,128)(2,1)S(1)}, u32[]{:S(2)}, u32[]{:S(2)}) async-start(bf16[32,2,640]{2,1,0:T(2,128)(2,1)} %reshape.447), calls=%async_computation.1 | async-start | bytes 163840 | tf_op jit(solution)/shard_map/all_to_all | solution.py:88
  76.6 3.8 %copy-start.1 = (f32[20,5136]{1,0:T(8,128)S(1)}, f32[20,5136]{1,0:T(8,128)}, u32[]{:S(2)}) copy-start(f32[20,5136]{1,0:T(8,128)} %sub.33) | copy-start | bytes 1232644
  80.4 2.1 %copy-start.2 = (pred[5136]{0:T(1024)(128)(4,1)S(1)}, pred[5136]{0:T(1024)(128)(4,1)}, u32[]{:S(2)}) copy-start(pred[5136]{0:T(1024)(128)(4,1)} %iota_compare_fusion.2) | copy-start | bytes 15412

commit v11 on v6

--- a/solution.py
+++ b/solution.py
@@ -4,6 +4,7 @@
 import jax.numpy as jnp
 import numpy as np
 from jax import lax
+from jax.experimental import pallas as pl
 from jax.sharding import Mesh
 from jax.sharding import PartitionSpec as P
 
@@ -39,19 +40,43 @@
     return rhs, cosp[:ablocks], sinp[:ablocks]
 
 
+def synth_kernel(lhs_ref, rhs_ref, cos_ref, sin_ref, o_ref):
+    fields = o_ref.shape[0]
+    part = jnp.dot(lhs_ref[...], rhs_ref[...], preferred_element_type=jnp.float32)
+    acc = jnp.zeros(o_ref.shape, jnp.float32)
+    for a in range(cos_ref.shape[0]):
+        re = part[2 * a * fields:(2 * a + 1) * fields]
+        im = part[(2 * a + 1) * fields:(2 * a + 2) * fields]
+        acc = acc + re * cos_ref[a:a + 1, :] - im * sin_ref[a:a + 1, :]
+    o_ref[...] = acc
+
+
 def row_synthesis(coef_row, rhs, cosp, sinp, points):
     fields = coef_row.shape[1]
     waves = coef_row.shape[2]
     ablocks = waves // 64
-    lon_idx = jnp.arange(rhs.shape[-1], dtype=jnp.int32)
+    lon = rhs.shape[-1]
+    lon_idx = jnp.arange(lon, dtype=jnp.int32)
     blocks = coef_row.reshape(2, fields, ablocks, 64)
     c0 = blocks[0]
     c1 = blocks[1]
     lhs = jnp.stack(
         [jnp.concatenate([c0, -c1], -1), jnp.concatenate([c1, c0], -1)], 0
     )
-    part = jnp.einsum("dfab,bi->dfai", lhs, rhs, preferred_element_type=jnp.float32)
-    total = jnp.sum(part[0] * cosp[None] - part[1] * sinp[None], axis=1)
+    lhs = jnp.transpose(lhs, (2, 0, 1, 3)).reshape(ablocks * 2 * fields, 128)
+    tile = 512
+    total = pl.pallas_call(
+        synth_kernel,
+        grid=(pl.cdiv(lon, tile),),
+        in_specs=[
+            pl.BlockSpec((ablocks * 2 * fields, 128), lambda i: (0, 0)),
+            pl.BlockSpec((128, tile), lambda i: (0, i)),
+            pl.BlockSpec((ablocks, tile), lambda i: (0, i)),
+            pl.BlockSpec((ablocks, tile), lambda i: (0, i)),
+        ],
+        out_specs=pl.BlockSpec((fields, tile), lambda i: (0, i)),
+        out_shape=jax.ShapeDtypeStruct((fields, lon), jnp.float32),
+    )(lhs, rhs, cosp, sinp)
     return jnp.where(lon_idx[None, :] < points, total, jnp.zeros_like(total))
 
 

time: 84.9 us -> 89.5 us (1.054)
  Pallas kernels: 0 us -> 8.13 us
  waiting for transfers between devices: 26.8 us -> 20.1 us
  local copies, waits for them, and re-layouts: 8.25 us -> 11.7 us
  other arithmetic: 15.9 us -> 18.9 us
  matrix products: 9.22 us -> 6.38 us
    pallas_call x0 -> x1, Pallas kernels: none -> 8.13 us  [row_synthesis(): pl.pallas_call(synth_kernel, grid=(pl.cdiv(lon, tile),), in_specs=[pl.Blo...]
    all_to_all x1, waiting for transfers between devices: 20.6 us -> 13.8 us  [on_device(): lax.all_to_all(spec_v, ('lev_g', 'lev_r'), split_axis=0, concat_axis=0, t...]
    dot_general x1 -> x0, matrix products: 2.3 us -> none  [row_synthesis(): jnp.einsum('dfab,bi->dfai', lhs, rhs, preferred_element_type=jnp.float32)]
    add x1, local copies, waits for them, and re-layouts: 0.15 us -> 1.96 us  [compose(): sin = s1[:, None] * c0[None] + c1[:, None] * s0[None]]
    reduce_sum x1 -> x0, other arithmetic: 1.79 us -> none  [row_synthesis(): total = jnp.sum(part[0] * cosp[None] - part[1] * sinp[None], axis=1)]
    select_n x1, other arithmetic: 2.2 us -> 3.63 us  [on_device(): jnp.where(even_mask, legendre, zeros)]
    broadcast_in_dim x1, other arithmetic: 0.09 us -> 1.16 us  [on_device(): tables = tuple((t[None] for t in row_tables(row_points[0], waves)))]
    sub x1, local copies, waits for them, and re-layouts: 0.94 us -> 1.95 us  [compose(): cos = c1[:, None] * c0[None] - s1[:, None] * s0[None]]
  transfers between devices with their start and end apart: 2 -> 2, of which waited for: 2 -> 2; matrix products, arithmetic and copies ran while one was open for 19% -> 26% of each run, Pallas kernels for 0% -> 0%
where the time goes in v11:
time: 89.5 us; the launch traced here: 88.8 us
  waiting for transfers between devices  20.1 us (22%)
  other arithmetic  18.9 us (21%)
  local copies, waits for them, and re-layouts  11.7 us (13%)
  blocking collectives  10.1 us (11%)
  starting transfers between devices  9.31 us (10%)
  Pallas kernels  8.13 us (9%)
  matrix products  6.38 us (7%)
  between operations  4.08 us (5%)
    all_to_all x1, waiting for transfers between devices, on_device(): lax.all_to_all(spec_v, ('lev_g', 'lev_r'), split_axis=0, concat_axis=0, t...  13.8 us
    all_to_all x1, blocking collectives, on_device(): lax.all_to_all(grid, 'lev_r', split_axis=1, concat_axis=0, tiled=True)  10.1 us
    pallas_call x1, Pallas kernels, row_synthesis(): pl.pallas_call(synth_kernel, grid=(pl.cdiv(lon, tile),), in_specs=[pl.Blo...  8.13 us
    cos x3, other arithmetic, trig_pair(): return (jnp.cos(theta), jnp.sin(theta))  7.65 us
    all_to_all x1, waiting for transfers between devices, on_device(): lax.all_to_all(fourier, ('wave', 'lev_g', 'lev_r'), split_axis=0, concat_...  6.32 us
    all_to_all x1, starting transfers between devices, on_device(): lax.all_to_all(spec_v, ('lev_g', 'lev_r'), split_axis=0, concat_axis=0, t...  5.3 us
    dot_general x1, matrix products, on_device(): jnp.einsum('lscfk,sjk->sclfj', gathered, leg2, preferred_element_type=jnp...  4.97 us
    all_to_all x1, starting transfers between devices, on_device(): lax.all_to_all(fourier, ('wave', 'lev_g', 'lev_r'), split_axis=0, concat_...  4 us
  transfers between devices with their start and end apart: 2, of which 2 were waited for; matrix products, arithmetic and copies ran while one was open for 26% of the time, Pallas kernels for 0%

profile of v11, /device:TPU:0, one launch (start us, length us, event | category | flops | bytes accessed | tf_op | source)
XLA Modules:
  0.0 88.8 jit_solution(11537652797214954726)
XLA Ops:
  0.0 5.3 %all-to-all-start = ((bf16[8,40,2,2,1280]{4,3,2,1,0:T(2,128)(2,1)}), bf16[8,40,2,2,1280]{4,3,2,1,0:T(2,128)(2,1)S(1)}, u32[]{:S(2)}, u32[]{:S(2)}) async-start(bf16[8,40,2,2,1280]{4,3,2,1,0:T(2,128)(2,1)} %bitcast.64), calls=%async_computation | async-start | bytes 6553600 | tf_op jit(solution)/shard_map/all_to_all | solution.py:94
  10.4 3.0 %fusion.54 = (f32[8,5136]{1,0:T(8,128)S(1)}, f32[8,5136]{1,0:T(8,128)}) fusion(f32[]{:T(128)S(6)} %convert_element_type.74, pred[]{:T(512)S(6)} %lt.110, s32[]{:T(128)S(6)} %select_n.129, s32[8]{0:T(128)S(1)} %iota_multiply_fusion.2), kind=kLoop, calls=%fused_computation.74 | loop fusion | flops 451968 | bytes 328745 | tf_op jit(solution)/shard_map/cos | solution.py:19
  13.4 2.3 %fusion.50 = (f32[5,5136]{1,0:T(8,128)S(1)}, f32[5,5136]{1,0:T(8,128)S(1)}) fusion(f32[]{:T(128)S(6)} %convert_element_type.74, pred[]{:T(512)S(6)} %lt.110, s32[]{:T(128)S(6)} %select_n.129, s32[5]{0:T(128)S(1)} %iota_multiply_fusion.1), kind=kLoop, calls=%fused_computation.70 | loop fusion | flops 282480 | bytes 205469 | tf_op jit(solution)/shard_map/cos | solution.py:19
  15.7 2.3 %fusion.56 = (f32[4,5136]{1,0:T(4,128)S(1)}, f32[4,5136]{1,0:T(4,128)S(1)}) fusion(f32[]{:T(128)S(6)} %convert_element_type.74, pred[]{:T(512)S(6)} %lt.110, s32[]{:T(128)S(6)} %select_n.129, s32[4]{0:T(128)S(1)} %iota_multiply_fusion), kind=kLoop, calls=%fused_computation.76 | loop fusion | flops 225984 | bytes 164377 | tf_op jit(solution)/shard_map/cos | solution.py:19
  18.1 1.1 %multiply_add_fusion = (f32[5,4,5136]{2,1,0:T(4,128)}, f32[5,4,5136]{2,1,0:T(4,128)}) fusion(f32[4,5136]{1,0:T(4,128)S(1)} %get-tuple-element.41, f32[5,5136]{1,0:T(8,128)S(1)} %get-tuple-element.39, f32[4,5136]{1,0:T(4,128)S(1)} %get-tuple-element.40, f32[5,5136]{1,0:T(8,128)S(1)} %get-tuple-element.38), kind=kLoop, calls=%fused_computation.22 | loop fusion | flops 616320 | bytes 1191552 | tf_op jit(solution)/shard_map/add | solution.py:26
  19.2 2.0 %add.126 = f32[1,20,5136]{2,1,0:T(8,128)} reshape(f32[5,4,5136]{2,1,0:T(4,128)} %get-tuple-element.30) | data formatting | bytes 821760 | tf_op jit(solution)/shard_map/add | solution.py:26
  21.1 2.0 %sub.32 = f32[1,20,5136]{2,1,0:T(8,128)} reshape(f32[5,4,5136]{2,1,0:T(4,128)} %get-tuple-element.31) | data formatting | bytes 821760 | tf_op jit(solution)/shard_map/sub | solution.py:25
  23.4 3.6 %broadcast_select_fusion.1 = (bf16[40,16,1280]{2,1,0:T(8,128)(2,1)}, bf16[40,16,1280]{2,1,0:T(8,128)(2,1)}) fusion(bf16[40,16,1280]{2,1,0:T(8,128)(2,1)} %param.6, pred[40,1280]{1,0:T(8,128)(4,1)S(1)} %get-tuple-element.36, pred[40,1280]{1,0:T(8,128)(4,1)S(1)} %get-tuple-element.37), kind=kLoop, calls=%fused_computation.14 | loop fusion | flops 1638400 | bytes 5017600 | tf_op jit(solution)/shard_map/jit(_where)/select_n | solution.py:112
  27.0 2.3 %fusion.51 = (f32[8,5136]{1,0:T(8,128)S(1)}, f32[8,5136]{1,0:T(8,128)S(1)}) fusion(f32[]{:T(128)S(6)} %convert_element_type.74, pred[]{:T(512)S(6)} %lt.110, s32[]{:T(128)S(6)} %select_n.129), kind=kLoop, calls=%fused_computation.71 | loop fusion | flops 451968 | bytes 328713 | tf_op jit(solution)/shard_map/sin | solution.py:19
  29.6 1.2 %maximum_bitcast_fusion.2 = bf16[1,128,5136]{2,1,0:T(8,128)(2,1)} fusion(bf16[64,5136]{1,0:T(8,128)(2,1)S(1)} %get-tuple-element.27, bf16[64,5136]{1,0:T(8,128)(2,1)S(1)} %get-tuple-element.26), kind=kLoop, calls=%fused_computation.15 | loop fusion | flops 2629632 | bytes 2629632 | tf_op jit(solution)/shard_map/broadcast_in_dim | solution.py:100
  30.8 13.8 %all-to-all-done = bf16[8,40,2,2,1280]{4,3,2,1,0:T(2,128)(2,1)S(1)} async-done(((bf16[8,40,2,2,1280]{4,3,2,1,0:T(2,128)(2,1)}), bf16[8,40,2,2,1280]{4,3,2,1,0:T(2,128)(2,1)S(1)}, u32[]{:S(2)}, u32[]{:S(2)}) %all-to-all-start) | async-done | bytes 3276832 | tf_op jit(solution)/shard_map/all_to_all | solution.py:94
  44.6 5.0 %fusion.14 = f32[40,2,8,2,32]{4,2,3,1,0:T(8,128)} fusion(bf16[8,40,2,2,1280]{4,3,2,1,0:T(2,128)(2,1)S(1)} %all-to-all-done, bf16[40,16,1280]{2,1,0:T(8,128)(2,1)} %get-tuple-element.25, bf16[40,16,1280]{2,1,0:T(8,128)(2,1)} %get-tuple-element.24), kind=kOutput, calls=%fused_computation.18 | convolution fusion | flops 111411200 | bytes 6717440 | tf_op jit(solution)/shard_map/lscfk,sjk->sclfj/dot_general | solution.py:114
  49.6 1.4 %copy.18 = f32[40,2,8,2,32]{0,4,3,2,1:T(8,128)S(1)} copy(f32[40,2,8,2,32]{4,2,3,1,0:T(8,128)} %fusion.14) | data formatting | bytes 327680 | tf_op jit(solution)/shard_map/lscfk,sjk->sclfj/transpose | solution.py:114
  52.5 1.0 %reshape.509 = bf16[32,2,640]{2,1,0:T(2,128)(2,1)} reshape(bf16[32,1,2,16,40]{4,3,2,1,0:T(8,128)(2,1)S(1)} %bitcast.74) | data formatting | bytes 163840
  53.5 4.0 %all-to-all-start.1 = ((bf16[32,2,640]{2,1,0:T(2,128)(2,1)}), bf16[32,2,640]{2,1,0:T(2,128)(2,1)S(1)}, u32[]{:S(2)}, u32[]{:S(2)}) async-start(bf16[32,2,640]{2,1,0:T(2,128)(2,1)} %reshape.509), calls=%async_computation.1 | async-start | bytes 163840 | tf_op jit(solution)/shard_map/all_to_all | solution.py:127
  57.5 0.6 iota_compare_fusion.2
  58.2 0.6 select_select_fusion
  58.8 6.3 %all-to-all-done.1 = bf16[32,2,640]{2,1,0:T(2,128)(2,1)S(1)} async-done(((bf16[32,2,640]{2,1,0:T(2,128)(2,1)}), bf16[32,2,640]{2,1,0:T(2,128)(2,1)S(1)}, u32[]{:S(2)}, u32[]{:S(2)}) %all-to-all-start.1) | async-done | bytes 81952 | tf_op jit(solution)/shard_map/all_to_all | solution.py:127
  66.0 1.4 %fusion.11 = bf16[2,16,1280]{2,1,0:T(8,128)(2,1)S(1)} fusion(bf16[2,16,1280]{2,1,0:T(8,128)(2,1)S(1)} %reshape.465, s32[1280]{0:T(1024)S(1)} %copy-done.1, f32[1280]{0:T(1024)S(1)} %select_select_fusion), kind=kOutput, calls=%fused_computation.12 | convolution fusion | flops 106577920 | bytes 174080 | tf_op jit(solution)/shard_map/cfrs,sm->cfrm/dot_general | solution.py:133
  67.9 0.7 copy.22
  68.6 8.1 %shard_map.55 = f32[16,5136]{1,0:T(8,128)} custom-call(bf16[640,128]{1,0:T(8,128)(2,1)} %bitcast.75, bf16[128,5136]{1,0:T(8,128)(2,1)} %bitcast.63, f32[20,5136]{1,0:T(8,128)} %bitcast.71, f32[20,5136]{1,0:T(8,128)} %bitcast.70), custom_call_target="tpu_custom_call" | custom-call | tf_op jit(solution)/shard_map/pallas_call | solution.py:68
  76.7 1.0 %broadcast_select_fusion.2 = f32[16,5136]{1,0:T(8,128)S(1)} fusion(f32[16,5136]{1,0:T(8,128)} %shard_map.55, pred[5136]{0:T(1024)(128)(4,1)S(1)} %iota_compare_fusion.2), kind=kLoop, calls=%fused_computation.42 | loop fusion | flops 82176 | bytes 662544 | tf_op jit(solution)/shard_map/jit(_where)/select_n | solution.py:80
  77.9 10.1 %all_to_all.19 = f32[1,8,2,5136]{3,2,0,1:T(2,128)S(1)} all-to-all(f32[1,8,2,5136]{3,2,0,1:T(2,128)S(1)} %bitcast.72), channel_id=1, replica_groups=mesh['wave'=4,'lev'=8] {'lev'}, dimensions={1} | all-to-all | bytes 657408 | tf_op jit(solution)/shard_map/all_to_all | solution.py:145
  88.0 0.7 copy.36
  (38 shorter events, 4.8 us)
Async XLA Ops:
  0.0 5.3 %copy-start.3 = (s32[32]{0:T(128)S(1)}, s32[32]{0:T(128)}, u32[]{:S(2)}) copy-start(s32[32]{0:T(128)} %param.9) | copy-start | bytes 388
  0.0 7.8 %copy-start.2 = (s32[32]{0:T(128)S(1)}, s32[32]{0:T(128)}, u32[]{:S(2)}) copy-start(s32[32]{0:T(128)} %param.8) | copy-start | bytes 388
  0.0 44.6 %all-to-all-start = ((bf16[8,40,2,2,1280]{4,3,2,1,0:T(2,128)(2,1)}), bf16[8,40,2,2,1280]{4,3,2,1,0:T(2,128)(2,1)S(1)}, u32[]{:S(2)}, u32[]{:S(2)}) async-start(bf16[8,40,2,2,1280]{4,3,2,1,0:T(2,128)(2,1)} %bitcast.64), calls=%async_computation | async-start | bytes 6553600 | tf_op jit(solution)/shard_map/all_to_all | solution.py:94
  18.1 5.1 %copy-start.1 = (s32[1280]{0:T(1024)S(1)}, s32[1280]{0:T(1024)}, u32[]{:S(2)}) copy-start(s32[1280]{0:T(1024)} %param.7) | copy-start | bytes 15364
  23.4 5.9 %copy-start = (f32[8,5136]{1,0:T(8,128)S(1)}, f32[8,5136]{1,0:T(8,128)}, u32[]{:S(2)}) copy-start(f32[8,5136]{1,0:T(8,128)} %get-tuple-element.43) | copy-start | bytes 493060
  53.5 11.6 %all-to-all-start.1 = ((bf16[32,2,640]{2,1,0:T(2,128)(2,1)}), bf16[32,2,640]{2,1,0:T(2,128)(2,1)S(1)}, u32[]{:S(2)}, u32[]{:S(2)}) async-start(bf16[32,2,640]{2,1,0:T(2,128)(2,1)} %reshape.509), calls=%async_computation.1 | async-start | bytes 163840 | tf_op jit(solution)/shard_map/all_to_all | solution.py:127

commit v12 on v11

--- a/solution.py
+++ b/solution.py
@@ -64,7 +64,7 @@
         [jnp.concatenate([c0, -c1], -1), jnp.concatenate([c1, c0], -1)], 0
     )
     lhs = jnp.transpose(lhs, (2, 0, 1, 3)).reshape(ablocks * 2 * fields, 128)
-    tile = 512
+    tile = 1024
     total = pl.pallas_call(
         synth_kernel,
         grid=(pl.cdiv(lon, tile),),

time: 89.5 us -> 87.1 us (0.973)
  Pallas kernels: 8.13 us -> 5.81 us
    pallas_call x1, Pallas kernels: 8.13 us -> 5.81 us  [row_synthesis(): pl.pallas_call(synth_kernel, grid=(pl.cdiv(lon, tile),), in_specs=[pl.Blo...]
where the time goes in v12:
time: 87.1 us; the launch traced here: 86.4 us
  waiting for transfers between devices  20.1 us (23%)
  other arithmetic  18.9 us (22%)
  local copies, waits for them, and re-layouts  11.7 us (13%)
  blocking collectives  10.1 us (12%)
  starting transfers between devices  9.31 us (11%)
  matrix products  6.38 us (7%)
  Pallas kernels  5.81 us (7%)
  between operations  4.08 us (5%)
    all_to_all x1, waiting for transfers between devices, on_device(): lax.all_to_all(spec_v, ('lev_g', 'lev_r'), split_axis=0, concat_axis=0, t...  13.8 us
    all_to_all x1, blocking collectives, on_device(): lax.all_to_all(grid, 'lev_r', split_axis=1, concat_axis=0, tiled=True)  10.1 us
    cos x3, other arithmetic, trig_pair(): return (jnp.cos(theta), jnp.sin(theta))  7.65 us
    all_to_all x1, waiting for transfers between devices, on_device(): lax.all_to_all(fourier, ('wave', 'lev_g', 'lev_r'), split_axis=0, concat_...  6.32 us
    pallas_call x1, Pallas kernels, row_synthesis(): pl.pallas_call(synth_kernel, grid=(pl.cdiv(lon, tile),), in_specs=[pl.Blo...  5.81 us
    all_to_all x1, starting transfers between devices, on_device(): lax.all_to_all(spec_v, ('lev_g', 'lev_r'), split_axis=0, concat_axis=0, t...  5.3 us
    dot_general x1, matrix products, on_device(): jnp.einsum('lscfk,sjk->sclfj', gathered, leg2, preferred_element_type=jnp...  4.97 us
    all_to_all x1, starting transfers between devices, on_device(): lax.all_to_all(fourier, ('wave', 'lev_g', 'lev_r'), split_axis=0, concat_...  4 us
  transfers between devices with their start and end apart: 2, of which 2 were waited for; matrix products, arithmetic and copies ran while one was open for 26% of the time, Pallas kernels for 0%

profile of v12, /device:TPU:0, one launch (start us, length us, event | category | flops | bytes accessed | tf_op | source)
XLA Modules:
  0.0 86.4 jit_solution(6007959555284538211)
XLA Ops:
  0.0 5.3 %all-to-all-start = ((bf16[8,40,2,2,1280]{4,3,2,1,0:T(2,128)(2,1)}), bf16[8,40,2,2,1280]{4,3,2,1,0:T(2,128)(2,1)S(1)}, u32[]{:S(2)}, u32[]{:S(2)}) async-start(bf16[8,40,2,2,1280]{4,3,2,1,0:T(2,128)(2,1)} %bitcast.64), calls=%async_computation | async-start | bytes 6553600 | tf_op jit(solution)/shard_map/all_to_all | solution.py:94
  10.4 3.0 %fusion.54 = (f32[8,5136]{1,0:T(8,128)S(1)}, f32[8,5136]{1,0:T(8,128)}) fusion(f32[]{:T(128)S(6)} %convert_element_type.74, pred[]{:T(512)S(6)} %lt.110, s32[]{:T(128)S(6)} %select_n.129, s32[8]{0:T(128)S(1)} %iota_multiply_fusion.2), kind=kLoop, calls=%fused_computation.74 | loop fusion | flops 451968 | bytes 328745 | tf_op jit(solution)/shard_map/cos | solution.py:19
  13.4 2.3 %fusion.50 = (f32[5,5136]{1,0:T(8,128)S(1)}, f32[5,5136]{1,0:T(8,128)S(1)}) fusion(f32[]{:T(128)S(6)} %convert_element_type.74, pred[]{:T(512)S(6)} %lt.110, s32[]{:T(128)S(6)} %select_n.129, s32[5]{0:T(128)S(1)} %iota_multiply_fusion.1), kind=kLoop, calls=%fused_computation.70 | loop fusion | flops 282480 | bytes 205469 | tf_op jit(solution)/shard_map/cos | solution.py:19
  15.7 2.3 %fusion.56 = (f32[4,5136]{1,0:T(4,128)S(1)}, f32[4,5136]{1,0:T(4,128)S(1)}) fusion(f32[]{:T(128)S(6)} %convert_element_type.74, pred[]{:T(512)S(6)} %lt.110, s32[]{:T(128)S(6)} %select_n.129, s32[4]{0:T(128)S(1)} %iota_multiply_fusion), kind=kLoop, calls=%fused_computation.76 | loop fusion | flops 225984 | bytes 164377 | tf_op jit(solution)/shard_map/cos | solution.py:19
  18.1 1.1 %multiply_add_fusion = (f32[5,4,5136]{2,1,0:T(4,128)}, f32[5,4,5136]{2,1,0:T(4,128)}) fusion(f32[4,5136]{1,0:T(4,128)S(1)} %get-tuple-element.41, f32[5,5136]{1,0:T(8,128)S(1)} %get-tuple-element.39, f32[4,5136]{1,0:T(4,128)S(1)} %get-tuple-element.40, f32[5,5136]{1,0:T(8,128)S(1)} %get-tuple-element.38), kind=kLoop, calls=%fused_computation.22 | loop fusion | flops 616320 | bytes 1191552 | tf_op jit(solution)/shard_map/add | solution.py:26
  19.2 2.0 %add.126 = f32[1,20,5136]{2,1,0:T(8,128)} reshape(f32[5,4,5136]{2,1,0:T(4,128)} %get-tuple-element.30) | data formatting | bytes 821760 | tf_op jit(solution)/shard_map/add | solution.py:26
  21.1 2.0 %sub.32 = f32[1,20,5136]{2,1,0:T(8,128)} reshape(f32[5,4,5136]{2,1,0:T(4,128)} %get-tuple-element.31) | data formatting | bytes 821760 | tf_op jit(solution)/shard_map/sub | solution.py:25
  23.4 3.6 %broadcast_select_fusion.1 = (bf16[40,16,1280]{2,1,0:T(8,128)(2,1)}, bf16[40,16,1280]{2,1,0:T(8,128)(2,1)}) fusion(bf16[40,16,1280]{2,1,0:T(8,128)(2,1)} %param.6, pred[40,1280]{1,0:T(8,128)(4,1)S(1)} %get-tuple-element.36, pred[40,1280]{1,0:T(8,128)(4,1)S(1)} %get-tuple-element.37), kind=kLoop, calls=%fused_computation.14 | loop fusion | flops 1638400 | bytes 5017600 | tf_op jit(solution)/shard_map/jit(_where)/select_n | solution.py:112
  27.0 2.3 %fusion.51 = (f32[8,5136]{1,0:T(8,128)S(1)}, f32[8,5136]{1,0:T(8,128)S(1)}) fusion(f32[]{:T(128)S(6)} %convert_element_type.74, pred[]{:T(512)S(6)} %lt.110, s32[]{:T(128)S(6)} %select_n.129), kind=kLoop, calls=%fused_computation.71 | loop fusion | flops 451968 | bytes 328713 | tf_op jit(solution)/shard_map/sin | solution.py:19
  29.6 1.2 %maximum_bitcast_fusion.2 = bf16[1,128,5136]{2,1,0:T(8,128)(2,1)} fusion(bf16[64,5136]{1,0:T(8,128)(2,1)S(1)} %get-tuple-element.27, bf16[64,5136]{1,0:T(8,128)(2,1)S(1)} %get-tuple-element.26), kind=kLoop, calls=%fused_computation.15 | loop fusion | flops 2629632 | bytes 2629632 | tf_op jit(solution)/shard_map/broadcast_in_dim | solution.py:100
  30.8 13.8 %all-to-all-done = bf16[8,40,2,2,1280]{4,3,2,1,0:T(2,128)(2,1)S(1)} async-done(((bf16[8,40,2,2,1280]{4,3,2,1,0:T(2,128)(2,1)}), bf16[8,40,2,2,1280]{4,3,2,1,0:T(2,128)(2,1)S(1)}, u32[]{:S(2)}, u32[]{:S(2)}) %all-to-all-start) | async-done | bytes 3276832 | tf_op jit(solution)/shard_map/all_to_all | solution.py:94
  44.6 5.0 %fusion.14 = f32[40,2,8,2,32]{4,2,3,1,0:T(8,128)} fusion(bf16[8,40,2,2,1280]{4,3,2,1,0:T(2,128)(2,1)S(1)} %all-to-all-done, bf16[40,16,1280]{2,1,0:T(8,128)(2,1)} %get-tuple-element.25, bf16[40,16,1280]{2,1,0:T(8,128)(2,1)} %get-tuple-element.24), kind=kOutput, calls=%fused_computation.18 | convolution fusion | flops 111411200 | bytes 6717440 | tf_op jit(solution)/shard_map/lscfk,sjk->sclfj/dot_general | solution.py:114
  49.6 1.4 %copy.18 = f32[40,2,8,2,32]{0,4,3,2,1:T(8,128)S(1)} copy(f32[40,2,8,2,32]{4,2,3,1,0:T(8,128)} %fusion.14) | data formatting | bytes 327680 | tf_op jit(solution)/shard_map/lscfk,sjk->sclfj/transpose | solution.py:114
  52.5 1.0 %reshape.509 = bf16[32,2,640]{2,1,0:T(2,128)(2,1)} reshape(bf16[32,1,2,16,40]{4,3,2,1,0:T(8,128)(2,1)S(1)} %bitcast.74) | data formatting | bytes 163840
  53.5 4.0 %all-to-all-start.1 = ((bf16[32,2,640]{2,1,0:T(2,128)(2,1)}), bf16[32,2,640]{2,1,0:T(2,128)(2,1)S(1)}, u32[]{:S(2)}, u32[]{:S(2)}) async-start(bf16[32,2,640]{2,1,0:T(2,128)(2,1)} %reshape.509), calls=%async_computation.1 | async-start | bytes 163840 | tf_op jit(solution)/shard_map/all_to_all | solution.py:127
  57.5 0.6 iota_compare_fusion.2
  58.2 0.6 select_select_fusion
  58.8 6.3 %all-to-all-done.1 = bf16[32,2,640]{2,1,0:T(2,128)(2,1)S(1)} async-done(((bf16[32,2,640]{2,1,0:T(2,128)(2,1)}), bf16[32,2,640]{2,1,0:T(2,128)(2,1)S(1)}, u32[]{:S(2)}, u32[]{:S(2)}) %all-to-all-start.1) | async-done | bytes 81952 | tf_op jit(solution)/shard_map/all_to_all | solution.py:127
  66.0 1.4 %fusion.11 = bf16[2,16,1280]{2,1,0:T(8,128)(2,1)S(1)} fusion(bf16[2,16,1280]{2,1,0:T(8,128)(2,1)S(1)} %reshape.465, s32[1280]{0:T(1024)S(1)} %copy-done.1, f32[1280]{0:T(1024)S(1)} %select_select_fusion), kind=kOutput, calls=%fused_computation.12 | convolution fusion | flops 106577920 | bytes 174080 | tf_op jit(solution)/shard_map/cfrs,sm->cfrm/dot_general | solution.py:133
  67.9 0.7 copy.22
  68.6 5.8 %shard_map.55 = f32[16,5136]{1,0:T(8,128)} custom-call(bf16[640,128]{1,0:T(8,128)(2,1)} %bitcast.75, bf16[128,5136]{1,0:T(8,128)(2,1)} %bitcast.63, f32[20,5136]{1,0:T(8,128)} %bitcast.71, f32[20,5136]{1,0:T(8,128)} %bitcast.70), custom_call_target="tpu_custom_call" | custom-call | tf_op jit(solution)/shard_map/pallas_call | solution.py:68
  74.4 1.0 %broadcast_select_fusion.2 = f32[16,5136]{1,0:T(8,128)S(1)} fusion(f32[16,5136]{1,0:T(8,128)} %shard_map.55, pred[5136]{0:T(1024)(128)(4,1)S(1)} %iota_compare_fusion.2), kind=kLoop, calls=%fused_computation.42 | loop fusion | flops 82176 | bytes 662544 | tf_op jit(solution)/shard_map/jit(_where)/select_n | solution.py:80
  75.6 10.1 %all_to_all.19 = f32[1,8,2,5136]{3,2,0,1:T(2,128)S(1)} all-to-all(f32[1,8,2,5136]{3,2,0,1:T(2,128)S(1)} %bitcast.72), channel_id=1, replica_groups=mesh['wave'=4,'lev'=8] {'lev'}, dimensions={1} | all-to-all | bytes 657408 | tf_op jit(solution)/shard_map/all_to_all | solution.py:145
  85.7 0.7 copy.36
  (38 shorter events, 4.8 us)
Async XLA Ops:
  0.0 5.3 %copy-start.3 = (s32[32]{0:T(128)S(1)}, s32[32]{0:T(128)}, u32[]{:S(2)}) copy-start(s32[32]{0:T(128)} %param.9) | copy-start | bytes 388
  0.0 7.8 %copy-start.2 = (s32[32]{0:T(128)S(1)}, s32[32]{0:T(128)}, u32[]{:S(2)}) copy-start(s32[32]{0:T(128)} %param.8) | copy-start | bytes 388
  0.0 44.6 %all-to-all-start = ((bf16[8,40,2,2,1280]{4,3,2,1,0:T(2,128)(2,1)}), bf16[8,40,2,2,1280]{4,3,2,1,0:T(2,128)(2,1)S(1)}, u32[]{:S(2)}, u32[]{:S(2)}) async-start(bf16[8,40,2,2,1280]{4,3,2,1,0:T(2,128)(2,1)} %bitcast.64), calls=%async_computation | async-start | bytes 6553600 | tf_op jit(solution)/shard_map/all_to_all | solution.py:94
  18.1 5.1 %copy-start.1 = (s32[1280]{0:T(1024)S(1)}, s32[1280]{0:T(1024)}, u32[]{:S(2)}) copy-start(s32[1280]{0:T(1024)} %param.7) | copy-start | bytes 15364
  23.4 5.9 %copy-start = (f32[8,5136]{1,0:T(8,128)S(1)}, f32[8,5136]{1,0:T(8,128)}, u32[]{:S(2)}) copy-start(f32[8,5136]{1,0:T(8,128)} %get-tuple-element.43) | copy-start | bytes 493060
  53.5 11.6 %all-to-all-start.1 = ((bf16[32,2,640]{2,1,0:T(2,128)(2,1)}), bf16[32,2,640]{2,1,0:T(2,128)(2,1)S(1)}, u32[]{:S(2)}, u32[]{:S(2)}) async-start(bf16[32,2,640]{2,1,0:T(2,128)(2,1)} %reshape.509), calls=%async_computation.1 | async-start | bytes 163840 | tf_op jit(solution)/shard_map/all_to_all | solution.py:127

commit v13 on v12

--- a/solution.py
+++ b/solution.py
@@ -42,12 +42,13 @@
 
 def synth_kernel(lhs_ref, rhs_ref, cos_ref, sin_ref, o_ref):
     fields = o_ref.shape[0]
-    part = jnp.dot(lhs_ref[...], rhs_ref[...], preferred_element_type=jnp.float32)
+    rhs = rhs_ref[...]
     acc = jnp.zeros(o_ref.shape, jnp.float32)
     for a in range(cos_ref.shape[0]):
-        re = part[2 * a * fields:(2 * a + 1) * fields]
-        im = part[(2 * a + 1) * fields:(2 * a + 2) * fields]
-        acc = acc + re * cos_ref[a:a + 1, :] - im * sin_ref[a:a + 1, :]
+        part = jnp.dot(
+            lhs_ref[2 * a * fields:(2 * a + 2) * fields, :], rhs, preferred_element_type=jnp.float32
+        )
+        acc = acc + part[:fields] * cos_ref[a:a + 1, :] - part[fields:] * sin_ref[a:a + 1, :]
     o_ref[...] = acc
 
 

time: 87.1 us -> 88.4 us (1.015)
  Pallas kernels: 5.81 us -> 7.15 us
    pallas_call x1, Pallas kernels: 5.81 us -> 7.15 us  [row_synthesis(): pl.pallas_call(synth_kernel, grid=(pl.cdiv(lon, tile),), in_specs=[pl.Blo...]
where the time goes in v13:
time: 88.4 us; the launch traced here: 87.8 us
  waiting for transfers between devices  20.1 us (23%)
  other arithmetic  18.9 us (21%)
  local copies, waits for them, and re-layouts  11.7 us (13%)
  blocking collectives  10.1 us (11%)
  starting transfers between devices  9.31 us (11%)
  Pallas kernels  7.15 us (8%)
  matrix products  6.38 us (7%)
  between operations  4.08 us (5%)
    all_to_all x1, waiting for transfers between devices, on_device(): lax.all_to_all(spec_v, ('lev_g', 'lev_r'), split_axis=0, concat_axis=0, t...  13.8 us
    all_to_all x1, blocking collectives, on_device(): lax.all_to_all(grid, 'lev_r', split_axis=1, concat_axis=0, tiled=True)  10.1 us
    cos x3, other arithmetic, trig_pair(): return (jnp.cos(theta), jnp.sin(theta))  7.65 us
    pallas_call x1, Pallas kernels, row_synthesis(): pl.pallas_call(synth_kernel, grid=(pl.cdiv(lon, tile),), in_specs=[pl.Blo...  7.15 us
    all_to_all x1, waiting for transfers between devices, on_device(): lax.all_to_all(fourier, ('wave', 'lev_g', 'lev_r'), split_axis=0, concat_...  6.32 us
    all_to_all x1, starting transfers between devices, on_device(): lax.all_to_all(spec_v, ('lev_g', 'lev_r'), split_axis=0, concat_axis=0, t...  5.3 us
    dot_general x1, matrix products, on_device(): jnp.einsum('lscfk,sjk->sclfj', gathered, leg2, preferred_element_type=jnp...  4.97 us
    all_to_all x1, starting transfers between devices, on_device(): lax.all_to_all(fourier, ('wave', 'lev_g', 'lev_r'), split_axis=0, concat_...  4 us
  transfers between devices with their start and end apart: 2, of which 2 were waited for; matrix products, arithmetic and copies ran while one was open for 26% of the time, Pallas kernels for 0%

profile of v13, /device:TPU:0, one launch (start us, length us, event | category | flops | bytes accessed | tf_op | source)
XLA Modules:
  0.0 87.8 jit_solution(17409996232692833181)
XLA Ops:
  0.0 5.3 %all-to-all-start = ((bf16[8,40,2,2,1280]{4,3,2,1,0:T(2,128)(2,1)}), bf16[8,40,2,2,1280]{4,3,2,1,0:T(2,128)(2,1)S(1)}, u32[]{:S(2)}, u32[]{:S(2)}) async-start(bf16[8,40,2,2,1280]{4,3,2,1,0:T(2,128)(2,1)} %bitcast.64), calls=%async_computation | async-start | bytes 6553600 | tf_op jit(solution)/shard_map/all_to_all | solution.py:95
  10.4 3.0 %fusion.54 = (f32[8,5136]{1,0:T(8,128)S(1)}, f32[8,5136]{1,0:T(8,128)}) fusion(f32[]{:T(128)S(6)} %convert_element_type.74, pred[]{:T(512)S(6)} %lt.110, s32[]{:T(128)S(6)} %select_n.129, s32[8]{0:T(128)S(1)} %iota_multiply_fusion.2), kind=kLoop, calls=%fused_computation.74 | loop fusion | flops 451968 | bytes 328745 | tf_op jit(solution)/shard_map/cos | solution.py:19
  13.4 2.3 %fusion.50 = (f32[5,5136]{1,0:T(8,128)S(1)}, f32[5,5136]{1,0:T(8,128)S(1)}) fusion(f32[]{:T(128)S(6)} %convert_element_type.74, pred[]{:T(512)S(6)} %lt.110, s32[]{:T(128)S(6)} %select_n.129, s32[5]{0:T(128)S(1)} %iota_multiply_fusion.1), kind=kLoop, calls=%fused_computation.70 | loop fusion | flops 282480 | bytes 205469 | tf_op jit(solution)/shard_map/cos | solution.py:19
  15.7 2.3 %fusion.56 = (f32[4,5136]{1,0:T(4,128)S(1)}, f32[4,5136]{1,0:T(4,128)S(1)}) fusion(f32[]{:T(128)S(6)} %convert_element_type.74, pred[]{:T(512)S(6)} %lt.110, s32[]{:T(128)S(6)} %select_n.129, s32[4]{0:T(128)S(1)} %iota_multiply_fusion), kind=kLoop, calls=%fused_computation.76 | loop fusion | flops 225984 | bytes 164377 | tf_op jit(solution)/shard_map/cos | solution.py:19
  18.1 1.1 %multiply_add_fusion = (f32[5,4,5136]{2,1,0:T(4,128)}, f32[5,4,5136]{2,1,0:T(4,128)}) fusion(f32[4,5136]{1,0:T(4,128)S(1)} %get-tuple-element.41, f32[5,5136]{1,0:T(8,128)S(1)} %get-tuple-element.39, f32[4,5136]{1,0:T(4,128)S(1)} %get-tuple-element.40, f32[5,5136]{1,0:T(8,128)S(1)} %get-tuple-element.38), kind=kLoop, calls=%fused_computation.22 | loop fusion | flops 616320 | bytes 1191552 | tf_op jit(solution)/shard_map/add | solution.py:26
  19.2 2.0 %add.126 = f32[1,20,5136]{2,1,0:T(8,128)} reshape(f32[5,4,5136]{2,1,0:T(4,128)} %get-tuple-element.30) | data formatting | bytes 821760 | tf_op jit(solution)/shard_map/add | solution.py:26
  21.1 2.0 %sub.32 = f32[1,20,5136]{2,1,0:T(8,128)} reshape(f32[5,4,5136]{2,1,0:T(4,128)} %get-tuple-element.31) | data formatting | bytes 821760 | tf_op jit(solution)/shard_map/sub | solution.py:25
  23.4 3.6 %broadcast_select_fusion.1 = (bf16[40,16,1280]{2,1,0:T(8,128)(2,1)}, bf16[40,16,1280]{2,1,0:T(8,128)(2,1)}) fusion(bf16[40,16,1280]{2,1,0:T(8,128)(2,1)} %param.6, pred[40,1280]{1,0:T(8,128)(4,1)S(1)} %get-tuple-element.36, pred[40,1280]{1,0:T(8,128)(4,1)S(1)} %get-tuple-element.37), kind=kLoop, calls=%fused_computation.14 | loop fusion | flops 1638400 | bytes 5017600 | tf_op jit(solution)/shard_map/jit(_where)/select_n | solution.py:113
  27.0 2.3 %fusion.51 = (f32[8,5136]{1,0:T(8,128)S(1)}, f32[8,5136]{1,0:T(8,128)S(1)}) fusion(f32[]{:T(128)S(6)} %convert_element_type.74, pred[]{:T(512)S(6)} %lt.110, s32[]{:T(128)S(6)} %select_n.129), kind=kLoop, calls=%fused_computation.71 | loop fusion | flops 451968 | bytes 328713 | tf_op jit(solution)/shard_map/sin | solution.py:19
  29.6 1.2 %maximum_bitcast_fusion.2 = bf16[1,128,5136]{2,1,0:T(8,128)(2,1)} fusion(bf16[64,5136]{1,0:T(8,128)(2,1)S(1)} %get-tuple-element.27, bf16[64,5136]{1,0:T(8,128)(2,1)S(1)} %get-tuple-element.26), kind=kLoop, calls=%fused_computation.15 | loop fusion | flops 2629632 | bytes 2629632 | tf_op jit(solution)/shard_map/broadcast_in_dim | solution.py:101
  30.8 13.8 %all-to-all-done = bf16[8,40,2,2,1280]{4,3,2,1,0:T(2,128)(2,1)S(1)} async-done(((bf16[8,40,2,2,1280]{4,3,2,1,0:T(2,128)(2,1)}), bf16[8,40,2,2,1280]{4,3,2,1,0:T(2,128)(2,1)S(1)}, u32[]{:S(2)}, u32[]{:S(2)}) %all-to-all-start) | async-done | bytes 3276832 | tf_op jit(solution)/shard_map/all_to_all | solution.py:95
  44.6 5.0 %fusion.14 = f32[40,2,8,2,32]{4,2,3,1,0:T(8,128)} fusion(bf16[8,40,2,2,1280]{4,3,2,1,0:T(2,128)(2,1)S(1)} %all-to-all-done, bf16[40,16,1280]{2,1,0:T(8,128)(2,1)} %get-tuple-element.25, bf16[40,16,1280]{2,1,0:T(8,128)(2,1)} %get-tuple-element.24), kind=kOutput, calls=%fused_computation.18 | convolution fusion | flops 111411200 | bytes 6717440 | tf_op jit(solution)/shard_map/lscfk,sjk->sclfj/dot_general | solution.py:115
  49.6 1.4 %copy.18 = f32[40,2,8,2,32]{0,4,3,2,1:T(8,128)S(1)} copy(f32[40,2,8,2,32]{4,2,3,1,0:T(8,128)} %fusion.14) | data formatting | bytes 327680 | tf_op jit(solution)/shard_map/lscfk,sjk->sclfj/transpose | solution.py:115
  52.5 1.0 %reshape.509 = bf16[32,2,640]{2,1,0:T(2,128)(2,1)} reshape(bf16[32,1,2,16,40]{4,3,2,1,0:T(8,128)(2,1)S(1)} %bitcast.74) | data formatting | bytes 163840
  53.5 4.0 %all-to-all-start.1 = ((bf16[32,2,640]{2,1,0:T(2,128)(2,1)}), bf16[32,2,640]{2,1,0:T(2,128)(2,1)S(1)}, u32[]{:S(2)}, u32[]{:S(2)}) async-start(bf16[32,2,640]{2,1,0:T(2,128)(2,1)} %reshape.509), calls=%async_computation.1 | async-start | bytes 163840 | tf_op jit(solution)/shard_map/all_to_all | solution.py:128
  57.5 0.6 iota_compare_fusion.2
  58.2 0.6 select_select_fusion
  58.8 6.3 %all-to-all-done.1 = bf16[32,2,640]{2,1,0:T(2,128)(2,1)S(1)} async-done(((bf16[32,2,640]{2,1,0:T(2,128)(2,1)}), bf16[32,2,640]{2,1,0:T(2,128)(2,1)S(1)}, u32[]{:S(2)}, u32[]{:S(2)}) %all-to-all-start.1) | async-done | bytes 81952 | tf_op jit(solution)/shard_map/all_to_all | solution.py:128
  66.0 1.4 %fusion.11 = bf16[2,16,1280]{2,1,0:T(8,128)(2,1)S(1)} fusion(bf16[2,16,1280]{2,1,0:T(8,128)(2,1)S(1)} %reshape.465, s32[1280]{0:T(1024)S(1)} %copy-done.1, f32[1280]{0:T(1024)S(1)} %select_select_fusion), kind=kOutput, calls=%fused_computation.12 | convolution fusion | flops 106577920 | bytes 174080 | tf_op jit(solution)/shard_map/cfrs,sm->cfrm/dot_general | solution.py:134
  67.9 0.7 copy.22
  68.6 7.2 %shard_map.55 = f32[16,5136]{1,0:T(8,128)} custom-call(bf16[640,128]{1,0:T(8,128)(2,1)} %bitcast.75, bf16[128,5136]{1,0:T(8,128)(2,1)} %bitcast.63, f32[20,5136]{1,0:T(8,128)} %bitcast.71, f32[20,5136]{1,0:T(8,128)} %bitcast.70), custom_call_target="tpu_custom_call" | custom-call | tf_op jit(solution)/shard_map/pallas_call | solution.py:69
  75.7 1.0 %broadcast_select_fusion.2 = f32[16,5136]{1,0:T(8,128)S(1)} fusion(f32[16,5136]{1,0:T(8,128)} %shard_map.55, pred[5136]{0:T(1024)(128)(4,1)S(1)} %iota_compare_fusion.2), kind=kLoop, calls=%fused_computation.42 | loop fusion | flops 82176 | bytes 662544 | tf_op jit(solution)/shard_map/jit(_where)/select_n | solution.py:81
  77.0 10.1 %all_to_all.19 = f32[1,8,2,5136]{3,2,0,1:T(2,128)S(1)} all-to-all(f32[1,8,2,5136]{3,2,0,1:T(2,128)S(1)} %bitcast.72), channel_id=1, replica_groups=mesh['wave'=4,'lev'=8] {'lev'}, dimensions={1} | all-to-all | bytes 657408 | tf_op jit(solution)/shard_map/all_to_all | solution.py:146
  87.1 0.7 copy.36
  (38 shorter events, 4.8 us)
Async XLA Ops:
  0.0 5.3 %copy-start.3 = (s32[32]{0:T(128)S(1)}, s32[32]{0:T(128)}, u32[]{:S(2)}) copy-start(s32[32]{0:T(128)} %param.9) | copy-start | bytes 388
  0.0 7.8 %copy-start.2 = (s32[32]{0:T(128)S(1)}, s32[32]{0:T(128)}, u32[]{:S(2)}) copy-start(s32[32]{0:T(128)} %param.8) | copy-start | bytes 388
  0.0 44.6 %all-to-all-start = ((bf16[8,40,2,2,1280]{4,3,2,1,0:T(2,128)(2,1)}), bf16[8,40,2,2,1280]{4,3,2,1,0:T(2,128)(2,1)S(1)}, u32[]{:S(2)}, u32[]{:S(2)}) async-start(bf16[8,40,2,2,1280]{4,3,2,1,0:T(2,128)(2,1)} %bitcast.64), calls=%async_computation | async-start | bytes 6553600 | tf_op jit(solution)/shard_map/all_to_all | solution.py:95
  18.1 5.1 %copy-start.1 = (s32[1280]{0:T(1024)S(1)}, s32[1280]{0:T(1024)}, u32[]{:S(2)}) copy-start(s32[1280]{0:T(1024)} %param.7) | copy-start | bytes 15364
  23.4 5.9 %copy-start = (f32[8,5136]{1,0:T(8,128)S(1)}, f32[8,5136]{1,0:T(8,128)}, u32[]{:S(2)}) copy-start(f32[8,5136]{1,0:T(8,128)} %get-tuple-element.43) | copy-start | bytes 493060
  53.5 11.6 %all-to-all-start.1 = ((bf16[32,2,640]{2,1,0:T(2,128)(2,1)}), bf16[32,2,640]{2,1,0:T(2,128)(2,1)S(1)}, u32[]{:S(2)}, u32[]{:S(2)}) async-start(bf16[32,2,640]{2,1,0:T(2,128)(2,1)} %reshape.509), calls=%async_computation.1 | async-start | bytes 163840 | tf_op jit(solution)/shard_map/all_to_all | solution.py:128

commit v14 on v3

--- a/solution.py
+++ b/solution.py
@@ -76,18 +76,17 @@
     leg2 = jnp.concatenate(
         [jnp.where(even_mask, legendre, zeros), jnp.where(odd_mask, legendre, zeros)], 1
     )
-    sums = jnp.einsum("lscfk,sjk->sclfj", gathered, leg2, preferred_element_type=jnp.float32)
-    sums = sums.reshape(per_dev, 2, fields, 2, nlath)
+    sums = jnp.einsum("lscfk,sjk->jclfs", gathered, leg2, preferred_element_type=jnp.float32)
+    sums = sums.reshape(2 * nlath, 2, fields, per_dev)
     north = band_rows < nlath
     lat_idx = jnp.where(north, band_rows, band_rows - nlath)
     parity_sign = jnp.where(north, 1.0, -1.0).astype(jnp.float32)
-    fourier = (sums[:, :, :, 0][..., lat_idx] + parity_sign * sums[:, :, :, 1][..., lat_idx]).astype(
+    fourier = (sums[lat_idx] + parity_sign[:, None, None, None] * sums[nlath + lat_idx]).astype(
         jnp.bfloat16
     )
-    rows = band_rows.shape[0]
     fpg = fields // n_g
-    fourier = fourier.reshape(per_dev, 2, n_g, fpg, n_wave, n_r, rows_per_dev)
-    fourier = jnp.transpose(fourier, (4, 2, 5, 1, 3, 6, 0))
+    fourier = fourier.reshape(n_wave, n_r, rows_per_dev, 2, n_g, fpg, per_dev)
+    fourier = jnp.transpose(fourier, (0, 4, 1, 3, 5, 2, 6))
     fourier = fourier.reshape(n_wave * n_g * n_r, 2, fpg, rows_per_dev, per_dev)
     banded = lax.all_to_all(
         fourier, ("wave", "lev_g", "lev_r"), split_axis=0, concat_axis=0, tiled=True

time: 84.7 us -> 84.8 us (level)
    unnamed x29 -> x27, local copies, waits for them, and re-layouts: 2.34 us -> 2.17 us
  transfers between devices with their start and end apart: 2 -> 2, of which waited for: 2 -> 2; matrix products, arithmetic and copies ran while one was open for 33% -> 32% of each run, Pallas kernels for 0% -> 0%
where the time goes in v14:
time: 84.8 us; the launch traced here: 84.2 us
  other arithmetic  22.6 us (27%)
  waiting for transfers between devices  15.5 us (18%)
  local copies, waits for them, and re-layouts  12.9 us (15%)
  blocking collectives  10.9 us (13%)
  starting transfers between devices  9.31 us (11%)
  matrix products  8.82 us (10%)
  between operations  4.16 us (5%)
    all_to_all x1, waiting for transfers between devices, on_device(): lax.all_to_all(spec_v, ('lev_g', 'lev_r'), split_axis=0, concat_axis=0, t...  15 us
    all_to_all x1, blocking collectives, on_device(): lax.all_to_all(grid, 'lev_r', split_axis=1, concat_axis=0, tiled=True)  10.9 us
    cos x3, other arithmetic, trig_pair(): return (jnp.cos(theta), jnp.sin(theta))  9.05 us
    all_to_all x1, starting transfers between devices, on_device(): lax.all_to_all(spec_v, ('lev_g', 'lev_r'), split_axis=0, concat_axis=0, t...  5.3 us
    dot_general x1, matrix products, on_device(): jnp.einsum('lscfk,sjk->jclfs', gathered, leg2, preferred_element_type=jnp...  4.98 us
    all_to_all x1, starting transfers between devices, on_device(): lax.all_to_all(fourier, ('wave', 'lev_g', 'lev_r'), split_axis=0, concat_...  4 us
    select_n x1, other arithmetic, on_device(): jnp.where(even_mask, legendre, zeros)  3.68 us
    sin x1, other arithmetic, trig_pair(): return (jnp.cos(theta), jnp.sin(theta))  2.94 us
  transfers between devices with their start and end apart: 2, of which 2 were waited for; matrix products, arithmetic and copies ran while one was open for 32% of the time, Pallas kernels for 0%

profile of v14, /device:TPU:0, one launch (start us, length us, event | category | flops | bytes accessed | tf_op | source)
XLA Modules:
  0.0 84.2 jit_solution(5165375423201117076)
XLA Ops:
  0.0 5.3 %all-to-all-start = ((bf16[8,40,2,2,1280]{4,3,2,1,0:T(2,128)(2,1)}), bf16[8,40,2,2,1280]{4,3,2,1,0:T(2,128)(2,1)S(1)}, u32[]{:S(2)}, u32[]{:S(2)}) async-start(bf16[8,40,2,2,1280]{4,3,2,1,0:T(2,128)(2,1)} %bitcast.79), calls=%async_computation | async-start | bytes 6553600 | tf_op jit(solution)/shard_map/all_to_all | solution.py:67
  7.9 0.6 dynamic-slice.2
  10.4 2.9 %fusion.64 = (f32[8,5136]{1,0:T(8,128)S(1)}, f32[8,5136]{1,0:T(8,128)}) fusion(f32[]{:T(128)S(6)} %convert_element_type.76, pred[]{:T(512)S(6)} %lt.117, s32[]{:T(128)S(6)} %select_n.144), kind=kLoop, calls=%fused_computation.83 | loop fusion | flops 451968 | bytes 328713 | tf_op jit(solution)/shard_map/sin | solution.py:18
  13.4 3.1 %fusion.67 = (f32[8,5136]{1,0:T(8,128)}, f32[8,5136]{1,0:T(8,128)}) fusion(f32[]{:T(128)S(6)} %convert_element_type.76, pred[]{:T(512)S(6)} %lt.117, s32[]{:T(128)S(6)} %select_n.144, s32[8]{0:T(128)S(1)} %iota_multiply_fusion.2), kind=kLoop, calls=%fused_computation.86 | loop fusion | flops 451968 | bytes 328745 | tf_op jit(solution)/shard_map/cos | solution.py:18
  16.4 3.0 %fusion.63 = (f32[5,5136]{1,0:T(8,128)}, f32[5,5136]{1,0:T(8,128)}) fusion(f32[]{:T(128)S(6)} %convert_element_type.76, pred[]{:T(512)S(6)} %lt.117, s32[]{:T(128)S(6)} %select_n.144, s32[5]{0:T(128)S(1)} %iota_multiply_fusion.1), kind=kLoop, calls=%fused_computation.82 | loop fusion | flops 282480 | bytes 205469 | tf_op jit(solution)/shard_map/cos | solution.py:18
  19.5 3.0 %fusion.69 = (f32[4,5136]{1,0:T(4,128)S(1)}, f32[4,5136]{1,0:T(4,128)}) fusion(f32[]{:T(128)S(6)} %convert_element_type.76, pred[]{:T(512)S(6)} %lt.117, s32[]{:T(128)S(6)} %select_n.144, s32[4]{0:T(128)S(1)} %iota_multiply_fusion), kind=kLoop, calls=%fused_computation.88 | loop fusion | flops 225984 | bytes 164377 | tf_op jit(solution)/shard_map/cos | solution.py:18
  22.4 0.8 dynamic-slice_subtract_fusion
  23.4 3.7 %broadcast_select_fusion.1 = (bf16[40,16,1280]{2,1,0:T(8,128)(2,1)}, bf16[40,16,1280]{2,1,0:T(8,128)(2,1)}) fusion(bf16[40,16,1280]{2,1,0:T(8,128)(2,1)} %param.6, pred[40,1280]{1,0:T(8,128)(4,1)S(1)} %get-tuple-element.32, pred[40,1280]{1,0:T(8,128)(4,1)S(1)} %get-tuple-element.33), kind=kLoop, calls=%fused_computation.20 | loop fusion | flops 1638400 | bytes 5017600 | tf_op jit(solution)/shard_map/jit(_where)/select_n | solution.py:77
  27.1 1.1 %multiply_subtract_fusion = (f32[5,4,5136]{2,1,0:T(4,128)}, f32[5,4,5136]{2,1,0:T(4,128)}) fusion(f32[4,5136]{1,0:T(4,128)S(1)} %copy-done.8, f32[5,5136]{1,0:T(8,128)S(1)} %copy-done.7, f32[4,5136]{1,0:T(4,128)S(1)} %get-tuple-element.28, f32[5,5136]{1,0:T(8,128)S(1)} %copy-done.6), kind=kLoop, calls=%fused_computation.34 | loop fusion | flops 616320 | bytes 1191552 | tf_op jit(solution)/shard_map/sub | solution.py:24
  28.2 1.4 %fusion.24 = (bf16[64,5136]{1,0:T(8,128)(2,1)}, bf16[64,5136]{1,0:T(8,128)(2,1)}) fusion(f32[8,5136]{1,0:T(8,128)S(1)} %get-tuple-element.36, f32[8,5136]{1,0:T(8,128)S(1)} %copy-done.5, f32[8,5136]{1,0:T(8,128)S(1)} %copy-done.3, f32[8,5136]{1,0:T(8,128)S(1)} %copy-done.4), kind=kLoop, calls=%fused_computation.28 | loop fusion | flops 2629632 | bytes 1972224 | tf_op jit(solution)/shard_map/convert_element_type | solution.py:36
  29.6 15.0 %all-to-all-done = bf16[8,40,2,2,1280]{4,3,2,1,0:T(2,128)(2,1)S(1)} async-done(((bf16[8,40,2,2,1280]{4,3,2,1,0:T(2,128)(2,1)}), bf16[8,40,2,2,1280]{4,3,2,1,0:T(2,128)(2,1)S(1)}, u32[]{:S(2)}, u32[]{:S(2)}) %all-to-all-start) | async-done | bytes 3276832 | tf_op jit(solution)/shard_map/all_to_all | solution.py:67
  44.6 5.0 %fusion.21 = f32[32,2,8,2,40]{0,2,3,1,4:T(8,128)} fusion(bf16[8,40,2,2,1280]{4,3,2,1,0:T(2,128)(2,1)S(1)} %all-to-all-done, bf16[40,16,1280]{2,1,0:T(8,128)(2,1)} %get-tuple-element.17, bf16[40,16,1280]{2,1,0:T(8,128)(2,1)} %get-tuple-element.16), kind=kOutput, calls=%fused_computation.27 | convolution fusion | flops 111411200 | bytes 6717440 | tf_op jit(solution)/shard_map/lscfk,sjk->jclfs/dot_general | solution.py:79
  49.6 1.4 %copy.17 = f32[32,2,8,2,40]{4,0,3,2,1:T(8,128)S(1)} copy(f32[32,2,8,2,40]{0,2,3,1,4:T(8,128)} %fusion.21) | data formatting | bytes 327680 | tf_op jit(solution)/shard_map/lscfk,sjk->jclfs/transpose | solution.py:79
  52.7 1.0 %reshape.472 = bf16[32,2,640]{2,1,0:T(2,128)(2,1)} reshape(bf16[32,1,2,16,40]{4,3,2,1,0:T(8,128)(2,1)S(1)} %fusion.78) | data formatting | bytes 163840
  53.7 4.0 %all-to-all-start.1 = ((bf16[32,2,640]{2,1,0:T(2,128)(2,1)}), bf16[32,2,640]{2,1,0:T(2,128)(2,1)S(1)}, u32[]{:S(2)}, u32[]{:S(2)}) async-start(bf16[32,2,640]{2,1,0:T(2,128)(2,1)} %reshape.472), calls=%async_computation.1 | async-start | bytes 163840 | tf_op jit(solution)/shard_map/all_to_all | solution.py:91
  58.3 1.3 %copy.22 = bf16[64,5136]{0,1:T(8,128)(2,1)S(1)} copy(bf16[64,5136]{1,0:T(8,128)(2,1)S(1)} %copy-done.1) | data formatting | bytes 1314816 | tf_op jit(solution)/shard_map/convert_element_type | solution.py:36
  59.7 1.3 %copy.23 = bf16[64,5136]{0,1:T(8,128)(2,1)S(1)} copy(bf16[64,5136]{1,0:T(8,128)(2,1)S(1)} %copy-done) | data formatting | bytes 1314816 | tf_op jit(solution)/shard_map/convert_element_type | solution.py:37
  61.0 1.2 %add.137 = f32[20,5136]{1,0:T(8,128)S(1)} reshape(f32[5,4,5136]{2,1,0:T(4,128)} %get-tuple-element.21) | data formatting | bytes 821760 | tf_op jit(solution)/shard_map/add | solution.py:25
  62.1 1.9 %sub.33 = f32[20,5136]{1,0:T(8,128)} reshape(f32[5,4,5136]{2,1,0:T(4,128)} %get-tuple-element.20) | data formatting | bytes 821760 | tf_op jit(solution)/shard_map/sub | solution.py:24
  66.2 1.4 %fusion.15 = bf16[2,16,1280]{2,1,0:T(8,128)(2,1)S(1)} fusion(bf16[2,16,1280]{2,1,0:T(8,128)(2,1)S(1)} %reshape.428, s32[1280]{0:T(1024)S(1)} %copy-done.9, f32[1280]{0:T(1024)S(1)} %select_select_fusion), kind=kOutput, calls=%fused_computation.18 | convolution fusion | flops 106577920 | bytes 174080 | tf_op jit(solution)/shard_map/cfrs,sm->cfrm/dot_general | solution.py:97
  68.0 2.4 %fusion.18 = f32[2,16,20,5136]{3,2,1,0:T(8,128)S(1)} fusion(bf16[64,5136]{0,1:T(8,128)(2,1)S(1)} %copy.23, bf16[64,5136]{0,1:T(8,128)(2,1)S(1)} %copy.22, bf16[1,16,20,128]{3,2,1,0:T(8,128)(2,1)S(1)} %get-tuple-element.23, bf16[1,16,20,128]{3,2,1,0:T(8,128)(2,1)S(1)} %get-tuple-element.22), kind=kOutput, calls=%fused_computation.24 | convolution fusion | flops 844193792 | bytes 14626816 | tf_op jit(solution)/shard_map/dfab,bi->dfai/dot_general | solution.py:51
  70.5 1.8 %fusion.2 = f32[16,5136]{1,0:T(8,128)S(1)} fusion(f32[2,16,20,5136]{3,2,1,0:T(8,128)S(1)} %fusion.18, f32[20,5136]{1,0:T(8,128)S(1)} %add.137, f32[20,5136]{1,0:T(8,128)S(1)} %copy-done.2), kind=kLoop, calls=%fused_computation.5 | loop fusion | flops 6491904 | bytes 14298624 | tf_op jit(solution)/shard_map/reduce_sum | solution.py:52
  72.6 10.9 %all_to_all.19 = f32[1,8,2,5136]{3,2,0,1:T(2,128)S(1)} all-to-all(f32[1,8,2,5136]{3,2,0,1:T(2,128)S(1)} %broadcast_select_fusion.2), channel_id=1, replica_groups=mesh['wave'=4,'lev'=8] {'lev'}, dimensions={1} | all-to-all | bytes 657408 | tf_op jit(solution)/shard_map/all_to_all | solution.py:112
  83.5 0.7 copy.32
  (51 shorter events, 5.8 us)
Async XLA Ops:
  0.0 5.3 %copy-start.10 = (s32[32]{0:T(128)S(1)}, s32[32]{0:T(128)}, u32[]{:S(2)}) copy-start(s32[32]{0:T(128)} %param.9) | copy-start | bytes 388
  0.0 7.9 %copy-start.11 = (s32[32]{0:T(128)S(1)}, s32[32]{0:T(128)}, u32[]{:S(2)}) copy-start(s32[32]{0:T(128)} %param.8) | copy-start | bytes 388
  0.0 44.6 %all-to-all-start = ((bf16[8,40,2,2,1280]{4,3,2,1,0:T(2,128)(2,1)}), bf16[8,40,2,2,1280]{4,3,2,1,0:T(2,128)(2,1)S(1)}, u32[]{:S(2)}, u32[]{:S(2)}) async-start(bf16[8,40,2,2,1280]{4,3,2,1,0:T(2,128)(2,1)} %bitcast.79), calls=%async_computation | async-start | bytes 6553600 | tf_op jit(solution)/shard_map/all_to_all | solution.py:67
  23.3 3.7 %copy-start.6 = (f32[5,5136]{1,0:T(8,128)S(1)}, f32[5,5136]{1,0:T(8,128)}, u32[]{:S(2)}) copy-start(f32[5,5136]{1,0:T(8,128)} %get-tuple-element.26) | copy-start | bytes 308164
  23.3 3.7 %copy-start.7 = (f32[5,5136]{1,0:T(8,128)S(1)}, f32[5,5136]{1,0:T(8,128)}, u32[]{:S(2)}) copy-start(f32[5,5136]{1,0:T(8,128)} %get-tuple-element.27) | copy-start | bytes 308164
  23.4 3.7 %copy-start.8 = (f32[4,5136]{1,0:T(4,128)S(1)}, f32[4,5136]{1,0:T(4,128)}, u32[]{:S(2)}) copy-start(f32[4,5136]{1,0:T(4,128)} %get-tuple-element.29) | copy-start | bytes 246532
  23.4 4.8 %copy-start.3 = (f32[8,5136]{1,0:T(8,128)S(1)}, f32[8,5136]{1,0:T(8,128)}, u32[]{:S(2)}) copy-start(f32[8,5136]{1,0:T(8,128)} %get-tuple-element.37) | copy-start | bytes 493060
  23.4 4.8 %copy-start.4 = (f32[8,5136]{1,0:T(8,128)S(1)}, f32[8,5136]{1,0:T(8,128)}, u32[]{:S(2)}) copy-start(f32[8,5136]{1,0:T(8,128)} %get-tuple-element.34) | copy-start | bytes 493060
  23.4 4.8 %copy-start.5 = (f32[8,5136]{1,0:T(8,128)S(1)}, f32[8,5136]{1,0:T(8,128)}, u32[]{:S(2)}) copy-start(f32[8,5136]{1,0:T(8,128)} %get-tuple-element.35) | copy-start | bytes 493060
  51.9 6.4 %copy-start.1 = (bf16[64,5136]{1,0:T(8,128)(2,1)S(1)}, bf16[64,5136]{1,0:T(8,128)(2,1)}, u32[]{:S(2)}) copy-start(bf16[64,5136]{1,0:T(8,128)(2,1)} %get-tuple-element.18) | copy-start | bytes 1972228
  52.5 7.1 %copy-start = (bf16[64,5136]{1,0:T(8,128)(2,1)S(1)}, bf16[64,5136]{1,0:T(8,128)(2,1)}, u32[]{:S(2)}) copy-start(bf16[64,5136]{1,0:T(8,128)(2,1)} %get-tuple-element.19) | copy-start | bytes 1972228
  53.7 11.6 %all-to-all-start.1 = ((bf16[32,2,640]{2,1,0:T(2,128)(2,1)}), bf16[32,2,640]{2,1,0:T(2,128)(2,1)S(1)}, u32[]{:S(2)}, u32[]{:S(2)}) async-start(bf16[32,2,640]{2,1,0:T(2,128)(2,1)} %reshape.472), calls=%async_computation.1 | async-start | bytes 163840 | tf_op jit(solution)/shard_map/all_to_all | solution.py:91
  61.0 5.2 %copy-start.9 = (s32[1280]{0:T(1024)S(1)}, s32[1280]{0:T(1024)}, u32[]{:S(2)}) copy-start(s32[1280]{0:T(1024)} %param.7) | copy-start | bytes 15364
  68.0 2.4 %copy-start.2 = (f32[20,5136]{1,0:T(8,128)S(1)}, f32[20,5136]{1,0:T(8,128)}, u32[]{:S(2)}) copy-start(f32[20,5136]{1,0:T(8,128)} %sub.33) | copy-start | bytes 1232644

commit v15 on v3

--- a/solution.py
+++ b/solution.py
@@ -94,14 +94,16 @@
     )
     banded = jnp.transpose(banded, (1, 2, 3, 0, 4)).reshape(2, fpg, rows_per_dev, -1)
     wave_idx = jnp.arange(waves, dtype=jnp.int32)
-    onehot = (slot_wave[:, None] == wave_idx[None, :]).astype(jnp.bfloat16)
-    coef = jnp.einsum("cfrs,sm->cfrm", banded, onehot, preferred_element_type=jnp.float32)
     first_row = (lax.axis_index("wave") * n_r + lax.axis_index("lev_r")) * rows_per_dev
     my_rows = lax.dynamic_slice_in_dim(band_rows, first_row, rows_per_dev)
     row_points = row_lons[my_rows]
     keep = 2 * wave_idx[None, :] < row_points[:, None]
-    factor = jnp.where(keep, jnp.where(wave_idx[None, :] == 0, 1.0, 2.0), 0.0).astype(jnp.float32)
-    coef = (coef * factor[None, None]).astype(jnp.bfloat16)
+    factor = jnp.where(keep, jnp.where(wave_idx[None, :] == 0, 2.0, 4.0), 0.0) / 2.0
+    onehot = jnp.where(
+        slot_wave[None, :, None] == wave_idx[None, None, :], factor[:, None, :], 0.0
+    ).astype(jnp.bfloat16)
+    coef = jnp.einsum("cfrs,rsm->cfrm", banded, onehot, preferred_element_type=jnp.float32)
+    coef = coef.astype(jnp.bfloat16)
     coef_rows = jnp.moveaxis(coef, 2, 0)
     if rows_per_dev == 1:
         grid = row_synthesis(coef_rows[0], row_points[0])[None]

time: 84.7 us -> 84 us (level)
  no operation moved by 1% of the time
where the time goes in v15:
time: 84 us; the launch traced here: 83.5 us
  other arithmetic  22.6 us (27%)
  waiting for transfers between devices  15.4 us (18%)
  local copies, waits for them, and re-layouts  12.9 us (15%)
  blocking collectives  10.9 us (13%)
  starting transfers between devices  9.31 us (11%)
  matrix products  8.15 us (10%)
  between operations  4.24 us (5%)
    all_to_all x1, waiting for transfers between devices, on_device(): lax.all_to_all(spec_v, ('lev_g', 'lev_r'), split_axis=0, concat_axis=0, t...  14.9 us
    all_to_all x1, blocking collectives, on_device(): lax.all_to_all(grid, 'lev_r', split_axis=1, concat_axis=0, tiled=True)  10.9 us
    cos x3, other arithmetic, trig_pair(): return (jnp.cos(theta), jnp.sin(theta))  9.06 us
    all_to_all x1, starting transfers between devices, on_device(): lax.all_to_all(spec_v, ('lev_g', 'lev_r'), split_axis=0, concat_axis=0, t...  5.3 us
    dot_general x1, matrix products, on_device(): jnp.einsum('lscfk,sjk->sclfj', gathered, leg2, preferred_element_type=jnp...  4.98 us
    all_to_all x1, starting transfers between devices, on_device(): lax.all_to_all(fourier, ('wave', 'lev_g', 'lev_r'), split_axis=0, concat_...  4 us
    select_n x1, other arithmetic, on_device(): jnp.where(even_mask, legendre, zeros)  3.67 us
    sin x1, other arithmetic, trig_pair(): return (jnp.cos(theta), jnp.sin(theta))  2.94 us
  transfers between devices with their start and end apart: 2, of which 2 were waited for; matrix products, arithmetic and copies ran while one was open for 33% of the time, Pallas kernels for 0%

profile of v15, /device:TPU:0, one launch (start us, length us, event | category | flops | bytes accessed | tf_op | source)
XLA Modules:
  0.0 83.5 jit_solution(3571429176018482174)
XLA Ops:
  0.0 5.3 %all-to-all-start = ((bf16[8,40,2,2,1280]{4,3,2,1,0:T(2,128)(2,1)}), bf16[8,40,2,2,1280]{4,3,2,1,0:T(2,128)(2,1)S(1)}, u32[]{:S(2)}, u32[]{:S(2)}) async-start(bf16[8,40,2,2,1280]{4,3,2,1,0:T(2,128)(2,1)} %bitcast.85), calls=%async_computation | async-start | bytes 6553600 | tf_op jit(solution)/shard_map/all_to_all | solution.py:67
  10.5 2.9 %fusion.60 = (f32[8,5136]{1,0:T(8,128)S(1)}, f32[8,5136]{1,0:T(8,128)}) fusion(f32[]{:T(128)S(6)} %convert_element_type.90, pred[]{:T(512)S(6)} %lt.114, s32[]{:T(128)S(6)} %select_n.150), kind=kLoop, calls=%fused_computation.82 | loop fusion | flops 451968 | bytes 328713 | tf_op jit(solution)/shard_map/sin | solution.py:18
  13.5 3.1 %fusion.63 = (f32[8,5136]{1,0:T(8,128)}, f32[8,5136]{1,0:T(8,128)}) fusion(f32[]{:T(128)S(6)} %convert_element_type.90, pred[]{:T(512)S(6)} %lt.114, s32[]{:T(128)S(6)} %select_n.150, s32[8]{0:T(128)S(1)} %iota_multiply_fusion.2), kind=kLoop, calls=%fused_computation.85 | loop fusion | flops 451968 | bytes 328745 | tf_op jit(solution)/shard_map/cos | solution.py:18
  16.5 3.0 %fusion.59 = (f32[5,5136]{1,0:T(8,128)}, f32[5,5136]{1,0:T(8,128)}) fusion(f32[]{:T(128)S(6)} %convert_element_type.90, pred[]{:T(512)S(6)} %lt.114, s32[]{:T(128)S(6)} %select_n.150, s32[5]{0:T(128)S(1)} %iota_multiply_fusion.1), kind=kLoop, calls=%fused_computation.81 | loop fusion | flops 282480 | bytes 205469 | tf_op jit(solution)/shard_map/cos | solution.py:18
  19.6 3.0 %fusion.65 = (f32[4,5136]{1,0:T(4,128)S(1)}, f32[4,5136]{1,0:T(4,128)}) fusion(f32[]{:T(128)S(6)} %convert_element_type.90, pred[]{:T(512)S(6)} %lt.114, s32[]{:T(128)S(6)} %select_n.150, s32[4]{0:T(128)S(1)} %iota_multiply_fusion), kind=kLoop, calls=%fused_computation.87 | loop fusion | flops 225984 | bytes 164377 | tf_op jit(solution)/shard_map/cos | solution.py:18
  22.5 0.8 dynamic-slice_subtract_fusion
  23.5 3.7 %broadcast_select_fusion.1 = (bf16[40,16,1280]{2,1,0:T(8,128)(2,1)}, bf16[40,16,1280]{2,1,0:T(8,128)(2,1)}) fusion(bf16[40,16,1280]{2,1,0:T(8,128)(2,1)} %param.6, pred[40,1280]{1,0:T(8,128)(4,1)S(1)} %get-tuple-element.32, pred[40,1280]{1,0:T(8,128)(4,1)S(1)} %get-tuple-element.33), kind=kLoop, calls=%fused_computation.20 | loop fusion | flops 1638400 | bytes 5017600 | tf_op jit(solution)/shard_map/jit(_where)/select_n | solution.py:77
  27.2 1.1 %multiply_subtract_fusion = (f32[5,4,5136]{2,1,0:T(4,128)}, f32[5,4,5136]{2,1,0:T(4,128)}) fusion(f32[4,5136]{1,0:T(4,128)S(1)} %copy-done.8, f32[5,5136]{1,0:T(8,128)S(1)} %copy-done.7, f32[4,5136]{1,0:T(4,128)S(1)} %get-tuple-element.30, f32[5,5136]{1,0:T(8,128)S(1)} %copy-done.6), kind=kLoop, calls=%fused_computation.32 | loop fusion | flops 616320 | bytes 1191552 | tf_op jit(solution)/shard_map/sub | solution.py:24
  28.3 1.4 %fusion.23 = (bf16[64,5136]{1,0:T(8,128)(2,1)}, bf16[64,5136]{1,0:T(8,128)(2,1)}) fusion(f32[8,5136]{1,0:T(8,128)S(1)} %get-tuple-element.36, f32[8,5136]{1,0:T(8,128)S(1)} %copy-done.5, f32[8,5136]{1,0:T(8,128)S(1)} %copy-done.3, f32[8,5136]{1,0:T(8,128)S(1)} %copy-done.4), kind=kLoop, calls=%fused_computation.28 | loop fusion | flops 2629632 | bytes 1972224 | tf_op jit(solution)/shard_map/convert_element_type | solution.py:36
  29.7 14.9 %all-to-all-done = bf16[8,40,2,2,1280]{4,3,2,1,0:T(2,128)(2,1)S(1)} async-done(((bf16[8,40,2,2,1280]{4,3,2,1,0:T(2,128)(2,1)}), bf16[8,40,2,2,1280]{4,3,2,1,0:T(2,128)(2,1)S(1)}, u32[]{:S(2)}, u32[]{:S(2)}) %all-to-all-start) | async-done | bytes 3276832 | tf_op jit(solution)/shard_map/all_to_all | solution.py:67
  44.6 5.0 %fusion.20 = f32[40,2,8,2,32]{4,2,3,1,0:T(8,128)} fusion(bf16[8,40,2,2,1280]{4,3,2,1,0:T(2,128)(2,1)S(1)} %all-to-all-done, bf16[40,16,1280]{2,1,0:T(8,128)(2,1)} %get-tuple-element.17, bf16[40,16,1280]{2,1,0:T(8,128)(2,1)} %get-tuple-element.16), kind=kOutput, calls=%fused_computation.27 | convolution fusion | flops 111411200 | bytes 6717440 | tf_op jit(solution)/shard_map/lscfk,sjk->sclfj/dot_general | solution.py:79
  49.6 1.4 %copy.17 = f32[40,2,8,2,32]{0,4,3,2,1:T(8,128)S(1)} copy(f32[40,2,8,2,32]{4,2,3,1,0:T(8,128)} %fusion.20) | data formatting | bytes 327680 | tf_op jit(solution)/shard_map/lscfk,sjk->sclfj/transpose | solution.py:79
  52.6 1.0 %reshape.512 = bf16[32,2,640]{2,1,0:T(2,128)(2,1)} reshape(bf16[32,1,2,16,40]{4,3,2,1,0:T(8,128)(2,1)S(1)} %bitcast.92) | data formatting | bytes 163840
  53.6 4.0 %all-to-all-start.1 = ((bf16[32,2,640]{2,1,0:T(2,128)(2,1)}), bf16[32,2,640]{2,1,0:T(2,128)(2,1)S(1)}, u32[]{:S(2)}, u32[]{:S(2)}) async-start(bf16[32,2,640]{2,1,0:T(2,128)(2,1)} %reshape.512), calls=%async_computation.1 | async-start | bytes 163840 | tf_op jit(solution)/shard_map/all_to_all | solution.py:92
  57.6 0.6 select_multiply_fusion
  58.2 1.3 %copy.21 = bf16[64,5136]{0,1:T(8,128)(2,1)S(1)} copy(bf16[64,5136]{1,0:T(8,128)(2,1)S(1)} %copy-done.1) | data formatting | bytes 1314816 | tf_op jit(solution)/shard_map/convert_element_type | solution.py:36
  59.6 1.3 %copy.22 = bf16[64,5136]{0,1:T(8,128)(2,1)S(1)} copy(bf16[64,5136]{1,0:T(8,128)(2,1)S(1)} %copy-done) | data formatting | bytes 1314816 | tf_op jit(solution)/shard_map/convert_element_type | solution.py:37
  60.9 1.2 %add.125 = f32[20,5136]{1,0:T(8,128)S(1)} reshape(f32[5,4,5136]{2,1,0:T(4,128)} %get-tuple-element.23) | data formatting | bytes 821760 | tf_op jit(solution)/shard_map/add | solution.py:25
  62.1 2.0 %sub.33 = f32[20,5136]{1,0:T(8,128)} reshape(f32[5,4,5136]{2,1,0:T(4,128)} %get-tuple-element.22) | data formatting | bytes 821760 | tf_op jit(solution)/shard_map/sub | solution.py:24
  66.1 0.7 fusion.14
  67.2 2.4 %fusion.17 = f32[2,16,20,5136]{3,2,1,0:T(8,128)S(1)} fusion(bf16[64,5136]{0,1:T(8,128)(2,1)S(1)} %copy.22, bf16[64,5136]{0,1:T(8,128)(2,1)S(1)} %copy.21, bf16[1,16,20,128]{3,2,1,0:T(8,128)(2,1)S(1)} %get-tuple-element.25, bf16[1,16,20,128]{3,2,1,0:T(8,128)(2,1)S(1)} %get-tuple-element.24), kind=kOutput, calls=%fused_computation.24 | convolution fusion | flops 844193792 | bytes 14626816 | tf_op jit(solution)/shard_map/dfab,bi->dfai/dot_general | solution.py:51
  69.7 1.8 %fusion.2 = f32[16,5136]{1,0:T(8,128)S(1)} fusion(f32[2,16,20,5136]{3,2,1,0:T(8,128)S(1)} %fusion.17, f32[20,5136]{1,0:T(8,128)S(1)} %add.125, f32[20,5136]{1,0:T(8,128)S(1)} %copy-done.2), kind=kLoop, calls=%fused_computation.5 | loop fusion | flops 6491904 | bytes 14298624 | tf_op jit(solution)/shard_map/reduce_sum | solution.py:52
  71.8 10.9 %all_to_all.19 = f32[1,8,2,5136]{3,2,0,1:T(2,128)S(1)} all-to-all(f32[1,8,2,5136]{3,2,0,1:T(2,128)S(1)} %broadcast_select_fusion.2), channel_id=1, replica_groups=mesh['wave'=4,'lev'=8] {'lev'}, dimensions={1} | all-to-all | bytes 657408 | tf_op jit(solution)/shard_map/all_to_all | solution.py:115
  82.8 0.7 copy.37
  (54 shorter events, 5.8 us)
Async XLA Ops:
  0.0 5.3 %copy-start.10 = (s32[32]{0:T(128)S(1)}, s32[32]{0:T(128)}, u32[]{:S(2)}) copy-start(s32[32]{0:T(128)} %param.9) | copy-start | bytes 388
  0.0 7.9 %copy-start.11 = (s32[32]{0:T(128)S(1)}, s32[32]{0:T(128)}, u32[]{:S(2)}) copy-start(s32[32]{0:T(128)} %param.8) | copy-start | bytes 388
  0.0 44.6 %all-to-all-start = ((bf16[8,40,2,2,1280]{4,3,2,1,0:T(2,128)(2,1)}), bf16[8,40,2,2,1280]{4,3,2,1,0:T(2,128)(2,1)S(1)}, u32[]{:S(2)}, u32[]{:S(2)}) async-start(bf16[8,40,2,2,1280]{4,3,2,1,0:T(2,128)(2,1)} %bitcast.85), calls=%async_computation | async-start | bytes 6553600 | tf_op jit(solution)/shard_map/all_to_all | solution.py:67
  23.4 3.7 %copy-start.6 = (f32[5,5136]{1,0:T(8,128)S(1)}, f32[5,5136]{1,0:T(8,128)}, u32[]{:S(2)}) copy-start(f32[5,5136]{1,0:T(8,128)} %get-tuple-element.28) | copy-start | bytes 308164
  23.4 3.7 %copy-start.7 = (f32[5,5136]{1,0:T(8,128)S(1)}, f32[5,5136]{1,0:T(8,128)}, u32[]{:S(2)}) copy-start(f32[5,5136]{1,0:T(8,128)} %get-tuple-element.29) | copy-start | bytes 308164
  23.5 3.7 %copy-start.8 = (f32[4,5136]{1,0:T(4,128)S(1)}, f32[4,5136]{1,0:T(4,128)}, u32[]{:S(2)}) copy-start(f32[4,5136]{1,0:T(4,128)} %get-tuple-element.31) | copy-start | bytes 246532
  23.5 4.8 %copy-start.3 = (f32[8,5136]{1,0:T(8,128)S(1)}, f32[8,5136]{1,0:T(8,128)}, u32[]{:S(2)}) copy-start(f32[8,5136]{1,0:T(8,128)} %get-tuple-element.37) | copy-start | bytes 493060
  23.5 4.8 %copy-start.4 = (f32[8,5136]{1,0:T(8,128)S(1)}, f32[8,5136]{1,0:T(8,128)}, u32[]{:S(2)}) copy-start(f32[8,5136]{1,0:T(8,128)} %get-tuple-element.34) | copy-start | bytes 493060
  23.5 4.8 %copy-start.5 = (f32[8,5136]{1,0:T(8,128)S(1)}, f32[8,5136]{1,0:T(8,128)}, u32[]{:S(2)}) copy-start(f32[8,5136]{1,0:T(8,128)} %get-tuple-element.35) | copy-start | bytes 493060
  51.8 6.4 %copy-start.1 = (bf16[64,5136]{1,0:T(8,128)(2,1)S(1)}, bf16[64,5136]{1,0:T(8,128)(2,1)}, u32[]{:S(2)}) copy-start(bf16[64,5136]{1,0:T(8,128)(2,1)} %get-tuple-element.18) | copy-start | bytes 1972228
  52.4 7.1 %copy-start = (bf16[64,5136]{1,0:T(8,128)(2,1)S(1)}, bf16[64,5136]{1,0:T(8,128)(2,1)}, u32[]{:S(2)}) copy-start(bf16[64,5136]{1,0:T(8,128)(2,1)} %get-tuple-element.19) | copy-start | bytes 1972228
  53.6 11.6 %all-to-all-start.1 = ((bf16[32,2,640]{2,1,0:T(2,128)(2,1)}), bf16[32,2,640]{2,1,0:T(2,128)(2,1)S(1)}, u32[]{:S(2)}, u32[]{:S(2)}) async-start(bf16[32,2,640]{2,1,0:T(2,128)(2,1)} %reshape.512), calls=%async_computation.1 | async-start | bytes 163840 | tf_op jit(solution)/shard_map/all_to_all | solution.py:92
  60.9 5.2 %copy-start.9 = (s32[1280]{0:T(1024)S(1)}, s32[1280]{0:T(1024)}, u32[]{:S(2)}) copy-start(s32[1280]{0:T(1024)} %param.7) | copy-start | bytes 15364
  67.2 2.4 %copy-start.2 = (f32[20,5136]{1,0:T(8,128)S(1)}, f32[20,5136]{1,0:T(8,128)}, u32[]{:S(2)}) copy-start(f32[20,5136]{1,0:T(8,128)} %sub.33) | copy-start | bytes 1232644

commit v16 on v15

--- a/solution.py
+++ b/solution.py
@@ -77,13 +77,17 @@
         [jnp.where(even_mask, legendre, zeros), jnp.where(odd_mask, legendre, zeros)], 1
     )
     sums = jnp.einsum("lscfk,sjk->sclfj", gathered, leg2, preferred_element_type=jnp.float32)
-    sums = sums.reshape(per_dev, 2, fields, 2, nlath)
+    sums = sums.reshape(per_dev, 2, fields, 2 * nlath)
     north = band_rows < nlath
     lat_idx = jnp.where(north, band_rows, band_rows - nlath)
-    parity_sign = jnp.where(north, 1.0, -1.0).astype(jnp.float32)
-    fourier = (sums[:, :, :, 0][..., lat_idx] + parity_sign * sums[:, :, :, 1][..., lat_idx]).astype(
-        jnp.bfloat16
+    j2 = jnp.arange(2 * nlath, dtype=jnp.int32)[:, None]
+    sel = jnp.where(j2 == lat_idx[None, :], 1.0, 0.0) + jnp.where(
+        j2 == nlath + lat_idx[None, :], jnp.where(north, 1.0, -1.0)[None, :], 0.0
     )
+    fourier = jnp.einsum(
+        "scfj,jp->scfp", sums, sel, precision=lax.Precision.HIGHEST,
+        preferred_element_type=jnp.float32,
+    ).astype(jnp.bfloat16)
     rows = band_rows.shape[0]
     fpg = fields // n_g
     fourier = fourier.reshape(per_dev, 2, n_g, fpg, n_wave, n_r, rows_per_dev)

time: 84 us -> 83.3 us (level)
  local copies, waits for them, and re-layouts: 12.9 us -> 11.6 us
    gather x2 -> x0, local copies, waits for them, and re-layouts: 1.16 us -> none  [the longest x1 0.58 us: on_device(): sums[:, :, :, 0][..., lat_idx]]
    unnamed x29 -> x27, local copies, waits for them, and re-layouts: 2.34 us -> 2.18 us
where the time goes in v16:
time: 83.3 us; the launch traced here: 82.8 us
  other arithmetic  22.5 us (27%)
  waiting for transfers between devices  15.5 us (19%)
  local copies, waits for them, and re-layouts  11.6 us (14%)
  blocking collectives  10.9 us (13%)
  starting transfers between devices  9.3 us (11%)
  matrix products  8.76 us (11%)
  between operations  4.15 us (5%)
    all_to_all x1, waiting for transfers between devices, on_device(): lax.all_to_all(spec_v, ('lev_g', 'lev_r'), split_axis=0, concat_axis=0, t...  15 us
    all_to_all x1, blocking collectives, on_device(): lax.all_to_all(grid, 'lev_r', split_axis=1, concat_axis=0, tiled=True)  10.9 us
    cos x3, other arithmetic, trig_pair(): return (jnp.cos(theta), jnp.sin(theta))  9.06 us
    all_to_all x1, starting transfers between devices, on_device(): lax.all_to_all(spec_v, ('lev_g', 'lev_r'), split_axis=0, concat_axis=0, t...  5.3 us
    dot_general x1, matrix products, on_device(): jnp.einsum('lscfk,sjk->sclfj', gathered, leg2, preferred_element_type=jnp...  4.99 us
    all_to_all x1, starting transfers between devices, on_device(): lax.all_to_all(fourier, ('wave', 'lev_g', 'lev_r'), split_axis=0, concat_...  4 us
    select_n x1, other arithmetic, on_device(): jnp.where(even_mask, legendre, zeros)  3.64 us
    sin x1, other arithmetic, trig_pair(): return (jnp.cos(theta), jnp.sin(theta))  2.94 us
  transfers between devices with their start and end apart: 2, of which 2 were waited for; matrix products, arithmetic and copies ran while one was open for 33% of the time, Pallas kernels for 0%

profile of v16, /device:TPU:0, one launch (start us, length us, event | category | flops | bytes accessed | tf_op | source)
XLA Modules:
  0.0 82.8 jit_solution(6043936887507259313)
XLA Ops:
  0.0 5.3 %all-to-all-start = ((bf16[8,40,2,2,1280]{4,3,2,1,0:T(2,128)(2,1)}), bf16[8,40,2,2,1280]{4,3,2,1,0:T(2,128)(2,1)S(1)}, u32[]{:S(2)}, u32[]{:S(2)}) async-start(bf16[8,40,2,2,1280]{4,3,2,1,0:T(2,128)(2,1)} %bitcast.81), calls=%async_computation | async-start | bytes 6553600 | tf_op jit(solution)/shard_map/all_to_all | solution.py:67
  10.4 2.9 %fusion.61 = (f32[8,5136]{1,0:T(8,128)S(1)}, f32[8,5136]{1,0:T(8,128)}) fusion(f32[]{:T(128)S(6)} %convert_element_type.83, pred[]{:T(512)S(6)} %lt.109, s32[]{:T(128)S(6)} %select_n.155), kind=kLoop, calls=%fused_computation.79 | loop fusion | flops 451968 | bytes 328713 | tf_op jit(solution)/shard_map/sin | solution.py:18
  13.4 3.1 %fusion.64 = (f32[8,5136]{1,0:T(8,128)}, f32[8,5136]{1,0:T(8,128)}) fusion(f32[]{:T(128)S(6)} %convert_element_type.83, pred[]{:T(512)S(6)} %lt.109, s32[]{:T(128)S(6)} %select_n.155, s32[8]{0:T(128)S(1)} %iota_multiply_fusion.2), kind=kLoop, calls=%fused_computation.82 | loop fusion | flops 451968 | bytes 328745 | tf_op jit(solution)/shard_map/cos | solution.py:18
  16.4 3.0 %fusion.60 = (f32[5,5136]{1,0:T(8,128)}, f32[5,5136]{1,0:T(8,128)}) fusion(f32[]{:T(128)S(6)} %convert_element_type.83, pred[]{:T(512)S(6)} %lt.109, s32[]{:T(128)S(6)} %select_n.155, s32[5]{0:T(128)S(1)} %iota_multiply_fusion.1), kind=kLoop, calls=%fused_computation.78 | loop fusion | flops 282480 | bytes 205469 | tf_op jit(solution)/shard_map/cos | solution.py:18
  19.5 3.0 %fusion.66 = (f32[4,5136]{1,0:T(4,128)S(1)}, f32[4,5136]{1,0:T(4,128)}) fusion(f32[]{:T(128)S(6)} %convert_element_type.83, pred[]{:T(512)S(6)} %lt.109, s32[]{:T(128)S(6)} %select_n.155, s32[4]{0:T(128)S(1)} %iota_multiply_fusion), kind=kLoop, calls=%fused_computation.84 | loop fusion | flops 225984 | bytes 164377 | tf_op jit(solution)/shard_map/cos | solution.py:18
  22.4 0.8 dynamic-slice_subtract_fusion
  23.4 3.6 %broadcast_select_fusion.1 = (bf16[40,16,1280]{2,1,0:T(8,128)(2,1)}, bf16[40,16,1280]{2,1,0:T(8,128)(2,1)}) fusion(bf16[40,16,1280]{2,1,0:T(8,128)(2,1)} %param.6, pred[40,1280]{1,0:T(8,128)(4,1)S(1)} %get-tuple-element.32, pred[40,1280]{1,0:T(8,128)(4,1)S(1)} %get-tuple-element.33), kind=kLoop, calls=%fused_computation.18 | loop fusion | flops 1638400 | bytes 5017600 | tf_op jit(solution)/shard_map/jit(_where)/select_n | solution.py:77
  27.1 1.1 %multiply_subtract_fusion = (f32[5,4,5136]{2,1,0:T(4,128)}, f32[5,4,5136]{2,1,0:T(4,128)}) fusion(f32[4,5136]{1,0:T(4,128)S(1)} %copy-done.8, f32[5,5136]{1,0:T(8,128)S(1)} %copy-done.7, f32[4,5136]{1,0:T(4,128)S(1)} %get-tuple-element.28, f32[5,5136]{1,0:T(8,128)S(1)} %copy-done.6), kind=kLoop, calls=%fused_computation.31 | loop fusion | flops 616320 | bytes 1191552 | tf_op jit(solution)/shard_map/sub | solution.py:24
  28.2 1.4 %fusion.24 = (bf16[64,5136]{1,0:T(8,128)(2,1)}, bf16[64,5136]{1,0:T(8,128)(2,1)}) fusion(f32[8,5136]{1,0:T(8,128)S(1)} %get-tuple-element.36, f32[8,5136]{1,0:T(8,128)S(1)} %copy-done.5, f32[8,5136]{1,0:T(8,128)S(1)} %copy-done.3, f32[8,5136]{1,0:T(8,128)S(1)} %copy-done.4), kind=kLoop, calls=%fused_computation.28 | loop fusion | flops 2629632 | bytes 1972224 | tf_op jit(solution)/shard_map/convert_element_type | solution.py:36
  29.6 15.0 %all-to-all-done = bf16[8,40,2,2,1280]{4,3,2,1,0:T(2,128)(2,1)S(1)} async-done(((bf16[8,40,2,2,1280]{4,3,2,1,0:T(2,128)(2,1)}), bf16[8,40,2,2,1280]{4,3,2,1,0:T(2,128)(2,1)S(1)}, u32[]{:S(2)}, u32[]{:S(2)}) %all-to-all-start) | async-done | bytes 3276832 | tf_op jit(solution)/shard_map/all_to_all | solution.py:67
  44.6 5.0 %fusion.20 = f32[40,2,8,2,32]{4,2,3,1,0:T(8,128)} fusion(bf16[8,40,2,2,1280]{4,3,2,1,0:T(2,128)(2,1)S(1)} %all-to-all-done, bf16[40,16,1280]{2,1,0:T(8,128)(2,1)} %get-tuple-element.17, bf16[40,16,1280]{2,1,0:T(8,128)(2,1)} %get-tuple-element.16), kind=kOutput, calls=%fused_computation.25 | convolution fusion | flops 111411200 | bytes 6717440 | tf_op jit(solution)/shard_map/lscfk,sjk->sclfj/dot_general | solution.py:79
  49.6 1.5 %copy.14 = f32[40,2,8,2,32]{0,4,3,2,1:T(8,128)S(1)} copy(f32[40,2,8,2,32]{4,2,3,1,0:T(8,128)} %fusion.20) | data formatting | bytes 327680 | tf_op jit(solution)/shard_map/lscfk,sjk->sclfj/transpose | solution.py:79
  51.9 1.0 %reshape.476 = bf16[32,2,640]{2,1,0:T(2,128)(2,1)} reshape(bf16[32,1,2,16,40]{4,3,2,1,0:T(8,128)(2,1)S(1)} %bitcast.84) | data formatting | bytes 163840
  52.9 4.0 %all-to-all-start.1 = ((bf16[32,2,640]{2,1,0:T(2,128)(2,1)}), bf16[32,2,640]{2,1,0:T(2,128)(2,1)S(1)}, u32[]{:S(2)}, u32[]{:S(2)}) async-start(bf16[32,2,640]{2,1,0:T(2,128)(2,1)} %reshape.476), calls=%async_computation.1 | async-start | bytes 163840 | tf_op jit(solution)/shard_map/all_to_all | solution.py:96
  56.9 0.6 select_multiply_fusion
  57.5 1.3 %copy.17 = bf16[64,5136]{0,1:T(8,128)(2,1)S(1)} copy(bf16[64,5136]{1,0:T(8,128)(2,1)S(1)} %copy-done.1) | data formatting | bytes 1314816 | tf_op jit(solution)/shard_map/convert_element_type | solution.py:36
  58.9 1.3 %copy.18 = bf16[64,5136]{0,1:T(8,128)(2,1)S(1)} copy(bf16[64,5136]{1,0:T(8,128)(2,1)S(1)} %copy-done) | data formatting | bytes 1314816 | tf_op jit(solution)/shard_map/convert_element_type | solution.py:37
  60.2 1.2 %add.119 = f32[20,5136]{1,0:T(8,128)S(1)} reshape(f32[5,4,5136]{2,1,0:T(4,128)} %get-tuple-element.21) | data formatting | bytes 821760 | tf_op jit(solution)/shard_map/add | solution.py:25
  61.3 2.0 %sub.33 = f32[20,5136]{1,0:T(8,128)} reshape(f32[5,4,5136]{2,1,0:T(4,128)} %get-tuple-element.20) | data formatting | bytes 821760 | tf_op jit(solution)/shard_map/sub | solution.py:24
  65.4 0.7 fusion.14
  66.5 2.4 %fusion.17 = f32[2,16,20,5136]{3,2,1,0:T(8,128)S(1)} fusion(bf16[64,5136]{0,1:T(8,128)(2,1)S(1)} %copy.18, bf16[64,5136]{0,1:T(8,128)(2,1)S(1)} %copy.17, bf16[1,16,20,128]{3,2,1,0:T(8,128)(2,1)S(1)} %get-tuple-element.23, bf16[1,16,20,128]{3,2,1,0:T(8,128)(2,1)S(1)} %get-tuple-element.22), kind=kOutput, calls=%fused_computation.22 | convolution fusion | flops 844193792 | bytes 14626816 | tf_op jit(solution)/shard_map/dfab,bi->dfai/dot_general | solution.py:51
  69.0 1.8 %fusion.2 = f32[16,5136]{1,0:T(8,128)S(1)} fusion(f32[2,16,20,5136]{3,2,1,0:T(8,128)S(1)} %fusion.17, f32[20,5136]{1,0:T(8,128)S(1)} %add.119, f32[20,5136]{1,0:T(8,128)S(1)} %copy-done.2), kind=kLoop, calls=%fused_computation.3 | loop fusion | flops 6491904 | bytes 14298624 | tf_op jit(solution)/shard_map/reduce_sum | solution.py:52
  71.1 10.9 %all_to_all.19 = f32[1,8,2,5136]{3,2,0,1:T(2,128)S(1)} all-to-all(f32[1,8,2,5136]{3,2,0,1:T(2,128)S(1)} %broadcast_select_fusion.2), channel_id=1, replica_groups=mesh['wave'=4,'lev'=8] {'lev'}, dimensions={1} | all-to-all | bytes 657408 | tf_op jit(solution)/shard_map/all_to_all | solution.py:119
  82.1 0.7 copy.28
  (48 shorter events, 4.9 us)
Async XLA Ops:
  0.0 5.3 %copy-start.11 = (s32[32]{0:T(128)S(1)}, s32[32]{0:T(128)}, u32[]{:S(2)}) copy-start(s32[32]{0:T(128)} %param.9) | copy-start | bytes 388
  0.0 7.9 %copy-start.10 = (s32[32]{0:T(128)S(1)}, s32[32]{0:T(128)}, u32[]{:S(2)}) copy-start(s32[32]{0:T(128)} %param.8) | copy-start | bytes 388
  0.0 44.6 %all-to-all-start = ((bf16[8,40,2,2,1280]{4,3,2,1,0:T(2,128)(2,1)}), bf16[8,40,2,2,1280]{4,3,2,1,0:T(2,128)(2,1)S(1)}, u32[]{:S(2)}, u32[]{:S(2)}) async-start(bf16[8,40,2,2,1280]{4,3,2,1,0:T(2,128)(2,1)} %bitcast.81), calls=%async_computation | async-start | bytes 6553600 | tf_op jit(solution)/shard_map/all_to_all | solution.py:67
  22.4 4.6 %copy-start.6 = (f32[5,5136]{1,0:T(8,128)S(1)}, f32[5,5136]{1,0:T(8,128)}, u32[]{:S(2)}) copy-start(f32[5,5136]{1,0:T(8,128)} %get-tuple-element.26) | copy-start | bytes 308164
  22.4 4.6 %copy-start.7 = (f32[5,5136]{1,0:T(8,128)S(1)}, f32[5,5136]{1,0:T(8,128)}, u32[]{:S(2)}) copy-start(f32[5,5136]{1,0:T(8,128)} %get-tuple-element.27) | copy-start | bytes 308164
  22.4 4.6 %copy-start.8 = (f32[4,5136]{1,0:T(4,128)S(1)}, f32[4,5136]{1,0:T(4,128)}, u32[]{:S(2)}) copy-start(f32[4,5136]{1,0:T(4,128)} %get-tuple-element.29) | copy-start | bytes 246532
  23.4 4.8 %copy-start.3 = (f32[8,5136]{1,0:T(8,128)S(1)}, f32[8,5136]{1,0:T(8,128)}, u32[]{:S(2)}) copy-start(f32[8,5136]{1,0:T(8,128)} %get-tuple-element.37) | copy-start | bytes 493060
  23.4 4.8 %copy-start.4 = (f32[8,5136]{1,0:T(8,128)S(1)}, f32[8,5136]{1,0:T(8,128)}, u32[]{:S(2)}) copy-start(f32[8,5136]{1,0:T(8,128)} %get-tuple-element.34) | copy-start | bytes 493060
  23.4 4.8 %copy-start.5 = (f32[8,5136]{1,0:T(8,128)S(1)}, f32[8,5136]{1,0:T(8,128)}, u32[]{:S(2)}) copy-start(f32[8,5136]{1,0:T(8,128)} %get-tuple-element.35) | copy-start | bytes 493060
  49.6 7.9 %copy-start.1 = (bf16[64,5136]{1,0:T(8,128)(2,1)S(1)}, bf16[64,5136]{1,0:T(8,128)(2,1)}, u32[]{:S(2)}) copy-start(bf16[64,5136]{1,0:T(8,128)(2,1)} %get-tuple-element.18) | copy-start | bytes 1972228
  49.6 9.3 %copy-start = (bf16[64,5136]{1,0:T(8,128)(2,1)S(1)}, bf16[64,5136]{1,0:T(8,128)(2,1)}, u32[]{:S(2)}) copy-start(bf16[64,5136]{1,0:T(8,128)(2,1)} %get-tuple-element.19) | copy-start | bytes 1972228
  52.9 11.6 %all-to-all-start.1 = ((bf16[32,2,640]{2,1,0:T(2,128)(2,1)}), bf16[32,2,640]{2,1,0:T(2,128)(2,1)S(1)}, u32[]{:S(2)}, u32[]{:S(2)}) async-start(bf16[32,2,640]{2,1,0:T(2,128)(2,1)} %reshape.476), calls=%async_computation.1 | async-start | bytes 163840 | tf_op jit(solution)/shard_map/all_to_all | solution.py:96
  58.9 6.5 %copy-start.9 = (s32[1280]{0:T(1024)S(1)}, s32[1280]{0:T(1024)}, u32[]{:S(2)}) copy-start(s32[1280]{0:T(1024)} %param.7) | copy-start | bytes 15364
  66.5 2.4 %copy-start.2 = (f32[20,5136]{1,0:T(8,128)S(1)}, f32[20,5136]{1,0:T(8,128)}, u32[]{:S(2)}) copy-start(f32[20,5136]{1,0:T(8,128)} %sub.33) | copy-start | bytes 1232644

commit v17 on v16

--- a/solution.py
+++ b/solution.py
@@ -76,18 +76,17 @@
     leg2 = jnp.concatenate(
         [jnp.where(even_mask, legendre, zeros), jnp.where(odd_mask, legendre, zeros)], 1
     )
-    sums = jnp.einsum("lscfk,sjk->sclfj", gathered, leg2, preferred_element_type=jnp.float32)
-    sums = sums.reshape(per_dev, 2, fields, 2 * nlath)
     north = band_rows < nlath
     lat_idx = jnp.where(north, band_rows, band_rows - nlath)
     j2 = jnp.arange(2 * nlath, dtype=jnp.int32)[:, None]
     sel = jnp.where(j2 == lat_idx[None, :], 1.0, 0.0) + jnp.where(
         j2 == nlath + lat_idx[None, :], jnp.where(north, 1.0, -1.0)[None, :], 0.0
     )
-    fourier = jnp.einsum(
-        "scfj,jp->scfp", sums, sel, precision=lax.Precision.HIGHEST,
-        preferred_element_type=jnp.float32,
+    leg_rows = jnp.einsum(
+        "sjk,jp->spk", leg2, sel.astype(jnp.bfloat16), preferred_element_type=jnp.float32
     ).astype(jnp.bfloat16)
+    sums = jnp.einsum("lscfk,spk->sclfp", gathered, leg_rows, preferred_element_type=jnp.float32)
+    fourier = sums.reshape(per_dev, 2, fields, band_rows.shape[0]).astype(jnp.bfloat16)
     rows = band_rows.shape[0]
     fpg = fields // n_g
     fourier = fourier.reshape(per_dev, 2, n_g, fpg, n_wave, n_r, rows_per_dev)

time: 83.3 us -> 84.2 us (1.011)
    transpose x2 -> x0, local copies, waits for them, and re-layouts: 1.65 us -> none  [the longest x1 1.54 us: on_device(): jnp.einsum('lscfk,sjk->sclfj', gathered, leg2, preferred_element_type=jnp...]
    convert_element_type x0 -> x1, local copies, waits for them, and re-layouts: none -> 1.4 us  [on_device(): sums.reshape(per_dev, 2, fields, band_rows.shape[0]).astype(jnp.bfloat16)]
    convert_element_type x1, local copies, waits for them, and re-layouts: 1.31 us -> 2.17 us  [row_synthesis(): cosb = cos_t.astype(jnp.bfloat16)]
    dot_general x2 -> x1, matrix products: 5.6 us -> 5.87 us  [on_device(): jnp.einsum('lscfk,spk->sclfp', gathered, leg_rows, preferred_element_type...]
    unnamed x27 -> x29, local copies, waits for them, and re-layouts: 2.18 us -> 2.17 us
  transfers between devices with their start and end apart: 2 -> 2, of which waited for: 2 -> 1; matrix products, arithmetic and copies ran while one was open for 33% -> 33% of each run, Pallas kernels for 0% -> 0%
where the time goes in v17:
time: 84.2 us; the launch traced here: 83.6 us
  other arithmetic  22.2 us (26%)
  waiting for transfers between devices  15.4 us (18%)
  local copies, waits for them, and re-layouts  12.3 us (15%)
  blocking collectives  11.5 us (14%)
  starting transfers between devices  9.32 us (11%)
  matrix products  9.04 us (11%)
  between operations  3.96 us (5%)
    all_to_all x1, waiting for transfers between devices, on_device(): lax.all_to_all(spec_v, ('lev_g', 'lev_r'), split_axis=0, concat_axis=0, t...  15.4 us
    all_to_all x1, blocking collectives, on_device(): lax.all_to_all(grid, 'lev_r', split_axis=1, concat_axis=0, tiled=True)  11.5 us
    cos x3, other arithmetic, trig_pair(): return (jnp.cos(theta), jnp.sin(theta))  9.05 us
    dot_general x1, matrix products, on_device(): jnp.einsum('lscfk,spk->sclfp', gathered, leg_rows, preferred_element_type...  5.87 us
    all_to_all x1, starting transfers between devices, on_device(): lax.all_to_all(spec_v, ('lev_g', 'lev_r'), split_axis=0, concat_axis=0, t...  5.32 us
    all_to_all x1, starting transfers between devices, on_device(): lax.all_to_all(fourier, ('wave', 'lev_g', 'lev_r'), split_axis=0, concat_...  4 us
    select_n x1, other arithmetic, on_device(): jnp.where(even_mask, legendre, zeros)  3.64 us
    sin x1, other arithmetic, trig_pair(): return (jnp.cos(theta), jnp.sin(theta))  2.94 us
  transfers between devices with their start and end apart: 2, of which 1 were waited for; matrix products, arithmetic and copies ran while one was open for 33% of the time, Pallas kernels for 0%

profile of v17, /device:TPU:0, one launch (start us, length us, event | category | flops | bytes accessed | tf_op | source)
XLA Modules:
  0.0 83.6 jit_solution(3995987548690318448)
XLA Ops:
  0.0 5.3 %all-to-all-start = ((bf16[8,40,2,2,1280]{4,3,2,1,0:T(2,128)(2,1)}), bf16[8,40,2,2,1280]{4,3,2,1,0:T(2,128)(2,1)S(1)}, u32[]{:S(2)}, u32[]{:S(2)}) async-start(bf16[8,40,2,2,1280]{4,3,2,1,0:T(2,128)(2,1)} %bitcast.81), calls=%async_computation | async-start | bytes 6553600 | tf_op jit(solution)/shard_map/all_to_all | solution.py:67
  5.9 0.6 dynamic_slice.6
  8.4 0.6 dynamic-slice.2
  10.8 2.9 %fusion.67 = (f32[8,5136]{1,0:T(8,128)S(1)}, f32[8,5136]{1,0:T(8,128)}) fusion(f32[]{:T(128)S(6)} %convert_element_type.110, pred[]{:T(512)S(6)} %lt.109, s32[]{:T(128)S(6)} %select_n.155), kind=kLoop, calls=%fused_computation.80 | loop fusion | flops 451968 | bytes 328713 | tf_op jit(solution)/shard_map/sin | solution.py:18
  13.7 3.1 %fusion.70 = (f32[8,5136]{1,0:T(8,128)}, f32[8,5136]{1,0:T(8,128)}) fusion(f32[]{:T(128)S(6)} %convert_element_type.110, pred[]{:T(512)S(6)} %lt.109, s32[]{:T(128)S(6)} %select_n.155, s32[8]{0:T(128)S(1)} %iota_multiply_fusion.2), kind=kLoop, calls=%fused_computation.83 | loop fusion | flops 451968 | bytes 328745 | tf_op jit(solution)/shard_map/cos | solution.py:18
  16.8 3.0 %fusion.66 = (f32[5,5136]{1,0:T(8,128)}, f32[5,5136]{1,0:T(8,128)}) fusion(f32[]{:T(128)S(6)} %convert_element_type.110, pred[]{:T(512)S(6)} %lt.109, s32[]{:T(128)S(6)} %select_n.155, s32[5]{0:T(128)S(1)} %iota_multiply_fusion.1), kind=kLoop, calls=%fused_computation.79 | loop fusion | flops 282480 | bytes 205469 | tf_op jit(solution)/shard_map/cos | solution.py:18
  19.8 3.0 %fusion.72 = (f32[4,5136]{1,0:T(4,128)S(1)}, f32[4,5136]{1,0:T(4,128)}) fusion(f32[]{:T(128)S(6)} %convert_element_type.110, pred[]{:T(512)S(6)} %lt.109, s32[]{:T(128)S(6)} %select_n.155, s32[4]{0:T(128)S(1)} %iota_multiply_fusion), kind=kLoop, calls=%fused_computation.85 | loop fusion | flops 225984 | bytes 164377 | tf_op jit(solution)/shard_map/cos | solution.py:18
  23.0 3.6 %broadcast_select_fusion.1 = (bf16[40,16,1280]{2,1,0:T(8,128)(2,1)}, bf16[40,16,1280]{2,1,0:T(8,128)(2,1)}) fusion(bf16[40,16,1280]{2,1,0:T(8,128)(2,1)} %param.6, pred[40,1280]{1,0:T(8,128)(4,1)S(1)} %get-tuple-element.32, pred[40,1280]{1,0:T(8,128)(4,1)S(1)} %get-tuple-element.33), kind=kLoop, calls=%fused_computation.20 | loop fusion | flops 1638400 | bytes 5017600 | tf_op jit(solution)/shard_map/jit(_where)/select_n | solution.py:77
  26.7 1.1 %multiply_subtract_fusion = (f32[5,4,5136]{2,1,0:T(4,128)}, f32[5,4,5136]{2,1,0:T(4,128)}) fusion(f32[4,5136]{1,0:T(4,128)S(1)} %copy-done.7, f32[5,5136]{1,0:T(8,128)S(1)} %copy-done.6, f32[4,5136]{1,0:T(4,128)S(1)} %get-tuple-element.28, f32[5,5136]{1,0:T(8,128)S(1)} %copy-done.5), kind=kLoop, calls=%fused_computation.32 | loop fusion | flops 616320 | bytes 1191552 | tf_op jit(solution)/shard_map/sub | solution.py:24
  27.8 1.4 %fusion.30 = (bf16[64,5136]{1,0:T(8,128)(2,1)}, bf16[64,5136]{1,0:T(8,128)(2,1)}) fusion(f32[8,5136]{1,0:T(8,128)S(1)} %get-tuple-element.36, f32[8,5136]{1,0:T(8,128)S(1)} %copy-done.4, f32[8,5136]{1,0:T(8,128)S(1)} %copy-done.2, f32[8,5136]{1,0:T(8,128)S(1)} %copy-done.3), kind=kLoop, calls=%fused_computation.29 | loop fusion | flops 2629632 | bytes 1972224 | tf_op jit(solution)/shard_map/convert_element_type | solution.py:36
  29.2 15.4 %all-to-all-done = bf16[8,40,2,2,1280]{4,3,2,1,0:T(2,128)(2,1)S(1)} async-done(((bf16[8,40,2,2,1280]{4,3,2,1,0:T(2,128)(2,1)}), bf16[8,40,2,2,1280]{4,3,2,1,0:T(2,128)(2,1)S(1)}, u32[]{:S(2)}, u32[]{:S(2)}) %all-to-all-start) | async-done | bytes 3276832 | tf_op jit(solution)/shard_map/all_to_all | solution.py:67
  44.6 5.9 %fusion.25 = bf16[40,2,8,2,32]{4,2,3,1,0:T(8,128)(2,1)} fusion(bf16[8,40,2,2,1280]{4,3,2,1,0:T(2,128)(2,1)S(1)} %all-to-all-done, bf16[40,16,1280]{2,1,0:T(8,128)(2,1)} %get-tuple-element.17, bf16[40,16,1280]{2,1,0:T(8,128)(2,1)} %get-tuple-element.16, f32[32]{0:T(128)S(1)} %compare_select_fusion, s32[32]{0:T(128)S(1)} %copy-done.12, s32[32]{0:T(128)S(1)} %copy-done.11), kind=kOutput, calls=%fused_computation.28 | convolution fusion | flops 217954304 | bytes 6635904 | tf_op jit(solution)/shard_map/lscfk,spk->sclfp/dot_general | solution.py:88
  50.5 1.4 %copy.14 = bf16[40,2,8,2,32]{0,4,3,2,1:T(8,128)(2,1)S(1)} copy(bf16[40,2,8,2,32]{4,2,3,1,0:T(8,128)(2,1)} %fusion.25) | data formatting | bytes 163840 | tf_op jit(solution)/shard_map/convert_element_type | solution.py:89
  52.0 1.0 %reshape.481 = bf16[32,2,640]{2,1,0:T(2,128)(2,1)} reshape(bf16[32,1,2,16,40]{4,3,2,1,0:T(8,128)(2,1)S(1)} %bitcast.84) | data formatting | bytes 163840
  53.0 4.0 %all-to-all-start.1 = ((bf16[32,2,640]{2,1,0:T(2,128)(2,1)}), bf16[32,2,640]{2,1,0:T(2,128)(2,1)S(1)}, u32[]{:S(2)}, u32[]{:S(2)}) async-start(bf16[32,2,640]{2,1,0:T(2,128)(2,1)} %reshape.481), calls=%async_computation.1 | async-start | bytes 163840 | tf_op jit(solution)/shard_map/all_to_all | solution.py:95
  57.6 2.2 %copy.17 = bf16[64,5136]{0,1:T(8,128)(2,1)S(1)} copy(bf16[64,5136]{1,0:T(8,128)(2,1)} %get-tuple-element.18) | data formatting | bytes 1314816 | tf_op jit(solution)/shard_map/convert_element_type | solution.py:36
  59.8 1.3 %copy.18 = bf16[64,5136]{0,1:T(8,128)(2,1)S(1)} copy(bf16[64,5136]{1,0:T(8,128)(2,1)S(1)} %copy-done) | data formatting | bytes 1314816 | tf_op jit(solution)/shard_map/convert_element_type | solution.py:37
  61.1 1.2 %add.119 = f32[20,5136]{1,0:T(8,128)S(1)} reshape(f32[5,4,5136]{2,1,0:T(4,128)} %get-tuple-element.21) | data formatting | bytes 821760 | tf_op jit(solution)/shard_map/add | solution.py:25
  62.2 1.9 %sub.33 = f32[20,5136]{1,0:T(8,128)} reshape(f32[5,4,5136]{2,1,0:T(4,128)} %get-tuple-element.20) | data formatting | bytes 821760 | tf_op jit(solution)/shard_map/sub | solution.py:24
  65.7 0.7 fusion.16
  66.8 2.4 %fusion.19 = f32[2,16,20,5136]{3,2,1,0:T(8,128)S(1)} fusion(bf16[64,5136]{0,1:T(8,128)(2,1)S(1)} %copy.18, bf16[64,5136]{0,1:T(8,128)(2,1)S(1)} %copy.17, bf16[1,16,20,128]{3,2,1,0:T(8,128)(2,1)S(1)} %get-tuple-element.23, bf16[1,16,20,128]{3,2,1,0:T(8,128)(2,1)S(1)} %get-tuple-element.22), kind=kOutput, calls=%fused_computation.24 | convolution fusion | flops 844193792 | bytes 14626816 | tf_op jit(solution)/shard_map/dfab,bi->dfai/dot_general | solution.py:51
  69.3 1.8 %fusion.2 = f32[16,5136]{1,0:T(8,128)S(1)} fusion(f32[2,16,20,5136]{3,2,1,0:T(8,128)S(1)} %fusion.19, f32[20,5136]{1,0:T(8,128)S(1)} %add.119, f32[20,5136]{1,0:T(8,128)S(1)} %copy-done.1), kind=kLoop, calls=%fused_computation.3 | loop fusion | flops 6491904 | bytes 14298624 | tf_op jit(solution)/shard_map/reduce_sum | solution.py:52
  71.4 11.5 %all_to_all.19 = f32[1,8,2,5136]{3,2,0,1:T(2,128)S(1)} all-to-all(f32[1,8,2,5136]{3,2,0,1:T(2,128)S(1)} %broadcast_select_fusion.2), channel_id=1, replica_groups=mesh['wave'=4,'lev'=8] {'lev'}, dimensions={1} | all-to-all | bytes 657408 | tf_op jit(solution)/shard_map/all_to_all | solution.py:118
  82.9 0.7 copy.31
  (49 shorter events, 3.7 us)
Async XLA Ops:
  0.0 5.3 %copy-start.10 = (s32[32]{0:T(128)S(1)}, s32[32]{0:T(128)}, u32[]{:S(2)}) copy-start(s32[32]{0:T(128)} %param.9) | copy-start | bytes 388
  0.0 8.4 %copy-start.9 = (s32[32]{0:T(128)S(1)}, s32[32]{0:T(128)}, u32[]{:S(2)}) copy-start(s32[32]{0:T(128)} %param.8) | copy-start | bytes 388
  0.0 22.8 %copy-start.8 = (s32[1280]{0:T(1024)S(1)}, s32[1280]{0:T(1024)}, u32[]{:S(2)}) copy-start(s32[1280]{0:T(1024)} %param.7) | copy-start | bytes 15364
  0.0 44.6 %all-to-all-start = ((bf16[8,40,2,2,1280]{4,3,2,1,0:T(2,128)(2,1)}), bf16[8,40,2,2,1280]{4,3,2,1,0:T(2,128)(2,1)S(1)}, u32[]{:S(2)}, u32[]{:S(2)}) async-start(bf16[8,40,2,2,1280]{4,3,2,1,0:T(2,128)(2,1)} %bitcast.81), calls=%async_computation | async-start | bytes 6553600 | tf_op jit(solution)/shard_map/all_to_all | solution.py:67
  22.8 3.9 %copy-start.5 = (f32[5,5136]{1,0:T(8,128)S(1)}, f32[5,5136]{1,0:T(8,128)}, u32[]{:S(2)}) copy-start(f32[5,5136]{1,0:T(8,128)} %get-tuple-element.26) | copy-start | bytes 308164
  22.8 3.9 %copy-start.6 = (f32[5,5136]{1,0:T(8,128)S(1)}, f32[5,5136]{1,0:T(8,128)}, u32[]{:S(2)}) copy-start(f32[5,5136]{1,0:T(8,128)} %get-tuple-element.27) | copy-start | bytes 308164
  22.8 3.9 %copy-start.7 = (f32[4,5136]{1,0:T(4,128)S(1)}, f32[4,5136]{1,0:T(4,128)}, u32[]{:S(2)}) copy-start(f32[4,5136]{1,0:T(4,128)} %get-tuple-element.29) | copy-start | bytes 246532
  23.0 4.8 %copy-start.2 = (f32[8,5136]{1,0:T(8,128)S(1)}, f32[8,5136]{1,0:T(8,128)}, u32[]{:S(2)}) copy-start(f32[8,5136]{1,0:T(8,128)} %get-tuple-element.37) | copy-start | bytes 493060
  23.0 4.8 %copy-start.3 = (f32[8,5136]{1,0:T(8,128)S(1)}, f32[8,5136]{1,0:T(8,128)}, u32[]{:S(2)}) copy-start(f32[8,5136]{1,0:T(8,128)} %get-tuple-element.34) | copy-start | bytes 493060
  23.0 4.8 %copy-start.4 = (f32[8,5136]{1,0:T(8,128)S(1)}, f32[8,5136]{1,0:T(8,128)}, u32[]{:S(2)}) copy-start(f32[8,5136]{1,0:T(8,128)} %get-tuple-element.35) | copy-start | bytes 493060
  26.7 17.9 %copy-start.11 = (s32[32]{0:T(128)S(1)}, s32[32]{0:T(128)}, u32[]{:S(2)}) copy-start(s32[32]{0:T(128)} %get-tuple-element.30) | copy-start | bytes 388
  26.7 17.9 %copy-start.12 = (s32[32]{0:T(128)S(1)}, s32[32]{0:T(128)}, u32[]{:S(2)}) copy-start(s32[32]{0:T(128)} %get-tuple-element.31) | copy-start | bytes 388
  50.5 9.3 %copy-start = (bf16[64,5136]{1,0:T(8,128)(2,1)S(1)}, bf16[64,5136]{1,0:T(8,128)(2,1)}, u32[]{:S(2)}) copy-start(bf16[64,5136]{1,0:T(8,128)(2,1)} %get-tuple-element.19) | copy-start | bytes 1972228
  53.0 11.8 %all-to-all-start.1 = ((bf16[32,2,640]{2,1,0:T(2,128)(2,1)}), bf16[32,2,640]{2,1,0:T(2,128)(2,1)S(1)}, u32[]{:S(2)}, u32[]{:S(2)}) async-start(bf16[32,2,640]{2,1,0:T(2,128)(2,1)} %reshape.481), calls=%async_computation.1 | async-start | bytes 163840 | tf_op jit(solution)/shard_map/all_to_all | solution.py:95
  66.8 2.4 %copy-start.1 = (f32[20,5136]{1,0:T(8,128)S(1)}, f32[20,5136]{1,0:T(8,128)}, u32[]{:S(2)}) copy-start(f32[20,5136]{1,0:T(8,128)} %sub.33) | copy-start | bytes 1232644

commit v18 on v16

--- a/solution.py
+++ b/solution.py
@@ -50,7 +50,7 @@
     rhs = jnp.concatenate([cosb, sinb], 0)
     part = jnp.einsum("dfab,bi->dfai", lhs, rhs, preferred_element_type=jnp.float32)
     total = jnp.sum(part[0] * cosp[None] - part[1] * sinp[None], axis=1)
-    return jnp.where(lon_idx[None, :] < points, total, jnp.zeros_like(total))
+    return total
 
 
 def on_device(spec, legendre, slot_wave, row_lons, band_rows, rows_per_dev):
@@ -117,7 +117,11 @@
     fpd = fpg // n_r
     grid = grid.reshape(rows_per_dev, n_r, fpd, lon)
     grid = lax.all_to_all(grid, "lev_r", split_axis=1, concat_axis=0, tiled=True)
-    return grid.reshape(n_r * rows_per_dev, fpd, lon)
+    grid = grid.reshape(n_r * rows_per_dev, fpd, lon)
+    group_rows = lax.dynamic_slice_in_dim(band_rows, lax.axis_index("wave") * n_r * rows_per_dev, n_r * rows_per_dev)
+    group_points = row_lons[group_rows]
+    lon_idx = jnp.arange(lon, dtype=jnp.int32)
+    return jnp.where(lon_idx[None, None, :] < group_points[:, None, None], grid, jnp.zeros_like(grid))
 
 
 def solution(mesh):

time: 83.3 us -> 84.5 us (1.014)
  blocking collectives: 10.9 us -> 0 us
  waiting for transfers between devices: 15.5 us -> 21.8 us
  starting transfers between devices: 9.3 us -> 12.7 us
  other arithmetic: 22.5 us -> 24.1 us
    all_to_all x1 -> x0, blocking collectives: 10.9 us -> none  [on_device(): lax.all_to_all(grid, 'lev_r', split_axis=1, concat_axis=0, tiled=True)]
    all_to_all x0 -> x1, waiting for transfers between devices: none -> 7.63 us  [on_device(): lax.all_to_all(grid, 'lev_r', split_axis=1, concat_axis=0, tiled=True)]
    all_to_all x0 -> x1, starting transfers between devices: none -> 3.44 us  [on_device(): lax.all_to_all(grid, 'lev_r', split_axis=1, concat_axis=0, tiled=True)]
    select_n x1 -> x2, other arithmetic: 0.16 us -> 1.69 us  [the longest x1 0.96 us: on_device(): jnp.where(lon_idx[None, None, :] < group_points[:, None, None], grid, jnp...]
    all_to_all x1, waiting for transfers between devices: 15 us -> 13.7 us  [on_device(): lax.all_to_all(spec_v, ('lev_g', 'lev_r'), split_axis=0, concat_axis=0, t...]
    another operation x0 -> x1, local copies, waits for them, and re-layouts: none -> 0.92 us  [on_device(): grid = grid.reshape(rows_per_dev, n_r, fpd, lon)]
    unnamed x27 -> x28, local copies, waits for them, and re-layouts: 2.18 us -> 1.45 us
  transfers between devices with their start and end apart: 2 -> 3, of which waited for: 2 -> 3; matrix products, arithmetic and copies ran while one was open for 33% -> 34% of each run, Pallas kernels for 0% -> 0%
where the time goes in v18:
time: 84.5 us; the launch traced here: 83.9 us
  other arithmetic  24.1 us (29%)
  waiting for transfers between devices  21.8 us (26%)
  starting transfers between devices  12.7 us (15%)
  local copies, waits for them, and re-layouts  12.3 us (15%)
  matrix products  8.83 us (10%)
  between operations  4.13 us (5%)
    all_to_all x1, waiting for transfers between devices, on_device(): lax.all_to_all(spec_v, ('lev_g', 'lev_r'), split_axis=0, concat_axis=0, t...  13.7 us
    cos x3, other arithmetic, trig_pair(): return (jnp.cos(theta), jnp.sin(theta))  9.11 us
    all_to_all x1, waiting for transfers between devices, on_device(): lax.all_to_all(grid, 'lev_r', split_axis=1, concat_axis=0, tiled=True)  7.63 us
    all_to_all x1, starting transfers between devices, on_device(): lax.all_to_all(spec_v, ('lev_g', 'lev_r'), split_axis=0, concat_axis=0, t...  5.3 us
    dot_general x1, matrix products, on_device(): jnp.einsum('lscfk,sjk->sclfj', gathered, leg2, preferred_element_type=jnp...  5.06 us
    all_to_all x1, starting transfers between devices, on_device(): lax.all_to_all(fourier, ('wave', 'lev_g', 'lev_r'), split_axis=0, concat_...  4.01 us
    select_n x1, other arithmetic, on_device(): jnp.where(even_mask, legendre, zeros)  3.7 us
    all_to_all x1, starting transfers between devices, on_device(): lax.all_to_all(grid, 'lev_r', split_axis=1, concat_axis=0, tiled=True)  3.44 us
  transfers between devices with their start and end apart: 3, of which 3 were waited for; matrix products, arithmetic and copies ran while one was open for 34% of the time, Pallas kernels for 0%

profile of v18, /device:TPU:0, one launch (start us, length us, event | category | flops | bytes accessed | tf_op | source)
XLA Modules:
  0.0 83.9 jit_solution(9334935666903959589)
XLA Ops:
  0.0 5.3 %all-to-all-start = ((bf16[8,40,2,2,1280]{4,3,2,1,0:T(2,128)(2,1)}), bf16[8,40,2,2,1280]{4,3,2,1,0:T(2,128)(2,1)S(1)}, u32[]{:S(2)}, u32[]{:S(2)}) async-start(bf16[8,40,2,2,1280]{4,3,2,1,0:T(2,128)(2,1)} %bitcast.82), calls=%async_computation | async-start | bytes 6553600 | tf_op jit(solution)/shard_map/all_to_all | solution.py:67
  11.0 2.9 %fusion.61 = (f32[8,5136]{1,0:T(8,128)S(1)}, f32[8,5136]{1,0:T(8,128)}) fusion(f32[]{:T(128)S(6)} %convert_element_type.83, pred[]{:T(512)S(6)} %lt.128, s32[]{:T(128)S(6)} %select_n.156), kind=kLoop, calls=%fused_computation.81 | loop fusion | flops 451968 | bytes 328713 | tf_op jit(solution)/shard_map/sin | solution.py:18
  13.9 3.1 %fusion.64 = (f32[8,5136]{1,0:T(8,128)}, f32[8,5136]{1,0:T(8,128)}) fusion(f32[]{:T(128)S(6)} %convert_element_type.83, pred[]{:T(512)S(6)} %lt.128, s32[]{:T(128)S(6)} %select_n.156, s32[8]{0:T(128)S(1)} %iota_multiply_fusion.2), kind=kLoop, calls=%fused_computation.84 | loop fusion | flops 451968 | bytes 328745 | tf_op jit(solution)/shard_map/cos | solution.py:18
  17.0 3.1 %fusion.60 = (f32[5,5136]{1,0:T(8,128)}, f32[5,5136]{1,0:T(8,128)}) fusion(f32[]{:T(128)S(6)} %convert_element_type.83, pred[]{:T(512)S(6)} %lt.128, s32[]{:T(128)S(6)} %select_n.156, s32[5]{0:T(128)S(1)} %iota_multiply_fusion.1), kind=kLoop, calls=%fused_computation.80 | loop fusion | flops 282480 | bytes 205469 | tf_op jit(solution)/shard_map/cos | solution.py:18
  20.0 3.0 %fusion.66 = (f32[4,5136]{1,0:T(4,128)S(1)}, f32[4,5136]{1,0:T(4,128)}) fusion(f32[]{:T(128)S(6)} %convert_element_type.83, pred[]{:T(512)S(6)} %lt.128, s32[]{:T(128)S(6)} %select_n.156, s32[4]{0:T(128)S(1)} %iota_multiply_fusion), kind=kLoop, calls=%fused_computation.86 | loop fusion | flops 225984 | bytes 164377 | tf_op jit(solution)/shard_map/cos | solution.py:18
  23.0 0.8 dynamic-slice_subtract_fusion
  23.9 3.7 %broadcast_select_fusion.1 = (bf16[40,16,1280]{2,1,0:T(8,128)(2,1)}, bf16[40,16,1280]{2,1,0:T(8,128)(2,1)}) fusion(bf16[40,16,1280]{2,1,0:T(8,128)(2,1)} %param.6, pred[40,1280]{1,0:T(8,128)(4,1)S(1)} %get-tuple-element.32, pred[40,1280]{1,0:T(8,128)(4,1)S(1)} %get-tuple-element.33), kind=kLoop, calls=%fused_computation.19 | loop fusion | flops 1638400 | bytes 5017600 | tf_op jit(solution)/shard_map/jit(_where)/select_n | solution.py:77
  28.4 1.1 %multiply_subtract_fusion = (f32[5,4,5136]{2,1,0:T(4,128)}, f32[5,4,5136]{2,1,0:T(4,128)}) fusion(f32[4,5136]{1,0:T(4,128)S(1)} %copy-done.9, f32[5,5136]{1,0:T(8,128)S(1)} %copy-done.8, f32[4,5136]{1,0:T(4,128)S(1)} %get-tuple-element.28, f32[5,5136]{1,0:T(8,128)S(1)} %copy-done.7), kind=kLoop, calls=%fused_computation.32 | loop fusion | flops 616320 | bytes 1191552 | tf_op jit(solution)/shard_map/sub | solution.py:24
  29.5 1.4 %fusion.24 = (bf16[64,5136]{1,0:T(8,128)(2,1)}, bf16[64,5136]{1,0:T(8,128)(2,1)}) fusion(f32[8,5136]{1,0:T(8,128)S(1)} %get-tuple-element.38, f32[8,5136]{1,0:T(8,128)S(1)} %copy-done.6, f32[8,5136]{1,0:T(8,128)S(1)} %copy-done.4, f32[8,5136]{1,0:T(8,128)S(1)} %copy-done.5), kind=kLoop, calls=%fused_computation.29 | loop fusion | flops 2629632 | bytes 1972224 | tf_op jit(solution)/shard_map/convert_element_type | solution.py:36
  30.9 13.7 %all-to-all-done = bf16[8,40,2,2,1280]{4,3,2,1,0:T(2,128)(2,1)S(1)} async-done(((bf16[8,40,2,2,1280]{4,3,2,1,0:T(2,128)(2,1)}), bf16[8,40,2,2,1280]{4,3,2,1,0:T(2,128)(2,1)S(1)}, u32[]{:S(2)}, u32[]{:S(2)}) %all-to-all-start) | async-done | bytes 3276832 | tf_op jit(solution)/shard_map/all_to_all | solution.py:67
  44.6 5.1 %fusion.20 = f32[40,2,8,2,32]{4,2,3,1,0:T(8,128)} fusion(bf16[8,40,2,2,1280]{4,3,2,1,0:T(2,128)(2,1)S(1)} %all-to-all-done, bf16[40,16,1280]{2,1,0:T(8,128)(2,1)} %get-tuple-element.17, bf16[40,16,1280]{2,1,0:T(8,128)(2,1)} %get-tuple-element.16), kind=kOutput, calls=%fused_computation.26 | convolution fusion | flops 111411200 | bytes 6717440 | tf_op jit(solution)/shard_map/lscfk,sjk->sclfj/dot_general | solution.py:79
  49.7 1.5 %copy.14 = f32[40,2,8,2,32]{0,4,3,2,1:T(8,128)S(1)} copy(f32[40,2,8,2,32]{4,2,3,1,0:T(8,128)} %fusion.20) | data formatting | bytes 327680 | tf_op jit(solution)/shard_map/lscfk,sjk->sclfj/transpose | solution.py:79
  51.9 1.0 %reshape.486 = bf16[32,2,640]{2,1,0:T(2,128)(2,1)} reshape(bf16[32,1,2,16,40]{4,3,2,1,0:T(8,128)(2,1)S(1)} %bitcast.84) | data formatting | bytes 163840
  52.9 4.0 %all-to-all-start.1 = ((bf16[32,2,640]{2,1,0:T(2,128)(2,1)}), bf16[32,2,640]{2,1,0:T(2,128)(2,1)S(1)}, u32[]{:S(2)}, u32[]{:S(2)}) async-start(bf16[32,2,640]{2,1,0:T(2,128)(2,1)} %reshape.486), calls=%async_computation.1 | async-start | bytes 163840 | tf_op jit(solution)/shard_map/all_to_all | solution.py:96
  57.0 1.3 %copy.17 = bf16[64,5136]{0,1:T(8,128)(2,1)S(1)} copy(bf16[64,5136]{1,0:T(8,128)(2,1)S(1)} %copy-done.2) | data formatting | bytes 1314816 | tf_op jit(solution)/shard_map/convert_element_type | solution.py:36
  58.3 1.3 %copy.18 = bf16[64,5136]{0,1:T(8,128)(2,1)S(1)} copy(bf16[64,5136]{1,0:T(8,128)(2,1)S(1)} %copy-done.1) | data formatting | bytes 1314816 | tf_op jit(solution)/shard_map/convert_element_type | solution.py:37
  59.6 1.2 %add.127 = f32[20,5136]{1,0:T(8,128)S(1)} reshape(f32[5,4,5136]{2,1,0:T(4,128)} %get-tuple-element.21) | data formatting | bytes 821760 | tf_op jit(solution)/shard_map/add | solution.py:25
  60.8 2.0 %sub.33 = f32[20,5136]{1,0:T(8,128)} reshape(f32[5,4,5136]{2,1,0:T(4,128)} %get-tuple-element.20) | data formatting | bytes 821760 | tf_op jit(solution)/shard_map/sub | solution.py:24
  66.6 2.4 %fusion.17 = f32[2,16,20,5136]{3,2,1,0:T(8,128)S(1)} fusion(bf16[64,5136]{0,1:T(8,128)(2,1)S(1)} %copy.18, bf16[64,5136]{0,1:T(8,128)(2,1)S(1)} %copy.17, bf16[1,16,20,128]{3,2,1,0:T(8,128)(2,1)S(1)} %get-tuple-element.23, bf16[1,16,20,128]{3,2,1,0:T(8,128)(2,1)S(1)} %get-tuple-element.22), kind=kOutput, calls=%fused_computation.23 | convolution fusion | flops 844193792 | bytes 14626816 | tf_op jit(solution)/shard_map/dfab,bi->dfai/dot_general | solution.py:51
  69.1 1.8 %fusion.2 = f32[16,5136]{1,0:T(8,128)S(1)} fusion(f32[2,16,20,5136]{3,2,1,0:T(8,128)S(1)} %fusion.17, f32[20,5136]{1,0:T(8,128)S(1)} %add.127, f32[20,5136]{1,0:T(8,128)S(1)} %copy-done.3), kind=kLoop, calls=%fused_computation.4 | loop fusion | flops 6491904 | bytes 14298624 | tf_op jit(solution)/shard_map/reduce_sum | solution.py:52
  70.9 0.9 %reshape_broadcast_in_dim.3 = f32[1,8,2,5136]{3,2,0,1:T(2,128)} reshape(f32[16,5136]{1,0:T(8,128)S(1)} %fusion.2) | data formatting | bytes 657408 | tf_op jit(solution)/shard_map/reshape;broadcast_in_dim | solution.py:118
  71.8 3.4 %all-to-all-start.2 = ((f32[1,8,2,5136]{3,2,0,1:T(2,128)}), f32[1,8,2,5136]{3,2,0,1:T(2,128)S(1)}, u32[]{:S(2)}, u32[]{:S(2)}) async-start(f32[1,8,2,5136]{3,2,0,1:T(2,128)} %reshape_broadcast_in_dim.3), calls=%async_computation.2 | async-start | bytes 671744 | tf_op jit(solution)/shard_map/all_to_all | solution.py:119
  75.3 7.6 %all-to-all-done.2 = f32[1,8,2,5136]{3,2,0,1:T(2,128)S(1)} async-done(((f32[1,8,2,5136]{3,2,0,1:T(2,128)}), f32[1,8,2,5136]{3,2,0,1:T(2,128)S(1)}, u32[]{:S(2)}, u32[]{:S(2)}) %all-to-all-start.2) | async-done | bytes 328736 | tf_op jit(solution)/shard_map/all_to_all | solution.py:119
  83.0 1.0 %bitcast_select_fusion = f32[8,2,5136]{2,1,0:T(2,128)} fusion(f32[1,8,2,5136]{3,2,0,1:T(2,128)S(1)} %all-to-all-done.2, pred[8,5136]{1,0:T(8,128)(4,1)S(1)} %iota_compare_fusion.2), kind=kLoop, calls=%fused_computation.33 | loop fusion | flops 82176 | bytes 698496 | tf_op jit(solution)/shard_map/jit(_where)/select_n | solution.py:124
  (53 shorter events, 7.3 us)
Async XLA Ops:
  0.0 5.3 %copy-start.12 = (s32[32]{0:T(128)S(1)}, s32[32]{0:T(128)}, u32[]{:S(2)}) copy-start(s32[32]{0:T(128)} %param.9) | copy-start | bytes 388
  0.0 8.4 %copy-start = (s32[32]{0:T(128)S(1)}, s32[32]{0:T(128)}, u32[]{:S(2)}) copy-start(s32[32]{0:T(128)} %param.8) | copy-start | bytes 388
  0.0 44.6 %all-to-all-start = ((bf16[8,40,2,2,1280]{4,3,2,1,0:T(2,128)(2,1)}), bf16[8,40,2,2,1280]{4,3,2,1,0:T(2,128)(2,1)S(1)}, u32[]{:S(2)}, u32[]{:S(2)}) async-start(bf16[8,40,2,2,1280]{4,3,2,1,0:T(2,128)(2,1)} %bitcast.82), calls=%async_computation | async-start | bytes 6553600 | tf_op jit(solution)/shard_map/all_to_all | solution.py:67
  23.8 4.6 %copy-start.7 = (f32[5,5136]{1,0:T(8,128)S(1)}, f32[5,5136]{1,0:T(8,128)}, u32[]{:S(2)}) copy-start(f32[5,5136]{1,0:T(8,128)} %get-tuple-element.26) | copy-start | bytes 308164
  23.8 4.6 %copy-start.8 = (f32[5,5136]{1,0:T(8,128)S(1)}, f32[5,5136]{1,0:T(8,128)}, u32[]{:S(2)}) copy-start(f32[5,5136]{1,0:T(8,128)} %get-tuple-element.27) | copy-start | bytes 308164
  23.8 4.6 %copy-start.9 = (f32[4,5136]{1,0:T(4,128)S(1)}, f32[4,5136]{1,0:T(4,128)}, u32[]{:S(2)}) copy-start(f32[4,5136]{1,0:T(4,128)} %get-tuple-element.29) | copy-start | bytes 246532
  23.9 5.6 %copy-start.4 = (f32[8,5136]{1,0:T(8,128)S(1)}, f32[8,5136]{1,0:T(8,128)}, u32[]{:S(2)}) copy-start(f32[8,5136]{1,0:T(8,128)} %get-tuple-element.39) | copy-start | bytes 493060
  23.9 5.6 %copy-start.5 = (f32[8,5136]{1,0:T(8,128)S(1)}, f32[8,5136]{1,0:T(8,128)}, u32[]{:S(2)}) copy-start(f32[8,5136]{1,0:T(8,128)} %get-tuple-element.34) | copy-start | bytes 493060
  23.9 5.5 %copy-start.6 = (f32[8,5136]{1,0:T(8,128)S(1)}, f32[8,5136]{1,0:T(8,128)}, u32[]{:S(2)}) copy-start(f32[8,5136]{1,0:T(8,128)} %get-tuple-element.35) | copy-start | bytes 493060
  44.6 6.6 %copy-start.10 = (f32[32]{0:T(128)S(1)}, f32[32]{0:T(128)}, u32[]{:S(2)}) copy-start(f32[32]{0:T(128)} %compare_select_fusion.1) | copy-start | bytes 388
  49.7 7.3 %copy-start.2 = (bf16[64,5136]{1,0:T(8,128)(2,1)S(1)}, bf16[64,5136]{1,0:T(8,128)(2,1)}, u32[]{:S(2)}) copy-start(bf16[64,5136]{1,0:T(8,128)(2,1)} %get-tuple-element.18) | copy-start | bytes 1972228
  49.7 8.6 %copy-start.1 = (bf16[64,5136]{1,0:T(8,128)(2,1)S(1)}, bf16[64,5136]{1,0:T(8,128)(2,1)}, u32[]{:S(2)}) copy-start(bf16[64,5136]{1,0:T(8,128)(2,1)} %get-tuple-element.19) | copy-start | bytes 1972228
  52.9 11.6 %all-to-all-start.1 = ((bf16[32,2,640]{2,1,0:T(2,128)(2,1)}), bf16[32,2,640]{2,1,0:T(2,128)(2,1)S(1)}, u32[]{:S(2)}, u32[]{:S(2)}) async-start(bf16[32,2,640]{2,1,0:T(2,128)(2,1)} %reshape.486), calls=%async_computation.1 | async-start | bytes 163840 | tf_op jit(solution)/shard_map/all_to_all | solution.py:96
  58.3 7.1 %copy-start.11 = (s32[1280]{0:T(1024)S(1)}, s32[1280]{0:T(1024)}, u32[]{:S(2)}) copy-start(s32[1280]{0:T(1024)} %param.7) | copy-start | bytes 15364
  66.6 2.4 %copy-start.3 = (f32[20,5136]{1,0:T(8,128)S(1)}, f32[20,5136]{1,0:T(8,128)}, u32[]{:S(2)}) copy-start(f32[20,5136]{1,0:T(8,128)} %sub.33) | copy-start | bytes 1232644
  71.8 11.2 %all-to-all-start.2 = ((f32[1,8,2,5136]{3,2,0,1:T(2,128)}), f32[1,8,2,5136]{3,2,0,1:T(2,128)S(1)}, u32[]{:S(2)}, u32[]{:S(2)}) async-start(f32[1,8,2,5136]{3,2,0,1:T(2,128)} %reshape_broadcast_in_dim.3), calls=%async_computation.2 | async-start | bytes 671744 | tf_op jit(solution)/shard_map/all_to_all | solution.py:119
